TPU v7x, 32 devices: a whole 2x2x4 slice. The times are simulated.
32 devices in a mesh: groups: 2 (over y), lon: 4 (over z), tm: 2 (over x), branch: 2 (over core).
Axes of the slice: x: 2, y: 2, z: 4, core: 2. Of those that a mesh axis runs over, the one named last changes fastest.
Arguments:
- queries: bfloat16 [4, 2, 32, 32, 1536], P(('groups', 'branch'), 'tm', None, 'lon'), parts along dimension 0
- keys: bfloat16 [4, 2, 32, 32, 1536], P(('groups', 'branch'), 'tm', None, 'lon'), parts along dimension 0
- values: bfloat16 [4, 2, 32, 32, 1536], P(('groups', 'branch'), 'tm', None, 'lon'), parts along dimension 0, may hold values from -6 to 6
- window_map: int32 [32, 15], P(('groups', 'lon')), parts along dimension 0, may hold values from 0 to 1, as said below
- frame_valid: int32 [4, 32], P('groups', 'lon'), parts along dimension 0, may hold values 0 or 1
Outputs:
- guided: bfloat16 [4, 32, 32, 1536], P(('groups', 'tm'), None, 'lon', 'branch'), parts along dimension 0
There are 2 independent parts, one for each index of `groups`. A program takes and returns all parts, laid end to end along the dimension named above; each array names one. Nothing has to cross between parts.
Inputs may be any that keep to these rules, and one draw needn't show every extreme that they name: `window_map`: entries are 0 or 1; entry 7 of every row, the query block itself, is 1.
All inputs are finite; a program needn't handle non-finite values. No bound on the sum of `frame_valid` on one device may be relied on, other than what follows from the above.
Results may differ from a plain program's by a relative error of at most 0.008.
Values may be sent and summed in bfloat16 or wider, within the bound.
No kernel may reach another device: no remote copies, remote signals or barrier semaphores. Data moves between devices by JAX's collectives and lax.ppermute only.
A program may use at most 64 MiB of HBM per device.

v0:
```python
import jax
import jax.numpy as jnp
from jax import lax
from jax.sharding import PartitionSpec as P

DH = 128
BLK = 2
REACH = 7
WIN = 15


guidance_weight = 5.0
masked_score = -1e30


def shifted(value, axis, by):
    count = lax.axis_size(axis)
    return lax.ppermute(value, axis, [(i, (i + by) % count) for i in range(count)])


def from_partner(value, axis, bit):
    return lax.ppermute(value, axis, [(i, i ^ 1 << bit) for i in range(lax.axis_size(axis))])


def attend_frames(query_rows, key_rows, value_rows, allowed, scale):
    scores = (
        jnp.einsum("fthd,gthd->thfg", query_rows, key_rows, preferred_element_type=jnp.float32)
        * scale
    )
    limited = jnp.where(allowed[:, None], scores, masked_score)
    maxima = jnp.max(limited, axis=-1, keepdims=True)
    weights = jnp.exp(limited - maxima)
    totals = jnp.sum(weights, axis=-1)
    result = jnp.einsum(
        "thfg,gthd->fthd",
        weights.astype(jnp.bfloat16),
        value_rows,
        preferred_element_type=jnp.float32,
    )
    return (result / jnp.transpose(totals, (2, 0, 1))[..., None]).astype(jnp.bfloat16)


def local(queries, keys, values, window_map, frame_valid):
    own_q = queries[0]
    own_k = keys[0]
    own_v = values[0]
    frames, lat_rows, columns, model_width = own_q.shape
    head_count = model_width // DH
    scale = DH ** (-0.5)
    reach_cols = REACH * BLK
    outer_cols = reach_cols - columns
    key_value = jnp.stack([own_k, own_v])
    received = {}
    for step_by in (1, -1, 2, -2):
        if step_by == 2:
            piece = key_value[:, :, :, columns - outer_cols :, :]
        elif step_by == -2:
            piece = key_value[:, :, :, :outer_cols, :]
        else:
            piece = key_value
        received[step_by] = shifted(piece, "lon", step_by)
    extended = jnp.concatenate(
        [received[2], received[1], key_value, received[-1], received[-2]], axis=3
    )
    ext_count = columns + 2 * reach_cols
    column_ids = jnp.arange(columns, dtype=jnp.int32)
    ext_ids = jnp.arange(ext_count, dtype=jnp.int32)
    slots = ext_ids[None, :] // BLK - column_ids[:, None] // BLK
    per_column_map = jnp.repeat(window_map, BLK, axis=0)
    picks = slots[:, :, None] == jnp.arange(WIN, dtype=jnp.int32)[None, None, :]
    active = jnp.any(picks & (per_column_map[:, None, :] > 0), axis=-1)
    allowed_keys = jnp.broadcast_to(
        active[None, :, None, :], (lat_rows, columns, lat_rows, ext_count)
    )
    allowed_keys = allowed_keys.reshape(lat_rows * columns, lat_rows * ext_count)
    query_flat = own_q.reshape(frames, lat_rows * columns, model_width)
    key_flat = extended[0].reshape(frames, lat_rows * ext_count, model_width)
    value_flat = extended[1].reshape(frames, lat_rows * ext_count, model_width)

    def per_head(head_index):
        start = head_index * DH
        query_head = lax.dynamic_slice_in_dim(query_flat, start, DH, 2)
        key_head = lax.dynamic_slice_in_dim(key_flat, start, DH, 2)
        value_head = lax.dynamic_slice_in_dim(value_flat, start, DH, 2)
        scores = (
            jnp.einsum("fqd,fkd->fqk", query_head, key_head, preferred_element_type=jnp.float32)
            * scale
        )
        limited = jnp.where(allowed_keys[None], scores, masked_score)
        maxima = jnp.max(limited, axis=-1, keepdims=True)
        weights = jnp.exp(limited - maxima)
        totals = jnp.sum(weights, axis=-1)
        result = jnp.einsum(
            "fqk,fkd->fqd",
            weights.astype(jnp.bfloat16),
            value_head,
            preferred_element_type=jnp.float32,
        )
        return result / totals[..., None]

    per_heads = lax.map(per_head, jnp.arange(head_count, dtype=jnp.int32))
    spatial = jnp.transpose(per_heads, (1, 2, 0, 3)).reshape(
        frames, lat_rows * columns, model_width
    )
    token_count = lat_rows * columns
    valid_tokens = jnp.transpose(jnp.tile(frame_valid, (1, lat_rows)))
    query_rows = own_q.reshape(frames, token_count, head_count, DH)
    key_rows = own_k.reshape(frames, token_count, head_count, DH)
    value_rows = own_v.reshape(frames, token_count, head_count, DH)
    moved_q, moved_k, moved_v = (
        lax.all_to_all(query_rows, "tm", split_axis=2, concat_axis=0, tiled=True),
        lax.all_to_all(key_rows, "tm", split_axis=2, concat_axis=0, tiled=True),
        lax.all_to_all(value_rows, "tm", split_axis=2, concat_axis=0, tiled=True),
    )
    total_frames = moved_q.shape[0]
    frame_ids = jnp.arange(total_frames, dtype=jnp.int32)
    same_frame = frame_ids[:, None] == frame_ids[None, :]
    allowed = (valid_tokens[:, None, :] > 0) | same_frame[None]
    result = attend_frames(moved_q, moved_k, moved_v, allowed, scale)
    temporal = lax.all_to_all(result, "tm", split_axis=0, concat_axis=2, tiled=True)
    temporal = temporal.reshape(frames, token_count, model_width).astype(jnp.float32)
    mixed = (
        (spatial + temporal).astype(jnp.bfloat16).reshape(frames, lat_rows, columns, model_width)
    )
    half_width = model_width // 2
    branch_index = lax.axis_index("branch")
    partner = from_partner(mixed, "branch", 0)
    is_conditional = branch_index == 0
    conditional = jnp.where(is_conditional, mixed, partner)
    unconditional = jnp.where(is_conditional, partner, mixed)
    conditional = lax.dynamic_slice_in_dim(conditional, branch_index * half_width, half_width, 3)
    unconditional = lax.dynamic_slice_in_dim(
        unconditional, branch_index * half_width, half_width, 3
    )
    conditional = conditional.astype(jnp.float32)
    unconditional = unconditional.astype(jnp.float32)
    return (unconditional + guidance_weight * (conditional - unconditional)).astype(jnp.bfloat16)


def solution(mesh):
    in_specs = (
        P(("groups", "branch"), "tm", None, "lon", None),
        P(("groups", "branch"), "tm", None, "lon", None),
        P(("groups", "branch"), "tm", None, "lon", None),
        P(("groups", "lon"), None),
        P("groups", "lon"),
    )
    out_specs = P(("groups", "tm"), None, "lon", "branch")
    return jax.shard_map(local, mesh=mesh, in_specs=in_specs, out_specs=out_specs, check_vma=False)
```

profile of v0, /device:TPU:0, one launch (start us, length us, event | category | flops | bytes accessed | tf_op | source)
XLA Modules:
  0.0 312.3 jit_solution(5808014139879188930)
XLA Ops:
  0.0 2.3 copy_dynamic-update-slice_fusion.3
  3.5 3.0 collective-permute-start.1
  6.5 2.0 collective-permute-start.2
  8.5 3.3 %fusion.32 = (bf16[2,1,32,6,1536]{4,2,3,1,0:T(8,128)(2,1)}, bf16[2,1,32,6,1536]{4,2,3,1,0:T(8,128)(2,1)}) fusion(bf16[2,1,32,8,1536]{4,2,3,1,0:T(8,128)(2,1)} %copy_dynamic-update-slice_fusion.1), kind=kLoop, calls=%fused_computation.64 | loop fusion | bytes 4718592 | tf_op jit(solution)/shard_map/slice | solution.py:58
  12.8 1.9 collective-permute-start.3
  16.4 4.3 %all-to-all-start = ((bf16[1,256,12,128]{3,1,0,2:T(8,128)(2,1)}), bf16[1,256,12,128]{3,1,0,2:T(8,128)(2,1)}, u32[]{:S(2)}, u32[]{:S(2)}) async-start(bf16[1,256,12,128]{3,1,0,2:T(8,128)(2,1)} %copy.103), calls=%async_computation | async-start | bytes 1572864 | tf_op jit(solution)/shard_map/all_to_all | solution.py:111
  20.7 1.5 reshape_squeeze.22
  22.8 2.3 copy.105
  26.3 4.7 %all-to-all-done = bf16[1,256,12,128]{3,1,0,2:T(8,128)(2,1)} async-done(((bf16[1,256,12,128]{3,1,0,2:T(8,128)(2,1)}), bf16[1,256,12,128]{3,1,0,2:T(8,128)(2,1)}, u32[]{:S(2)}, u32[]{:S(2)}) %all-to-all-start) | async-done | bytes 786464 | tf_op jit(solution)/shard_map/all_to_all | solution.py:111
  31.0 3.5 %all-to-all-start.1 = ((bf16[1,256,12,128]{3,1,0,2:T(8,128)(2,1)}), bf16[1,256,12,128]{3,1,0,2:T(8,128)(2,1)S(1)}, u32[]{:S(2)}, u32[]{:S(2)}) async-start(bf16[1,256,12,128]{3,1,0,2:T(8,128)(2,1)} %copy.105), calls=%async_computation.1 | async-start | bytes 1572864 | tf_op jit(solution)/shard_map/all_to_all | solution.py:112
  34.7 9.2 %all-to-all-done.1 = bf16[1,256,12,128]{3,1,0,2:T(8,128)(2,1)S(1)} async-done(((bf16[1,256,12,128]{3,1,0,2:T(8,128)(2,1)}), bf16[1,256,12,128]{3,1,0,2:T(8,128)(2,1)S(1)}, u32[]{:S(2)}, u32[]{:S(2)}) %all-to-all-start.1) | async-done | bytes 786464 | tf_op jit(solution)/shard_map/all_to_all | solution.py:112
  43.9 4.3 %all-to-all-start.2 = ((bf16[1,256,12,128]{3,1,0,2:T(8,128)(2,1)}), bf16[1,256,12,128]{3,1,0,2:T(8,128)(2,1)}, u32[]{:S(2)}, u32[]{:S(2)}) async-start(bf16[1,256,12,128]{3,1,0,2:T(8,128)(2,1)} %copy.108), calls=%async_computation.2 | async-start | bytes 1572864 | tf_op jit(solution)/shard_map/all_to_all | solution.py:113
  48.2 3.1 %fusion.23 = f32[256,6,2,2]{2,3,1,0:T(2,128)S(1)} fusion(bf16[1,256,2,6,128]{4,1,3,2,0:T(8,128)(2,1)} %bitcast.3, bf16[1,256,2,6,128]{4,1,3,2,0:T(8,128)(2,1)} %bitcast.70), kind=kOutput, calls=%fused_computation.32 | convolution fusion | flops 1572864 | bytes 1597440 | tf_op jit(solution)/shard_map/fthd,gthd->thfg/dot_general | solution.py:27
  53.2 3.6 %all-to-all-done.2 = bf16[1,256,12,128]{3,1,0,2:T(8,128)(2,1)} async-done(((bf16[1,256,12,128]{3,1,0,2:T(8,128)(2,1)}), bf16[1,256,12,128]{3,1,0,2:T(8,128)(2,1)}, u32[]{:S(2)}, u32[]{:S(2)}) %all-to-all-start.2) | async-done | bytes 786464 | tf_op jit(solution)/shard_map/all_to_all | solution.py:113
  56.8 2.9 fusion.24
  59.7 1.4 fusion.18
  61.0 3.7 %all-to-all-start.3 = ((bf16[2,256,6,128]{3,1,2,0:T(8,128)(2,1)}), bf16[2,256,6,128]{3,1,2,0:T(8,128)(2,1)S(1)}, u32[]{:S(2)}, u32[]{:S(2)}) async-start(bf16[2,256,6,128]{3,1,2,0:T(8,128)(2,1)} %fusion.18), calls=%async_computation.3 | async-start | bytes 1572864 | tf_op jit(solution)/shard_map/all_to_all | solution.py:120
  65.1 7.5 %all-to-all-done.3 = bf16[2,256,6,128]{3,1,2,0:T(8,128)(2,1)S(1)} async-done(((bf16[2,256,6,128]{3,1,2,0:T(8,128)(2,1)}), bf16[2,256,6,128]{3,1,2,0:T(8,128)(2,1)S(1)}, u32[]{:S(2)}, u32[]{:S(2)}) %all-to-all-start.3) | async-done | bytes 786464 | tf_op jit(solution)/shard_map/all_to_all | solution.py:120
  73.6 1.5 reshape.208
  75.2 77.7 %collective-permute-done = bf16[2,1,32,6,1536]{4,2,3,1,0:T(8,128)(2,1)} collective-permute-done((bf16[2,1,32,6,1536]{4,2,3,1,0:T(8,128)(2,1)}, bf16[2,1,32,6,1536]{4,2,3,1,0:T(8,128)(2,1)}, u32[]{:S(2)}, u32[]{:S(2)}) %collective-permute-start) | collective-permute-done | bytes 1179680 | tf_op jit(solution)/shard_map/ppermute | solution.py:18
  152.9 1.4 constant_dynamic-update-slice_fusion.3
  154.3 1.6 constant_dynamic-update-slice_fusion.2
  156.4 1.5 constant_dynamic-update-slice_fusion.1
  157.9 20.1 %collective-permute-done.3 = bf16[2,1,32,6,1536]{4,2,3,1,0:T(8,128)(2,1)} collective-permute-done((bf16[2,1,32,6,1536]{4,2,3,1,0:T(8,128)(2,1)}, bf16[2,1,32,6,1536]{4,2,3,1,0:T(8,128)(2,1)}, u32[]{:S(2)}, u32[]{:S(2)}) %collective-permute-start.3) | collective-permute-done | bytes 1179680 | tf_op jit(solution)/shard_map/ppermute | solution.py:18
  178.0 1.4 constant_dynamic-update-slice_fusion
  180.3 3.8 %copy.99 = bf16[1,1,32,36,1536]{4,3,2,1,0:T(8,128)(2,1)} copy(bf16[1,1,32,36,1536]{4,2,3,1,0:T(8,128)(2,1)S(1)} %get-tuple-element.77) | data formatting | bytes 7077888 | tf_op jit(solution)/shard_map/slice | solution.py:77
  184.1 5.7 %reshape_squeeze.19 = bf16[1,1152,1536]{2,1,0:T(8,128)(2,1)} reshape(bf16[1,1,32,36,1536]{4,3,2,1,0:T(8,128)(2,1)} %copy.99) | data formatting | bytes 7077888 | tf_op jit(solution)/shard_map/reshape;squeeze | solution.py:77
  189.7 3.8 %copy.100 = bf16[1,1,32,36,1536]{4,3,2,1,0:T(8,128)(2,1)} copy(bf16[1,1,32,36,1536]{4,2,3,1,0:T(8,128)(2,1)S(1)} %get-tuple-element.76) | data formatting | bytes 7077888 | tf_op jit(solution)/shard_map/slice | solution.py:78
  193.6 5.8 %reshape_squeeze.20 = bf16[1,1152,1536]{2,1,0:T(8,128)(2,1)} reshape(bf16[1,1,32,36,1536]{4,3,2,1,0:T(8,128)(2,1)} %copy.100) | data formatting | bytes 7077888 | tf_op jit(solution)/shard_map/reshape;squeeze | solution.py:78
  199.3 102.7 %while.11 = (s32[]{:T(128)}, f32[12,1,256,128]{3,2,1,0:T(8,128)S(1)}, s32[12]{0:T(128)S(1)}, bf16[1,256,1536]{2,1,0:T(8,128)(2,1)}, bf16[1,1152,1536]{2,1,0:T(8,...) while((s32[]{:T(128)}, ...), condition=%wide.region_4.5_spmd.clone, body=%wide.region_1.4_spmd.clone.sunk | while | flops 153091584 | bytes 5512139 | solution.py:101
  201.1 3.7 %broadcast_in_dim_reshape.6 = pred[256,1152]{1,0:T(32,128)(4,1)S(1)} reshape(pred[32,8,32,36]{3,2,1,0:T(32,128)(4,1)S(1)} %broadcast_in_dim.70) | data formatting | bytes 589824 | tf_op jit(solution)/shard_map/while/body/eval_jaxpr/broadcast_in_dim;reshape | solution.py:89
  204.7 1.5 fusion.42
  206.5 1.4 fusion.44
  209.6 3.7 %broadcast_in_dim_reshape.6 = pred[256,1152]{1,0:T(32,128)(4,1)S(1)} reshape(pred[32,8,32,36]{3,2,1,0:T(32,128)(4,1)S(1)} %broadcast_in_dim.70) | data formatting | bytes 589824 | tf_op jit(solution)/shard_map/while/body/eval_jaxpr/broadcast_in_dim;reshape | solution.py:89
  213.3 1.5 fusion.42
  218.2 3.7 %broadcast_in_dim_reshape.6 = pred[256,1152]{1,0:T(32,128)(4,1)S(1)} reshape(pred[32,8,32,36]{3,2,1,0:T(32,128)(4,1)S(1)} %broadcast_in_dim.70) | data formatting | bytes 589824 | tf_op jit(solution)/shard_map/while/body/eval_jaxpr/broadcast_in_dim;reshape | solution.py:89
  221.8 1.5 fusion.42
  223.6 1.4 fusion.44
  226.7 3.7 %broadcast_in_dim_reshape.6 = pred[256,1152]{1,0:T(32,128)(4,1)S(1)} reshape(pred[32,8,32,36]{3,2,1,0:T(32,128)(4,1)S(1)} %broadcast_in_dim.70) | data formatting | bytes 589824 | tf_op jit(solution)/shard_map/while/body/eval_jaxpr/broadcast_in_dim;reshape | solution.py:89
  230.4 1.5 fusion.42
  235.3 3.7 %broadcast_in_dim_reshape.6 = pred[256,1152]{1,0:T(32,128)(4,1)S(1)} reshape(pred[32,8,32,36]{3,2,1,0:T(32,128)(4,1)S(1)} %broadcast_in_dim.70) | data formatting | bytes 589824 | tf_op jit(solution)/shard_map/while/body/eval_jaxpr/broadcast_in_dim;reshape | solution.py:89
  239.0 1.5 fusion.42
  240.7 1.4 fusion.44
  243.9 3.7 %broadcast_in_dim_reshape.6 = pred[256,1152]{1,0:T(32,128)(4,1)S(1)} reshape(pred[32,8,32,36]{3,2,1,0:T(32,128)(4,1)S(1)} %broadcast_in_dim.70) | data formatting | bytes 589824 | tf_op jit(solution)/shard_map/while/body/eval_jaxpr/broadcast_in_dim;reshape | solution.py:89
  247.5 1.5 fusion.42
  252.4 3.7 %broadcast_in_dim_reshape.6 = pred[256,1152]{1,0:T(32,128)(4,1)S(1)} reshape(pred[32,8,32,36]{3,2,1,0:T(32,128)(4,1)S(1)} %broadcast_in_dim.70) | data formatting | bytes 589824 | tf_op jit(solution)/shard_map/while/body/eval_jaxpr/broadcast_in_dim;reshape | solution.py:89
  256.1 1.5 fusion.42
  257.9 1.4 fusion.44
  261.0 3.7 %broadcast_in_dim_reshape.6 = pred[256,1152]{1,0:T(32,128)(4,1)S(1)} reshape(pred[32,8,32,36]{3,2,1,0:T(32,128)(4,1)S(1)} %broadcast_in_dim.70) | data formatting | bytes 589824 | tf_op jit(solution)/shard_map/while/body/eval_jaxpr/broadcast_in_dim;reshape | solution.py:89
  264.6 1.5 fusion.42
  269.5 3.7 %broadcast_in_dim_reshape.6 = pred[256,1152]{1,0:T(32,128)(4,1)S(1)} reshape(pred[32,8,32,36]{3,2,1,0:T(32,128)(4,1)S(1)} %broadcast_in_dim.70) | data formatting | bytes 589824 | tf_op jit(solution)/shard_map/while/body/eval_jaxpr/broadcast_in_dim;reshape | solution.py:89
  273.2 1.5 fusion.42
  275.0 1.4 fusion.44
  278.1 3.7 %broadcast_in_dim_reshape.6 = pred[256,1152]{1,0:T(32,128)(4,1)S(1)} reshape(pred[32,8,32,36]{3,2,1,0:T(32,128)(4,1)S(1)} %broadcast_in_dim.70) | data formatting | bytes 589824 | tf_op jit(solution)/shard_map/while/body/eval_jaxpr/broadcast_in_dim;reshape | solution.py:89
  281.7 1.5 fusion.42
  286.6 3.7 %broadcast_in_dim_reshape.6 = pred[256,1152]{1,0:T(32,128)(4,1)S(1)} reshape(pred[32,8,32,36]{3,2,1,0:T(32,128)(4,1)S(1)} %broadcast_in_dim.70) | data formatting | bytes 589824 | tf_op jit(solution)/shard_map/while/body/eval_jaxpr/broadcast_in_dim;reshape | solution.py:89
  290.3 1.5 fusion.42
  292.1 1.4 fusion.44
  295.2 3.7 %broadcast_in_dim_reshape.6 = pred[256,1152]{1,0:T(32,128)(4,1)S(1)} reshape(pred[32,8,32,36]{3,2,1,0:T(32,128)(4,1)S(1)} %broadcast_in_dim.70) | data formatting | bytes 589824 | tf_op jit(solution)/shard_map/while/body/eval_jaxpr/broadcast_in_dim;reshape | solution.py:89
  298.8 1.5 fusion.42
  303.2 2.4 copy.102
  305.5 1.4 reshape.207
  306.9 2.1 add_convert_fusion
  309.1 2.3 collective-permute-done.4
  (94 shorter events, 37.3 us)
Async XLA Ops:
  0.0 2.3 copy-start.1
  3.5 11.3 %copy-start.3 = (bf16[1,1,32,8,1536]{4,3,2,1,0:T(8,128)(2,1)S(1)}, bf16[1,1,32,8,1536]{4,3,2,1,0:T(8,128)(2,1)}, u32[]{:S(2)}) copy-start(bf16[1,1,32,8,1536]{4,3,2,1,0:T(8,128)(2,1)} %param.7) | copy-start | bytes 2359300
  3.5 150.8 %collective-permute-start.1 = (bf16[2,1,32,8,1536]{4,2,3,1,0:T(8,128)(2,1)}, bf16[2,1,32,8,1536]{4,2,3,1,0:T(8,128)(2,1)}, u32[]{:S(2)}, u32[]{:S(2)}) collective-permute-start(bf16[2,1,32,8,1536]{4,2,3,1,0:T(8,128)(2,1)} %copy_dynamic-update-slice_fusion.1), channel_id=1, source_target_pairs={{0,4},{4,8},{8,12},{12,0},{1,5},{5,9},{9,13},{13,1},{2,6},{6,10},{... | collective-permute-start | bytes 4718600 | tf_op jit(solution)/shard_map/ppermute | solution.py:18
  6.5 149.9 %collective-permute-start.2 = (bf16[2,1,32,8,1536]{4,2,3,1,0:T(8,128)(2,1)}, bf16[2,1,32,8,1536]{4,2,3,1,0:T(8,128)(2,1)}, u32[]{:S(2)}, u32[]{:S(2)}) collective-permute-start(bf16[2,1,32,8,1536]{4,2,3,1,0:T(8,128)(2,1)} %copy_dynamic-update-slice_fusion.1), channel_id=1, source_target_pairs={{0,12},{4,0},{8,4},{12,8},{1,13},{5,1},{9,5},{13,9},{2,14},{6,2},{... | collective-permute-start | bytes 4718600 | tf_op jit(solution)/shard_map/ppermute | solution.py:18
  11.8 141.0 %collective-permute-start = (bf16[2,1,32,6,1536]{4,2,3,1,0:T(8,128)(2,1)}, bf16[2,1,32,6,1536]{4,2,3,1,0:T(8,128)(2,1)}, u32[]{:S(2)}, u32[]{:S(2)}) collective-permute-start(bf16[2,1,32,6,1536]{4,2,3,1,0:T(8,128)(2,1)} %get-tuple-element.79), channel_id=1, source_target_pairs={{0,8},{4,12},{8,0},{12,4},{1,9},{5,13},{9,1},{13,5},{2,10},{6,14},... | collective-permute-start | bytes 3538952 | tf_op jit(solution)/shard_map/ppermute | solution.py:18
  12.8 165.2 %collective-permute-start.3 = (bf16[2,1,32,6,1536]{4,2,3,1,0:T(8,128)(2,1)}, bf16[2,1,32,6,1536]{4,2,3,1,0:T(8,128)(2,1)}, u32[]{:S(2)}, u32[]{:S(2)}) collective-permute-start(bf16[2,1,32,6,1536]{4,2,3,1,0:T(8,128)(2,1)} %get-tuple-element.78), channel_id=1, source_target_pairs={{0,8},{4,12},{8,0},{12,4},{1,9},{5,13},{9,1},{13,5},{2,10},{6,14},... | collective-permute-start | bytes 3538952 | tf_op jit(solution)/shard_map/ppermute | solution.py:18
  15.3 5.4 %copy-start = (bf16[1,1,32,8,1536]{4,3,2,1,0:T(8,128)(2,1)S(1)}, bf16[1,1,32,8,1536]{4,3,2,1,0:T(8,128)(2,1)}, u32[]{:S(2)}) copy-start(bf16[1,1,32,8,1536]{4,3,2,1,0:T(8,128)(2,1)} %param.8) | copy-start | bytes 2359300
  16.4 14.6 %all-to-all-start = ((bf16[1,256,12,128]{3,1,0,2:T(8,128)(2,1)}), bf16[1,256,12,128]{3,1,0,2:T(8,128)(2,1)}, u32[]{:S(2)}, u32[]{:S(2)}) async-start(bf16[1,256,12,128]{3,1,0,2:T(8,128)(2,1)} %copy.103), calls=%async_computation | async-start | bytes 1572864 | tf_op jit(solution)/shard_map/all_to_all | solution.py:111
  22.2 2.9 copy-start.8
  25.2 9.4 %copy-start.7 = (s32[4,15]{1,0:T(4,128)S(1)}, s32[4,15]{1,0:T(4,128)}, u32[]{:S(2)}) copy-start(s32[4,15]{1,0:T(4,128)} %param.10) | copy-start | bytes 724
  31.0 12.8 %all-to-all-start.1 = ((bf16[1,256,12,128]{3,1,0,2:T(8,128)(2,1)}), bf16[1,256,12,128]{3,1,0,2:T(8,128)(2,1)S(1)}, u32[]{:S(2)}, u32[]{:S(2)}) async-start(bf16[1,256,12,128]{3,1,0,2:T(8,128)(2,1)} %copy.105), calls=%async_computation.1 | async-start | bytes 1572864 | tf_op jit(solution)/shard_map/all_to_all | solution.py:112
  43.9 4.3 %copy-start.6 = (bf16[1,256,12,128]{3,1,0,2:T(8,128)(2,1)}, bf16[1,256,12,128]{3,1,0,2:T(8,128)(2,1)S(1)}, u32[]{:S(2)}) copy-start(bf16[1,256,12,128]{3,1,0,2:T(8,128)(2,1)S(1)} %all-to-all-done.1) | copy-start | bytes 2359300
  43.9 12.9 %all-to-all-start.2 = ((bf16[1,256,12,128]{3,1,0,2:T(8,128)(2,1)}), bf16[1,256,12,128]{3,1,0,2:T(8,128)(2,1)}, u32[]{:S(2)}, u32[]{:S(2)}) async-start(bf16[1,256,12,128]{3,1,0,2:T(8,128)(2,1)} %copy.108), calls=%async_computation.2 | async-start | bytes 1572864 | tf_op jit(solution)/shard_map/all_to_all | solution.py:113
  61.0 11.5 %all-to-all-start.3 = ((bf16[2,256,6,128]{3,1,2,0:T(8,128)(2,1)}), bf16[2,256,6,128]{3,1,2,0:T(8,128)(2,1)S(1)}, u32[]{:S(2)}, u32[]{:S(2)}) async-start(bf16[2,256,6,128]{3,1,2,0:T(8,128)(2,1)} %fusion.18), calls=%async_computation.3 | async-start | bytes 1572864 | tf_op jit(solution)/shard_map/all_to_all | solution.py:120
  154.2 1.9 copy-start.2
  193.6 5.8 %copy-start.4 = (f32[12,1,256,128]{3,2,1,0:T(8,128)S(1)}, f32[12,1,256,128]{3,2,1,0:T(8,128)}, u32[]{:S(2)}) copy-start(f32[12,1,256,128]{3,2,1,0:T(8,128)} %custom-call.2) | copy-start | bytes 4718596
  302.0 1.2 copy-start.5
  309.0 2.4 collective-permute-start.4
where the time goes:
time: 314 us; the launch traced here: 312 us
  waiting for transfers between devices  125 us (40%)
  local copies, waits for them, and re-layouts  106 us (34%)
  matrix products  39.8 us (13%)
  starting transfers between devices  23.9 us (8%)
  other arithmetic  8.82 us (3%)
  loops' own time  8.19 us (3%)
    ppermute x4, waiting for transfers between devices, shifted(): lax.ppermute(value, axis, [(i, (i + by) % count) for i in range(count)])  97.8 us
    another operation x12, local copies, waits for them, and re-layouts, per_head(): limited = jnp.where(allowed_keys[None], scores, masked_score)  43.9 us
    dot_general x12, matrix products, per_head(): jnp.einsum('fqd,fkd->fqk', query_head, key_head, preferred_element_type=j...  17.5 us
    dot_general x12, matrix products, per_head(): jnp.einsum('fqk,fkd->fqd', weights.astype(jnp.bfloat16), value_head, pref...  16.3 us
    all_to_all x1, waiting for transfers between devices, local(): lax.all_to_all(key_rows, 'tm', split_axis=2, concat_axis=0, tiled=True)  9.18 us
    unnamed x24, local copies, waits for them, and re-layouts  8.51 us
    another operation x1, loops' own time, local(): per_heads = lax.map(per_head, jnp.arange(head_count, dtype=jnp.int32))  8.19 us
    ppermute x4, starting transfers between devices, shifted(): lax.ppermute(value, axis, [(i, (i + by) % count) for i in range(count)])  7.98 us
  transfers between devices with their start and end apart: 9, of which 7 were waited for; matrix products, arithmetic and copies ran while one was open for 9% of the time, Pallas kernels for 0%

commit v1 on v0

v1 whole, which is shorter than its diff:
```python
import functools

import jax
import jax.numpy as jnp
from jax import lax
from jax.experimental import pallas as pl
from jax.sharding import PartitionSpec as P

DH = 128
BLK = 2
REACH = 7
WIN = 15


guidance_weight = 5.0
masked_score = -1e30


def shifted(value, axis, by):
    count = lax.axis_size(axis)
    return lax.ppermute(value, axis, [(i, (i + by) % count) for i in range(count)])


def from_partner(value, axis, bit):
    return lax.ppermute(value, axis, [(i, i ^ 1 << bit) for i in range(lax.axis_size(axis))])


def spatial_kernel(q_ref, k_ref, v_ref, m_ref, o_ref, *, scale):
    scores = (
        lax.dot_general(
            q_ref[...], k_ref[...], (((1,), (1,)), ((), ())), preferred_element_type=jnp.float32
        )
        * scale
    )
    limited = jnp.where(m_ref[...] > 0, scores, masked_score)
    maxima = jnp.max(limited, axis=-1, keepdims=True)
    weights = jnp.exp(limited - maxima)
    totals = jnp.sum(weights, axis=-1, keepdims=True)
    result = jnp.dot(
        weights.astype(jnp.bfloat16), v_ref[...], preferred_element_type=jnp.float32
    )
    o_ref[...] = result / totals


def spatial_attention(query_flat, key_value_flat, mask, scale):
    frames, query_count, model_width = query_flat.shape
    key_count = key_value_flat.shape[2]
    head_count = model_width // DH
    return pl.pallas_call(
        functools.partial(spatial_kernel, scale=scale),
        grid=(frames, head_count),
        in_specs=[
            pl.BlockSpec((None, query_count, DH), lambda f, h: (f, 0, h)),
            pl.BlockSpec((None, None, key_count, DH), lambda f, h: (0, f, 0, h)),
            pl.BlockSpec((None, None, key_count, DH), lambda f, h: (1, f, 0, h)),
            pl.BlockSpec((query_count, key_count), lambda f, h: (0, 0)),
        ],
        out_specs=pl.BlockSpec((None, query_count, DH), lambda f, h: (f, 0, h)),
        out_shape=jax.ShapeDtypeStruct((frames, query_count, model_width), jnp.float32),
        cost_estimate=pl.CostEstimate(
            flops=4 * frames * query_count * key_count * model_width,
            transcendentals=frames * head_count * query_count * key_count,
            bytes_accessed=2 * model_width * frames * (query_count + 2 * key_count)
            + 4 * frames * query_count * model_width,
        ),
    )(query_flat, key_value_flat, key_value_flat, mask)


def temporal_attention(own_q, all_k, all_v, valid, own_ids, all_ids, scale):
    q32 = own_q.astype(jnp.float32)
    k32 = all_k.astype(jnp.float32)
    scores = jnp.sum(q32[:, None] * k32[None], axis=-1) * scale
    same = own_ids[:, None] == all_ids[None, :]
    allowed = (valid[None, :, :] > 0) | same[:, :, None]
    limited = jnp.where(allowed[..., None], scores, masked_score)
    maxima = jnp.max(limited, axis=1, keepdims=True)
    weights = jnp.exp(limited - maxima)
    totals = jnp.sum(weights, axis=1)
    rounded = weights.astype(jnp.bfloat16).astype(jnp.float32)
    result = jnp.sum(rounded[..., None] * all_v.astype(jnp.float32)[None], axis=1)
    return (result / totals[..., None]).astype(jnp.bfloat16)


def local(queries, keys, values, window_map, frame_valid):
    own_q = queries[0]
    own_k = keys[0]
    own_v = values[0]
    frames, lat_rows, columns, model_width = own_q.shape
    head_count = model_width // DH
    scale = DH ** (-0.5)
    reach_cols = REACH * BLK
    lon_count = lax.axis_size("lon")
    total_cols = lon_count * columns
    ext_count = columns + 2 * reach_cols
    key_value = jnp.stack([own_k, own_v])
    column_ids = jnp.arange(columns, dtype=jnp.int32)
    per_column_map = jnp.repeat(window_map, BLK, axis=0)
    if ext_count >= total_cols and WIN * BLK <= total_cols:
        extended = lax.all_gather(key_value, "lon", axis=3, tiled=True)
        key_cols = total_cols
        block_count = total_cols // BLK
        query_blocks = (lax.axis_index("lon") * columns + column_ids) // BLK
        key_blocks = jnp.arange(total_cols, dtype=jnp.int32) // BLK
        slots = (key_blocks[None, :] - query_blocks[:, None] + REACH) % block_count
    else:
        reach_devices = -(-reach_cols // columns)
        left_parts, right_parts = [], []
        for step_by in range(1, reach_devices + 1):
            need = min(columns, reach_cols - (step_by - 1) * columns)
            left_parts.insert(0, shifted(key_value[:, :, :, columns - need :, :], "lon", step_by))
            right_parts.append(shifted(key_value[:, :, :, :need, :], "lon", -step_by))
        extended = jnp.concatenate(left_parts + [key_value] + right_parts, axis=3)
        key_cols = ext_count
        ext_ids = jnp.arange(ext_count, dtype=jnp.int32)
        slots = ext_ids[None, :] // BLK - column_ids[:, None] // BLK
    picks = slots[:, :, None] == jnp.arange(WIN, dtype=jnp.int32)[None, None, :]
    active = jnp.any(picks & (per_column_map[:, None, :] > 0), axis=-1)
    mask = jnp.broadcast_to(
        active[None, :, None, :].astype(jnp.float32), (lat_rows, columns, lat_rows, key_cols)
    ).reshape(lat_rows * columns, lat_rows * key_cols)
    query_flat = own_q.reshape(frames, lat_rows * columns, model_width)
    key_value_flat = extended.reshape(2, frames, lat_rows * key_cols, model_width)
    spatial = spatial_attention(query_flat, key_value_flat, mask, scale)

    token_count = lat_rows * columns
    tm_count = lax.axis_size("tm")
    tm_index = lax.axis_index("tm")
    key_value_rows = key_value.reshape(2, frames, token_count, head_count, DH)
    pieces = [key_value_rows]
    for step_by in range(1, tm_count):
        pieces.append(shifted(key_value_rows, "tm", step_by))
    gathered = jnp.concatenate(pieces, axis=1)
    piece_ids = jnp.arange(tm_count * frames, dtype=jnp.int32)
    frame_ids = ((tm_index - piece_ids // frames) % tm_count) * frames + piece_ids % frames
    valid_tokens = jnp.take(jnp.tile(frame_valid, (1, lat_rows)), frame_ids, axis=0)
    temporal = temporal_attention(
        own_q.reshape(frames, token_count, head_count, DH),
        gathered[0],
        gathered[1],
        valid_tokens,
        frame_ids[:frames],
        frame_ids,
        scale,
    )
    temporal = temporal.reshape(frames, token_count, model_width).astype(jnp.float32)
    mixed = (
        (spatial + temporal).astype(jnp.bfloat16).reshape(frames, lat_rows, columns, model_width)
    )
    half_width = model_width // 2
    branch_index = lax.axis_index("branch")
    own_half = lax.dynamic_slice_in_dim(mixed, branch_index * half_width, half_width, 3)
    other_half = lax.dynamic_slice_in_dim(mixed, (1 - branch_index) * half_width, half_width, 3)
    partner = from_partner(other_half, "branch", 0)
    is_conditional = branch_index == 0
    conditional = jnp.where(is_conditional, own_half, partner).astype(jnp.float32)
    unconditional = jnp.where(is_conditional, partner, own_half).astype(jnp.float32)
    return (unconditional + guidance_weight * (conditional - unconditional)).astype(jnp.bfloat16)


def solution(mesh):
    in_specs = (
        P(("groups", "branch"), "tm", None, "lon", None),
        P(("groups", "branch"), "tm", None, "lon", None),
        P(("groups", "branch"), "tm", None, "lon", None),
        P(("groups", "lon"), None),
        P("groups", "lon"),
    )
    out_specs = P(("groups", "tm"), None, "lon", "branch")
    return jax.shard_map(local, mesh=mesh, in_specs=in_specs, out_specs=out_specs, check_vma=False)
```

time: 314 us -> 152 us (0.48)
  local copies, waits for them, and re-layouts: 106 us -> 23.4 us
  matrix products: 39.8 us -> 0 us
  waiting for transfers between devices: 125 us -> 90.5 us
  starting transfers between devices: 23.9 us -> 3.06 us
  between operations: 0.3 us -> 13.5 us
  Pallas kernels: 0 us -> 12.8 us
  loops' own time: 8.19 us -> 0 us
    ppermute x4 -> x1, waiting for transfers between devices: 97.8 us -> 24.1 us  [shifted(): lax.ppermute(value, axis, [(i, (i + by) % count) for i in range(count)])]
    all_gather x0 -> x1, waiting for transfers between devices: none -> 64.7 us  [local(): extended = lax.all_gather(key_value, 'lon', axis=3, tiled=True)]
    another operation x21 -> x2, local copies, waits for them, and re-layouts: 62.4 us -> 0.1 us  [local(): jnp.tile(frame_valid, (1, lat_rows))]
    dot_general x26 -> x0, matrix products: 39.8 us -> none  [the longest x12 17.5 us: per_head(): jnp.einsum('fqd,fkd->fqk', query_head, key_head, preferred_element_type=j...]
    all_to_all x4 -> x0, waiting for transfers between devices: 24.9 us -> none  [the longest x1 9.18 us: local(): lax.all_to_all(key_rows, 'tm', split_axis=2, concat_axis=0, tiled=True)]
    all_to_all x4 -> x0, starting transfers between devices: 15.9 us -> none  [the longest x1 4.32 us: local(): lax.all_to_all(query_rows, 'tm', split_axis=2, concat_axis=0, tiled=True)]
    pallas_call x0 -> x1, Pallas kernels: none -> 12.8 us  [spatial_attention(): pl.pallas_call(functools.partial(spatial_kernel, scale=scale), grid=(fram...]
    slice x4 -> x0, local copies, waits for them, and re-layouts: 11.8 us -> none  [the longest x2 4.67 us: local(): value_flat = extended[1].reshape(frames, lat_rows * ext_count, model_width)]
  transfers between devices with their start and end apart: 9 -> 3, of which waited for: 7 -> 3; matrix products, arithmetic and copies ran while one was open for 9% -> 17% of each run, Pallas kernels for 0% -> 0%
where the time goes in v1:
time: 152 us; the launch traced here: 151 us
  waiting for transfers between devices  90.5 us (60%)
  local copies, waits for them, and re-layouts  23.4 us (15%)
  between operations  13.5 us (9%)
  Pallas kernels  12.8 us (8%)
  other arithmetic  7.99 us (5%)
  starting transfers between devices  3.06 us (2%)
    all_gather x1, waiting for transfers between devices, local(): extended = lax.all_gather(key_value, 'lon', axis=3, tiled=True)  64.7 us
    ppermute x1, waiting for transfers between devices, shifted(): lax.ppermute(value, axis, [(i, (i + by) % count) for i in range(count)])  24.1 us
    pallas_call x1, Pallas kernels, spatial_attention(): pl.pallas_call(functools.partial(spatial_kernel, scale=scale), grid=(fram...  12.8 us
    reshape x1, local copies, waits for them, and re-layouts, local(): mask = jnp.broadcast_to(active[None, :, None, :].astype(jnp.float32), (la...  4.68 us
    reshape x2, local copies, waits for them, and re-layouts, local(): key_value_rows = key_value.reshape(2, frames, token_count, head_count, DH)  4.44 us
    convert_element_type x2, local copies, waits for them, and re-layouts, local(): temporal.reshape(frames, token_count, model_width).astype(jnp.float32)  3.57 us
  transfers between devices with their start and end apart: 3, of which 3 were waited for; matrix products, arithmetic and copies ran while one was open for 17% of the time, Pallas kernels for 0%

profile of v1, /device:TPU:0, one launch (start us, length us, event | category | flops | bytes accessed | tf_op | source)
XLA Modules:
  0.0 151.4 jit_solution(11796534828391479970)
XLA Ops:
  6.5 0.0 copy-start.3
  6.5 0.0 all-gather.2.cloned.1.call-start
  6.5 1.3 constant_dynamic-update-slice_fusion.1
  7.8 0.1 copy-done.3
  7.9 0.1 constant_dynamic-update-slice_fusion
  8.0 0.0 copy-start
  8.0 1.2 copy-done
  9.2 0.0 all-gather.2.cloned.1.call-update
  9.2 2.9 %reshape.302 = bf16[2,1,256,12,128]{4,3,2,0,1:T(8,128)(2,1)S(1)} reshape(bf16[2,1,32,8,1536]{4,3,2,1,0:T(8,128)(2,1)} %copy-done) | data formatting | bytes 3145728 | tf_op jit(solution)/shard_map/reshape | solution.py:128
  12.1 0.0 copy-start.5
  12.1 0.0 copy-start.2
  12.1 1.5 %copy.12 = bf16[2,1,256,12,128]{4,2,3,1,0:T(8,128)(2,1)} copy(bf16[2,1,256,12,128]{4,3,2,0,1:T(8,128)(2,1)S(1)} %reshape.302) | data formatting | bytes 3145728 | tf_op jit(solution)/shard_map/reshape | solution.py:128
  13.7 0.0 copy-start.4
  13.7 2.9 %collective-permute-start = (bf16[2,1,256,12,128]{4,2,3,1,0:T(8,128)(2,1)}, bf16[2,1,256,12,128]{4,2,3,1,0:T(8,128)(2,1)}, u32[]{:S(2)}, u32[]{:S(2)}) collective-permute-start(bf16[2,1,256,12,128]{4,2,3,1,0:T(8,128)(2,1)} %copy.12), channel_id=1, source_target_pairs={{0,2},{2,0},{1,3},{3,1},{4,6},{6,4},{5,7},{7,5},{8,10},{10,8},{9,1... | collective-permute-start | bytes 4718600 | tf_op jit(solution)/shard_map/ppermute | solution.py:21
  16.6 0.0 copy-done.5
  16.6 0.1 tile.10
  16.7 0.0 copy-done.2
  16.7 1.8 %reshape.304 = f32[256,12,128]{2,1,0:T(8,128)} reshape(bf16[1,1,32,8,1536]{4,3,2,1,0:T(8,128)(2,1)S(1)} %copy-done.2) | data formatting | bytes 2359296 | tf_op jit(solution)/shard_map/convert_element_type | solution.py:70
  18.5 0.0 copy-done.4
  18.5 0.1 copy.11
  18.6 0.1 add_select_fusion
  18.7 0.1 fusion.9
  18.8 2.6 %broadcast_in_dim.23 = f32[32,8,32,32]{3,2,1,0:T(8,128)} broadcast(f32[8,32]{1,0:T(8,128)S(1)} %convert_element_type.86), dimensions={1,3} | broadcast | bytes 1049600 | tf_op jit(solution)/shard_map/broadcast_in_dim | solution.py:118
  21.4 4.7 %reshape.301.m_ref = f32[256,1024]{1,0:T(8,128)} reshape(f32[32,8,32,32]{3,2,1,0:T(8,128)} %broadcast_in_dim.23) | data formatting | bytes 2097152 | tf_op jit(solution)/shard_map/reshape | solution.py:120
  26.1 0.6 gather_fusion
  26.6 0.1 compare_and_fusion
  26.7 0.4 constant_dynamic-update-slice_fusion.2
  27.1 0.0 copy-start.1
  27.1 0.1 compare_or_fusion
  27.2 24.1 %collective-permute-done = bf16[2,1,256,12,128]{4,2,3,1,0:T(8,128)(2,1)} collective-permute-done((bf16[2,1,256,12,128]{4,2,3,1,0:T(8,128)(2,1)}, bf16[2,1,256,12,128]{4,2,3,1,0:T(8,128)(2,1)}, u32[]{:S(2)}, u32[]{:S(2)}) %collective-permute-start) | collective-permute-done | bytes 1572896 | tf_op jit(solution)/shard_map/ppermute | solution.py:21
  51.3 2.6 %copy_dynamic-update-slice_fusion = bf16[2,2,256,12,128]{4,3,2,0,1:T(8,128)(2,1)S(1)} fusion(bf16[2,2,256,12,128]{4,3,2,0,1:T(8,128)(2,1)S(1)} %constant_dynamic-update-slice_fusion.2, bf16[2,1,256,12,128]{4,2,3,1,0:T(8,128)(2,1)} %collective-permute-done), kind=kLoop, calls=%fused_computation.3 | loop fusion | bytes 3670016 | tf_op jit(solution)/shard_map/concatenate | solution.py:132
  53.9 0.0 copy-done.1
  53.9 1.2 multiply_reduce_fusion.1
  55.1 0.1 fusion.4
  55.3 0.1 fusion.5
  55.4 2.9 %multiply_reduce_fusion = f32[256,12,128]{2,1,0:T(8,128)S(1)} fusion(bf16[2,2,256,12,128]{4,3,2,0,1:T(8,128)(2,1)S(1)} %copy_dynamic-update-slice_fusion, f32[2,256,12]{2,1,0:T(8,128)S(1)} %get-tuple-element.6), kind=kLoop, calls=%fused_computation.1 | loop fusion | flops 1966080 | bytes 3170304 | tf_op jit(solution)/shard_map/reduce_sum | solution.py:80
  58.4 0.7 fusion
  59.1 1.7 %copy.14 = f32[256,12,128]{0,2,1:T(8,128)} copy(f32[256,12,128]{2,1,0:T(8,128)S(1)} %fusion) | data formatting | bytes 3145728 | tf_op jit(solution)/shard_map/convert_element_type | solution.py:145
  60.8 1.9 %copy.15 = f32[1,256,1536]{2,1,0:T(8,128)S(1)} copy(f32[1,256,1536]{1,2,0:T(8,128)} %bitcast.17) | data formatting | bytes 3145728 | tf_op jit(solution)/shard_map/convert_element_type | solution.py:145
  62.7 64.7 %all-gather.2.cloned.1.call-done = bf16[2,1,32,32,1536]{4,3,2,1,0:T(8,128)(2,1)} async-done(((bf16[2,1,32,8,1536]{4,3,2,1,0:T(8,128)(2,1)}), bf16[2,1,32,32,1536]{4,3,2,1,0:T(8,128)(2,1)}) %all-gather.2.cloned.1.call-update) | async-done | bytes 6291472 | tf_op jit(solution)/shard_map/all_gather | solution.py:99
  127.4 12.8 %shard_map.55 = f32[1,256,1536]{2,1,0:T(8,128)} custom-call(bf16[1,256,1536]{2,1,0:T(8,128)(2,1)} %bitcast.18, bf16[2,1,1024,1536]{3,2,1,0:T(8,128)(2,1)} %bitcast.15, bf16[2,1,1024,1536]{3,2,1,0:T(8,128)(2,1)} %bitcast.16, f32[256,1024]{1,0:T(8,128)} %reshape.301.m_ref), custom_call_target="tpu_custom_call" | custom-call | flops 1610612736 | bytes 8650752 | tf_op jit(solution)/shard_map/pallas_call | solution.py:49
  140.2 1.6 %fusion.3 = bf16[1,32,8,1536]{3,2,1,0:T(8,128)(2,1)S(1)} fusion(f32[1,256,1536]{2,1,0:T(8,128)} %shard_map.55, f32[1,256,1536]{2,1,0:T(8,128)S(1)} %copy.15), kind=kLoop, calls=%fused_computation.11 | loop fusion | flops 786432 | bytes 3932160 | tf_op jit(solution)/shard_map/reshape | solution.py:147
  141.9 0.1 collective-permute-start.1
  142.0 1.7 %collective-permute-done.1 = bf16[1,32,8,768]{3,2,1,0:T(8,128)(2,1)S(1)} collective-permute-done((bf16[1,32,8,768]{3,2,1,0:T(8,128)(2,1)S(1)}, bf16[1,32,8,768]{3,2,1,0:T(8,128)(2,1)S(1)}, u32[]{:S(2)}, u32[]{:S(2)}) %collective-permute-start.1) | collective-permute-done | bytes 393248 | tf_op jit(solution)/shard_map/ppermute | solution.py:25
  143.7 0.9 fusion.2
  (11 shorter events, 0.1 us)
Async XLA Ops:
  6.5 1.4 copy-start.3
  6.5 120.9 %all-gather.2.cloned.1.call-start = ((), (), s32[]{:S(2)}) async-start(), calls=%async_computation | async-start | bytes 7864320 | tf_op jit(solution)/shard_map/all_gather | solution.py:99
  8.0 1.2 copy-start
  12.1 4.5 %copy-start.5 = (s32[2,8]{1,0:T(2,128)S(1)}, s32[2,8]{1,0:T(2,128)}, u32[]{:S(2)}) copy-start(s32[2,8]{1,0:T(2,128)} %param.9) | copy-start | bytes 196
  12.1 4.6 %copy-start.2 = (bf16[1,1,32,8,1536]{4,3,2,1,0:T(8,128)(2,1)S(1)}, bf16[1,1,32,8,1536]{4,3,2,1,0:T(8,128)(2,1)}, u32[]{:S(2)}) copy-start(bf16[1,1,32,8,1536]{4,3,2,1,0:T(8,128)(2,1)} %param.5) | copy-start | bytes 2359300
  13.7 4.8 %copy-start.4 = (s32[4,15]{1,0:T(4,128)S(1)}, s32[4,15]{1,0:T(4,128)}, u32[]{:S(2)}) copy-start(s32[4,15]{1,0:T(4,128)} %param.8) | copy-start | bytes 724
  13.7 37.6 %collective-permute-start = (bf16[2,1,256,12,128]{4,2,3,1,0:T(8,128)(2,1)}, bf16[2,1,256,12,128]{4,2,3,1,0:T(8,128)(2,1)}, u32[]{:S(2)}, u32[]{:S(2)}) collective-permute-start(bf16[2,1,256,12,128]{4,2,3,1,0:T(8,128)(2,1)} %copy.12), channel_id=1, source_target_pairs={{0,2},{2,0},{1,3},{3,1},{4,6},{6,4},{5,7},{7,5},{8,10},{10,8},{9,1... | collective-permute-start | bytes 4718600 | tf_op jit(solution)/shard_map/ppermute | solution.py:21
  27.1 26.9 %copy-start.1 = (f32[256,12,128]{2,1,0:T(8,128)S(1)}, f32[256,12,128]{2,1,0:T(8,128)}, u32[]{:S(2)}) copy-start(f32[256,12,128]{2,1,0:T(8,128)} %reshape.304) | copy-start | bytes 4718596
  141.9 1.8 %collective-permute-start.1 = (bf16[1,32,8,768]{3,2,1,0:T(8,128)(2,1)S(1)}, bf16[1,32,8,768]{3,2,1,0:T(8,128)(2,1)S(1)}, u32[]{:S(2)}, u32[]{:S(2)}) collective-permute-start(bf16[1,32,8,768]{3,2,1,0:T(8,128)(2,1)S(1)} %constant_dynamic-slice_fusion), channel_id=1, source_target_pairs={{0,1},{1,0},{2,3},{3,2},{4,5},{5,4},{6,7},{7,6},{8,9},{9,8},{10,11... | collective-permute-start | bytes 1179656 | tf_op jit(solution)/shard_map/ppermute | solution.py:25
Sparse Core Ops, SparseCore 0:
  9.3 118.0 all-gather.1

commit v2 on v1

--- a/solution.py
+++ b/solution.py
@@ -76,9 +76,27 @@
     maxima = jnp.max(limited, axis=1, keepdims=True)
     weights = jnp.exp(limited - maxima)
     totals = jnp.sum(weights, axis=1)
-    rounded = weights.astype(jnp.bfloat16).astype(jnp.float32)
+    rounded = lax.reduce_precision(weights, exponent_bits=8, mantissa_bits=7)
     result = jnp.sum(rounded[..., None] * all_v.astype(jnp.float32)[None], axis=1)
-    return (result / totals[..., None]).astype(jnp.bfloat16)
+    result = lax.reduce_precision(result / totals[..., None], exponent_bits=8, mantissa_bits=7)
+    return result.astype(jnp.bfloat16)
+
+
+def line_gather(block, axis):
+    count = lax.axis_size(axis)
+    index = lax.axis_index(axis)
+    left, right = {}, {}
+    from_left = from_right = block
+    for step in range(1, count):
+        from_left = lax.ppermute(from_left, axis, [(s, s + 1) for s in range(step - 1, count - 1)])
+        from_right = lax.ppermute(
+            from_right, axis, [(s, s - 1) for s in range(1, count - step + 1)]
+        )
+        left[step], right[step] = from_left, from_right
+    relative = [block]
+    for d in range(1, count):
+        relative.append(jnp.where(index + d < count, right[d], left[count - d]))
+    return relative
 
 
 def local(queries, keys, values, window_map, frame_valid):
@@ -96,11 +114,12 @@
     column_ids = jnp.arange(columns, dtype=jnp.int32)
     per_column_map = jnp.repeat(window_map, BLK, axis=0)
     if ext_count >= total_cols and WIN * BLK <= total_cols:
-        extended = lax.all_gather(key_value, "lon", axis=3, tiled=True)
+        extended = jnp.concatenate(line_gather(key_value, "lon"), axis=3)
         key_cols = total_cols
         block_count = total_cols // BLK
-        query_blocks = (lax.axis_index("lon") * columns + column_ids) // BLK
-        key_blocks = jnp.arange(total_cols, dtype=jnp.int32) // BLK
+        first_col = lax.axis_index("lon") * columns
+        query_blocks = (first_col + column_ids) // BLK
+        key_blocks = ((first_col + jnp.arange(total_cols, dtype=jnp.int32)) % total_cols) // BLK
         slots = (key_blocks[None, :] - query_blocks[:, None] + REACH) % block_count
     else:
         reach_devices = -(-reach_cols // columns)

time: 152 us -> 144 us (0.947)
  waiting for transfers between devices: 90.5 us -> 68.7 us
  between operations: 13.5 us -> 0.22 us
  starting transfers between devices: 3.06 us -> 16.3 us
  other arithmetic: 7.99 us -> 19 us
  local copies, waits for them, and re-layouts: 23.4 us -> 25.3 us
    ppermute x0 -> x6, waiting for transfers between devices: none -> 67 us  [the longest x3 67 us: line_gather(): lax.ppermute(from_right, axis, [(s, s - 1) for s in range(1, count - step...]
    all_gather x1 -> x0, waiting for transfers between devices: 64.7 us -> none  [local(): extended = lax.all_gather(key_value, 'lon', axis=3, tiled=True)]
    ppermute x1, waiting for transfers between devices: 24.1 us -> 0.01 us  [shifted(): lax.ppermute(value, axis, [(i, (i + by) % count) for i in range(count)])]
    ppermute x0 -> x6, starting transfers between devices: none -> 14.3 us  [the longest x3 10.4 us: line_gather(): lax.ppermute(from_left, axis, [(s, s + 1) for s in range(step - 1, count...]
    select_n x2 -> x5, other arithmetic: 0.01 us -> 4.77 us  [the longest x3 4.75 us: line_gather(): relative.append(jnp.where(index + d < count, right[d], left[count - d]))]
    concatenate x0 -> x1, other arithmetic: none -> 4.49 us  [local(): extended = jnp.concatenate(line_gather(key_value, 'lon'), axis=3)]
    reduce_sum x1, other arithmetic: 1.17 us -> 2.91 us  [temporal_attention(): scores = jnp.sum(q32[:, None] * k32[None], axis=-1) * scale]
    unnamed x14 -> x12, local copies, waits for them, and re-layouts: 2.93 us -> 4.1 us
  transfers between devices with their start and end apart: 3 -> 8, of which waited for: 3 -> 4; matrix products, arithmetic and copies ran while one was open for 17% -> 23% of each run, Pallas kernels for 0% -> 0%
where the time goes in v2:
time: 144 us; the launch traced here: 142 us
  waiting for transfers between devices  68.7 us (48%)
  local copies, waits for them, and re-layouts  25.3 us (18%)
  other arithmetic  19 us (13%)
  starting transfers between devices  16.3 us (11%)
  Pallas kernels  12.9 us (9%)
    ppermute x3, waiting for transfers between devices, line_gather(): lax.ppermute(from_right, axis, [(s, s - 1) for s in range(1, count - step...  67 us
    pallas_call x1, Pallas kernels, spatial_attention(): pl.pallas_call(functools.partial(spatial_kernel, scale=scale), grid=(fram...  12.9 us
    ppermute x3, starting transfers between devices, line_gather(): lax.ppermute(from_left, axis, [(s, s + 1) for s in range(step - 1, count...  10.4 us
    select_n x3, other arithmetic, line_gather(): relative.append(jnp.where(index + d < count, right[d], left[count - d]))  4.75 us
    reshape x1, local copies, waits for them, and re-layouts, local(): mask = jnp.broadcast_to(active[None, :, None, :].astype(jnp.float32), (la...  4.66 us
    concatenate x1, other arithmetic, local(): extended = jnp.concatenate(line_gather(key_value, 'lon'), axis=3)  4.49 us
    reshape x2, local copies, waits for them, and re-layouts, local(): key_value_rows = key_value.reshape(2, frames, token_count, head_count, DH)  4.45 us
    unnamed x12, local copies, waits for them, and re-layouts  4.1 us
  transfers between devices with their start and end apart: 8, of which 4 were waited for; matrix products, arithmetic and copies ran while one was open for 23% of the time, Pallas kernels for 0%

profile of v2, /device:TPU:0, one launch (start us, length us, event | category | flops | bytes accessed | tf_op | source)
XLA Modules:
  0.0 142.3 jit_solution(1762452895160906449)
XLA Ops:
  0.0 0.0 copy-start.2
  0.0 2.2 %constant_dynamic-update-slice_fusion.1 = bf16[2,1,32,8,1536]{4,3,2,1,0:T(8,128)(2,1)} fusion(bf16[1,1,32,8,1536]{4,3,2,1,0:T(8,128)(2,1)} %param.6), kind=kLoop, calls=%fused_computation.25 | loop fusion | bytes 1572864
  2.2 0.0 copy-done.2
  2.2 0.9 constant_dynamic-update-slice_fusion
  3.1 1.3 collective-permute-start
  4.4 6.7 %collective-permute-start.1 = (bf16[2,1,32,8,1536]{4,3,2,1,0:T(8,128)(2,1)}, bf16[2,1,32,8,1536]{4,3,2,1,0:T(8,128)(2,1)}, u32[]{:S(2)}, u32[]{:S(2)}) collective-permute-start(bf16[2,1,32,8,1536]{4,3,2,1,0:T(8,128)(2,1)} %constant_dynamic-update-slice_fusion), channel_id=1, source_target_pairs={{0,4},{4,8},{8,12},{1,5},{5,9},{9,13},{2,6},{6,10},{10,14},{3,7},{... | collective-permute-start | bytes 4718600 | tf_op jit(solution)/shard_map/ppermute | solution.py:91
  11.1 2.9 %reshape.322 = bf16[2,1,256,12,128]{4,3,2,0,1:T(8,128)(2,1)S(1)} reshape(bf16[2,1,32,8,1536]{4,3,2,1,0:T(8,128)(2,1)} %constant_dynamic-update-slice_fusion) | data formatting | bytes 3145728 | tf_op jit(solution)/shard_map/reshape | solution.py:147
  14.0 0.0 copy-start.3
  14.1 1.6 %copy.12 = bf16[2,1,256,12,128]{4,2,3,1,0:T(8,128)(2,1)} copy(bf16[2,1,256,12,128]{4,3,2,0,1:T(8,128)(2,1)S(1)} %reshape.322) | data formatting | bytes 3145728 | tf_op jit(solution)/shard_map/reshape | solution.py:147
  15.6 1.9 %collective-permute-start.6 = (bf16[2,1,256,12,128]{4,2,3,1,0:T(8,128)(2,1)}, bf16[2,1,256,12,128]{4,2,3,1,0:T(8,128)(2,1)}, u32[]{:S(2)}, u32[]{:S(2)}) collective-permute-start(bf16[2,1,256,12,128]{4,2,3,1,0:T(8,128)(2,1)} %copy.12), channel_id=1, source_target_pairs={{0,2},{2,0},{1,3},{3,1},{4,6},{6,4},{5,7},{7,5},{8,10},{10,8},{9,1... | collective-permute-start | bytes 4718600 | tf_op jit(solution)/shard_map/ppermute | solution.py:21
  17.5 0.0 copy-done.3
  17.6 0.1 copy.11
  17.7 25.0 %collective-permute-done = bf16[2,1,32,8,1536]{4,3,2,1,0:T(8,128)(2,1)} collective-permute-done((bf16[2,1,32,8,1536]{4,3,2,1,0:T(8,128)(2,1)}, bf16[2,1,32,8,1536]{4,3,2,1,0:T(8,128)(2,1)}, u32[]{:S(2)}, u32[]{:S(2)}) %collective-permute-start) | collective-permute-done | bytes 1572896 | tf_op jit(solution)/shard_map/ppermute | solution.py:92
  42.8 1.3 collective-permute-start.4
  44.1 0.1 add_select_fusion
  44.1 0.1 fusion.8
  44.2 1.7 %constant_dynamic-update-slice_fusion.2 = bf16[2,2,256,12,128]{4,3,2,0,1:T(8,128)(2,1)} fusion(bf16[2,1,256,12,128]{4,3,2,0,1:T(8,128)(2,1)S(1)} %reshape.322), kind=kLoop, calls=%fused_computation.26 | loop fusion | bytes 3670016
  45.9 0.0 collective-permute-done.1
  45.9 1.9 %collective-permute-start.2 = (bf16[2,1,32,8,1536]{4,3,2,1,0:T(8,128)(2,1)}, bf16[2,1,32,8,1536]{4,3,2,1,0:T(8,128)(2,1)}, u32[]{:S(2)}, u32[]{:S(2)}) collective-permute-start(bf16[2,1,32,8,1536]{4,3,2,1,0:T(8,128)(2,1)} %collective-permute-done.1), channel_id=1, source_target_pairs={{4,8},{8,12},{5,9},{9,13},{6,10},{10,14},{7,11},{11,15},{20,24},{2... | collective-permute-start | bytes 4718600 | tf_op jit(solution)/shard_map/ppermute | solution.py:91
  47.9 2.5 %broadcast_in_dim.23 = f32[32,8,32,32]{3,2,1,0:T(8,128)} broadcast(f32[8,32]{1,0:T(8,128)S(1)} %convert_element_type.68), dimensions={1,3} | broadcast | bytes 1049600 | tf_op jit(solution)/shard_map/broadcast_in_dim | solution.py:137
  50.4 0.0 copy-start.1
  50.4 4.7 %reshape.321.m_ref = f32[256,1024]{1,0:T(8,128)} reshape(f32[32,8,32,32]{3,2,1,0:T(8,128)} %broadcast_in_dim.23) | data formatting | bytes 2097152 | tf_op jit(solution)/shard_map/reshape | solution.py:139
  55.0 0.0 copy-done.1
  55.0 0.0 copy-start.4
  55.0 0.5 reshape.324
  55.5 0.2 copy-done.4
  55.7 0.1 tile.10
  55.8 0.6 gather_fusion
  56.4 0.1 compare_or_fusion
  56.4 0.0 collective-permute-done.6
  56.4 3.8 %copy_dynamic-update-slice_fusion = bf16[2,2,256,12,128]{4,3,2,0,1:T(8,128)(2,1)} fusion(bf16[2,2,256,12,128]{4,3,2,0,1:T(8,128)(2,1)} %constant_dynamic-update-slice_fusion.2, bf16[2,1,256,12,128]{4,2,3,1,0:T(8,128)(2,1)} %collective-permute-done.6), kind=kLoop, calls=%fused_computation.4 | loop fusion | bytes 3670016 | tf_op jit(solution)/shard_map/concatenate | solution.py:151
  60.2 0.0 copy-start
  60.2 2.9 %multiply_reduce_fusion.1 = f32[2,256,12]{2,1,0:T(8,128)S(1)} fusion(bf16[2,2,256,12,128]{4,3,2,0,1:T(8,128)(2,1)} %copy_dynamic-update-slice_fusion, f32[256,12,128]{2,1,0:T(8,128)S(1)} %reshape.324), kind=kLoop, calls=%fused_computation.3 | loop fusion | flops 2353152 | bytes 3170304 | tf_op jit(solution)/shard_map/reduce_sum | solution.py:72
  63.2 17.4 %collective-permute-done.4 = bf16[2,1,32,8,1536]{4,3,2,1,0:T(8,128)(2,1)} collective-permute-done((bf16[2,1,32,8,1536]{4,3,2,1,0:T(8,128)(2,1)}, bf16[2,1,32,8,1536]{4,3,2,1,0:T(8,128)(2,1)}, u32[]{:S(2)}, u32[]{:S(2)}) %collective-permute-start.4) | collective-permute-done | bytes 1572896 | tf_op jit(solution)/shard_map/ppermute | solution.py:92
  80.5 1.3 collective-permute-start.5
  81.8 0.1 fusion.4
  82.0 0.1 fusion.5
  82.1 0.0 copy-done
  82.1 2.9 %multiply_reduce_fusion = f32[256,12,128]{2,1,0:T(8,128)S(1)} fusion(bf16[2,2,256,12,128]{4,3,2,0,1:T(8,128)(2,1)S(1)} %copy-done, f32[2,256,12]{2,1,0:T(8,128)S(1)} %get-tuple-element.6), kind=kLoop, calls=%fused_computation.2 | loop fusion | flops 1966080 | bytes 3170304 | tf_op jit(solution)/shard_map/reduce_sum | solution.py:80
  85.1 0.0 collective-permute-done.2
  85.1 1.8 %collective-permute-start.3 = (bf16[2,1,32,8,1536]{4,3,2,1,0:T(8,128)(2,1)}, bf16[2,1,32,8,1536]{4,3,2,1,0:T(8,128)(2,1)}, u32[]{:S(2)}, u32[]{:S(2)}) collective-permute-start(bf16[2,1,32,8,1536]{4,3,2,1,0:T(8,128)(2,1)} %collective-permute-done.2), channel_id=1, source_target_pairs={{8,12},{9,13},{10,14},{11,15},{24,28},{25,29},{26,30},{27,31}} | collective-permute-start | bytes 4718600 | tf_op jit(solution)/shard_map/ppermute | solution.py:91
  86.9 0.7 fusion
  87.6 1.7 %copy.14 = f32[256,12,128]{0,2,1:T(8,128)} copy(f32[256,12,128]{2,1,0:T(8,128)S(1)} %fusion) | data formatting | bytes 3145728 | tf_op jit(solution)/shard_map/convert_element_type | solution.py:164
  89.3 1.9 %copy.15 = f32[1,256,1536]{2,1,0:T(8,128)S(1)} copy(f32[1,256,1536]{1,2,0:T(8,128)} %bitcast.17) | data formatting | bytes 3145728 | tf_op jit(solution)/shard_map/convert_element_type | solution.py:164
  91.2 1.6 %broadcast_select_fusion.1 = bf16[2,1,32,8,1536]{4,3,2,1,0:T(8,128)(2,1)S(1)} fusion(bf16[2,1,32,8,1536]{4,3,2,1,0:T(8,128)(2,1)} %collective-permute-done.4, bf16[2,1,32,8,1536]{4,3,2,1,0:T(8,128)(2,1)} %collective-permute-done.2, pred[]{:T(512)S(6)} %lt.53), kind=kLoop, calls=%fused_computation.8 | loop fusion | flops 786432 | bytes 4718593 | tf_op jit(solution)/shard_map/jit(_where)/select_n | solution.py:98
  92.8 24.6 %collective-permute-done.5 = bf16[2,1,32,8,1536]{4,3,2,1,0:T(8,128)(2,1)} collective-permute-done((bf16[2,1,32,8,1536]{4,3,2,1,0:T(8,128)(2,1)}, bf16[2,1,32,8,1536]{4,3,2,1,0:T(8,128)(2,1)}, u32[]{:S(2)}, u32[]{:S(2)}) %collective-permute-start.5) | collective-permute-done | bytes 1572896 | tf_op jit(solution)/shard_map/ppermute | solution.py:92
  117.4 1.6 %broadcast_select_fusion = bf16[2,1,32,8,1536]{4,3,2,1,0:T(8,128)(2,1)S(1)} fusion(bf16[2,1,32,8,1536]{4,3,2,1,0:T(8,128)(2,1)} %collective-permute-done.5, bf16[2,1,32,8,1536]{4,3,2,1,0:T(8,128)(2,1)} %collective-permute-done.1, pred[]{:T(512)S(6)} %lt.54), kind=kLoop, calls=%fused_computation.7 | loop fusion | flops 786432 | bytes 4718593 | tf_op jit(solution)/shard_map/jit(_where)/select_n | solution.py:98
  119.0 0.0 collective-permute-done.3
  119.0 1.6 %broadcast_select_fusion.2 = bf16[2,1,32,8,1536]{4,3,2,1,0:T(8,128)(2,1)S(1)} fusion(bf16[2,1,32,8,1536]{4,3,2,1,0:T(8,128)(2,1)} %collective-permute-done, bf16[2,1,32,8,1536]{4,3,2,1,0:T(8,128)(2,1)} %collective-permute-done.3, pred[]{:T(512)S(6)} %lt.52), kind=kLoop, calls=%fused_computation.9 | loop fusion | flops 786432 | bytes 4718593 | tf_op jit(solution)/shard_map/jit(_where)/select_n | solution.py:98
  120.6 4.5 %pad_maximum_fusion = bf16[2,1,32,32,1536]{4,3,2,1,0:T(8,128)(2,1)} fusion(bf16[2,1,32,8,1536]{4,3,2,1,0:T(8,128)(2,1)S(1)} %broadcast_select_fusion, bf16[2,1,32,8,1536]{4,3,2,1,0:T(8,128)(2,1)S(1)} %broadcast_select_fusion.1, bf16[2,1,32,8,1536]{4,3,2,1,0:T(8,128)(2,1)S(1)} %broadcast_select_fusion.2, ...), kind=kLoop, calls=%fused_computation.1 | loop fusion | flops 25165824 | bytes 12582912 | tf_op jit(solution)/shard_map/concatenate | solution.py:117
  125.1 12.9 %shard_map.55 = f32[1,256,1536]{2,1,0:T(8,128)} custom-call(bf16[1,256,1536]{2,1,0:T(8,128)(2,1)} %bitcast.18, bf16[2,1,1024,1536]{3,2,1,0:T(8,128)(2,1)} %bitcast.15, bf16[2,1,1024,1536]{3,2,1,0:T(8,128)(2,1)} %bitcast.16, f32[256,1024]{1,0:T(8,128)} %reshape.321.m_ref), custom_call_target="tpu_custom_call" | custom-call | flops 1610612736 | bytes 8650752 | tf_op jit(solution)/shard_map/pallas_call | solution.py:49
  137.9 1.6 %fusion.3 = bf16[1,32,8,1536]{3,2,1,0:T(8,128)(2,1)S(1)} fusion(f32[1,256,1536]{2,1,0:T(8,128)} %shard_map.55, f32[1,256,1536]{2,1,0:T(8,128)S(1)} %copy.15), kind=kLoop, calls=%fused_computation.15 | loop fusion | flops 786432 | bytes 3932160 | tf_op jit(solution)/shard_map/reshape | solution.py:166
  139.6 0.1 collective-permute-start.7
  139.7 1.7 %collective-permute-done.7 = bf16[1,32,8,768]{3,2,1,0:T(8,128)(2,1)S(1)} collective-permute-done((bf16[1,32,8,768]{3,2,1,0:T(8,128)(2,1)S(1)}, bf16[1,32,8,768]{3,2,1,0:T(8,128)(2,1)S(1)}, u32[]{:S(2)}, u32[]{:S(2)}) %collective-permute-start.7) | collective-permute-done | bytes 393248 | tf_op jit(solution)/shard_map/ppermute | solution.py:25
  141.4 0.9 fusion.2
  (12 shorter events, 0.2 us)
Async XLA Ops:
  0.0 2.2 %copy-start.2 = (bf16[1,1,32,8,1536]{4,3,2,1,0:T(8,128)(2,1)S(1)}, bf16[1,1,32,8,1536]{4,3,2,1,0:T(8,128)(2,1)}, u32[]{:S(2)}) copy-start(bf16[1,1,32,8,1536]{4,3,2,1,0:T(8,128)(2,1)} %param.7) | copy-start | bytes 2359300
  3.1 39.6 %collective-permute-start = (bf16[2,1,32,8,1536]{4,3,2,1,0:T(8,128)(2,1)}, bf16[2,1,32,8,1536]{4,3,2,1,0:T(8,128)(2,1)}, u32[]{:S(2)}, u32[]{:S(2)}) collective-permute-start(bf16[2,1,32,8,1536]{4,3,2,1,0:T(8,128)(2,1)} %constant_dynamic-update-slice_fusion), channel_id=1, source_target_pairs={{4,0},{8,4},{12,8},{5,1},{9,5},{13,9},{6,2},{10,6},{14,10},{7,3},{... | collective-permute-start | bytes 4718600 | tf_op jit(solution)/shard_map/ppermute | solution.py:92
  4.4 41.5 %collective-permute-start.1 = (bf16[2,1,32,8,1536]{4,3,2,1,0:T(8,128)(2,1)}, bf16[2,1,32,8,1536]{4,3,2,1,0:T(8,128)(2,1)}, u32[]{:S(2)}, u32[]{:S(2)}) collective-permute-start(bf16[2,1,32,8,1536]{4,3,2,1,0:T(8,128)(2,1)} %constant_dynamic-update-slice_fusion), channel_id=1, source_target_pairs={{0,4},{4,8},{8,12},{1,5},{5,9},{9,13},{2,6},{6,10},{10,14},{3,7},{... | collective-permute-start | bytes 4718600 | tf_op jit(solution)/shard_map/ppermute | solution.py:91
  14.0 3.5 %copy-start.3 = (s32[4,15]{1,0:T(4,128)S(1)}, s32[4,15]{1,0:T(4,128)}, u32[]{:S(2)}) copy-start(s32[4,15]{1,0:T(4,128)} %param.8) | copy-start | bytes 724
  15.6 40.8 %collective-permute-start.6 = (bf16[2,1,256,12,128]{4,2,3,1,0:T(8,128)(2,1)}, bf16[2,1,256,12,128]{4,2,3,1,0:T(8,128)(2,1)}, u32[]{:S(2)}, u32[]{:S(2)}) collective-permute-start(bf16[2,1,256,12,128]{4,2,3,1,0:T(8,128)(2,1)} %copy.12), channel_id=1, source_target_pairs={{0,2},{2,0},{1,3},{3,1},{4,6},{6,4},{5,7},{7,5},{8,10},{10,8},{9,1... | collective-permute-start | bytes 4718600 | tf_op jit(solution)/shard_map/ppermute | solution.py:21
  42.8 37.8 %collective-permute-start.4 = (bf16[2,1,32,8,1536]{4,3,2,1,0:T(8,128)(2,1)}, bf16[2,1,32,8,1536]{4,3,2,1,0:T(8,128)(2,1)}, u32[]{:S(2)}, u32[]{:S(2)}) collective-permute-start(bf16[2,1,32,8,1536]{4,3,2,1,0:T(8,128)(2,1)} %collective-permute-done), channel_id=1, source_target_pairs={{4,0},{8,4},{5,1},{9,5},{6,2},{10,6},{7,3},{11,7},{20,16},{24,20},... | collective-permute-start | bytes 4718600 | tf_op jit(solution)/shard_map/ppermute | solution.py:92
  45.9 39.1 %collective-permute-start.2 = (bf16[2,1,32,8,1536]{4,3,2,1,0:T(8,128)(2,1)}, bf16[2,1,32,8,1536]{4,3,2,1,0:T(8,128)(2,1)}, u32[]{:S(2)}, u32[]{:S(2)}) collective-permute-start(bf16[2,1,32,8,1536]{4,3,2,1,0:T(8,128)(2,1)} %collective-permute-done.1), channel_id=1, source_target_pairs={{4,8},{8,12},{5,9},{9,13},{6,10},{10,14},{7,11},{11,15},{20,24},{2... | collective-permute-start | bytes 4718600 | tf_op jit(solution)/shard_map/ppermute | solution.py:91
  50.4 4.7 %copy-start.1 = (bf16[1,1,32,8,1536]{4,3,2,1,0:T(8,128)(2,1)S(1)}, bf16[1,1,32,8,1536]{4,3,2,1,0:T(8,128)(2,1)}, u32[]{:S(2)}) copy-start(bf16[1,1,32,8,1536]{4,3,2,1,0:T(8,128)(2,1)} %param.5) | copy-start | bytes 2359300
  55.0 0.7 copy-start.4
  60.2 21.9 %copy-start = (bf16[2,2,256,12,128]{4,3,2,0,1:T(8,128)(2,1)S(1)}, bf16[2,2,256,12,128]{4,3,2,0,1:T(8,128)(2,1)}, u32[]{:S(2)}) copy-start(bf16[2,2,256,12,128]{4,3,2,0,1:T(8,128)(2,1)} %copy_dynamic-update-slice_fusion) | copy-start | bytes 9437188
  80.5 36.9 %collective-permute-start.5 = (bf16[2,1,32,8,1536]{4,3,2,1,0:T(8,128)(2,1)}, bf16[2,1,32,8,1536]{4,3,2,1,0:T(8,128)(2,1)}, u32[]{:S(2)}, u32[]{:S(2)}) collective-permute-start(bf16[2,1,32,8,1536]{4,3,2,1,0:T(8,128)(2,1)} %collective-permute-done.4), channel_id=1, source_target_pairs={{4,0},{5,1},{6,2},{7,3},{20,16},{21,17},{22,18},{23,19}} | collective-permute-start | bytes 4718600 | tf_op jit(solution)/shard_map/ppermute | solution.py:92
  85.1 33.9 %collective-permute-start.3 = (bf16[2,1,32,8,1536]{4,3,2,1,0:T(8,128)(2,1)}, bf16[2,1,32,8,1536]{4,3,2,1,0:T(8,128)(2,1)}, u32[]{:S(2)}, u32[]{:S(2)}) collective-permute-start(bf16[2,1,32,8,1536]{4,3,2,1,0:T(8,128)(2,1)} %collective-permute-done.2), channel_id=1, source_target_pairs={{8,12},{9,13},{10,14},{11,15},{24,28},{25,29},{26,30},{27,31}} | collective-permute-start | bytes 4718600 | tf_op jit(solution)/shard_map/ppermute | solution.py:91
  139.6 1.8 %collective-permute-start.7 = (bf16[1,32,8,768]{3,2,1,0:T(8,128)(2,1)S(1)}, bf16[1,32,8,768]{3,2,1,0:T(8,128)(2,1)S(1)}, u32[]{:S(2)}, u32[]{:S(2)}) collective-permute-start(bf16[1,32,8,768]{3,2,1,0:T(8,128)(2,1)S(1)} %constant_dynamic-slice_fusion), channel_id=1, source_target_pairs={{0,1},{1,0},{2,3},{3,2},{4,5},{5,4},{6,7},{7,6},{8,9},{9,8},{10,11... | collective-permute-start | bytes 1179656 | tf_op jit(solution)/shard_map/ppermute | solution.py:25

commit v3 on v2

--- a/solution.py
+++ b/solution.py
@@ -25,7 +25,7 @@
     return lax.ppermute(value, axis, [(i, i ^ 1 << bit) for i in range(lax.axis_size(axis))])
 
 
-def spatial_kernel(q_ref, k_ref, v_ref, m_ref, o_ref, *, scale):
+def spatial_kernel(q_ref, k_ref, v_ref, m_ref, o_ref, lse_ref, *, scale):
     scores = (
         lax.dot_general(
             q_ref[...], k_ref[...], (((1,), (1,)), ((), ())), preferred_element_type=jnp.float32
@@ -40,6 +40,7 @@
         weights.astype(jnp.bfloat16), v_ref[...], preferred_element_type=jnp.float32
     )
     o_ref[...] = result / totals
+    lse_ref[...] = maxima + jnp.log(totals)
 
 
 def spatial_attention(query_flat, key_value_flat, mask, scale):
@@ -55,8 +56,14 @@
             pl.BlockSpec((None, None, key_count, DH), lambda f, h: (1, f, 0, h)),
             pl.BlockSpec((query_count, key_count), lambda f, h: (0, 0)),
         ],
-        out_specs=pl.BlockSpec((None, query_count, DH), lambda f, h: (f, 0, h)),
-        out_shape=jax.ShapeDtypeStruct((frames, query_count, model_width), jnp.float32),
+        out_specs=[
+            pl.BlockSpec((None, query_count, DH), lambda f, h: (f, 0, h)),
+            pl.BlockSpec((None, None, query_count, 1), lambda f, h: (f, h, 0, 0)),
+        ],
+        out_shape=[
+            jax.ShapeDtypeStruct((frames, query_count, model_width), jnp.float32),
+            jax.ShapeDtypeStruct((frames, head_count, query_count, 1), jnp.float32),
+        ],
         cost_estimate=pl.CostEstimate(
             flops=4 * frames * query_count * key_count * model_width,
             transcendentals=frames * head_count * query_count * key_count,
@@ -99,6 +106,92 @@
     return relative
 
 
+def window_mask(query_cols, key_cols, column_map, total_cols, lat_rows):
+    block_count = total_cols // BLK
+    slots = (key_cols[None, :] // BLK - query_cols[:, None] // BLK + REACH) % block_count
+    picks = slots[:, :, None] == jnp.arange(WIN, dtype=jnp.int32)[None, None, :]
+    return jnp.any(picks & (column_map[:, None, :] > 0), axis=-1)
+
+
+def expand_mask(active, lat_rows):
+    query_cols, key_cols = active.shape
+    return jnp.broadcast_to(
+        active[None, :, None, :].astype(jnp.float32), (lat_rows, query_cols, lat_rows, key_cols)
+    ).reshape(lat_rows * query_cols, lat_rows * key_cols)
+
+
+def flat_keys(blocks):
+    joined = jnp.concatenate(blocks, axis=3)
+    two, frames, lat_rows, cols, model_width = joined.shape
+    return joined.reshape(two, frames, lat_rows * cols, model_width)
+
+
+def spatial_line_of_four(own_q, key_value, window_map, scale):
+    frames, lat_rows, columns, model_width = own_q.shape
+    head_count = model_width // DH
+    count = 4
+    total_cols = count * columns
+    index = lax.axis_index("lon")
+    is_middle = (index >= 1) & (index <= count - 2)
+    from_left = lax.ppermute(key_value, "lon", [(0, 1), (1, 2), (2, 3)])
+    from_right = lax.ppermute(key_value, "lon", [(3, 2), (2, 1), (1, 0)])
+    onward = jnp.where(index == 1, from_left, from_right)
+    two_away = lax.ppermute(onward, "lon", [(1, 2), (2, 1)])
+    held_q, _ = lax.optimization_barrier((own_q, from_left))
+    guest_q = lax.ppermute(held_q, "lon", [(0, 1), (3, 2)])
+    guest_map = lax.ppermute(window_map, "lon", [(0, 1), (3, 2)])
+
+    column_ids = jnp.arange(columns, dtype=jnp.int32)
+    guest_device = jnp.where(index == 1, 0, count - 1)
+    near_block = jnp.where(index == 1, index + 1, index - 1)
+    far_block = (index + 2) % count
+    guest_key_cols = jnp.concatenate([near_block * columns + column_ids, far_block * columns + column_ids])
+    guest_active = window_mask(
+        guest_device * columns + column_ids,
+        guest_key_cols,
+        jnp.repeat(guest_map, BLK, axis=0),
+        total_cols,
+        lat_rows,
+    ) & is_middle
+    guest_near = jnp.where(index == 1, from_right, from_left)
+    guest_out, guest_lse = spatial_attention(
+        guest_q.reshape(frames, lat_rows * columns, model_width),
+        flat_keys([guest_near, two_away]),
+        expand_mask(guest_active, lat_rows),
+        scale,
+    )
+    returned, returned_lse = lax.ppermute(
+        (guest_out.astype(jnp.bfloat16), guest_lse.reshape(frames, head_count, lat_rows * columns)),
+        "lon",
+        [(1, 0), (2, 3)],
+    )
+
+    rel_cols = ((index - 1) * columns + jnp.arange(total_cols, dtype=jnp.int32)) % total_cols
+    rel_block = jnp.arange(total_cols, dtype=jnp.int32) // columns
+    block_valid = jnp.stack([index >= 1, index >= 0, index <= count - 2, is_middle])
+    own_active = window_mask(
+        index * columns + column_ids, rel_cols, jnp.repeat(window_map, BLK, axis=0), total_cols, lat_rows
+    ) & block_valid[rel_block][None, :]
+    own_out, own_lse = spatial_attention(
+        own_q.reshape(frames, lat_rows * columns, model_width),
+        flat_keys([from_left, key_value, from_right, two_away]),
+        expand_mask(own_active, lat_rows),
+        scale,
+    )
+    own_lse = jnp.transpose(own_lse[..., 0], (0, 2, 1))[..., None]
+    returned_lse = jnp.transpose(returned_lse, (0, 2, 1))[..., None]
+    top = jnp.maximum(own_lse, returned_lse)
+    own_weight = jnp.exp(own_lse - top)
+    returned_weight = jnp.exp(returned_lse - top)
+    shape4 = (frames, lat_rows * columns, head_count, DH)
+    joined = (
+        own_weight * own_out.reshape(shape4)
+        + returned_weight * returned.astype(jnp.float32).reshape(shape4)
+    ) / (own_weight + returned_weight)
+    spatial = jnp.where(is_middle, own_out, joined.reshape(own_out.shape))
+    return spatial
+
+
 def local(queries, keys, values, window_map, frame_valid):
     own_q = queries[0]
     own_k = keys[0]
@@ -113,33 +206,36 @@
     key_value = jnp.stack([own_k, own_v])
     column_ids = jnp.arange(columns, dtype=jnp.int32)
     per_column_map = jnp.repeat(window_map, BLK, axis=0)
-    if ext_count >= total_cols and WIN * BLK <= total_cols:
-        extended = jnp.concatenate(line_gather(key_value, "lon"), axis=3)
-        key_cols = total_cols
-        block_count = total_cols // BLK
-        first_col = lax.axis_index("lon") * columns
-        query_blocks = (first_col + column_ids) // BLK
-        key_blocks = ((first_col + jnp.arange(total_cols, dtype=jnp.int32)) % total_cols) // BLK
-        slots = (key_blocks[None, :] - query_blocks[:, None] + REACH) % block_count
+    full_ring = ext_count >= total_cols and WIN * BLK <= total_cols
+    if full_ring and lon_count == 4:
+        spatial = spatial_line_of_four(own_q, key_value, window_map, scale)
     else:
-        reach_devices = -(-reach_cols // columns)
-        left_parts, right_parts = [], []
-        for step_by in range(1, reach_devices + 1):
-            need = min(columns, reach_cols - (step_by - 1) * columns)
-            left_parts.insert(0, shifted(key_value[:, :, :, columns - need :, :], "lon", step_by))
-            right_parts.append(shifted(key_value[:, :, :, :need, :], "lon", -step_by))
-        extended = jnp.concatenate(left_parts + [key_value] + right_parts, axis=3)
-        key_cols = ext_count
-        ext_ids = jnp.arange(ext_count, dtype=jnp.int32)
-        slots = ext_ids[None, :] // BLK - column_ids[:, None] // BLK
-    picks = slots[:, :, None] == jnp.arange(WIN, dtype=jnp.int32)[None, None, :]
-    active = jnp.any(picks & (per_column_map[:, None, :] > 0), axis=-1)
-    mask = jnp.broadcast_to(
-        active[None, :, None, :].astype(jnp.float32), (lat_rows, columns, lat_rows, key_cols)
-    ).reshape(lat_rows * columns, lat_rows * key_cols)
-    query_flat = own_q.reshape(frames, lat_rows * columns, model_width)
-    key_value_flat = extended.reshape(2, frames, lat_rows * key_cols, model_width)
-    spatial = spatial_attention(query_flat, key_value_flat, mask, scale)
+        if full_ring:
+            extended = jnp.concatenate(line_gather(key_value, "lon"), axis=3)
+            key_cols = total_cols
+            block_count = total_cols // BLK
+            first_col = lax.axis_index("lon") * columns
+            query_blocks = (first_col + column_ids) // BLK
+            key_blocks = ((first_col + jnp.arange(total_cols, dtype=jnp.int32)) % total_cols) // BLK
+            slots = (key_blocks[None, :] - query_blocks[:, None] + REACH) % block_count
+        else:
+            reach_devices = -(-reach_cols // columns)
+            left_parts, right_parts = [], []
+            for step_by in range(1, reach_devices + 1):
+                need = min(columns, reach_cols - (step_by - 1) * columns)
+                left_parts.insert(
+                    0, shifted(key_value[:, :, :, columns - need :, :], "lon", step_by)
+                )
+                right_parts.append(shifted(key_value[:, :, :, :need, :], "lon", -step_by))
+            extended = jnp.concatenate(left_parts + [key_value] + right_parts, axis=3)
+            key_cols = ext_count
+            ext_ids = jnp.arange(ext_count, dtype=jnp.int32)
+            slots = ext_ids[None, :] // BLK - column_ids[:, None] // BLK
+        picks = slots[:, :, None] == jnp.arange(WIN, dtype=jnp.int32)[None, None, :]
+        active = jnp.any(picks & (per_column_map[:, None, :] > 0), axis=-1)
+        query_flat = own_q.reshape(frames, lat_rows * columns, model_width)
+        key_value_flat = extended.reshape(2, frames, lat_rows * key_cols, model_width)
+        spatial = spatial_attention(query_flat, key_value_flat, expand_mask(active, lat_rows), scale)[0]
 
     token_count = lat_rows * columns
     tm_count = lax.axis_size("tm")

time: 144 us -> 158 us (1.097)
  the two profiles are of different devices: /device:TPU:0 before, /device:TPU:17 now
where the time goes in v3:
time: 158 us; the launch traced here: 156 us
  local copies, waits for them, and re-layouts  45.4 us (29%)
  waiting for transfers between devices  39 us (25%)
  other arithmetic  30.3 us (19%)
  Pallas kernels  23.9 us (15%)
  starting transfers between devices  17.5 us (11%)
    pallas_call x2, Pallas kernels, spatial_attention(): pl.pallas_call(functools.partial(spatial_kernel, scale=scale), grid=(fram...  23.9 us
    ppermute x1, waiting for transfers between devices, spatial_line_of_four(): two_away = lax.ppermute(onward, 'lon', [(1, 2), (2, 1)])  21.3 us
    ppermute x1, waiting for transfers between devices, spatial_line_of_four(): guest_map = lax.ppermute(window_map, 'lon', [(0, 1), (3, 2)])  16.3 us
    concatenate x2, other arithmetic, flat_keys(): joined = jnp.concatenate(blocks, axis=3)  10.3 us
    reshape x2, local copies, waits for them, and re-layouts, expand_mask(): return jnp.broadcast_to(active[None, :, None, :].astype(jnp.float32), (la...  9.69 us
    broadcast_in_dim x2, local copies, waits for them, and re-layouts, expand_mask(): jnp.broadcast_to(active[None, :, None, :].astype(jnp.float32), (lat_rows,...  4.97 us
    unnamed x16, local copies, waits for them, and re-layouts  4.74 us
    reshape x2, local copies, waits for them, and re-layouts, local(): key_value_rows = key_value.reshape(2, frames, token_count, head_count, DH)  4.48 us
  transfers between devices with their start and end apart: 9, of which 3 were waited for; matrix products, arithmetic and copies ran while one was open for 41% of the time, Pallas kernels for 8%

profile of v3, /device:TPU:17, one launch (start us, length us, event | category | flops | bytes accessed | tf_op | source)
XLA Modules:
  0.0 156.4 jit_solution(6978628819987836115)
XLA Ops:
  0.0 2.1 %constant_dynamic-update-slice_fusion.1 = bf16[2,1,32,8,1536]{4,3,2,1,0:T(8,128)(2,1)} fusion(bf16[1,1,32,8,1536]{4,3,2,1,0:T(8,128)(2,1)} %param.6), kind=kLoop, calls=%fused_computation.33 | loop fusion | bytes 1572864
  2.1 1.0 constant_dynamic-update-slice_fusion
  3.1 3.2 %collective-permute-start = (bf16[2,1,32,8,1536]{4,3,2,1,0:T(8,128)(2,1)}, bf16[2,1,32,8,1536]{4,3,2,1,0:T(8,128)(2,1)}, u32[]{:S(2)}, u32[]{:S(2)}) collective-permute-start(bf16[2,1,32,8,1536]{4,3,2,1,0:T(8,128)(2,1)} %constant_dynamic-update-slice_fusion), channel_id=1, source_target_pairs={{0,4},{4,8},{8,12},{1,5},{5,9},{9,13},{2,6},{6,10},{10,14},{3,7},{... | collective-permute-start | bytes 4718600 | tf_op jit(solution)/shard_map/ppermute | solution.py:136
  6.3 2.1 %collective-permute-start.1 = (bf16[2,1,32,8,1536]{4,3,2,1,0:T(8,128)(2,1)}, bf16[2,1,32,8,1536]{4,3,2,1,0:T(8,128)(2,1)}, u32[]{:S(2)}, u32[]{:S(2)}) collective-permute-start(bf16[2,1,32,8,1536]{4,3,2,1,0:T(8,128)(2,1)} %constant_dynamic-update-slice_fusion), channel_id=1, source_target_pairs={{12,8},{8,4},{4,0},{13,9},{9,5},{5,1},{14,10},{10,6},{6,2},{15,11}... | collective-permute-start | bytes 4718600 | tf_op jit(solution)/shard_map/ppermute | solution.py:137
  8.4 1.3 collective-permute-start.4
  9.7 2.9 %reshape.667 = bf16[2,1,256,12,128]{4,3,2,0,1:T(8,128)(2,1)S(1)} reshape(bf16[2,1,32,8,1536]{4,3,2,1,0:T(8,128)(2,1)} %constant_dynamic-update-slice_fusion) | data formatting | bytes 3145728 | tf_op jit(solution)/shard_map/reshape | solution.py:243
  12.6 1.6 %copy.28 = bf16[2,1,256,12,128]{4,2,3,1,0:T(8,128)(2,1)} copy(bf16[2,1,256,12,128]{4,3,2,0,1:T(8,128)(2,1)S(1)} %reshape.667) | data formatting | bytes 3145728 | tf_op jit(solution)/shard_map/reshape | solution.py:243
  14.2 1.2 collective-permute-start.7
  15.4 0.0 copy-start.6
  15.4 1.7 %constant_dynamic-update-slice_fusion.2 = bf16[2,2,256,12,128]{4,3,2,0,1:T(8,128)(2,1)} fusion(bf16[2,1,256,12,128]{4,3,2,0,1:T(8,128)(2,1)S(1)} %reshape.667), kind=kLoop, calls=%fused_computation.34 | loop fusion | bytes 3670016
  17.2 0.1 copy.22
  17.4 0.1 tile.10
  17.5 0.1 add_select_fusion.1
  17.6 0.1 fusion.8
  17.7 0.6 gather_fusion
  18.3 0.1 compare_or_fusion
  18.4 2.5 %broadcast_in_dim.31 = f32[32,8,32,32]{3,2,1,0:T(8,128)} broadcast(f32[8,32]{1,0:T(8,128)S(1)} %and_convert_fusion.1), dimensions={1,3} | broadcast | bytes 1049600 | tf_op jit(solution)/shard_map/broadcast_in_dim | solution.py:118
  20.9 4.6 %reshape.662.m_ref = f32[256,1024]{1,0:T(8,128)} reshape(f32[32,8,32,32]{3,2,1,0:T(8,128)} %broadcast_in_dim.31) | data formatting | bytes 2097152 | tf_op jit(solution)/shard_map/reshape | solution.py:120
  25.4 1.6 reshape.669
  27.0 0.1 and_select_fusion.3
  27.1 0.1 add_select_fusion
  27.2 16.3 %collective-permute-done.4 = s32[4,15]{1,0:T(4,128)S(1)} collective-permute-done((s32[4,15]{1,0:T(4,128)S(1)}, s32[4,15]{1,0:T(4,128)S(1)}, u32[]{:S(2)}, u32[]{:S(2)}) %collective-permute-start.4) | collective-permute-done | bytes 272 | tf_op jit(solution)/shard_map/ppermute | solution.py:142
  43.5 0.1 copy.23
  43.6 0.1 fusion.10
  43.7 2.5 %broadcast_in_dim.34 = f32[32,8,32,16]{3,2,1,0:T(8,128)} broadcast(f32[8,16]{1,0:T(8,128)S(1)} %and_convert_fusion), dimensions={1,3} | broadcast | bytes 524800 | tf_op jit(solution)/shard_map/broadcast_in_dim | solution.py:118
  46.2 5.1 %reshape.665.m_ref = f32[256,512]{1,0:T(8,128)} reshape(f32[32,8,32,16]{3,2,1,0:T(8,128)} %broadcast_in_dim.34) | data formatting | bytes 1048576 | tf_op jit(solution)/shard_map/reshape | solution.py:120
  51.3 0.0 collective-permute-done
  51.3 0.0 collective-permute-done.1
  51.3 3.9 %broadcast_select_fusion = (bf16[2,1,32,8,1536]{4,3,2,1,0:T(8,128)(2,1)}, bf16[2,1,32,8,1536]{4,3,2,1,0:T(8,128)(2,1)}) fusion(bf16[2,1,32,8,1536]{4,3,2,1,0:T(8,128)(2,1)} %collective-permute-done.1, bf16[2,1,32,8,1536]{4,3,2,1,0:T(8,128)(2,1)} %collective-permute-done, pred[]{:T(512)S(6)} %eq.63), kind=kLoop, calls=%fused_computation.8 | loop fusion | flops 1572864 | bytes 6291457 | tf_op jit(solution)/shard_map/jit(_where)/select_n | solution.py:156
  55.2 1.9 %collective-permute-start.2 = (bf16[2,1,32,8,1536]{4,3,2,1,0:T(8,128)(2,1)}, bf16[2,1,32,8,1536]{4,3,2,1,0:T(8,128)(2,1)}, u32[]{:S(2)}, u32[]{:S(2)}) collective-permute-start(bf16[2,1,32,8,1536]{4,3,2,1,0:T(8,128)(2,1)} %get-tuple-element.19), channel_id=1, source_target_pairs={{4,8},{8,4},{5,9},{9,5},{6,10},{10,6},{7,11},{11,7},{20,24},{24,20... | collective-permute-start | bytes 4718600 | tf_op jit(solution)/shard_map/ppermute | solution.py:139
  57.2 1.5 collective-permute-start.3
  58.6 0.0 collective-permute-done.7
  58.7 2.6 %copy_dynamic-update-slice_fusion = bf16[2,2,256,12,128]{4,3,2,0,1:T(8,128)(2,1)S(1)} fusion(bf16[2,2,256,12,128]{4,3,2,0,1:T(8,128)(2,1)S(1)} %copy-done, bf16[2,1,256,12,128]{4,2,3,1,0:T(8,128)(2,1)} %collective-permute-done.7), kind=kLoop, calls=%fused_computation.5 | loop fusion | bytes 3670016 | tf_op jit(solution)/shard_map/concatenate | solution.py:247
  61.3 1.2 multiply_reduce_fusion.1
  62.5 0.1 fusion.4
  62.7 0.1 fusion.5
  62.8 2.9 %multiply_reduce_fusion = f32[256,12,128]{2,1,0:T(8,128)S(1)} fusion(bf16[2,2,256,12,128]{4,3,2,0,1:T(8,128)(2,1)S(1)} %copy_dynamic-update-slice_fusion, f32[2,256,12]{2,1,0:T(8,128)S(1)} %get-tuple-element.21), kind=kLoop, calls=%fused_computation.2 | loop fusion | flops 1966080 | bytes 3170304 | tf_op jit(solution)/shard_map/reduce_sum | solution.py:87
  65.8 0.7 fusion
  66.5 1.7 %copy.30 = f32[256,12,128]{0,2,1:T(8,128)} copy(f32[256,12,128]{2,1,0:T(8,128)S(1)} %fusion) | data formatting | bytes 3145728 | tf_op jit(solution)/shard_map/convert_element_type | solution.py:260
  68.2 2.0 %copy.31 = f32[1,256,1536]{2,1,0:T(8,128)S(1)} copy(f32[1,256,1536]{1,2,0:T(8,128)} %bitcast.44) | data formatting | bytes 3145728 | tf_op jit(solution)/shard_map/convert_element_type | solution.py:260
  70.2 21.3 %collective-permute-done.2 = bf16[2,1,32,8,1536]{4,3,2,1,0:T(8,128)(2,1)} collective-permute-done((bf16[2,1,32,8,1536]{4,3,2,1,0:T(8,128)(2,1)}, bf16[2,1,32,8,1536]{4,3,2,1,0:T(8,128)(2,1)}, u32[]{:S(2)}, u32[]{:S(2)}) %collective-permute-start.2) | collective-permute-done | bytes 1572896 | tf_op jit(solution)/shard_map/ppermute | solution.py:139
  91.5 3.6 %pad_maximum_fusion.1 = bf16[2,1,32,16,1536]{4,3,2,1,0:T(8,128)(2,1)} fusion(bf16[2,1,32,8,1536]{4,3,2,1,0:T(8,128)(2,1)} %collective-permute-done.2, bf16[2,1,32,8,1536]{4,3,2,1,0:T(8,128)(2,1)S(1)} %copy-done.1), kind=kLoop, calls=%fused_computation.4 | loop fusion | flops 6291456 | bytes 6291456 | tf_op jit(solution)/shard_map/concatenate | solution.py:124
  95.1 0.0 collective-permute-done.3
  95.1 11.0 %shard_map.56 = (f32[1,256,1536]{2,1,0:T(8,128)}, f32[1,12,256,1]{3,2,1,0:T(8,128)}) custom-call(bf16[1,256,1536]{2,1,0:T(8,128)(2,1)} %bitcast.5.q_ref, bf16[2,1,512,1536]{3,2,1,0:T(8,128)(2,1)} %bitcast.42, bf16[2,1,512,1536]{3,2,1,0:T(8,128)(2,1)} %bitcast.43, f32[256,512]{1,0:T(8,128)} %reshape.665.m_ref), custom_call_target="tpu_custom_call" | custom-call | flops 805306368 | bytes 5505024 | tf_op jit(solution)/shard_map/pallas_call | solution.py:50
  106.1 2.0 %reduce.7 = f32[12,256]{1,0:T(8,128)S(1)} reduce(f32[1,12,256,1]{3,2,1,0:T(8,128)} %get-tuple-element.13, f32[]{:T(128)} %constant.207), dimensions={0,3}, to_apply=%get-tuple-element.13.reduce_sub_computation | reduce | bytes 24580 | tf_op jit(solution)/shard_map/pallas_call | solution.py:50
  108.1 1.3 collective-permute-start.5
  109.4 1.0 convert_element_type.84
  110.4 2.2 %collective-permute-start.6 = (bf16[1,256,1536]{2,1,0:T(8,128)(2,1)}, bf16[1,256,1536]{2,1,0:T(8,128)(2,1)}, u32[]{:S(2)}, u32[]{:S(2)}) collective-permute-start(bf16[1,256,1536]{2,1,0:T(8,128)(2,1)} %convert_element_type.84), channel_id=1, source_target_pairs={{4,0},{8,12},{5,1},{9,13},{6,2},{10,14},{7,3},{11,15},{20,16},{24,... | collective-permute-start | bytes 2359304 | tf_op jit(solution)/shard_map/ppermute | solution.py:163
  112.6 6.7 %pad_maximum_fusion = bf16[2,1,32,32,1536]{4,3,2,1,0:T(8,128)(2,1)} fusion(bf16[2,1,32,8,1536]{4,3,2,1,0:T(8,128)(2,1)} %collective-permute-done.2, bf16[2,1,32,8,1536]{4,3,2,1,0:T(8,128)(2,1)} %collective-permute-done.1, bf16[2,1,32,8,1536]{4,3,2,1,0:T(8,128)(2,1)} %constant_dynamic-update-slice_fusion, bf16[2,1,32,8,1536]{4,3,2,1,0:T(8,128)(2,1)} %collective-permute-done), kind=kLoop, calls=%fused_computation.1 | loop fusion | flops 25165824 | bytes 12582912 | tf_op jit(solution)/shard_map/concatenate | solution.py:124
  119.3 12.9 %shard_map.55 = (f32[1,256,1536]{2,1,0:T(8,128)}, f32[1,12,256,1]{3,2,1,0:T(8,128)}) custom-call(bf16[1,256,1536]{2,1,0:T(8,128)(2,1)} %bitcast.q_ref, bf16[2,1,1024,1536]{3,2,1,0:T(8,128)(2,1)} %bitcast.40, bf16[2,1,1024,1536]{3,2,1,0:T(8,128)(2,1)} %bitcast.41, f32[256,1024]{1,0:T(8,128)} %reshape.662.m_ref), custom_call_target="tpu_custom_call" | custom-call | flops 1610612736 | bytes 8650752 | tf_op jit(solution)/shard_map/pallas_call | solution.py:50
  132.2 1.9 %reduce.6 = f32[12,256]{1,0:T(8,128)S(1)} reduce(f32[1,12,256,1]{3,2,1,0:T(8,128)} %get-tuple-element.11, f32[]{:T(128)} %constant.207), dimensions={0,3}, to_apply=%get-tuple-element.11.reduce_sub_computation | reduce | bytes 24580 | tf_op jit(solution)/shard_map/pallas_call | solution.py:50
  134.1 0.0 collective-permute-done.5
  134.1 1.3 mul.97
  135.4 1.9 %copy.25 = f32[1,256,1536]{2,1,0:T(8,128)S(1)} copy(f32[1,256,1536]{1,2,0:T(8,128)} %bitcast.45) | data formatting | bytes 3145728 | tf_op jit(solution)/shard_map/mul | solution.py:188
  137.3 1.3 mul.100
  138.6 3.0 %copy.26 = f32[1,256,1536]{2,1,0:T(8,128)} copy(f32[1,256,1536]{1,2,0:T(8,128)} %bitcast.46) | data formatting | bytes 3145728 | tf_op jit(solution)/shard_map/mul | solution.py:189
  141.6 1.3 div.96
  142.8 3.0 %copy.27 = f32[1,256,1536]{2,1,0:T(8,128)} copy(f32[1,256,1536]{1,2,0:T(8,128)} %bitcast.47) | data formatting | bytes 3145728 | tf_op jit(solution)/shard_map/div | solution.py:187
  145.9 0.0 collective-permute-done.6
  145.9 3.5 %fusion.3 = bf16[1,32,8,1536]{3,2,1,0:T(8,128)(2,1)S(1)} fusion(f32[1,256,1536]{2,1,0:T(8,128)S(1)} %copy.31, f32[1,256,1536]{2,1,0:T(8,128)} %get-tuple-element.10, f32[1,256,1536]{2,1,0:T(8,128)} %copy.27, f32[1,256,1536]{2,1,0:T(8,128)} %copy.26, bf16[1,256,1536]{2,1,0:T(8,128)(2,1)} %collective-permute-done.6, f32[1,256,1536]{2,1,0:T(8,128)S(1)} %copy.25, ...), kind=kLoop, calls=%fused_computation.15 | loop fusion | flops 3145728 | bytes 9437185 | tf_op jit(solution)/shard_map/reshape | solution.py:262
  149.4 0.9 copy-done.2
  150.3 2.8 %collective-permute-start.8 = (bf16[1,32,8,768]{3,2,1,0:T(8,128)(2,1)S(1)}, bf16[1,32,8,768]{3,2,1,0:T(8,128)(2,1)S(1)}, u32[]{:S(2)}, u32[]{:S(2)}) collective-permute-start(bf16[1,32,8,768]{3,2,1,0:T(8,128)(2,1)S(1)} %constant_dynamic-slice_fusion), channel_id=1, source_target_pairs={{0,1},{1,0},{2,3},{3,2},{4,5},{5,4},{6,7},{7,6},{8,9},{9,8},{10,11... | collective-permute-start | bytes 1179656 | tf_op jit(solution)/shard_map/ppermute | solution.py:25
  153.1 1.3 collective-permute-done.8
  154.5 1.9 %fusion.2 = bf16[1,32,8,768]{3,2,1,0:T(8,128)(2,1)} fusion(bf16[1,32,8,768]{3,2,1,0:T(8,128)(2,1)S(1)} %collective-permute-done.8, bf16[1,32,8,1536]{3,2,1,0:T(8,128)(2,1)} %copy-done.2, s32[]{:T(128)S(6)} %select_n.249, pred[]{:T(512)S(6)} %eq.62), kind=kLoop, calls=%fused_computation.14 | loop fusion | flops 1572864 | bytes 1179653 | tf_op jit(solution)/shard_map/convert_element_type | solution.py:272
  (33 shorter events, 0.3 us)
Async XLA Ops:
  0.0 2.1 %copy-start.4 = (bf16[1,1,32,8,1536]{4,3,2,1,0:T(8,128)(2,1)S(1)}, bf16[1,1,32,8,1536]{4,3,2,1,0:T(8,128)(2,1)}, u32[]{:S(2)}) copy-start(bf16[1,1,32,8,1536]{4,3,2,1,0:T(8,128)(2,1)} %param.7) | copy-start | bytes 2359300
  0.0 8.4 %copy-start.5 = (s32[4,15]{1,0:T(4,128)S(1)}, s32[4,15]{1,0:T(4,128)}, u32[]{:S(2)}) copy-start(s32[4,15]{1,0:T(4,128)} %param.8) | copy-start | bytes 724
  3.1 48.2 %collective-permute-start = (bf16[2,1,32,8,1536]{4,3,2,1,0:T(8,128)(2,1)}, bf16[2,1,32,8,1536]{4,3,2,1,0:T(8,128)(2,1)}, u32[]{:S(2)}, u32[]{:S(2)}) collective-permute-start(bf16[2,1,32,8,1536]{4,3,2,1,0:T(8,128)(2,1)} %constant_dynamic-update-slice_fusion), channel_id=1, source_target_pairs={{0,4},{4,8},{8,12},{1,5},{5,9},{9,13},{2,6},{6,10},{10,14},{3,7},{... | collective-permute-start | bytes 4718600 | tf_op jit(solution)/shard_map/ppermute | solution.py:136
  6.3 45.0 %collective-permute-start.1 = (bf16[2,1,32,8,1536]{4,3,2,1,0:T(8,128)(2,1)}, bf16[2,1,32,8,1536]{4,3,2,1,0:T(8,128)(2,1)}, u32[]{:S(2)}, u32[]{:S(2)}) collective-permute-start(bf16[2,1,32,8,1536]{4,3,2,1,0:T(8,128)(2,1)} %constant_dynamic-update-slice_fusion), channel_id=1, source_target_pairs={{12,8},{8,4},{4,0},{13,9},{9,5},{5,1},{14,10},{10,6},{6,2},{15,11}... | collective-permute-start | bytes 4718600 | tf_op jit(solution)/shard_map/ppermute | solution.py:137
  8.4 35.1 %collective-permute-start.4 = (s32[4,15]{1,0:T(4,128)S(1)}, s32[4,15]{1,0:T(4,128)S(1)}, u32[]{:S(2)}, u32[]{:S(2)}) collective-permute-start(s32[4,15]{1,0:T(4,128)S(1)} %copy-done.5), channel_id=1, source_target_pairs={{0,4},{12,8},{1,5},{13,9},{2,6},{14,10},{3,7},{15,11},{16,20},{28,... | collective-permute-start | bytes 728 | tf_op jit(solution)/shard_map/ppermute | solution.py:142
  14.2 44.5 %collective-permute-start.7 = (bf16[2,1,256,12,128]{4,2,3,1,0:T(8,128)(2,1)}, bf16[2,1,256,12,128]{4,2,3,1,0:T(8,128)(2,1)}, u32[]{:S(2)}, u32[]{:S(2)}) collective-permute-start(bf16[2,1,256,12,128]{4,2,3,1,0:T(8,128)(2,1)} %copy.28), channel_id=1, source_target_pairs={{0,2},{2,0},{1,3},{3,1},{4,6},{6,4},{5,7},{7,5},{8,10},{10,8},{9,1... | collective-permute-start | bytes 4718600 | tf_op jit(solution)/shard_map/ppermute | solution.py:21
  15.4 2.0 %copy-start.6 = (s32[2,8]{1,0:T(2,128)S(1)}, s32[2,8]{1,0:T(2,128)}, u32[]{:S(2)}) copy-start(s32[2,8]{1,0:T(2,128)} %param.9) | copy-start | bytes 196
  51.3 7.3 %copy-start = (bf16[2,2,256,12,128]{4,3,2,0,1:T(8,128)(2,1)S(1)}, bf16[2,2,256,12,128]{4,3,2,0,1:T(8,128)(2,1)}, u32[]{:S(2)}) copy-start(bf16[2,2,256,12,128]{4,3,2,0,1:T(8,128)(2,1)} %constant_dynamic-update-slice_fusion.2) | copy-start | bytes 9437188
  55.2 36.2 %collective-permute-start.2 = (bf16[2,1,32,8,1536]{4,3,2,1,0:T(8,128)(2,1)}, bf16[2,1,32,8,1536]{4,3,2,1,0:T(8,128)(2,1)}, u32[]{:S(2)}, u32[]{:S(2)}) collective-permute-start(bf16[2,1,32,8,1536]{4,3,2,1,0:T(8,128)(2,1)} %get-tuple-element.19), channel_id=1, source_target_pairs={{4,8},{8,4},{5,9},{9,5},{6,10},{10,6},{7,11},{11,7},{20,24},{24,20... | collective-permute-start | bytes 4718600 | tf_op jit(solution)/shard_map/ppermute | solution.py:139
  57.2 38.0 %collective-permute-start.3 = (bf16[1,32,8,1536]{3,2,1,0:T(8,128)(2,1)}, bf16[1,32,8,1536]{3,2,1,0:T(8,128)(2,1)}, u32[]{:S(2)}, u32[]{:S(2)}) collective-permute-start(bf16[1,32,8,1536]{3,2,1,0:T(8,128)(2,1)} %bitcast.4), channel_id=1, source_target_pairs={{0,4},{12,8},{1,5},{13,9},{2,6},{14,10},{3,7},{15,11},{16,20},{28,... | collective-permute-start | bytes 2359304 | tf_op jit(solution)/shard_map/ppermute | solution.py:141
  68.2 23.3 %copy-start.1 = (bf16[2,1,32,8,1536]{4,3,2,1,0:T(8,128)(2,1)S(1)}, bf16[2,1,32,8,1536]{4,3,2,1,0:T(8,128)(2,1)}, u32[]{:S(2)}) copy-start(bf16[2,1,32,8,1536]{4,3,2,1,0:T(8,128)(2,1)} %get-tuple-element.18) | copy-start | bytes 4718596
  106.1 3.3 %copy-start.3 = (f32[1,256,1536]{2,1,0:T(8,128)S(1)}, f32[1,256,1536]{2,1,0:T(8,128)}, u32[]{:S(2)}) copy-start(f32[1,256,1536]{2,1,0:T(8,128)} %get-tuple-element.14) | copy-start | bytes 4718596
  108.1 26.0 %collective-permute-start.5 = (f32[1,12,256]{2,1,0:T(8,128)S(1)}, f32[1,12,256]{2,1,0:T(8,128)S(1)}, u32[]{:S(2)}, u32[]{:S(2)}) collective-permute-start(f32[1,12,256]{2,1,0:T(8,128)S(1)} %bitcast.48), channel_id=1, source_target_pairs={{4,0},{8,12},{5,1},{9,13},{6,2},{10,14},{7,3},{11,15},{20,16},{24,... | collective-permute-start | bytes 36872 | tf_op jit(solution)/shard_map/ppermute | solution.py:163
  110.4 35.5 %collective-permute-start.6 = (bf16[1,256,1536]{2,1,0:T(8,128)(2,1)}, bf16[1,256,1536]{2,1,0:T(8,128)(2,1)}, u32[]{:S(2)}, u32[]{:S(2)}) collective-permute-start(bf16[1,256,1536]{2,1,0:T(8,128)(2,1)} %convert_element_type.84), channel_id=1, source_target_pairs={{4,0},{8,12},{5,1},{9,13},{6,2},{10,14},{7,3},{11,15},{20,16},{24,... | collective-permute-start | bytes 2359304 | tf_op jit(solution)/shard_map/ppermute | solution.py:163
  149.4 0.9 copy-start.2
  150.3 4.2 %collective-permute-start.8 = (bf16[1,32,8,768]{3,2,1,0:T(8,128)(2,1)S(1)}, bf16[1,32,8,768]{3,2,1,0:T(8,128)(2,1)S(1)}, u32[]{:S(2)}, u32[]{:S(2)}) collective-permute-start(bf16[1,32,8,768]{3,2,1,0:T(8,128)(2,1)S(1)} %constant_dynamic-slice_fusion), channel_id=1, source_target_pairs={{0,1},{1,0},{2,3},{3,2},{4,5},{5,4},{6,7},{7,6},{8,9},{9,8},{10,11... | collective-permute-start | bytes 1179656 | tf_op jit(solution)/shard_map/ppermute | solution.py:25

commit v4 on v3

--- a/solution.py
+++ b/solution.py
@@ -25,44 +25,59 @@
     return lax.ppermute(value, axis, [(i, i ^ 1 << bit) for i in range(lax.axis_size(axis))])
 
 
+def group_width(model_width):
+    for width in (512, 384, 256):
+        if model_width % width == 0:
+            return width
+    return DH
+
+
 def spatial_kernel(q_ref, k_ref, v_ref, m_ref, o_ref, lse_ref, *, scale):
-    scores = (
-        lax.dot_general(
-            q_ref[...], k_ref[...], (((1,), (1,)), ((), ())), preferred_element_type=jnp.float32
-        )
-        * scale
-    )
-    limited = jnp.where(m_ref[...] > 0, scores, masked_score)
-    maxima = jnp.max(limited, axis=-1, keepdims=True)
-    weights = jnp.exp(limited - maxima)
-    totals = jnp.sum(weights, axis=-1, keepdims=True)
-    result = jnp.dot(
-        weights.astype(jnp.bfloat16), v_ref[...], preferred_element_type=jnp.float32
-    )
-    o_ref[...] = result / totals
-    lse_ref[...] = maxima + jnp.log(totals)
+    allowed = m_ref[...] > 0
+    for head in range(q_ref.shape[-1] // DH):
+        lanes = slice(head * DH, (head + 1) * DH)
+        scores = (
+            lax.dot_general(
+                q_ref[:, lanes],
+                k_ref[:, lanes],
+                (((1,), (1,)), ((), ())),
+                preferred_element_type=jnp.float32,
+            )
+            * scale
+        )
+        limited = jnp.where(allowed, scores, masked_score)
+        maxima = jnp.max(limited, axis=-1, keepdims=True)
+        weights = jnp.exp(limited - maxima)
+        totals = jnp.sum(weights, axis=-1, keepdims=True)
+        result = jnp.dot(
+            weights.astype(jnp.bfloat16), v_ref[:, lanes], preferred_element_type=jnp.float32
+        )
+        o_ref[:, lanes] = result / totals
+        lse_ref[:, head : head + 1] = maxima + jnp.log(totals)
 
 
 def spatial_attention(query_flat, key_value_flat, mask, scale):
     frames, query_count, model_width = query_flat.shape
     key_count = key_value_flat.shape[2]
     head_count = model_width // DH
+    width = group_width(model_width)
+    groups = model_width // width
     return pl.pallas_call(
         functools.partial(spatial_kernel, scale=scale),
-        grid=(frames, head_count),
+        grid=(frames, groups),
         in_specs=[
-            pl.BlockSpec((None, query_count, DH), lambda f, h: (f, 0, h)),
-            pl.BlockSpec((None, None, key_count, DH), lambda f, h: (0, f, 0, h)),
-            pl.BlockSpec((None, None, key_count, DH), lambda f, h: (1, f, 0, h)),
-            pl.BlockSpec((query_count, key_count), lambda f, h: (0, 0)),
+            pl.BlockSpec((None, query_count, width), lambda f, g: (f, 0, g)),
+            pl.BlockSpec((None, None, key_count, width), lambda f, g: (0, f, 0, g)),
+            pl.BlockSpec((None, None, key_count, width), lambda f, g: (1, f, 0, g)),
+            pl.BlockSpec((query_count, key_count), lambda f, g: (0, 0)),
         ],
         out_specs=[
-            pl.BlockSpec((None, query_count, DH), lambda f, h: (f, 0, h)),
-            pl.BlockSpec((None, None, query_count, 1), lambda f, h: (f, h, 0, 0)),
+            pl.BlockSpec((None, query_count, width), lambda f, g: (f, 0, g)),
+            pl.BlockSpec((None, None, query_count, width // DH), lambda f, g: (f, g, 0, 0)),
         ],
         out_shape=[
             jax.ShapeDtypeStruct((frames, query_count, model_width), jnp.float32),
-            jax.ShapeDtypeStruct((frames, head_count, query_count, 1), jnp.float32),
+            jax.ShapeDtypeStruct((frames, groups, query_count, width // DH), jnp.float32),
         ],
         cost_estimate=pl.CostEstimate(
             flops=4 * frames * query_count * key_count * model_width,
@@ -71,6 +86,42 @@
             + 4 * frames * query_count * model_width,
         ),
     )(query_flat, key_value_flat, key_value_flat, mask)
+
+
+def combine_kernel(*refs):
+    *parts, temporal_ref, mixed_ref = refs
+    outs, lses = parts[0::2], parts[1::2]
+    for head in range(mixed_ref.shape[-1] // DH):
+        lanes = slice(head * DH, (head + 1) * DH)
+        logs = [lse[:, head : head + 1] for lse in lses]
+        top = functools.reduce(jnp.maximum, logs)
+        weights = [jnp.exp(log - top) for log in logs]
+        total = functools.reduce(jnp.add, weights)
+        value = functools.reduce(
+            jnp.add,
+            [w * o[:, lanes].astype(jnp.float32) for w, o in zip(weights, outs)],
+        )
+        mixed_ref[:, lanes] = (value / total + temporal_ref[:, lanes].astype(jnp.float32)).astype(
+            mixed_ref.dtype
+        )
+
+
+def combine_partials(partials, temporal):
+    frames, query_count, model_width = temporal.shape
+    width = group_width(model_width)
+    groups = model_width // width
+    big = pl.BlockSpec((None, query_count, width), lambda f, g: (f, 0, g))
+    small = pl.BlockSpec((None, None, query_count, width // DH), lambda f, g: (f, g, 0, 0))
+    operands = []
+    for out, lse in partials:
+        operands += [out, lse]
+    return pl.pallas_call(
+        combine_kernel,
+        grid=(frames, groups),
+        in_specs=[big, small] * len(partials) + [big],
+        out_specs=big,
+        out_shape=jax.ShapeDtypeStruct((frames, query_count, model_width), jnp.bfloat16),
+    )(*operands, temporal)
 
 
 def temporal_attention(own_q, all_k, all_v, valid, own_ids, all_ids, scale):
@@ -128,24 +179,43 @@
 
 def spatial_line_of_four(own_q, key_value, window_map, scale):
     frames, lat_rows, columns, model_width = own_q.shape
-    head_count = model_width // DH
     count = 4
     total_cols = count * columns
     index = lax.axis_index("lon")
     is_middle = (index >= 1) & (index <= count - 2)
+    column_ids = jnp.arange(columns, dtype=jnp.int32)
+    own_map = jnp.repeat(window_map, BLK, axis=0)
+    own_cols = index * columns + column_ids
+    query_flat = own_q.reshape(frames, lat_rows * columns, model_width)
+
     from_left = lax.ppermute(key_value, "lon", [(0, 1), (1, 2), (2, 3)])
     from_right = lax.ppermute(key_value, "lon", [(3, 2), (2, 1), (1, 0)])
+    guest_map = lax.ppermute(window_map, "lon", [(0, 1), (3, 2)])
+
+    near_cols = ((index - 1) * columns + jnp.arange(3 * columns, dtype=jnp.int32)) % total_cols
+    near_valid = jnp.stack([index >= 1, index >= 0, index <= count - 2])
+    near_active = window_mask(own_cols, near_cols, own_map, total_cols, lat_rows) & jnp.repeat(
+        near_valid, columns
+    )[None, :]
+    near_part = spatial_attention(
+        query_flat,
+        flat_keys([from_left, key_value, from_right]),
+        expand_mask(near_active, lat_rows),
+        scale,
+    )
+
     onward = jnp.where(index == 1, from_left, from_right)
     two_away = lax.ppermute(onward, "lon", [(1, 2), (2, 1)])
     held_q, _ = lax.optimization_barrier((own_q, from_left))
     guest_q = lax.ppermute(held_q, "lon", [(0, 1), (3, 2)])
-    guest_map = lax.ppermute(window_map, "lon", [(0, 1), (3, 2)])
-
-    column_ids = jnp.arange(columns, dtype=jnp.int32)
+    near_part, two_away, guest_q = lax.optimization_barrier((near_part, two_away, guest_q))
+
     guest_device = jnp.where(index == 1, 0, count - 1)
     near_block = jnp.where(index == 1, index + 1, index - 1)
     far_block = (index + 2) % count
-    guest_key_cols = jnp.concatenate([near_block * columns + column_ids, far_block * columns + column_ids])
+    guest_key_cols = jnp.concatenate(
+        [near_block * columns + column_ids, far_block * columns + column_ids]
+    )
     guest_active = window_mask(
         guest_device * columns + column_ids,
         guest_key_cols,
@@ -160,36 +230,22 @@
         expand_mask(guest_active, lat_rows),
         scale,
     )
+    lse_shape = guest_lse.shape
     returned, returned_lse = lax.ppermute(
-        (guest_out.astype(jnp.bfloat16), guest_lse.reshape(frames, head_count, lat_rows * columns)),
+        (guest_out.astype(jnp.bfloat16), jnp.swapaxes(guest_lse, 2, 3)),
         "lon",
         [(1, 0), (2, 3)],
     )
-
-    rel_cols = ((index - 1) * columns + jnp.arange(total_cols, dtype=jnp.int32)) % total_cols
-    rel_block = jnp.arange(total_cols, dtype=jnp.int32) // columns
-    block_valid = jnp.stack([index >= 1, index >= 0, index <= count - 2, is_middle])
-    own_active = window_mask(
-        index * columns + column_ids, rel_cols, jnp.repeat(window_map, BLK, axis=0), total_cols, lat_rows
-    ) & block_valid[rel_block][None, :]
-    own_out, own_lse = spatial_attention(
-        own_q.reshape(frames, lat_rows * columns, model_width),
-        flat_keys([from_left, key_value, from_right, two_away]),
-        expand_mask(own_active, lat_rows),
-        scale,
-    )
-    own_lse = jnp.transpose(own_lse[..., 0], (0, 2, 1))[..., None]
-    returned_lse = jnp.transpose(returned_lse, (0, 2, 1))[..., None]
-    top = jnp.maximum(own_lse, returned_lse)
-    own_weight = jnp.exp(own_lse - top)
-    returned_weight = jnp.exp(returned_lse - top)
-    shape4 = (frames, lat_rows * columns, head_count, DH)
-    joined = (
-        own_weight * own_out.reshape(shape4)
-        + returned_weight * returned.astype(jnp.float32).reshape(shape4)
-    ) / (own_weight + returned_weight)
-    spatial = jnp.where(is_middle, own_out, joined.reshape(own_out.shape))
-    return spatial
+    returned_lse = jnp.where(is_middle, masked_score, jnp.swapaxes(returned_lse, 2, 3))
+    assert returned_lse.shape == lse_shape
+
+    far_active = window_mask(
+        own_cols, far_block * columns + column_ids, own_map, total_cols, lat_rows
+    ) & is_middle
+    far_part = spatial_attention(
+        query_flat, flat_keys([two_away]), expand_mask(far_active, lat_rows), scale
+    )
+    return [near_part, far_part, (returned, returned_lse)]
 
 
 def local(queries, keys, values, window_map, frame_valid):
@@ -208,7 +264,7 @@
     per_column_map = jnp.repeat(window_map, BLK, axis=0)
     full_ring = ext_count >= total_cols and WIN * BLK <= total_cols
     if full_ring and lon_count == 4:
-        spatial = spatial_line_of_four(own_q, key_value, window_map, scale)
+        partials = spatial_line_of_four(own_q, key_value, window_map, scale)
     else:
         if full_ring:
             extended = jnp.concatenate(line_gather(key_value, "lon"), axis=3)
@@ -235,7 +291,9 @@
         active = jnp.any(picks & (per_column_map[:, None, :] > 0), axis=-1)
         query_flat = own_q.reshape(frames, lat_rows * columns, model_width)
         key_value_flat = extended.reshape(2, frames, lat_rows * key_cols, model_width)
-        spatial = spatial_attention(query_flat, key_value_flat, expand_mask(active, lat_rows), scale)[0]
+        partials = [
+            spatial_attention(query_flat, key_value_flat, expand_mask(active, lat_rows), scale)
+        ]
 
     token_count = lat_rows * columns
     tm_count = lax.axis_size("tm")
@@ -257,10 +315,8 @@
         frame_ids,
         scale,
     )
-    temporal = temporal.reshape(frames, token_count, model_width).astype(jnp.float32)
-    mixed = (
-        (spatial + temporal).astype(jnp.bfloat16).reshape(frames, lat_rows, columns, model_width)
-    )
+    temporal = temporal.reshape(frames, token_count, model_width)
+    mixed = combine_partials(partials, temporal).reshape(frames, lat_rows, columns, model_width)
     half_width = model_width // 2
     branch_index = lax.axis_index("branch")
     own_half = lax.dynamic_slice_in_dim(mixed, branch_index * half_width, half_width, 3)

time: 158 us -> 137 us (0.87)
  the two profiles are of different devices: /device:TPU:17 before, /device:TPU:0 now
where the time goes in v4:
time: 137 us
  local copies, waits for them, and re-layouts  41.9 us (31%)
  Pallas kernels  26 us (19%)
  other arithmetic  25.7 us (19%)
  starting transfers between devices  23.1 us (17%)
  waiting for transfers between devices  19.6 us (14%)
    pallas_call x3, Pallas kernels, spatial_attention(): pl.pallas_call(functools.partial(spatial_kernel, scale=scale), grid=(fram...  20.6 us
    reshape x3, local copies, waits for them, and re-layouts, expand_mask(): return jnp.broadcast_to(active[None, :, None, :].astype(jnp.float32), (la...  14.5 us
    ppermute x2, waiting for transfers between devices, spatial_line_of_four(): lax.ppermute((guest_out.astype(jnp.bfloat16), jnp.swapaxes(guest_lse, 2,...  13.7 us
    ppermute x1, starting transfers between devices, spatial_line_of_four(): guest_q = lax.ppermute(held_q, 'lon', [(0, 1), (3, 2)])  7.44 us
    broadcast_in_dim x3, local copies, waits for them, and re-layouts, expand_mask(): jnp.broadcast_to(active[None, :, None, :].astype(jnp.float32), (lat_rows,...  7.34 us
    concatenate x2, other arithmetic, flat_keys(): joined = jnp.concatenate(blocks, axis=3)  7.11 us
    ppermute x1, starting transfers between devices, spatial_line_of_four(): from_left = lax.ppermute(key_value, 'lon', [(0, 1), (1, 2), (2, 3)])  6.76 us
    pallas_call x1, Pallas kernels, combine_partials(): pl.pallas_call(combine_kernel, grid=(frames, groups), in_specs=[big, smal...  5.37 us
  transfers between devices with their start and end apart: 9, of which 3 were waited for; matrix products, arithmetic and copies ran while one was open for 41% of the time, Pallas kernels for 10%

profile of v4, /device:TPU:0, one launch (start us, length us, event | category | flops | bytes accessed | tf_op | source)
XLA Modules:
  0.0 136.6 jit_solution(3638249833006455666)
XLA Ops:
  0.0 2.1 %constant_dynamic-update-slice_fusion.1 = bf16[2,1,32,8,1536]{4,3,2,1,0:T(8,128)(2,1)} fusion(bf16[1,1,32,8,1536]{4,3,2,1,0:T(8,128)(2,1)} %param.6), kind=kLoop, calls=%fused_computation.29 | loop fusion | bytes 1572864
  2.1 0.9 constant_dynamic-update-slice_fusion
  3.1 1.3 collective-permute-start.1
  4.4 6.8 %collective-permute-start = (bf16[2,1,32,8,1536]{4,3,2,1,0:T(8,128)(2,1)}, bf16[2,1,32,8,1536]{4,3,2,1,0:T(8,128)(2,1)}, u32[]{:S(2)}, u32[]{:S(2)}) collective-permute-start(bf16[2,1,32,8,1536]{4,3,2,1,0:T(8,128)(2,1)} %constant_dynamic-update-slice_fusion), channel_id=1, source_target_pairs={{0,4},{4,8},{8,12},{1,5},{5,9},{9,13},{2,6},{6,10},{10,14},{3,7},{... | collective-permute-start | bytes 4718600 | tf_op jit(solution)/shard_map/ppermute | solution.py:191
  11.1 2.7 %collective-permute-start.4 = (s32[4,15]{1,0:T(4,128)S(1)}, s32[4,15]{1,0:T(4,128)S(1)}, u32[]{:S(2)}, u32[]{:S(2)}) collective-permute-start(s32[4,15]{1,0:T(4,128)S(1)} %copy-done.6), channel_id=1, source_target_pairs={{0,4},{12,8},{1,5},{13,9},{2,6},{14,10},{3,7},{15,11},{16,20},{28,... | collective-permute-start | bytes 728 | tf_op jit(solution)/shard_map/ppermute | solution.py:193
  13.9 2.9 %reshape.629 = bf16[2,1,256,12,128]{4,3,2,0,1:T(8,128)(2,1)S(1)} reshape(bf16[2,1,32,8,1536]{4,3,2,1,0:T(8,128)(2,1)} %constant_dynamic-update-slice_fusion) | data formatting | bytes 3145728 | tf_op jit(solution)/shard_map/reshape | solution.py:301
  16.8 1.6 %copy.13 = bf16[2,1,256,12,128]{4,2,3,1,0:T(8,128)(2,1)} copy(bf16[2,1,256,12,128]{4,3,2,0,1:T(8,128)(2,1)S(1)} %reshape.629) | data formatting | bytes 3145728 | tf_op jit(solution)/shard_map/reshape | solution.py:301
  18.4 1.5 %collective-permute-start.7 = (bf16[2,1,256,12,128]{4,2,3,1,0:T(8,128)(2,1)}, bf16[2,1,256,12,128]{4,2,3,1,0:T(8,128)(2,1)}, u32[]{:S(2)}, u32[]{:S(2)}) collective-permute-start(bf16[2,1,256,12,128]{4,2,3,1,0:T(8,128)(2,1)} %copy.13), channel_id=1, source_target_pairs={{0,2},{2,0},{1,3},{3,1},{4,6},{6,4},{5,7},{7,5},{8,10},{10,8},{9,1... | collective-permute-start | bytes 4718600 | tf_op jit(solution)/shard_map/ppermute | solution.py:21
  19.9 1.7 %constant_dynamic-update-slice_fusion.2 = bf16[2,2,256,12,128]{4,3,2,0,1:T(8,128)(2,1)} fusion(bf16[2,1,256,12,128]{4,3,2,0,1:T(8,128)(2,1)S(1)} %reshape.629), kind=kLoop, calls=%fused_computation.30 | loop fusion | bytes 3670016
  21.7 0.1 copy.11
  21.8 0.1 pad_add_fusion
  21.9 0.1 broadcast_in_dim.35
  22.0 0.1 and.261
  22.1 0.1 add_select_fusion.2
  22.1 0.1 add_select_fusion.1
  22.2 0.3 fusion.10
  22.5 0.1 tile.10
  22.6 0.1 fusion.6
  22.7 0.6 gather_fusion
  23.4 0.1 compare_or_fusion
  23.5 2.4 %broadcast_in_dim.36 = f32[32,8,32,24]{3,2,1,0:T(8,128)} broadcast(f32[8,24]{1,0:T(8,128)S(1)} %and_convert_fusion.2), dimensions={1,3} | broadcast | bytes 787200 | tf_op jit(solution)/shard_map/broadcast_in_dim | solution.py:169
  25.9 4.6 %reshape.623.m_ref = f32[256,768]{1,0:T(8,128)} reshape(f32[32,8,32,24]{3,2,1,0:T(8,128)} %broadcast_in_dim.36) | data formatting | bytes 1572864 | tf_op jit(solution)/shard_map/reshape | solution.py:171
  30.5 2.4 %broadcast_in_dim.37 = f32[32,8,32,8]{3,2,1,0:T(8,128)} broadcast(f32[8,8]{1,0:T(8,128)S(1)} %and_convert_fusion.1), dimensions={1,3} | broadcast | bytes 262400 | tf_op jit(solution)/shard_map/broadcast_in_dim | solution.py:169
  33.0 4.8 %reshape.625.m_ref = f32[256,256]{1,0:T(8,128)} reshape(f32[32,8,32,8]{3,2,1,0:T(8,128)} %broadcast_in_dim.37) | data formatting | bytes 524288 | tf_op jit(solution)/shard_map/reshape | solution.py:171
  37.7 1.8 %reshape.631 = f32[256,12,128]{2,1,0:T(8,128)} reshape(bf16[1,1,32,8,1536]{4,3,2,1,0:T(8,128)(2,1)S(1)} %copy-done.1) | data formatting | bytes 2359296 | tf_op jit(solution)/shard_map/convert_element_type | solution.py:128
  39.6 0.1 and_select_fusion.3
  39.7 0.1 add_select_fusion
  39.8 4.1 %collective-permute-done.4 = s32[4,15]{1,0:T(4,128)S(1)} collective-permute-done((s32[4,15]{1,0:T(4,128)S(1)}, s32[4,15]{1,0:T(4,128)S(1)}, u32[]{:S(2)}, u32[]{:S(2)}) %collective-permute-start.4) | collective-permute-done | bytes 272 | tf_op jit(solution)/shard_map/ppermute | solution.py:193
  43.9 0.1 copy.12
  44.0 0.1 fusion.8
  44.1 0.0 collective-permute-done.1
  44.1 0.0 collective-permute-done
  44.2 3.7 %broadcast_select_fusion = (bf16[2,1,32,8,1536]{4,3,2,1,0:T(8,128)(2,1)}, bf16[2,1,32,8,1536]{4,3,2,1,0:T(8,128)(2,1)}) fusion(bf16[2,1,32,8,1536]{4,3,2,1,0:T(8,128)(2,1)} %collective-permute-done.1, bf16[2,1,32,8,1536]{4,3,2,1,0:T(8,128)(2,1)} %collective-permute-done, pred[]{:T(512)S(6)} %eq.81), kind=kLoop, calls=%fused_computation.7 | loop fusion | flops 1572864 | bytes 6291457 | tf_op jit(solution)/shard_map/jit(_where)/select_n | solution.py:226
  47.9 0.7 collective-permute-start.2
  48.7 2.4 %broadcast_in_dim.39 = f32[32,8,32,16]{3,2,1,0:T(8,128)} broadcast(f32[8,16]{1,0:T(8,128)S(1)} %and_convert_fusion), dimensions={1,3} | broadcast | bytes 524800 | tf_op jit(solution)/shard_map/broadcast_in_dim | solution.py:169
  51.1 5.1 %reshape.628.m_ref = f32[256,512]{1,0:T(8,128)} reshape(f32[32,8,32,16]{3,2,1,0:T(8,128)} %broadcast_in_dim.39) | data formatting | bytes 1048576 | tf_op jit(solution)/shard_map/reshape | solution.py:171
  56.2 7.4 %collective-permute-start.3 = (bf16[1,32,8,1536]{3,2,1,0:T(8,128)(2,1)S(1)}, bf16[1,32,8,1536]{3,2,1,0:T(8,128)(2,1)S(1)}, u32[]{:S(2)}, u32[]{:S(2)}) collective-permute-start(bf16[1,32,8,1536]{3,2,1,0:T(8,128)(2,1)S(1)} %bitcast.36), channel_id=1, source_target_pairs={{0,4},{12,8},{1,5},{13,9},{2,6},{14,10},{3,7},{15,11},{16,20},{28,... | collective-permute-start | bytes 2359304 | tf_op jit(solution)/shard_map/ppermute | solution.py:210
  63.6 0.0 collective-permute-done.7
  63.7 3.9 %copy_dynamic-update-slice_fusion = bf16[2,2,256,12,128]{4,3,2,0,1:T(8,128)(2,1)} fusion(bf16[2,2,256,12,128]{4,3,2,0,1:T(8,128)(2,1)} %constant_dynamic-update-slice_fusion.2, bf16[2,1,256,12,128]{4,2,3,1,0:T(8,128)(2,1)} %collective-permute-done.7), kind=kLoop, calls=%fused_computation.5 | loop fusion | bytes 3670016 | tf_op jit(solution)/shard_map/concatenate | solution.py:305
  67.6 4.8 %pad_maximum_fusion = bf16[2,1,32,24,1536]{4,3,2,1,0:T(8,128)(2,1)} fusion(bf16[2,1,32,8,1536]{4,3,2,1,0:T(8,128)(2,1)} %collective-permute-done.1, bf16[2,1,32,8,1536]{4,3,2,1,0:T(8,128)(2,1)} %constant_dynamic-update-slice_fusion, bf16[2,1,32,8,1536]{4,3,2,1,0:T(8,128)(2,1)} %collective-permute-done), kind=kLoop, calls=%fused_computation.1 | loop fusion | flops 14155776 | bytes 9437184 | tf_op jit(solution)/shard_map/concatenate | solution.py:175
  72.3 8.5 %shard_map.55 = (f32[1,256,1536]{2,1,0:T(8,128)}, f32[1,3,256,4]{3,2,1,0:T(8,128)}) custom-call(bf16[1,256,1536]{2,1,0:T(8,128)(2,1)} %bitcast.34, bf16[2,1,768,1536]{3,2,1,0:T(8,128)(2,1)} %bitcast.28, bf16[2,1,768,1536]{3,2,1,0:T(8,128)(2,1)} %bitcast.29, f32[256,768]{1,0:T(8,128)} %reshape.623.m_ref), custom_call_target="tpu_custom_call" | custom-call | flops 1207959552 | bytes 7077888 | tf_op jit(solution)/shard_map/pallas_call | solution.py:65
  80.8 3.5 %multiply_reduce_fusion.1 = f32[2,256,12]{2,1,0:T(8,128)S(1)} fusion(bf16[2,2,256,12,128]{4,3,2,0,1:T(8,128)(2,1)} %copy_dynamic-update-slice_fusion, f32[256,12,128]{2,1,0:T(8,128)} %reshape.631), kind=kLoop, calls=%fused_computation.3 | loop fusion | flops 2353152 | bytes 3170304 | tf_op jit(solution)/shard_map/reduce_sum | solution.py:130
  84.3 0.1 fusion.2
  84.5 0.1 fusion.3
  84.6 0.0 collective-permute-done.3
  84.6 0.0 collective-permute-done.2
  84.7 2.3 %pad_maximum_fusion.1 = bf16[2,1,32,16,1536]{4,3,2,1,0:T(8,128)(2,1)} fusion(bf16[2,1,32,8,1536]{4,3,2,1,0:T(8,128)(2,1)S(1)} %collective-permute-done.2, bf16[2,1,32,8,1536]{4,3,2,1,0:T(8,128)(2,1)S(1)} %copy-done.2), kind=kLoop, calls=%fused_computation.4 | loop fusion | flops 6291456 | bytes 6291456 | tf_op jit(solution)/shard_map/concatenate | solution.py:175
  87.0 6.9 %shard_map.57 = (f32[1,256,1536]{2,1,0:T(8,128)}, f32[1,3,256,4]{3,2,1,0:T(8,128)}) custom-call(bf16[1,256,1536]{2,1,0:T(8,128)(2,1)} %bitcast.40, bf16[2,1,512,1536]{3,2,1,0:T(8,128)(2,1)} %bitcast.30, bf16[2,1,512,1536]{3,2,1,0:T(8,128)(2,1)} %bitcast.31, f32[256,512]{1,0:T(8,128)} %reshape.628.m_ref), custom_call_target="tpu_custom_call" | custom-call | flops 805306368 | bytes 5505024 | tf_op jit(solution)/shard_map/pallas_call | solution.py:65
  93.8 2.4 %convert_element_type.74 = bf16[1,256,1536]{2,1,0:T(8,128)(2,1)} convert(f32[1,256,1536]{2,1,0:T(8,128)} %get-tuple-element.25) | non-fusion elementwise | flops 393216 | bytes 2359296 | tf_op jit(solution)/shard_map/convert_element_type | solution.py:235
  96.2 1.3 collective-permute-start.5
  97.5 4.2 %multiply_reduce_fusion = f32[256,12,128]{2,1,0:T(8,128)S(1)} fusion(bf16[2,2,256,12,128]{4,3,2,0,1:T(8,128)(2,1)} %copy_dynamic-update-slice_fusion, f32[2,256,12]{2,1,0:T(8,128)S(1)} %get-tuple-element.30), kind=kLoop, calls=%fused_computation.2 | loop fusion | flops 1966080 | bytes 3170304 | tf_op jit(solution)/shard_map/reduce_sum | solution.py:138
  101.7 0.7 reduce-precision_convert_fusion
  102.5 0.9 copy.15
  103.3 1.2 copy.16.refs_6_
  104.5 1.3 collective-permute-start.6
  105.8 5.3 %shard_map.56 = (f32[1,256,1536]{2,1,0:T(8,128)}, f32[1,3,256,4]{3,2,1,0:T(8,128)}) custom-call(bf16[1,256,1536]{2,1,0:T(8,128)(2,1)} %bitcast.35, bf16[2,1,256,1536]{3,2,1,0:T(8,128)(2,1)} %bitcast.32, bf16[2,1,256,1536]{3,2,1,0:T(8,128)(2,1)} %bitcast.33, f32[256,256]{1,0:T(8,128)} %reshape.625.m_ref), custom_call_target="tpu_custom_call" | custom-call | flops 402653184 | bytes 3932160 | tf_op jit(solution)/shard_map/pallas_call | solution.py:65
  111.1 13.7 %collective-permute-done.6 = f32[1,3,4,256]{2,3,1,0:T(8,128)S(1)} collective-permute-done((f32[1,3,4,256]{2,3,1,0:T(8,128)S(1)}, f32[1,3,4,256]{2,3,1,0:T(8,128)S(1)}, u32[]{:S(2)}, u32[]{:S(2)}) %collective-permute-start.6) | collective-permute-done | bytes 12320 | tf_op jit(solution)/shard_map/ppermute | solution.py:234
  124.8 0.8 select_bitcast_fusion.refs_5_
  125.6 0.9 copy-done.4
  126.4 5.4 %shard_map.58 = bf16[1,256,1536]{2,1,0:T(8,128)(2,1)} custom-call(f32[1,256,1536]{2,1,0:T(8,128)} %get-tuple-element.19.refs_0_, f32[1,3,256,4]{3,2,1,0:T(8,128)} %get-tuple-element.20.refs_1_, f32[1,256,1536]{2,1,0:T(8,128)} %get-tuple-element.22.refs_2_, f32[1,3,256,4]{3,2,1,0:T(8,128)} %get-tuple-element.23.refs_3_, bf16[1,256,1536]{2,1,0:T(8,128)(2,1)} %copy-done.4, ...), custom_call_target="tpu_custom_call" | custom-call | tf_op jit(solution)/shard_map/pallas_call | solution.py:118
  131.8 1.0 constant_dynamic-slice_fusion
  132.8 0.1 collective-permute-start.8
  132.9 1.7 %collective-permute-done.8 = bf16[1,32,8,768]{3,2,1,0:T(8,128)(2,1)S(1)} collective-permute-done((bf16[1,32,8,768]{3,2,1,0:T(8,128)(2,1)S(1)}, bf16[1,32,8,768]{3,2,1,0:T(8,128)(2,1)S(1)}, u32[]{:S(2)}, u32[]{:S(2)}) %collective-permute-start.8) | collective-permute-done | bytes 393248 | tf_op jit(solution)/shard_map/ppermute | solution.py:25
  134.6 1.9 %fusion.1 = bf16[1,32,8,768]{3,2,1,0:T(8,128)(2,1)} fusion(bf16[1,32,8,768]{3,2,1,0:T(8,128)(2,1)S(1)} %collective-permute-done.8, bf16[1,32,8,1536]{3,2,1,0:T(8,128)(2,1)} %bitcast.39, s32[]{:T(128)S(6)} %select_n.251, pred[]{:T(512)S(6)} %eq.77), kind=kLoop, calls=%fused_computation.12 | loop fusion | flops 1572864 | bytes 1179653 | tf_op jit(solution)/shard_map/convert_element_type | solution.py:328
  (36 shorter events, 0.2 us)
Async XLA Ops:
  0.0 2.1 %copy-start.5 = (bf16[1,1,32,8,1536]{4,3,2,1,0:T(8,128)(2,1)S(1)}, bf16[1,1,32,8,1536]{4,3,2,1,0:T(8,128)(2,1)}, u32[]{:S(2)}) copy-start(bf16[1,1,32,8,1536]{4,3,2,1,0:T(8,128)(2,1)} %param.7) | copy-start | bytes 2359300
  0.0 11.1 %copy-start.6 = (s32[4,15]{1,0:T(4,128)S(1)}, s32[4,15]{1,0:T(4,128)}, u32[]{:S(2)}) copy-start(s32[4,15]{1,0:T(4,128)} %param.8) | copy-start | bytes 724
  3.1 41.1 %collective-permute-start.1 = (bf16[2,1,32,8,1536]{4,3,2,1,0:T(8,128)(2,1)}, bf16[2,1,32,8,1536]{4,3,2,1,0:T(8,128)(2,1)}, u32[]{:S(2)}, u32[]{:S(2)}) collective-permute-start(bf16[2,1,32,8,1536]{4,3,2,1,0:T(8,128)(2,1)} %constant_dynamic-update-slice_fusion), channel_id=1, source_target_pairs={{12,8},{8,4},{4,0},{13,9},{9,5},{5,1},{14,10},{10,6},{6,2},{15,11}... | collective-permute-start | bytes 4718600 | tf_op jit(solution)/shard_map/ppermute | solution.py:192
  4.4 39.8 %collective-permute-start = (bf16[2,1,32,8,1536]{4,3,2,1,0:T(8,128)(2,1)}, bf16[2,1,32,8,1536]{4,3,2,1,0:T(8,128)(2,1)}, u32[]{:S(2)}, u32[]{:S(2)}) collective-permute-start(bf16[2,1,32,8,1536]{4,3,2,1,0:T(8,128)(2,1)} %constant_dynamic-update-slice_fusion), channel_id=1, source_target_pairs={{0,4},{4,8},{8,12},{1,5},{5,9},{9,13},{2,6},{6,10},{10,14},{3,7},{... | collective-permute-start | bytes 4718600 | tf_op jit(solution)/shard_map/ppermute | solution.py:191
  11.1 32.8 %collective-permute-start.4 = (s32[4,15]{1,0:T(4,128)S(1)}, s32[4,15]{1,0:T(4,128)S(1)}, u32[]{:S(2)}, u32[]{:S(2)}) collective-permute-start(s32[4,15]{1,0:T(4,128)S(1)} %copy-done.6), channel_id=1, source_target_pairs={{0,4},{12,8},{1,5},{13,9},{2,6},{14,10},{3,7},{15,11},{16,20},{28,... | collective-permute-start | bytes 728 | tf_op jit(solution)/shard_map/ppermute | solution.py:193
  18.4 45.3 %collective-permute-start.7 = (bf16[2,1,256,12,128]{4,2,3,1,0:T(8,128)(2,1)}, bf16[2,1,256,12,128]{4,2,3,1,0:T(8,128)(2,1)}, u32[]{:S(2)}, u32[]{:S(2)}) collective-permute-start(bf16[2,1,256,12,128]{4,2,3,1,0:T(8,128)(2,1)} %copy.13), channel_id=1, source_target_pairs={{0,2},{2,0},{1,3},{3,1},{4,6},{6,4},{5,7},{7,5},{8,10},{10,8},{9,1... | collective-permute-start | bytes 4718600 | tf_op jit(solution)/shard_map/ppermute | solution.py:21
  19.9 2.7 %copy-start.7 = (s32[2,8]{1,0:T(2,128)S(1)}, s32[2,8]{1,0:T(2,128)}, u32[]{:S(2)}) copy-start(s32[2,8]{1,0:T(2,128)} %param.9) | copy-start | bytes 196
  33.0 4.8 %copy-start.1 = (bf16[1,1,32,8,1536]{4,3,2,1,0:T(8,128)(2,1)S(1)}, bf16[1,1,32,8,1536]{4,3,2,1,0:T(8,128)(2,1)}, u32[]{:S(2)}) copy-start(bf16[1,1,32,8,1536]{4,3,2,1,0:T(8,128)(2,1)} %param.5) | copy-start | bytes 2359300
  47.9 36.8 %collective-permute-start.2 = (bf16[2,1,32,8,1536]{4,3,2,1,0:T(8,128)(2,1)}, bf16[2,1,32,8,1536]{4,3,2,1,0:T(8,128)(2,1)S(1)}, u32[]{:S(2)}, u32[]{:S(2)}) collective-permute-start(bf16[2,1,32,8,1536]{4,3,2,1,0:T(8,128)(2,1)} %get-tuple-element.28), channel_id=1, source_target_pairs={{4,8},{8,4},{5,9},{9,5},{6,10},{10,6},{7,11},{11,7},{20,24},{24,20... | collective-permute-start | bytes 4718600 | tf_op jit(solution)/shard_map/ppermute | solution.py:208
  56.2 28.4 %collective-permute-start.3 = (bf16[1,32,8,1536]{3,2,1,0:T(8,128)(2,1)S(1)}, bf16[1,32,8,1536]{3,2,1,0:T(8,128)(2,1)S(1)}, u32[]{:S(2)}, u32[]{:S(2)}) collective-permute-start(bf16[1,32,8,1536]{3,2,1,0:T(8,128)(2,1)S(1)} %bitcast.36), channel_id=1, source_target_pairs={{0,4},{12,8},{1,5},{13,9},{2,6},{14,10},{3,7},{15,11},{16,20},{28,... | collective-permute-start | bytes 2359304 | tf_op jit(solution)/shard_map/ppermute | solution.py:210
  80.8 3.9 %copy-start.2 = (bf16[2,1,32,8,1536]{4,3,2,1,0:T(8,128)(2,1)S(1)}, bf16[2,1,32,8,1536]{4,3,2,1,0:T(8,128)(2,1)}, u32[]{:S(2)}) copy-start(bf16[2,1,32,8,1536]{4,3,2,1,0:T(8,128)(2,1)} %get-tuple-element.27) | copy-start | bytes 4718596
  84.6 2.4 %copy-start.3 = (bf16[1,32,8,1536]{3,2,1,0:T(8,128)(2,1)}, bf16[1,32,8,1536]{3,2,1,0:T(8,128)(2,1)S(1)}, u32[]{:S(2)}) copy-start(bf16[1,32,8,1536]{3,2,1,0:T(8,128)(2,1)S(1)} %collective-permute-done.3) | copy-start | bytes 2359300
  84.6 2.3 %copy-start = (bf16[2,1,32,8,1536]{4,3,2,1,0:T(8,128)(2,1)}, bf16[2,1,32,8,1536]{4,3,2,1,0:T(8,128)(2,1)S(1)}, u32[]{:S(2)}) copy-start(bf16[2,1,32,8,1536]{4,3,2,1,0:T(8,128)(2,1)S(1)} %collective-permute-done.2) | copy-start | bytes 4718596
  96.2 29.3 %collective-permute-start.5 = (bf16[1,256,1536]{2,1,0:T(8,128)(2,1)}, bf16[1,256,1536]{2,1,0:T(8,128)(2,1)S(1)}, u32[]{:S(2)}, u32[]{:S(2)}) collective-permute-start(bf16[1,256,1536]{2,1,0:T(8,128)(2,1)} %convert_element_type.74), channel_id=1, source_target_pairs={{4,0},{8,12},{5,1},{9,13},{6,2},{10,14},{7,3},{11,15},{20,16},{24,... | collective-permute-start | bytes 2359304 | tf_op jit(solution)/shard_map/ppermute | solution.py:234
  102.5 2.1 %copy-start.8 = (f32[1,3,256,4]{3,2,1,0:T(8,128)S(1)}, f32[1,3,256,4]{3,2,1,0:T(8,128)}, u32[]{:S(2)}) copy-start(f32[1,3,256,4]{3,2,1,0:T(8,128)} %get-tuple-element.26) | copy-start | bytes 36868
  104.5 20.3 %collective-permute-start.6 = (f32[1,3,4,256]{2,3,1,0:T(8,128)S(1)}, f32[1,3,4,256]{2,3,1,0:T(8,128)S(1)}, u32[]{:S(2)}, u32[]{:S(2)}) collective-permute-start(f32[1,3,4,256]{2,3,1,0:T(8,128)S(1)} %bitcast.42), channel_id=1, source_target_pairs={{4,0},{8,12},{5,1},{9,13},{6,2},{10,14},{7,3},{11,15},{20,16},{24,... | collective-permute-start | bytes 36872 | tf_op jit(solution)/shard_map/ppermute | solution.py:234
  125.6 0.9 copy-start.4
  132.8 1.8 %collective-permute-start.8 = (bf16[1,32,8,768]{3,2,1,0:T(8,128)(2,1)S(1)}, bf16[1,32,8,768]{3,2,1,0:T(8,128)(2,1)S(1)}, u32[]{:S(2)}, u32[]{:S(2)}) collective-permute-start(bf16[1,32,8,768]{3,2,1,0:T(8,128)(2,1)S(1)} %constant_dynamic-slice_fusion), channel_id=1, source_target_pairs={{0,1},{1,0},{2,3},{3,2},{4,5},{5,4},{6,7},{7,6},{8,9},{9,8},{10,11... | collective-permute-start | bytes 1179656 | tf_op jit(solution)/shard_map/ppermute | solution.py:25

commit v5 on v4

--- a/solution.py
+++ b/solution.py
@@ -52,11 +52,11 @@
         result = jnp.dot(
             weights.astype(jnp.bfloat16), v_ref[:, lanes], preferred_element_type=jnp.float32
         )
-        o_ref[:, lanes] = result / totals
+        o_ref[:, lanes] = (result / totals).astype(o_ref.dtype)
         lse_ref[:, head : head + 1] = maxima + jnp.log(totals)
 
 
-def spatial_attention(query_flat, key_value_flat, mask, scale):
+def spatial_attention(query_flat, key_value_flat, mask, scale, out_dtype=jnp.float32):
     frames, query_count, model_width = query_flat.shape
     key_count = key_value_flat.shape[2]
     head_count = model_width // DH
@@ -76,7 +76,7 @@
             pl.BlockSpec((None, None, query_count, width // DH), lambda f, g: (f, g, 0, 0)),
         ],
         out_shape=[
-            jax.ShapeDtypeStruct((frames, query_count, model_width), jnp.float32),
+            jax.ShapeDtypeStruct((frames, query_count, model_width), out_dtype),
             jax.ShapeDtypeStruct((frames, groups, query_count, width // DH), jnp.float32),
         ],
         cost_estimate=pl.CostEstimate(
@@ -204,8 +204,11 @@
         scale,
     )
 
-    onward = jnp.where(index == 1, from_left, from_right)
-    two_away = lax.ppermute(onward, "lon", [(1, 2), (2, 1)])
+    two_away = jnp.where(
+        index == 1,
+        lax.ppermute(from_right, "lon", [(2, 1)]),
+        lax.ppermute(from_left, "lon", [(1, 2)]),
+    )
     held_q, _ = lax.optimization_barrier((own_q, from_left))
     guest_q = lax.ppermute(held_q, "lon", [(0, 1), (3, 2)])
     near_part, two_away, guest_q = lax.optimization_barrier((near_part, two_away, guest_q))
@@ -229,10 +232,11 @@
         flat_keys([guest_near, two_away]),
         expand_mask(guest_active, lat_rows),
         scale,
+        jnp.bfloat16,
     )
     lse_shape = guest_lse.shape
     returned, returned_lse = lax.ppermute(
-        (guest_out.astype(jnp.bfloat16), jnp.swapaxes(guest_lse, 2, 3)),
+        (guest_out, jnp.swapaxes(guest_lse, 2, 3)),
         "lon",
         [(1, 0), (2, 3)],
     )

time: 137 us -> 144 us (1.051)
  waiting for transfers between devices: 19.6 us -> 30.5 us
  other arithmetic: 25.7 us -> 21.8 us
    ppermute x3 -> x4, waiting for transfers between devices: 13.7 us -> 23.5 us  [the longest x2 23.5 us: spatial_line_of_four(): lax.ppermute((guest_out, jnp.swapaxes(guest_lse, 2, 3)), 'lon', [(1, 0),...]
    ppermute x3 -> x4, starting transfers between devices: 3.31 us -> 6.21 us  [the longest x2 2.56 us: spatial_line_of_four(): lax.ppermute((guest_out, jnp.swapaxes(guest_lse, 2, 3)), 'lon', [(1, 0),...]
    convert_element_type x1 -> x0, other arithmetic: 2.37 us -> none  [spatial_line_of_four(): guest_out.astype(jnp.bfloat16)]
    ppermute x1, starting transfers between devices: 7.44 us -> 5.26 us  [spatial_line_of_four(): guest_q = lax.ppermute(held_q, 'lon', [(0, 1), (3, 2)])]
    select_n x1, other arithmetic: 3.73 us -> 1.59 us  [spatial_line_of_four(): guest_near = jnp.where(index == 1, from_right, from_left)]
    select_n x0 -> x1, other arithmetic: none -> 1.59 us  [spatial_line_of_four(): jnp.where(index == 1, lax.ppermute(from_right, 'lon', [(2, 1)]), lax.pper...]
    unnamed x20 -> x16, local copies, waits for them, and re-layouts: 4.78 us -> 4.99 us
  transfers between devices with their start and end apart: 9 -> 10, of which waited for: 3 -> 3; matrix products, arithmetic and copies ran while one was open for 41% -> 37% of each run, Pallas kernels for 10% -> 10%
where the time goes in v5:
time: 144 us; the launch traced here: 143 us
  local copies, waits for them, and re-layouts  40.8 us (28%)
  waiting for transfers between devices  30.5 us (21%)
  Pallas kernels  25.8 us (18%)
  starting transfers between devices  23.8 us (17%)
  other arithmetic  21.8 us (15%)
    ppermute x2, waiting for transfers between devices, spatial_line_of_four(): lax.ppermute((guest_out, jnp.swapaxes(guest_lse, 2, 3)), 'lon', [(1, 0),...  23.5 us
    pallas_call x3, Pallas kernels, spatial_attention(): pl.pallas_call(functools.partial(spatial_kernel, scale=scale), grid=(fram...  20.5 us
    reshape x3, local copies, waits for them, and re-layouts, expand_mask(): return jnp.broadcast_to(active[None, :, None, :].astype(jnp.float32), (la...  14.5 us
    broadcast_in_dim x3, local copies, waits for them, and re-layouts, expand_mask(): jnp.broadcast_to(active[None, :, None, :].astype(jnp.float32), (lat_rows,...  7.37 us
    concatenate x2, other arithmetic, flat_keys(): joined = jnp.concatenate(blocks, axis=3)  6.89 us
    ppermute x1, starting transfers between devices, spatial_line_of_four(): from_left = lax.ppermute(key_value, 'lon', [(0, 1), (1, 2), (2, 3)])  6.72 us
    pallas_call x1, Pallas kernels, combine_partials(): pl.pallas_call(combine_kernel, grid=(frames, groups), in_specs=[big, smal...  5.36 us
    ppermute x1, waiting for transfers between devices, spatial_line_of_four(): guest_map = lax.ppermute(window_map, 'lon', [(0, 1), (3, 2)])  5.32 us
  transfers between devices with their start and end apart: 10, of which 3 were waited for; matrix products, arithmetic and copies ran while one was open for 37% of the time, Pallas kernels for 10%

profile of v5, /device:TPU:0, one launch (start us, length us, event | category | flops | bytes accessed | tf_op | source)
XLA Modules:
  0.0 143.1 jit_solution(1622603110808438214)
XLA Ops:
  0.0 2.1 %constant_dynamic-update-slice_fusion.1 = bf16[2,1,32,8,1536]{4,3,2,1,0:T(8,128)(2,1)} fusion(bf16[1,1,32,8,1536]{4,3,2,1,0:T(8,128)(2,1)} %param.6), kind=kLoop, calls=%fused_computation.29 | loop fusion | bytes 1572864
  2.2 1.0 constant_dynamic-update-slice_fusion
  3.2 1.3 collective-permute-start.1
  4.5 6.7 %collective-permute-start = (bf16[2,1,32,8,1536]{4,3,2,1,0:T(8,128)(2,1)}, bf16[2,1,32,8,1536]{4,3,2,1,0:T(8,128)(2,1)}, u32[]{:S(2)}, u32[]{:S(2)}) collective-permute-start(bf16[2,1,32,8,1536]{4,3,2,1,0:T(8,128)(2,1)} %constant_dynamic-update-slice_fusion), channel_id=1, source_target_pairs={{0,4},{4,8},{8,12},{1,5},{5,9},{9,13},{2,6},{6,10},{10,14},{3,7},{... | collective-permute-start | bytes 4718600 | tf_op jit(solution)/shard_map/ppermute | solution.py:191
  11.2 2.8 %collective-permute-start.5 = (s32[4,15]{1,0:T(4,128)S(1)}, s32[4,15]{1,0:T(4,128)S(1)}, u32[]{:S(2)}, u32[]{:S(2)}) collective-permute-start(s32[4,15]{1,0:T(4,128)S(1)} %copy-done.4), channel_id=1, source_target_pairs={{0,4},{12,8},{1,5},{13,9},{2,6},{14,10},{3,7},{15,11},{16,20},{28,... | collective-permute-start | bytes 728 | tf_op jit(solution)/shard_map/ppermute | solution.py:193
  14.0 2.9 %reshape.629 = bf16[2,1,256,12,128]{4,3,2,0,1:T(8,128)(2,1)S(1)} reshape(bf16[2,1,32,8,1536]{4,3,2,1,0:T(8,128)(2,1)} %constant_dynamic-update-slice_fusion) | data formatting | bytes 3145728 | tf_op jit(solution)/shard_map/reshape | solution.py:305
  16.9 1.6 %copy.13 = bf16[2,1,256,12,128]{4,2,3,1,0:T(8,128)(2,1)} copy(bf16[2,1,256,12,128]{4,3,2,0,1:T(8,128)(2,1)S(1)} %reshape.629) | data formatting | bytes 3145728 | tf_op jit(solution)/shard_map/reshape | solution.py:305
  18.4 1.5 %collective-permute-start.8 = (bf16[2,1,256,12,128]{4,2,3,1,0:T(8,128)(2,1)}, bf16[2,1,256,12,128]{4,2,3,1,0:T(8,128)(2,1)}, u32[]{:S(2)}, u32[]{:S(2)}) collective-permute-start(bf16[2,1,256,12,128]{4,2,3,1,0:T(8,128)(2,1)} %copy.13), channel_id=1, source_target_pairs={{0,2},{2,0},{1,3},{3,1},{4,6},{6,4},{5,7},{7,5},{8,10},{10,8},{9,1... | collective-permute-start | bytes 4718600 | tf_op jit(solution)/shard_map/ppermute | solution.py:21
  19.9 1.7 %constant_dynamic-update-slice_fusion.2 = bf16[2,2,256,12,128]{4,3,2,0,1:T(8,128)(2,1)} fusion(bf16[2,1,256,12,128]{4,3,2,0,1:T(8,128)(2,1)S(1)} %reshape.629), kind=kLoop, calls=%fused_computation.30 | loop fusion | bytes 3670016
  21.8 0.1 copy.11
  21.9 0.1 pad_add_fusion
  21.9 0.1 broadcast_in_dim.35
  22.0 0.1 and.261
  22.1 0.1 add_select_fusion.2
  22.2 0.1 add_select_fusion.1
  22.3 0.3 fusion.10
  22.7 0.1 fusion.6
  22.8 0.1 and_select_fusion.3
  22.9 2.5 %broadcast_in_dim.36 = f32[32,8,32,24]{3,2,1,0:T(8,128)} broadcast(f32[8,24]{1,0:T(8,128)S(1)} %and_convert_fusion.2), dimensions={1,3} | broadcast | bytes 787200 | tf_op jit(solution)/shard_map/broadcast_in_dim | solution.py:169
  25.3 4.6 %reshape.623.m_ref = f32[256,768]{1,0:T(8,128)} reshape(f32[32,8,32,24]{3,2,1,0:T(8,128)} %broadcast_in_dim.36) | data formatting | bytes 1572864 | tf_op jit(solution)/shard_map/reshape | solution.py:171
  30.0 2.5 %broadcast_in_dim.37 = f32[32,8,32,8]{3,2,1,0:T(8,128)} broadcast(f32[8,8]{1,0:T(8,128)S(1)} %and_convert_fusion.1), dimensions={1,3} | broadcast | bytes 262400 | tf_op jit(solution)/shard_map/broadcast_in_dim | solution.py:169
  32.4 4.8 %reshape.625.m_ref = f32[256,256]{1,0:T(8,128)} reshape(f32[32,8,32,8]{3,2,1,0:T(8,128)} %broadcast_in_dim.37) | data formatting | bytes 524288 | tf_op jit(solution)/shard_map/reshape | solution.py:171
  37.2 0.5 reshape.631
  37.6 0.2 copy-done.5
  37.9 0.1 tile.10
  37.9 0.6 gather_fusion
  38.5 0.1 compare_or_fusion
  38.6 0.1 add_select_fusion
  38.7 5.3 %collective-permute-done.5 = s32[4,15]{1,0:T(4,128)S(1)} collective-permute-done((s32[4,15]{1,0:T(4,128)S(1)}, s32[4,15]{1,0:T(4,128)S(1)}, u32[]{:S(2)}, u32[]{:S(2)}) %collective-permute-start.5) | collective-permute-done | bytes 272 | tf_op jit(solution)/shard_map/ppermute | solution.py:193
  44.0 0.1 copy.12
  44.1 0.1 fusion.8
  44.2 2.5 %broadcast_in_dim.39 = f32[32,8,32,16]{3,2,1,0:T(8,128)} broadcast(f32[8,16]{1,0:T(8,128)S(1)} %and_convert_fusion), dimensions={1,3} | broadcast | bytes 524800 | tf_op jit(solution)/shard_map/broadcast_in_dim | solution.py:169
  46.7 5.1 %reshape.628.m_ref = f32[256,512]{1,0:T(8,128)} reshape(f32[32,8,32,16]{3,2,1,0:T(8,128)} %broadcast_in_dim.39) | data formatting | bytes 1048576 | tf_op jit(solution)/shard_map/reshape | solution.py:171
  51.8 0.0 collective-permute-done
  51.8 5.3 %collective-permute-start.4 = (bf16[1,32,8,1536]{3,2,1,0:T(8,128)(2,1)S(1)}, bf16[1,32,8,1536]{3,2,1,0:T(8,128)(2,1)}, u32[]{:S(2)}, u32[]{:S(2)}) collective-permute-start(bf16[1,32,8,1536]{3,2,1,0:T(8,128)(2,1)S(1)} %bitcast.36), channel_id=1, source_target_pairs={{0,4},{12,8},{1,5},{13,9},{2,6},{14,10},{3,7},{15,11},{16,20},{28,... | collective-permute-start | bytes 2359304 | tf_op jit(solution)/shard_map/ppermute | solution.py:213
  57.1 1.8 %collective-permute-start.3 = (bf16[2,1,32,8,1536]{4,3,2,1,0:T(8,128)(2,1)}, bf16[2,1,32,8,1536]{4,3,2,1,0:T(8,128)(2,1)}, u32[]{:S(2)}, u32[]{:S(2)}) collective-permute-start(bf16[2,1,32,8,1536]{4,3,2,1,0:T(8,128)(2,1)} %collective-permute-done), channel_id=1, source_target_pairs={{4,8},{5,9},{6,10},{7,11},{20,24},{21,25},{22,26},{23,27}} | collective-permute-start | bytes 4718600 | tf_op jit(solution)/shard_map/ppermute | solution.py:210
  58.9 1.8 %collective-permute-start.2 = (bf16[2,1,32,8,1536]{4,3,2,1,0:T(8,128)(2,1)}, bf16[2,1,32,8,1536]{4,3,2,1,0:T(8,128)(2,1)}, u32[]{:S(2)}, u32[]{:S(2)}) collective-permute-start(bf16[2,1,32,8,1536]{4,3,2,1,0:T(8,128)(2,1)} %collective-permute-done.1), channel_id=1, source_target_pairs={{8,4},{9,5},{10,6},{11,7},{24,20},{25,21},{26,22},{27,23}} | collective-permute-start | bytes 4718600 | tf_op jit(solution)/shard_map/ppermute | solution.py:209
  60.7 4.8 %pad_maximum_fusion = bf16[2,1,32,24,1536]{4,3,2,1,0:T(8,128)(2,1)} fusion(bf16[2,1,32,8,1536]{4,3,2,1,0:T(8,128)(2,1)} %collective-permute-done.1, bf16[2,1,32,8,1536]{4,3,2,1,0:T(8,128)(2,1)} %constant_dynamic-update-slice_fusion, bf16[2,1,32,8,1536]{4,3,2,1,0:T(8,128)(2,1)} %collective-permute-done), kind=kLoop, calls=%fused_computation.1 | loop fusion | flops 14155776 | bytes 9437184 | tf_op jit(solution)/shard_map/concatenate | solution.py:175
  65.5 8.5 %shard_map.55 = (f32[1,256,1536]{2,1,0:T(8,128)}, f32[1,3,256,4]{3,2,1,0:T(8,128)}) custom-call(bf16[1,256,1536]{2,1,0:T(8,128)(2,1)} %bitcast.34, bf16[2,1,768,1536]{3,2,1,0:T(8,128)(2,1)} %bitcast.28, bf16[2,1,768,1536]{3,2,1,0:T(8,128)(2,1)} %bitcast.29, f32[256,768]{1,0:T(8,128)} %reshape.623.m_ref), custom_call_target="tpu_custom_call" | custom-call | flops 1207959552 | bytes 7077888 | tf_op jit(solution)/shard_map/pallas_call | solution.py:65
  73.9 0.0 collective-permute-done.8
  74.0 3.9 %copy_dynamic-update-slice_fusion = bf16[2,2,256,12,128]{4,3,2,0,1:T(8,128)(2,1)} fusion(bf16[2,2,256,12,128]{4,3,2,0,1:T(8,128)(2,1)} %constant_dynamic-update-slice_fusion.2, bf16[2,1,256,12,128]{4,2,3,1,0:T(8,128)(2,1)} %collective-permute-done.8), kind=kLoop, calls=%fused_computation.5 | loop fusion | bytes 3670016 | tf_op jit(solution)/shard_map/concatenate | solution.py:309
  77.8 2.8 %multiply_reduce_fusion.1 = f32[2,256,12]{2,1,0:T(8,128)S(1)} fusion(bf16[2,2,256,12,128]{4,3,2,0,1:T(8,128)(2,1)} %copy_dynamic-update-slice_fusion, f32[256,12,128]{2,1,0:T(8,128)S(1)} %reshape.631), kind=kLoop, calls=%fused_computation.3 | loop fusion | flops 2353152 | bytes 3170304 | tf_op jit(solution)/shard_map/reduce_sum | solution.py:130
  80.6 0.1 fusion.2
  80.7 1.6 %broadcast_select_fusion = bf16[2,1,32,8,1536]{4,3,2,1,0:T(8,128)(2,1)S(1)} fusion(bf16[2,1,32,8,1536]{4,3,2,1,0:T(8,128)(2,1)} %collective-permute-done.1, bf16[2,1,32,8,1536]{4,3,2,1,0:T(8,128)(2,1)} %collective-permute-done, pred[]{:T(512)S(6)} %eq.81), kind=kLoop, calls=%fused_computation.7 | loop fusion | flops 786432 | bytes 4718593 | tf_op jit(solution)/shard_map/jit(_where)/select_n | solution.py:229
  82.3 0.1 fusion.3
  82.5 0.0 collective-permute-done.2
  82.5 1.6 %broadcast_select_fusion.1 = bf16[2,1,32,8,1536]{4,3,2,1,0:T(8,128)(2,1)S(1)} fusion(bf16[2,1,32,8,1536]{4,3,2,1,0:T(8,128)(2,1)} %collective-permute-done.2, bf16[2,1,32,8,1536]{4,3,2,1,0:T(8,128)(2,1)} %collective-permute-done.3, pred[]{:T(512)S(6)} %eq.81), kind=kLoop, calls=%fused_computation.8 | loop fusion | flops 786432 | bytes 4718593 | tf_op jit(solution)/shard_map/jit(_where)/select_n | solution.py:207
  84.1 2.1 %pad_maximum_fusion.1 = bf16[2,1,32,16,1536]{4,3,2,1,0:T(8,128)(2,1)} fusion(bf16[2,1,32,8,1536]{4,3,2,1,0:T(8,128)(2,1)S(1)} %broadcast_select_fusion.1, bf16[2,1,32,8,1536]{4,3,2,1,0:T(8,128)(2,1)S(1)} %broadcast_select_fusion), kind=kLoop, calls=%fused_computation.4 | loop fusion | flops 6291456 | bytes 6291456 | tf_op jit(solution)/shard_map/concatenate | solution.py:175
  86.2 6.7 %shard_map.57 = (bf16[1,256,1536]{2,1,0:T(8,128)(2,1)}, f32[1,3,256,4]{3,2,1,0:T(8,128)}) custom-call(bf16[1,256,1536]{2,1,0:T(8,128)(2,1)} %bitcast.7.q_ref, bf16[2,1,512,1536]{3,2,1,0:T(8,128)(2,1)} %bitcast.30, bf16[2,1,512,1536]{3,2,1,0:T(8,128)(2,1)} %bitcast.31, f32[256,512]{1,0:T(8,128)} %reshape.628.m_ref), custom_call_target="tpu_custom_call" | custom-call | flops 805306368 | bytes 5505024 | tf_op jit(solution)/shard_map/pallas_call | solution.py:65
  92.9 1.3 collective-permute-start.6
  94.2 4.2 %multiply_reduce_fusion = f32[256,12,128]{2,1,0:T(8,128)S(1)} fusion(bf16[2,2,256,12,128]{4,3,2,0,1:T(8,128)(2,1)} %copy_dynamic-update-slice_fusion, f32[2,256,12]{2,1,0:T(8,128)S(1)} %get-tuple-element.28), kind=kLoop, calls=%fused_computation.2 | loop fusion | flops 1966080 | bytes 3170304 | tf_op jit(solution)/shard_map/reduce_sum | solution.py:138
  98.4 0.7 reduce-precision_convert_fusion
  99.2 0.9 copy.15
  100.1 1.2 copy.16.refs_6_
  101.2 1.3 collective-permute-start.7
  102.5 5.3 %shard_map.56 = (f32[1,256,1536]{2,1,0:T(8,128)}, f32[1,3,256,4]{3,2,1,0:T(8,128)}) custom-call(bf16[1,256,1536]{2,1,0:T(8,128)(2,1)} %bitcast.35, bf16[2,1,256,1536]{3,2,1,0:T(8,128)(2,1)} %bitcast.32, bf16[2,1,256,1536]{3,2,1,0:T(8,128)(2,1)} %bitcast.33, f32[256,256]{1,0:T(8,128)} %reshape.625.m_ref), custom_call_target="tpu_custom_call" | custom-call | flops 402653184 | bytes 3932160 | tf_op jit(solution)/shard_map/pallas_call | solution.py:65
  107.8 23.5 %collective-permute-done.7 = f32[1,3,4,256]{2,3,1,0:T(8,128)S(1)} collective-permute-done((f32[1,3,4,256]{2,3,1,0:T(8,128)S(1)}, f32[1,3,4,256]{2,3,1,0:T(8,128)S(1)}, u32[]{:S(2)}, u32[]{:S(2)}) %collective-permute-start.7) | collective-permute-done | bytes 12320 | tf_op jit(solution)/shard_map/ppermute | solution.py:238
  131.3 0.8 select_bitcast_fusion.refs_5_
  132.1 0.9 copy-done.2
  133.0 5.4 %shard_map.58 = bf16[1,256,1536]{2,1,0:T(8,128)(2,1)} custom-call(f32[1,256,1536]{2,1,0:T(8,128)} %get-tuple-element.19.refs_0_, f32[1,3,256,4]{3,2,1,0:T(8,128)} %get-tuple-element.20.refs_1_, f32[1,256,1536]{2,1,0:T(8,128)} %get-tuple-element.22.refs_2_, f32[1,3,256,4]{3,2,1,0:T(8,128)} %get-tuple-element.23.refs_3_, bf16[1,256,1536]{2,1,0:T(8,128)(2,1)} %copy-done.2, ...), custom_call_target="tpu_custom_call" | custom-call | tf_op jit(solution)/shard_map/pallas_call | solution.py:118
  138.4 1.0 constant_dynamic-slice_fusion
  139.4 0.1 collective-permute-start.9
  139.5 1.7 %collective-permute-done.9 = bf16[1,32,8,768]{3,2,1,0:T(8,128)(2,1)S(1)} collective-permute-done((bf16[1,32,8,768]{3,2,1,0:T(8,128)(2,1)S(1)}, bf16[1,32,8,768]{3,2,1,0:T(8,128)(2,1)S(1)}, u32[]{:S(2)}, u32[]{:S(2)}) %collective-permute-start.9) | collective-permute-done | bytes 393248 | tf_op jit(solution)/shard_map/ppermute | solution.py:25
  141.2 1.9 %fusion.1 = bf16[1,32,8,768]{3,2,1,0:T(8,128)(2,1)} fusion(bf16[1,32,8,768]{3,2,1,0:T(8,128)(2,1)S(1)} %collective-permute-done.9, bf16[1,32,8,1536]{3,2,1,0:T(8,128)(2,1)} %bitcast.39, s32[]{:T(128)S(6)} %select_n.251, pred[]{:T(512)S(6)} %eq.77), kind=kLoop, calls=%fused_computation.12 | loop fusion | flops 1572864 | bytes 1179653 | tf_op jit(solution)/shard_map/convert_element_type | solution.py:332
  (34 shorter events, 0.2 us)
Async XLA Ops:
  0.0 2.2 %copy-start.3 = (bf16[1,1,32,8,1536]{4,3,2,1,0:T(8,128)(2,1)S(1)}, bf16[1,1,32,8,1536]{4,3,2,1,0:T(8,128)(2,1)}, u32[]{:S(2)}) copy-start(bf16[1,1,32,8,1536]{4,3,2,1,0:T(8,128)(2,1)} %param.7) | copy-start | bytes 2359300
  0.0 11.2 %copy-start.4 = (s32[4,15]{1,0:T(4,128)S(1)}, s32[4,15]{1,0:T(4,128)}, u32[]{:S(2)}) copy-start(s32[4,15]{1,0:T(4,128)} %param.8) | copy-start | bytes 724
  3.2 55.7 %collective-permute-start.1 = (bf16[2,1,32,8,1536]{4,3,2,1,0:T(8,128)(2,1)}, bf16[2,1,32,8,1536]{4,3,2,1,0:T(8,128)(2,1)}, u32[]{:S(2)}, u32[]{:S(2)}) collective-permute-start(bf16[2,1,32,8,1536]{4,3,2,1,0:T(8,128)(2,1)} %constant_dynamic-update-slice_fusion), channel_id=1, source_target_pairs={{12,8},{8,4},{4,0},{13,9},{9,5},{5,1},{14,10},{10,6},{6,2},{15,11}... | collective-permute-start | bytes 4718600 | tf_op jit(solution)/shard_map/ppermute | solution.py:192
  4.5 47.4 %collective-permute-start = (bf16[2,1,32,8,1536]{4,3,2,1,0:T(8,128)(2,1)}, bf16[2,1,32,8,1536]{4,3,2,1,0:T(8,128)(2,1)}, u32[]{:S(2)}, u32[]{:S(2)}) collective-permute-start(bf16[2,1,32,8,1536]{4,3,2,1,0:T(8,128)(2,1)} %constant_dynamic-update-slice_fusion), channel_id=1, source_target_pairs={{0,4},{4,8},{8,12},{1,5},{5,9},{9,13},{2,6},{6,10},{10,14},{3,7},{... | collective-permute-start | bytes 4718600 | tf_op jit(solution)/shard_map/ppermute | solution.py:191
  11.2 32.8 %collective-permute-start.5 = (s32[4,15]{1,0:T(4,128)S(1)}, s32[4,15]{1,0:T(4,128)S(1)}, u32[]{:S(2)}, u32[]{:S(2)}) collective-permute-start(s32[4,15]{1,0:T(4,128)S(1)} %copy-done.4), channel_id=1, source_target_pairs={{0,4},{12,8},{1,5},{13,9},{2,6},{14,10},{3,7},{15,11},{16,20},{28,... | collective-permute-start | bytes 728 | tf_op jit(solution)/shard_map/ppermute | solution.py:193
  18.4 55.5 %collective-permute-start.8 = (bf16[2,1,256,12,128]{4,2,3,1,0:T(8,128)(2,1)}, bf16[2,1,256,12,128]{4,2,3,1,0:T(8,128)(2,1)}, u32[]{:S(2)}, u32[]{:S(2)}) collective-permute-start(bf16[2,1,256,12,128]{4,2,3,1,0:T(8,128)(2,1)} %copy.13), channel_id=1, source_target_pairs={{0,2},{2,0},{1,3},{3,1},{4,6},{6,4},{5,7},{7,5},{8,10},{10,8},{9,1... | collective-permute-start | bytes 4718600 | tf_op jit(solution)/shard_map/ppermute | solution.py:21
  32.4 4.8 %copy-start.1 = (bf16[1,1,32,8,1536]{4,3,2,1,0:T(8,128)(2,1)S(1)}, bf16[1,1,32,8,1536]{4,3,2,1,0:T(8,128)(2,1)}, u32[]{:S(2)}) copy-start(bf16[1,1,32,8,1536]{4,3,2,1,0:T(8,128)(2,1)} %param.5) | copy-start | bytes 2359300
  37.2 0.7 copy-start.5
  51.8 32.3 %collective-permute-start.4 = (bf16[1,32,8,1536]{3,2,1,0:T(8,128)(2,1)S(1)}, bf16[1,32,8,1536]{3,2,1,0:T(8,128)(2,1)}, u32[]{:S(2)}, u32[]{:S(2)}) collective-permute-start(bf16[1,32,8,1536]{3,2,1,0:T(8,128)(2,1)S(1)} %bitcast.36), channel_id=1, source_target_pairs={{0,4},{12,8},{1,5},{13,9},{2,6},{14,10},{3,7},{15,11},{16,20},{28,... | collective-permute-start | bytes 2359304 | tf_op jit(solution)/shard_map/ppermute | solution.py:213
  57.1 25.4 %collective-permute-start.3 = (bf16[2,1,32,8,1536]{4,3,2,1,0:T(8,128)(2,1)}, bf16[2,1,32,8,1536]{4,3,2,1,0:T(8,128)(2,1)}, u32[]{:S(2)}, u32[]{:S(2)}) collective-permute-start(bf16[2,1,32,8,1536]{4,3,2,1,0:T(8,128)(2,1)} %collective-permute-done), channel_id=1, source_target_pairs={{4,8},{5,9},{6,10},{7,11},{20,24},{21,25},{22,26},{23,27}} | collective-permute-start | bytes 4718600 | tf_op jit(solution)/shard_map/ppermute | solution.py:210
  58.9 23.6 %collective-permute-start.2 = (bf16[2,1,32,8,1536]{4,3,2,1,0:T(8,128)(2,1)}, bf16[2,1,32,8,1536]{4,3,2,1,0:T(8,128)(2,1)}, u32[]{:S(2)}, u32[]{:S(2)}) collective-permute-start(bf16[2,1,32,8,1536]{4,3,2,1,0:T(8,128)(2,1)} %collective-permute-done.1), channel_id=1, source_target_pairs={{8,4},{9,5},{10,6},{11,7},{24,20},{25,21},{26,22},{27,23}} | collective-permute-start | bytes 4718600 | tf_op jit(solution)/shard_map/ppermute | solution.py:209
  84.1 2.1 %copy-start = (bf16[2,1,32,8,1536]{4,3,2,1,0:T(8,128)(2,1)}, bf16[2,1,32,8,1536]{4,3,2,1,0:T(8,128)(2,1)S(1)}, u32[]{:S(2)}) copy-start(bf16[2,1,32,8,1536]{4,3,2,1,0:T(8,128)(2,1)S(1)} %broadcast_select_fusion.1) | copy-start | bytes 4718596
  92.9 39.2 %collective-permute-start.6 = (bf16[1,256,1536]{2,1,0:T(8,128)(2,1)}, bf16[1,256,1536]{2,1,0:T(8,128)(2,1)S(1)}, u32[]{:S(2)}, u32[]{:S(2)}) collective-permute-start(bf16[1,256,1536]{2,1,0:T(8,128)(2,1)} %get-tuple-element.25), channel_id=1, source_target_pairs={{4,0},{8,12},{5,1},{9,13},{6,2},{10,14},{7,3},{11,15},{20,16},{24,... | collective-permute-start | bytes 2359304 | tf_op jit(solution)/shard_map/ppermute | solution.py:238
  99.2 2.1 %copy-start.6 = (f32[1,3,256,4]{3,2,1,0:T(8,128)S(1)}, f32[1,3,256,4]{3,2,1,0:T(8,128)}, u32[]{:S(2)}) copy-start(f32[1,3,256,4]{3,2,1,0:T(8,128)} %get-tuple-element.26) | copy-start | bytes 36868
  101.2 30.1 %collective-permute-start.7 = (f32[1,3,4,256]{2,3,1,0:T(8,128)S(1)}, f32[1,3,4,256]{2,3,1,0:T(8,128)S(1)}, u32[]{:S(2)}, u32[]{:S(2)}) collective-permute-start(f32[1,3,4,256]{2,3,1,0:T(8,128)S(1)} %bitcast.41), channel_id=1, source_target_pairs={{4,0},{8,12},{5,1},{9,13},{6,2},{10,14},{7,3},{11,15},{20,16},{24,... | collective-permute-start | bytes 36872 | tf_op jit(solution)/shard_map/ppermute | solution.py:238
  132.1 0.9 copy-start.2
  139.4 1.8 %collective-permute-start.9 = (bf16[1,32,8,768]{3,2,1,0:T(8,128)(2,1)S(1)}, bf16[1,32,8,768]{3,2,1,0:T(8,128)(2,1)S(1)}, u32[]{:S(2)}, u32[]{:S(2)}) collective-permute-start(bf16[1,32,8,768]{3,2,1,0:T(8,128)(2,1)S(1)} %constant_dynamic-slice_fusion), channel_id=1, source_target_pairs={{0,1},{1,0},{2,3},{3,2},{4,5},{5,4},{6,7},{7,6},{8,9},{9,8},{10,11... | collective-permute-start | bytes 1179656 | tf_op jit(solution)/shard_map/ppermute | solution.py:25

commit v6 on v5

--- a/solution.py
+++ b/solution.py
@@ -177,79 +177,92 @@
     return joined.reshape(two, frames, lat_rows * cols, model_width)
 
 
-def spatial_line_of_four(own_q, key_value, window_map, scale):
+def spatial_line_of_four(own_q, key_value, window_map, temporal, scale):
     frames, lat_rows, columns, model_width = own_q.shape
     count = 4
     total_cols = count * columns
+    half = model_width // 2
     index = lax.axis_index("lon")
+    branch_index = lax.axis_index("branch")
     is_middle = (index >= 1) & (index <= count - 2)
     column_ids = jnp.arange(columns, dtype=jnp.int32)
     own_map = jnp.repeat(window_map, BLK, axis=0)
     own_cols = index * columns + column_ids
-    query_flat = own_q.reshape(frames, lat_rows * columns, model_width)
-
-    from_left = lax.ppermute(key_value, "lon", [(0, 1), (1, 2), (2, 3)])
-    from_right = lax.ppermute(key_value, "lon", [(3, 2), (2, 1), (1, 0)])
     guest_map = lax.ppermute(window_map, "lon", [(0, 1), (3, 2)])
 
     near_cols = ((index - 1) * columns + jnp.arange(3 * columns, dtype=jnp.int32)) % total_cols
     near_valid = jnp.stack([index >= 1, index >= 0, index <= count - 2])
-    near_active = window_mask(own_cols, near_cols, own_map, total_cols, lat_rows) & jnp.repeat(
-        near_valid, columns
-    )[None, :]
-    near_part = spatial_attention(
-        query_flat,
-        flat_keys([from_left, key_value, from_right]),
-        expand_mask(near_active, lat_rows),
-        scale,
-    )
-
-    two_away = jnp.where(
-        index == 1,
-        lax.ppermute(from_right, "lon", [(2, 1)]),
-        lax.ppermute(from_left, "lon", [(1, 2)]),
-    )
-    held_q, _ = lax.optimization_barrier((own_q, from_left))
-    guest_q = lax.ppermute(held_q, "lon", [(0, 1), (3, 2)])
-    near_part, two_away, guest_q = lax.optimization_barrier((near_part, two_away, guest_q))
-
+    near_mask = expand_mask(
+        window_mask(own_cols, near_cols, own_map, total_cols, lat_rows)
+        & jnp.repeat(near_valid, columns)[None, :],
+        lat_rows,
+    )
     guest_device = jnp.where(index == 1, 0, count - 1)
     near_block = jnp.where(index == 1, index + 1, index - 1)
     far_block = (index + 2) % count
     guest_key_cols = jnp.concatenate(
         [near_block * columns + column_ids, far_block * columns + column_ids]
     )
-    guest_active = window_mask(
-        guest_device * columns + column_ids,
-        guest_key_cols,
-        jnp.repeat(guest_map, BLK, axis=0),
-        total_cols,
+    guest_mask = expand_mask(
+        window_mask(
+            guest_device * columns + column_ids,
+            guest_key_cols,
+            jnp.repeat(guest_map, BLK, axis=0),
+            total_cols,
+            lat_rows,
+        )
+        & is_middle,
         lat_rows,
-    ) & is_middle
-    guest_near = jnp.where(index == 1, from_right, from_left)
-    guest_out, guest_lse = spatial_attention(
-        guest_q.reshape(frames, lat_rows * columns, model_width),
-        flat_keys([guest_near, two_away]),
-        expand_mask(guest_active, lat_rows),
-        scale,
-        jnp.bfloat16,
-    )
-    lse_shape = guest_lse.shape
-    returned, returned_lse = lax.ppermute(
-        (guest_out, jnp.swapaxes(guest_lse, 2, 3)),
-        "lon",
-        [(1, 0), (2, 3)],
-    )
-    returned_lse = jnp.where(is_middle, masked_score, jnp.swapaxes(returned_lse, 2, 3))
-    assert returned_lse.shape == lse_shape
-
-    far_active = window_mask(
-        own_cols, far_block * columns + column_ids, own_map, total_cols, lat_rows
-    ) & is_middle
-    far_part = spatial_attention(
-        query_flat, flat_keys([two_away]), expand_mask(far_active, lat_rows), scale
-    )
-    return [near_part, far_part, (returned, returned_lse)]
+    )
+    far_mask = expand_mask(
+        window_mask(own_cols, far_block * columns + column_ids, own_map, total_cols, lat_rows)
+        & is_middle,
+        lat_rows,
+    )
+
+    mixed = []
+    previous = None
+    for chunk in range(2):
+        start = jnp.where(chunk == 0, 1 - branch_index, branch_index) * half
+        chunk_q = lax.dynamic_slice_in_dim(own_q, start, half, 3)
+        chunk_kv = lax.dynamic_slice_in_dim(key_value, start, half, 4)
+        if previous is not None:
+            chunk_kv, _ = lax.optimization_barrier((chunk_kv, previous))
+        query_flat = chunk_q.reshape(frames, lat_rows * columns, half)
+        from_left = lax.ppermute(chunk_kv, "lon", [(0, 1), (1, 2), (2, 3)])
+        from_right = lax.ppermute(chunk_kv, "lon", [(3, 2), (2, 1), (1, 0)])
+        previous = (from_left, from_right)
+        near_part = spatial_attention(
+            query_flat, flat_keys([from_left, chunk_kv, from_right]), near_mask, scale
+        )
+        two_away = jnp.where(
+            index == 1,
+            lax.ppermute(from_right, "lon", [(2, 1)]),
+            lax.ppermute(from_left, "lon", [(1, 2)]),
+        )
+        held_q, _ = lax.optimization_barrier((chunk_q, from_left))
+        guest_q = lax.ppermute(held_q, "lon", [(0, 1), (3, 2)])
+        near_part, two_away, guest_q = lax.optimization_barrier((near_part, two_away, guest_q))
+        guest_near = jnp.where(index == 1, from_right, from_left)
+        guest_out, guest_lse = spatial_attention(
+            guest_q.reshape(frames, lat_rows * columns, half),
+            flat_keys([guest_near, two_away]),
+            guest_mask,
+            scale,
+            jnp.bfloat16,
+        )
+        returned, returned_lse = lax.ppermute(
+            (guest_out, jnp.swapaxes(guest_lse, 2, 3)), "lon", [(1, 0), (2, 3)]
+        )
+        returned_lse = jnp.where(is_middle, masked_score, jnp.swapaxes(returned_lse, 2, 3))
+        far_part = spatial_attention(query_flat, flat_keys([two_away]), far_mask, scale)
+        chunk_temporal = lax.dynamic_slice_in_dim(temporal, start, half, 2)
+        mixed.append(
+            combine_partials(
+                [near_part, far_part, (returned, returned_lse)], chunk_temporal
+            ).reshape(frames, lat_rows, columns, half)
+        )
+    return mixed
 
 
 def local(queries, keys, values, window_map, frame_valid):
@@ -266,10 +279,29 @@
     key_value = jnp.stack([own_k, own_v])
     column_ids = jnp.arange(columns, dtype=jnp.int32)
     per_column_map = jnp.repeat(window_map, BLK, axis=0)
+    token_count = lat_rows * columns
+    tm_count = lax.axis_size("tm")
+    tm_index = lax.axis_index("tm")
+    key_value_rows = key_value.reshape(2, frames, token_count, head_count, DH)
+    pieces = [key_value_rows]
+    for step_by in range(1, tm_count):
+        pieces.append(shifted(key_value_rows, "tm", step_by))
+    gathered = jnp.concatenate(pieces, axis=1)
+    piece_ids = jnp.arange(tm_count * frames, dtype=jnp.int32)
+    frame_ids = ((tm_index - piece_ids // frames) % tm_count) * frames + piece_ids % frames
+    valid_tokens = jnp.take(jnp.tile(frame_valid, (1, lat_rows)), frame_ids, axis=0)
+    temporal = temporal_attention(
+        own_q.reshape(frames, token_count, head_count, DH),
+        gathered[0],
+        gathered[1],
+        valid_tokens,
+        frame_ids[:frames],
+        frame_ids,
+        scale,
+    )
+    temporal = temporal.reshape(frames, token_count, model_width)
     full_ring = ext_count >= total_cols and WIN * BLK <= total_cols
-    if full_ring and lon_count == 4:
-        partials = spatial_line_of_four(own_q, key_value, window_map, scale)
-    else:
+    if not (full_ring and lon_count == 4):
         if full_ring:
             extended = jnp.concatenate(line_gather(key_value, "lon"), axis=3)
             key_cols = total_cols
@@ -299,32 +331,18 @@
             spatial_attention(query_flat, key_value_flat, expand_mask(active, lat_rows), scale)
         ]
 
-    token_count = lat_rows * columns
-    tm_count = lax.axis_size("tm")
-    tm_index = lax.axis_index("tm")
-    key_value_rows = key_value.reshape(2, frames, token_count, head_count, DH)
-    pieces = [key_value_rows]
-    for step_by in range(1, tm_count):
-        pieces.append(shifted(key_value_rows, "tm", step_by))
-    gathered = jnp.concatenate(pieces, axis=1)
-    piece_ids = jnp.arange(tm_count * frames, dtype=jnp.int32)
-    frame_ids = ((tm_index - piece_ids // frames) % tm_count) * frames + piece_ids % frames
-    valid_tokens = jnp.take(jnp.tile(frame_valid, (1, lat_rows)), frame_ids, axis=0)
-    temporal = temporal_attention(
-        own_q.reshape(frames, token_count, head_count, DH),
-        gathered[0],
-        gathered[1],
-        valid_tokens,
-        frame_ids[:frames],
-        frame_ids,
-        scale,
-    )
-    temporal = temporal.reshape(frames, token_count, model_width)
-    mixed = combine_partials(partials, temporal).reshape(frames, lat_rows, columns, model_width)
     half_width = model_width // 2
     branch_index = lax.axis_index("branch")
-    own_half = lax.dynamic_slice_in_dim(mixed, branch_index * half_width, half_width, 3)
-    other_half = lax.dynamic_slice_in_dim(mixed, (1 - branch_index) * half_width, half_width, 3)
+    if full_ring and lon_count == 4:
+        other_half, own_half = spatial_line_of_four(own_q, key_value, window_map, temporal, scale)
+    else:
+        mixed = combine_partials(partials, temporal).reshape(
+            frames, lat_rows, columns, model_width
+        )
+        own_half = lax.dynamic_slice_in_dim(mixed, branch_index * half_width, half_width, 3)
+        other_half = lax.dynamic_slice_in_dim(
+            mixed, (1 - branch_index) * half_width, half_width, 3
+        )
     partner = from_partner(other_half, "branch", 0)
     is_conditional = branch_index == 0
     conditional = jnp.where(is_conditional, own_half, partner).astype(jnp.float32)

time: 144 us -> 157 us (1.090)
  waiting for transfers between devices: 30.5 us -> 5.98 us
  starting transfers between devices: 23.8 us -> 46.2 us
  Pallas kernels: 25.8 us -> 33.7 us
  other arithmetic: 21.8 us -> 27.3 us
  local copies, waits for them, and re-layouts: 40.8 us -> 42.6 us
    ppermute x2 -> x4, waiting for transfers between devices: 23.5 us -> 5.94 us  [spatial_line_of_four(): lax.ppermute((guest_out, jnp.swapaxes(guest_lse, 2, 3)), 'lon', [(1, 0),...]
    ppermute x1 -> x2, starting transfers between devices: 5.26 us -> 17.1 us  [spatial_line_of_four(): guest_q = lax.ppermute(held_q, 'lon', [(0, 1), (3, 2)])]
    pallas_call x3 -> x6, Pallas kernels: 20.5 us -> 27.3 us  [spatial_attention(): pl.pallas_call(functools.partial(spatial_kernel, scale=scale), grid=(fram...]
    ppermute x2 -> x4, starting transfers between devices: 8 us -> 14.6 us  [the longest x2 12 us: spatial_line_of_four(): from_left = lax.ppermute(chunk_kv, 'lon', [(0, 1), (1, 2), (2, 3)])]
    ppermute x1, waiting for transfers between devices: 5.32 us -> 0.01 us  [spatial_line_of_four(): guest_map = lax.ppermute(window_map, 'lon', [(0, 1), (3, 2)])]
    ppermute x2 -> x4, starting transfers between devices: 2.56 us -> 5.46 us  [spatial_line_of_four(): lax.ppermute((guest_out, jnp.swapaxes(guest_lse, 2, 3)), 'lon', [(1, 0),...]
    concatenate x2 -> x4, other arithmetic: 6.89 us -> 9.19 us  [flat_keys(): joined = jnp.concatenate(blocks, axis=3)]
    select_n x1 -> x2, other arithmetic: 1.59 us -> 3.32 us  [spatial_line_of_four(): guest_near = jnp.where(index == 1, from_right, from_left)]
  transfers between devices with their start and end apart: 10 -> 17, of which waited for: 3 -> 1; matrix products, arithmetic and copies ran while one was open for 37% -> 40% of each run, Pallas kernels for 10% -> 22%
where the time goes in v6:
time: 157 us; the launch traced here: 156 us
  starting transfers between devices  46.2 us (29%)
  local copies, waits for them, and re-layouts  42.6 us (27%)
  Pallas kernels  33.7 us (21%)
  other arithmetic  27.3 us (17%)
  waiting for transfers between devices  5.98 us (4%)
    pallas_call x6, Pallas kernels, spatial_attention(): pl.pallas_call(functools.partial(spatial_kernel, scale=scale), grid=(fram...  27.3 us
    ppermute x2, starting transfers between devices, spatial_line_of_four(): guest_q = lax.ppermute(held_q, 'lon', [(0, 1), (3, 2)])  17.1 us
    reshape x3, local copies, waits for them, and re-layouts, expand_mask(): return jnp.broadcast_to(active[None, :, None, :].astype(jnp.float32), (la...  14.4 us
    ppermute x2, starting transfers between devices, spatial_line_of_four(): from_left = lax.ppermute(chunk_kv, 'lon', [(0, 1), (1, 2), (2, 3)])  12 us
    concatenate x4, other arithmetic, flat_keys(): joined = jnp.concatenate(blocks, axis=3)  9.19 us
    broadcast_in_dim x3, local copies, waits for them, and re-layouts, expand_mask(): jnp.broadcast_to(active[None, :, None, :].astype(jnp.float32), (lat_rows,...  7.55 us
    pallas_call x2, Pallas kernels, combine_partials(): pl.pallas_call(combine_kernel, grid=(frames, groups), in_specs=[big, smal...  6.46 us
    unnamed x30, local copies, waits for them, and re-layouts  6.25 us
  transfers between devices with their start and end apart: 17, of which 1 were waited for; matrix products, arithmetic and copies ran while one was open for 40% of the time, Pallas kernels for 22%

profile of v6, /device:TPU:0, one launch (start us, length us, event | category | flops | bytes accessed | tf_op | source)
XLA Modules:
  0.0 156.2 jit_solution(8127558391037293169)
XLA Ops:
  0.0 1.2 constant_dynamic-update-slice_fusion.1
  1.2 1.2 constant_dynamic-update-slice_fusion
  2.4 1.4 constant_dynamic-slice_fusion.1
  3.8 1.3 collective-permute-start.1
  5.1 6.4 %collective-permute-start = (bf16[2,1,32,8,768]{4,3,2,1,0:T(8,128)(2,1)}, bf16[2,1,32,8,768]{4,3,2,1,0:T(8,128)(2,1)}, u32[]{:S(2)}, u32[]{:S(2)}) collective-permute-start(bf16[2,1,32,8,768]{4,3,2,1,0:T(8,128)(2,1)} %get-tuple-element.52), channel_id=1, source_target_pairs={{0,4},{4,8},{8,12},{1,5},{5,9},{9,13},{2,6},{6,10},{10,14},{3,7},{... | collective-permute-start | bytes 2359304 | tf_op jit(solution)/shard_map/ppermute | solution.py:232
  11.6 3.1 %collective-permute-start.5 = (s32[4,15]{1,0:T(4,128)S(1)}, s32[4,15]{1,0:T(4,128)S(1)}, u32[]{:S(2)}, u32[]{:S(2)}) collective-permute-start(s32[4,15]{1,0:T(4,128)S(1)} %copy-done.10), channel_id=1, source_target_pairs={{0,4},{12,8},{1,5},{13,9},{2,6},{14,10},{3,7},{15,11},{16,20},{28,... | collective-permute-start | bytes 728 | tf_op jit(solution)/shard_map/ppermute | solution.py:191
  14.6 2.9 %reshape.655 = bf16[2,1,256,12,128]{4,3,2,0,1:T(8,128)(2,1)S(1)} reshape(bf16[2,1,32,8,1536]{4,3,2,1,0:T(8,128)(2,1)} %copy-done.2) | data formatting | bytes 3145728 | tf_op jit(solution)/shard_map/reshape | solution.py:285
  17.5 1.5 copy.15
  19.1 1.5 collective-permute-start.8
  20.6 1.7 %constant_dynamic-update-slice_fusion.2 = bf16[2,2,256,12,128]{4,3,2,0,1:T(8,128)(2,1)} fusion(bf16[2,1,256,12,128]{4,3,2,0,1:T(8,128)(2,1)S(1)} %reshape.655), kind=kLoop, calls=%fused_computation.41 | loop fusion | bytes 3670016
  22.4 0.1 copy.13
  22.9 0.3 fusion.10
  23.6 0.6 gather_fusion
  24.3 1.1 dynamic-slice_bitcast_fusion
  25.4 0.5 reshape.663
  25.8 2.5 %broadcast_in_dim.40 = f32[32,8,32,24]{3,2,1,0:T(8,128)} broadcast(f32[8,24]{1,0:T(8,128)S(1)} %and_convert_fusion.2), dimensions={1,3} | broadcast | bytes 787200 | tf_op jit(solution)/shard_map/broadcast_in_dim | solution.py:169
  28.4 4.7 %reshape.649.m_ref = f32[256,768]{1,0:T(8,128)} reshape(f32[32,8,32,24]{3,2,1,0:T(8,128)} %broadcast_in_dim.40) | data formatting | bytes 1572864 | tf_op jit(solution)/shard_map/reshape | solution.py:171
  33.0 2.5 %broadcast_in_dim.41 = f32[32,8,32,8]{3,2,1,0:T(8,128)} broadcast(f32[8,8]{1,0:T(8,128)S(1)} %and_convert_fusion.1), dimensions={1,3} | broadcast | bytes 262400 | tf_op jit(solution)/shard_map/broadcast_in_dim | solution.py:169
  35.5 4.7 %reshape.651.m_ref = f32[256,256]{1,0:T(8,128)} reshape(f32[32,8,32,8]{3,2,1,0:T(8,128)} %broadcast_in_dim.41) | data formatting | bytes 524288 | tf_op jit(solution)/shard_map/reshape | solution.py:171
  40.4 0.7 collective-permute-start.2
  41.1 1.6 collective-permute-start.3
  42.7 2.5 %broadcast_in_dim.43 = f32[32,8,32,16]{3,2,1,0:T(8,128)} broadcast(f32[8,16]{1,0:T(8,128)S(1)} %and_convert_fusion), dimensions={1,3} | broadcast | bytes 524800 | tf_op jit(solution)/shard_map/broadcast_in_dim | solution.py:169
  45.3 5.1 %reshape.654.m_ref = f32[256,512]{1,0:T(8,128)} reshape(f32[32,8,32,16]{3,2,1,0:T(8,128)} %broadcast_in_dim.43) | data formatting | bytes 1048576 | tf_op jit(solution)/shard_map/reshape | solution.py:171
  50.4 6.5 %collective-permute-start.4 = (bf16[1,32,8,768]{3,2,1,0:T(8,128)(2,1)S(1)}, bf16[1,32,8,768]{3,2,1,0:T(8,128)(2,1)}, u32[]{:S(2)}, u32[]{:S(2)}) collective-permute-start(bf16[1,32,8,768]{3,2,1,0:T(8,128)(2,1)S(1)} %get-tuple-element.30), channel_id=1, source_target_pairs={{0,4},{12,8},{1,5},{13,9},{2,6},{14,10},{3,7},{15,11},{16,20},{28,... | collective-permute-start | bytes 1179656 | tf_op jit(solution)/shard_map/ppermute | solution.py:244
  56.9 1.3 collective-permute-start.11
  58.2 2.1 %broadcast_select_fusion.2 = bf16[2,1,32,8,768]{4,3,2,1,0:T(8,128)(2,1)} fusion(bf16[2,1,32,8,768]{4,3,2,1,0:T(8,128)(2,1)} %collective-permute-done.1, bf16[2,1,32,8,768]{4,3,2,1,0:T(8,128)(2,1)} %collective-permute-done, pred[]{:T(512)S(6)} %eq.83), kind=kLoop, calls=%fused_computation.15 | loop fusion | flops 393216 | bytes 2359297 | tf_op jit(solution)/shard_map/jit(_where)/select_n | solution.py:246
  60.3 3.2 %pad_maximum_fusion = bf16[2,1,32,24,768]{4,3,2,1,0:T(8,128)(2,1)} fusion(bf16[2,1,32,8,768]{4,3,2,1,0:T(8,128)(2,1)} %collective-permute-done.1, bf16[2,1,32,8,768]{4,3,2,1,0:T(8,128)(2,1)} %get-tuple-element.52, bf16[2,1,32,8,768]{4,3,2,1,0:T(8,128)(2,1)} %collective-permute-done), kind=kLoop, calls=%fused_computation.3 | loop fusion | flops 7077888 | bytes 4718592 | tf_op jit(solution)/shard_map/concatenate | solution.py:175
  63.5 5.5 %shard_map.55 = (f32[1,256,768]{2,1,0:T(8,128)}, f32[1,2,256,3]{3,2,1,0:T(8,128)}) custom-call(bf16[1,256,768]{2,1,0:T(8,128)(2,1)} %get-tuple-element.57.q_ref, bf16[2,1,768,768]{3,2,1,0:T(8,128)(2,1)} %bitcast.50, bf16[2,1,768,768]{3,2,1,0:T(8,128)(2,1)} %bitcast.51, f32[256,768]{1,0:T(8,128)} %reshape.649.m_ref), custom_call_target="tpu_custom_call" | custom-call | flops 603979776 | bytes 3538944 | tf_op jit(solution)/shard_map/pallas_call | solution.py:65
  69.1 5.6 %collective-permute-start.10 = (bf16[2,1,32,8,768]{4,3,2,1,0:T(8,128)(2,1)}, bf16[2,1,32,8,768]{4,3,2,1,0:T(8,128)(2,1)}, u32[]{:S(2)}, u32[]{:S(2)}) collective-permute-start(bf16[2,1,32,8,768]{4,3,2,1,0:T(8,128)(2,1)} %get-tuple-element.39), channel_id=1, source_target_pairs={{0,4},{4,8},{8,12},{1,5},{5,9},{9,13},{2,6},{6,10},{10,14},{3,7},{... | collective-permute-start | bytes 2359304 | tf_op jit(solution)/shard_map/ppermute | solution.py:232
  74.7 1.2 broadcast_select_fusion.3
  75.9 1.4 pad_maximum_fusion.2
  77.3 4.4 %shard_map.57 = (bf16[1,256,768]{2,1,0:T(8,128)(2,1)}, f32[1,2,256,3]{3,2,1,0:T(8,128)}) custom-call(bf16[1,256,768]{2,1,0:T(8,128)(2,1)} %bitcast.7.q_ref, bf16[2,1,512,768]{3,2,1,0:T(8,128)(2,1)} %bitcast.54, bf16[2,1,512,768]{3,2,1,0:T(8,128)(2,1)} %bitcast.55, f32[256,512]{1,0:T(8,128)} %reshape.654.m_ref), custom_call_target="tpu_custom_call" | custom-call | flops 402653184 | bytes 2752512 | tf_op jit(solution)/shard_map/pallas_call | solution.py:65
  81.7 1.3 collective-permute-start.6
  83.0 1.5 collective-permute-start.7
  84.5 3.8 %copy_dynamic-update-slice_fusion = bf16[2,2,256,12,128]{4,3,2,0,1:T(8,128)(2,1)} fusion(bf16[2,2,256,12,128]{4,3,2,0,1:T(8,128)(2,1)} %constant_dynamic-update-slice_fusion.2, bf16[2,1,256,12,128]{4,2,3,1,0:T(8,128)(2,1)} %collective-permute-done.8), kind=kLoop, calls=%fused_computation.5 | loop fusion | bytes 3670016 | tf_op jit(solution)/shard_map/concatenate | solution.py:289
  88.3 2.9 %multiply_reduce_fusion.1 = f32[2,256,12]{2,1,0:T(8,128)S(1)} fusion(bf16[2,2,256,12,128]{4,3,2,0,1:T(8,128)(2,1)} %copy_dynamic-update-slice_fusion, f32[256,12,128]{2,1,0:T(8,128)S(1)} %reshape.663), kind=kLoop, calls=%fused_computation.2 | loop fusion | flops 2353152 | bytes 3170304 | tf_op jit(solution)/shard_map/reduce_sum | solution.py:130
  91.2 0.1 fusion.2
  91.4 0.1 fusion.3
  91.5 2.9 %multiply_reduce_fusion = f32[256,12,128]{2,1,0:T(8,128)S(1)} fusion(bf16[2,2,256,12,128]{4,3,2,0,1:T(8,128)(2,1)S(1)} %copy-done.3, f32[2,256,12]{2,1,0:T(8,128)S(1)} %get-tuple-element.60), kind=kLoop, calls=%fused_computation.1 | loop fusion | flops 1966080 | bytes 3170304 | tf_op jit(solution)/shard_map/reduce_sum | solution.py:138
  94.5 0.7 reduce-precision_convert_fusion
  95.2 0.9 copy.17
  96.1 0.7 collective-permute-start.12
  96.8 1.6 collective-permute-start.13
  98.4 0.9 copy.20.refs_6_
  99.4 10.5 %collective-permute-start.14 = (bf16[1,32,8,768]{3,2,1,0:T(8,128)(2,1)}, bf16[1,32,8,768]{3,2,1,0:T(8,128)(2,1)}, u32[]{:S(2)}, u32[]{:S(2)}) collective-permute-start(bf16[1,32,8,768]{3,2,1,0:T(8,128)(2,1)} %get-tuple-element.42), channel_id=1, source_target_pairs={{0,4},{12,8},{1,5},{13,9},{2,6},{14,10},{3,7},{15,11},{16,20},{28,... | collective-permute-start | bytes 1179656 | tf_op jit(solution)/shard_map/ppermute | solution.py:244
  109.9 3.7 %shard_map.56 = (f32[1,256,768]{2,1,0:T(8,128)}, f32[1,2,256,3]{3,2,1,0:T(8,128)}) custom-call(bf16[1,256,768]{2,1,0:T(8,128)(2,1)} %get-tuple-element.57.q_ref, bf16[2,1,256,768]{3,2,1,0:T(8,128)(2,1)} %bitcast.56, bf16[2,1,256,768]{3,2,1,0:T(8,128)(2,1)} %bitcast.57, f32[256,256]{1,0:T(8,128)} %reshape.651.m_ref), custom_call_target="tpu_custom_call" | custom-call | flops 201326592 | bytes 1966080 | tf_op jit(solution)/shard_map/pallas_call | solution.py:65
  113.6 3.2 %pad_maximum_fusion.1 = bf16[2,1,32,24,768]{4,3,2,1,0:T(8,128)(2,1)} fusion(bf16[2,1,32,8,768]{4,3,2,1,0:T(8,128)(2,1)} %collective-permute-done.11, bf16[2,1,32,8,768]{4,3,2,1,0:T(8,128)(2,1)} %get-tuple-element.39, bf16[2,1,32,8,768]{4,3,2,1,0:T(8,128)(2,1)} %collective-permute-done.10), kind=kLoop, calls=%fused_computation.4 | loop fusion | flops 7077888 | bytes 4718592 | tf_op jit(solution)/shard_map/concatenate | solution.py:175
  116.8 1.2 broadcast_select_fusion
  118.0 5.6 %shard_map.59 = (f32[1,256,768]{2,1,0:T(8,128)}, f32[1,2,256,3]{3,2,1,0:T(8,128)}) custom-call(bf16[1,256,768]{2,1,0:T(8,128)(2,1)} %get-tuple-element.58.q_ref, bf16[2,1,768,768]{3,2,1,0:T(8,128)(2,1)} %bitcast.48, bf16[2,1,768,768]{3,2,1,0:T(8,128)(2,1)} %bitcast.49, f32[256,768]{1,0:T(8,128)} %reshape.649.m_ref), custom_call_target="tpu_custom_call" | custom-call | flops 603979776 | bytes 3538944 | tf_op jit(solution)/shard_map/pallas_call | solution.py:65
  123.6 1.7 %select_bitcast_fusion.1.refs_5_ = f32[1,2,256,3]{3,2,1,0:T(8,128)} fusion(f32[1,2,3,256]{2,3,1,0:T(8,128)} %collective-permute-done.7, pred[]{:T(512)S(6)} %and.269), kind=kLoop, calls=%fused_computation.26 | loop fusion | flops 1536 | bytes 12289 | tf_op jit(solution)/shard_map/jit(_where)/select_n | solution.py:257
  125.3 1.2 broadcast_select_fusion.1
  126.5 1.4 pad_maximum_fusion.3
  127.9 4.4 %shard_map.61 = (bf16[1,256,768]{2,1,0:T(8,128)(2,1)}, f32[1,2,256,3]{3,2,1,0:T(8,128)}) custom-call(bf16[1,256,768]{2,1,0:T(8,128)(2,1)} %bitcast.19.q_ref, bf16[2,1,512,768]{3,2,1,0:T(8,128)(2,1)} %bitcast.52, bf16[2,1,512,768]{3,2,1,0:T(8,128)(2,1)} %bitcast.53, f32[256,512]{1,0:T(8,128)} %reshape.654.m_ref), custom_call_target="tpu_custom_call" | custom-call | flops 402653184 | bytes 2752512 | tf_op jit(solution)/shard_map/pallas_call | solution.py:65
  132.3 1.4 collective-permute-start.15
  133.8 0.7 copy-done.8
  134.5 3.2 %shard_map.58 = bf16[1,256,768]{2,1,0:T(8,128)(2,1)} custom-call(f32[1,256,768]{2,1,0:T(8,128)} %get-tuple-element.31.refs_0_, f32[1,2,256,3]{3,2,1,0:T(8,128)} %get-tuple-element.32.refs_1_, f32[1,256,768]{2,1,0:T(8,128)} %get-tuple-element.34.refs_2_, f32[1,2,256,3]{3,2,1,0:T(8,128)} %get-tuple-element.35.refs_3_, bf16[1,256,768]{2,1,0:T(8,128)(2,1)} %copy-done.8, ...), custom_call_target="tpu_custom_call" | custom-call | tf_op jit(solution)/shard_map/pallas_call | solution.py:118
  137.7 0.9 copy.21.refs_6_
  138.7 1.3 collective-permute-start.16
  139.9 3.7 %shard_map.60 = (f32[1,256,768]{2,1,0:T(8,128)}, f32[1,2,256,3]{3,2,1,0:T(8,128)}) custom-call(bf16[1,256,768]{2,1,0:T(8,128)(2,1)} %get-tuple-element.58.q_ref, bf16[2,1,256,768]{3,2,1,0:T(8,128)(2,1)} %bitcast.58, bf16[2,1,256,768]{3,2,1,0:T(8,128)(2,1)} %bitcast.59, f32[256,256]{1,0:T(8,128)} %reshape.651.m_ref), custom_call_target="tpu_custom_call" | custom-call | flops 201326592 | bytes 1966080 | tf_op jit(solution)/shard_map/pallas_call | solution.py:65
  143.6 5.9 %collective-permute-done.16 = f32[1,2,3,256]{2,3,1,0:T(8,128)S(1)} collective-permute-done((f32[1,2,3,256]{2,3,1,0:T(8,128)S(1)}, f32[1,2,3,256]{2,3,1,0:T(8,128)S(1)}, u32[]{:S(2)}, u32[]{:S(2)}) %collective-permute-start.16) | collective-permute-done | bytes 6176 | tf_op jit(solution)/shard_map/ppermute | solution.py:254
  149.6 0.7 select_bitcast_fusion.refs_5_
  150.3 0.7 copy-done.9
  151.0 3.2 %shard_map.62 = bf16[1,256,768]{2,1,0:T(8,128)(2,1)} custom-call(f32[1,256,768]{2,1,0:T(8,128)} %get-tuple-element.43.refs_0_, f32[1,2,256,3]{3,2,1,0:T(8,128)} %get-tuple-element.44.refs_1_, f32[1,256,768]{2,1,0:T(8,128)} %get-tuple-element.46.refs_2_, f32[1,2,256,3]{3,2,1,0:T(8,128)} %get-tuple-element.47.refs_3_, bf16[1,256,768]{2,1,0:T(8,128)(2,1)} %copy-done.9, ...), custom_call_target="tpu_custom_call" | custom-call | tf_op jit(solution)/shard_map/pallas_call | solution.py:118
  154.3 1.9 %fusion.1 = bf16[1,32,8,768]{3,2,1,0:T(8,128)(2,1)} fusion(bf16[1,32,8,768]{3,2,1,0:T(8,128)(2,1)S(1)} %collective-permute-done.9, bf16[1,256,768]{2,1,0:T(8,128)(2,1)} %shard_map.62, pred[]{:T(512)S(6)} %eq.79), kind=kLoop, calls=%fused_computation.12 | loop fusion | flops 1572864 | bytes 1179649 | tf_op jit(solution)/shard_map/convert_element_type | solution.py:350
  (72 shorter events, 1.4 us)
Async XLA Ops:
  1.2 10.4 %copy-start.10 = (s32[4,15]{1,0:T(4,128)S(1)}, s32[4,15]{1,0:T(4,128)}, u32[]{:S(2)}) copy-start(s32[4,15]{1,0:T(4,128)} %param.8) | copy-start | bytes 724
  2.4 9.2 %copy-start.2 = (bf16[2,1,32,8,1536]{4,3,2,1,0:T(8,128)(2,1)}, bf16[2,1,32,8,1536]{4,3,2,1,0:T(8,128)(2,1)S(1)}, u32[]{:S(2)}) copy-start(bf16[2,1,32,8,1536]{4,3,2,1,0:T(8,128)(2,1)S(1)} %constant_dynamic-update-slice_fusion) | copy-start | bytes 4718596
  3.8 36.5 %collective-permute-start.1 = (bf16[2,1,32,8,768]{4,3,2,1,0:T(8,128)(2,1)}, bf16[2,1,32,8,768]{4,3,2,1,0:T(8,128)(2,1)}, u32[]{:S(2)}, u32[]{:S(2)}) collective-permute-start(bf16[2,1,32,8,768]{4,3,2,1,0:T(8,128)(2,1)} %get-tuple-element.52), channel_id=1, source_target_pairs={{12,8},{8,4},{4,0},{13,9},{9,5},{5,1},{14,10},{10,6},{6,2},{15,11}... | collective-permute-start | bytes 2359304 | tf_op jit(solution)/shard_map/ppermute | solution.py:233
  5.1 36.0 %collective-permute-start = (bf16[2,1,32,8,768]{4,3,2,1,0:T(8,128)(2,1)}, bf16[2,1,32,8,768]{4,3,2,1,0:T(8,128)(2,1)}, u32[]{:S(2)}, u32[]{:S(2)}) collective-permute-start(bf16[2,1,32,8,768]{4,3,2,1,0:T(8,128)(2,1)} %get-tuple-element.52), channel_id=1, source_target_pairs={{0,4},{4,8},{8,12},{1,5},{5,9},{9,13},{2,6},{6,10},{10,14},{3,7},{... | collective-permute-start | bytes 2359304 | tf_op jit(solution)/shard_map/ppermute | solution.py:232
  11.6 28.7 %collective-permute-start.5 = (s32[4,15]{1,0:T(4,128)S(1)}, s32[4,15]{1,0:T(4,128)S(1)}, u32[]{:S(2)}, u32[]{:S(2)}) collective-permute-start(s32[4,15]{1,0:T(4,128)S(1)} %copy-done.10), channel_id=1, source_target_pairs={{0,4},{12,8},{1,5},{13,9},{2,6},{14,10},{3,7},{15,11},{16,20},{28,... | collective-permute-start | bytes 728 | tf_op jit(solution)/shard_map/ppermute | solution.py:191
  19.1 4.1 %copy-start.11 = (s32[2,8]{1,0:T(2,128)S(1)}, s32[2,8]{1,0:T(2,128)}, u32[]{:S(2)}) copy-start(s32[2,8]{1,0:T(2,128)} %param.9) | copy-start | bytes 196
  19.1 5.2 %copy-start.5 = (bf16[1,1,32,8,1536]{4,3,2,1,0:T(8,128)(2,1)S(1)}, bf16[1,1,32,8,1536]{4,3,2,1,0:T(8,128)(2,1)}, u32[]{:S(2)}) copy-start(bf16[1,1,32,8,1536]{4,3,2,1,0:T(8,128)(2,1)} %param.5) | copy-start | bytes 2359300
  19.1 65.4 %collective-permute-start.8 = (bf16[2,1,256,12,128]{4,2,3,1,0:T(8,128)(2,1)}, bf16[2,1,256,12,128]{4,2,3,1,0:T(8,128)(2,1)}, u32[]{:S(2)}, u32[]{:S(2)}) collective-permute-start(bf16[2,1,256,12,128]{4,2,3,1,0:T(8,128)(2,1)} %copy.15), channel_id=1, source_target_pairs={{0,2},{2,0},{1,3},{3,1},{4,6},{6,4},{5,7},{7,5},{8,10},{10,8},{9,1... | collective-permute-start | bytes 4718600 | tf_op jit(solution)/shard_map/ppermute | solution.py:21
  22.3 3.1 %copy-start.6 = (bf16[1,1,32,8,1536]{4,3,2,1,0:T(8,128)(2,1)S(1)}, bf16[1,1,32,8,1536]{4,3,2,1,0:T(8,128)(2,1)}, u32[]{:S(2)}) copy-start(bf16[1,1,32,8,1536]{4,3,2,1,0:T(8,128)(2,1)} %param.5) | copy-start | bytes 2359300
  40.4 28.7 %collective-permute-start.2 = (bf16[2,1,32,8,768]{4,3,2,1,0:T(8,128)(2,1)}, bf16[2,1,32,8,768]{4,3,2,1,0:T(8,128)(2,1)S(1)}, u32[]{:S(2)}, u32[]{:S(2)}) collective-permute-start(bf16[2,1,32,8,768]{4,3,2,1,0:T(8,128)(2,1)} %collective-permute-done.1), channel_id=1, source_target_pairs={{8,4},{9,5},{10,6},{11,7},{24,20},{25,21},{26,22},{27,23}} | collective-permute-start | bytes 2359304 | tf_op jit(solution)/shard_map/ppermute | solution.py:240
  41.1 33.6 %collective-permute-start.3 = (bf16[2,1,32,8,768]{4,3,2,1,0:T(8,128)(2,1)}, bf16[2,1,32,8,768]{4,3,2,1,0:T(8,128)(2,1)}, u32[]{:S(2)}, u32[]{:S(2)}) collective-permute-start(bf16[2,1,32,8,768]{4,3,2,1,0:T(8,128)(2,1)} %collective-permute-done), channel_id=1, source_target_pairs={{4,8},{5,9},{6,10},{7,11},{20,24},{21,25},{22,26},{23,27}} | collective-permute-start | bytes 2359304 | tf_op jit(solution)/shard_map/ppermute | solution.py:241
  50.4 25.5 %collective-permute-start.4 = (bf16[1,32,8,768]{3,2,1,0:T(8,128)(2,1)S(1)}, bf16[1,32,8,768]{3,2,1,0:T(8,128)(2,1)}, u32[]{:S(2)}, u32[]{:S(2)}) collective-permute-start(bf16[1,32,8,768]{3,2,1,0:T(8,128)(2,1)S(1)} %get-tuple-element.30), channel_id=1, source_target_pairs={{0,4},{12,8},{1,5},{13,9},{2,6},{14,10},{3,7},{15,11},{16,20},{28,... | collective-permute-start | bytes 1179656 | tf_op jit(solution)/shard_map/ppermute | solution.py:244
  56.9 39.2 %collective-permute-start.11 = (bf16[2,1,32,8,768]{4,3,2,1,0:T(8,128)(2,1)}, bf16[2,1,32,8,768]{4,3,2,1,0:T(8,128)(2,1)}, u32[]{:S(2)}, u32[]{:S(2)}) collective-permute-start(bf16[2,1,32,8,768]{4,3,2,1,0:T(8,128)(2,1)} %get-tuple-element.39), channel_id=1, source_target_pairs={{12,8},{8,4},{4,0},{13,9},{9,5},{5,1},{14,10},{10,6},{6,2},{15,11}... | collective-permute-start | bytes 2359304 | tf_op jit(solution)/shard_map/ppermute | solution.py:233
  69.1 6.8 %copy-start.4 = (bf16[2,1,32,8,768]{4,3,2,1,0:T(8,128)(2,1)S(1)}, bf16[2,1,32,8,768]{4,3,2,1,0:T(8,128)(2,1)}, u32[]{:S(2)}) copy-start(bf16[2,1,32,8,768]{4,3,2,1,0:T(8,128)(2,1)} %broadcast_select_fusion.2) | copy-start | bytes 2359300
  69.1 5.6 %copy-start.7 = (bf16[2,1,32,8,768]{4,3,2,1,0:T(8,128)(2,1)}, bf16[2,1,32,8,768]{4,3,2,1,0:T(8,128)(2,1)S(1)}, u32[]{:S(2)}) copy-start(bf16[2,1,32,8,768]{4,3,2,1,0:T(8,128)(2,1)S(1)} %collective-permute-done.2) | copy-start | bytes 2359300
  69.1 27.8 %collective-permute-start.10 = (bf16[2,1,32,8,768]{4,3,2,1,0:T(8,128)(2,1)}, bf16[2,1,32,8,768]{4,3,2,1,0:T(8,128)(2,1)}, u32[]{:S(2)}, u32[]{:S(2)}) collective-permute-start(bf16[2,1,32,8,768]{4,3,2,1,0:T(8,128)(2,1)} %get-tuple-element.39), channel_id=1, source_target_pairs={{0,4},{4,8},{8,12},{1,5},{5,9},{9,13},{2,6},{6,10},{10,14},{3,7},{... | collective-permute-start | bytes 2359304 | tf_op jit(solution)/shard_map/ppermute | solution.py:232
  75.9 5.9 %copy-start = (bf16[2,1,32,8,768]{4,3,2,1,0:T(8,128)(2,1)}, bf16[2,1,32,8,768]{4,3,2,1,0:T(8,128)(2,1)S(1)}, u32[]{:S(2)}) copy-start(bf16[2,1,32,8,768]{4,3,2,1,0:T(8,128)(2,1)S(1)} %broadcast_select_fusion.3) | copy-start | bytes 2359300
  81.7 52.0 %collective-permute-start.6 = (bf16[1,256,768]{2,1,0:T(8,128)(2,1)}, bf16[1,256,768]{2,1,0:T(8,128)(2,1)S(1)}, u32[]{:S(2)}, u32[]{:S(2)}) collective-permute-start(bf16[1,256,768]{2,1,0:T(8,128)(2,1)} %get-tuple-element.37), channel_id=1, source_target_pairs={{4,0},{8,12},{5,1},{9,13},{6,2},{10,14},{7,3},{11,15},{20,16},{24,... | collective-permute-start | bytes 1179656 | tf_op jit(solution)/shard_map/ppermute | solution.py:254
  83.0 40.5 %collective-permute-start.7 = (f32[1,2,3,256]{2,3,1,0:T(8,128)}, f32[1,2,3,256]{2,3,1,0:T(8,128)}, u32[]{:S(2)}, u32[]{:S(2)}) collective-permute-start(f32[1,2,3,256]{2,3,1,0:T(8,128)} %bitcast.63), channel_id=1, source_target_pairs={{4,0},{8,12},{5,1},{9,13},{6,2},{10,14},{7,3},{11,15},{20,16},{24,... | collective-permute-start | bytes 18440 | tf_op jit(solution)/shard_map/ppermute | solution.py:254
  88.3 3.2 %copy-start.3 = (bf16[2,2,256,12,128]{4,3,2,0,1:T(8,128)(2,1)S(1)}, bf16[2,2,256,12,128]{4,3,2,0,1:T(8,128)(2,1)}, u32[]{:S(2)}) copy-start(bf16[2,2,256,12,128]{4,3,2,0,1:T(8,128)(2,1)} %copy_dynamic-update-slice_fusion) | copy-start | bytes 9437188
  96.1 29.2 %collective-permute-start.12 = (bf16[2,1,32,8,768]{4,3,2,1,0:T(8,128)(2,1)}, bf16[2,1,32,8,768]{4,3,2,1,0:T(8,128)(2,1)S(1)}, u32[]{:S(2)}, u32[]{:S(2)}) collective-permute-start(bf16[2,1,32,8,768]{4,3,2,1,0:T(8,128)(2,1)} %collective-permute-done.11), channel_id=1, source_target_pairs={{8,4},{9,5},{10,6},{11,7},{24,20},{25,21},{26,22},{27,23}} | collective-permute-start | bytes 2359304 | tf_op jit(solution)/shard_map/ppermute | solution.py:240
  96.8 28.4 %collective-permute-start.13 = (bf16[2,1,32,8,768]{4,3,2,1,0:T(8,128)(2,1)}, bf16[2,1,32,8,768]{4,3,2,1,0:T(8,128)(2,1)}, u32[]{:S(2)}, u32[]{:S(2)}) collective-permute-start(bf16[2,1,32,8,768]{4,3,2,1,0:T(8,128)(2,1)} %collective-permute-done.10), channel_id=1, source_target_pairs={{4,8},{5,9},{6,10},{7,11},{20,24},{21,25},{22,26},{23,27}} | collective-permute-start | bytes 2359304 | tf_op jit(solution)/shard_map/ppermute | solution.py:241
  99.4 27.1 %collective-permute-start.14 = (bf16[1,32,8,768]{3,2,1,0:T(8,128)(2,1)}, bf16[1,32,8,768]{3,2,1,0:T(8,128)(2,1)}, u32[]{:S(2)}, u32[]{:S(2)}) collective-permute-start(bf16[1,32,8,768]{3,2,1,0:T(8,128)(2,1)} %get-tuple-element.42), channel_id=1, source_target_pairs={{0,4},{12,8},{1,5},{13,9},{2,6},{14,10},{3,7},{15,11},{16,20},{28,... | collective-permute-start | bytes 1179656 | tf_op jit(solution)/shard_map/ppermute | solution.py:244
  126.5 5.8 %copy-start.1 = (bf16[2,1,32,8,768]{4,3,2,1,0:T(8,128)(2,1)}, bf16[2,1,32,8,768]{4,3,2,1,0:T(8,128)(2,1)S(1)}, u32[]{:S(2)}) copy-start(bf16[2,1,32,8,768]{4,3,2,1,0:T(8,128)(2,1)S(1)} %broadcast_select_fusion.1) | copy-start | bytes 2359300
  132.3 6.3 %copy-start.12 = (f32[1,2,256,3]{3,2,1,0:T(8,128)S(1)}, f32[1,2,256,3]{3,2,1,0:T(8,128)}, u32[]{:S(2)}) copy-start(f32[1,2,256,3]{3,2,1,0:T(8,128)} %get-tuple-element.50) | copy-start | bytes 18436
  132.3 18.0 %collective-permute-start.15 = (bf16[1,256,768]{2,1,0:T(8,128)(2,1)}, bf16[1,256,768]{2,1,0:T(8,128)(2,1)S(1)}, u32[]{:S(2)}, u32[]{:S(2)}) collective-permute-start(bf16[1,256,768]{2,1,0:T(8,128)(2,1)} %get-tuple-element.49), channel_id=1, source_target_pairs={{4,0},{8,12},{5,1},{9,13},{6,2},{10,14},{7,3},{11,15},{20,16},{24,... | collective-permute-start | bytes 1179656 | tf_op jit(solution)/shard_map/ppermute | solution.py:254
  133.8 0.7 copy-start.8
  137.7 16.6 %collective-permute-start.9 = (bf16[1,32,8,768]{3,2,1,0:T(8,128)(2,1)}, bf16[1,32,8,768]{3,2,1,0:T(8,128)(2,1)S(1)}, u32[]{:S(2)}, u32[]{:S(2)}) collective-permute-start(bf16[1,32,8,768]{3,2,1,0:T(8,128)(2,1)} %bitcast.61), channel_id=1, source_target_pairs={{0,1},{1,0},{2,3},{3,2},{4,5},{5,4},{6,7},{7,6},{8,9},{9,8},{10,11... | collective-permute-start | bytes 1179656 | tf_op jit(solution)/shard_map/ppermute | solution.py:25
  138.7 10.9 %collective-permute-start.16 = (f32[1,2,3,256]{2,3,1,0:T(8,128)S(1)}, f32[1,2,3,256]{2,3,1,0:T(8,128)S(1)}, u32[]{:S(2)}, u32[]{:S(2)}) collective-permute-start(f32[1,2,3,256]{2,3,1,0:T(8,128)S(1)} %bitcast.64), channel_id=1, source_target_pairs={{4,0},{8,12},{5,1},{9,13},{6,2},{10,14},{7,3},{11,15},{20,16},{24,... | collective-permute-start | bytes 18440 | tf_op jit(solution)/shard_map/ppermute | solution.py:254
  150.3 0.7 copy-start.9

commit v7 on v4

--- a/solution.py
+++ b/solution.py
@@ -204,29 +204,29 @@
         scale,
     )
 
-    onward = jnp.where(index == 1, from_left, from_right)
-    two_away = lax.ppermute(onward, "lon", [(1, 2), (2, 1)])
+    two_away = jnp.where(
+        index <= 1,
+        lax.ppermute(from_right, "lon", [(2, 1), (1, 0)]),
+        lax.ppermute(from_left, "lon", [(1, 2), (2, 3)]),
+    )
     held_q, _ = lax.optimization_barrier((own_q, from_left))
     guest_q = lax.ppermute(held_q, "lon", [(0, 1), (3, 2)])
     near_part, two_away, guest_q = lax.optimization_barrier((near_part, two_away, guest_q))
 
     guest_device = jnp.where(index == 1, 0, count - 1)
-    near_block = jnp.where(index == 1, index + 1, index - 1)
     far_block = (index + 2) % count
-    guest_key_cols = jnp.concatenate(
-        [near_block * columns + column_ids, far_block * columns + column_ids]
-    )
+    far_cols = far_block * columns + column_ids
     guest_active = window_mask(
         guest_device * columns + column_ids,
-        guest_key_cols,
+        far_cols,
         jnp.repeat(guest_map, BLK, axis=0),
         total_cols,
         lat_rows,
     ) & is_middle
-    guest_near = jnp.where(index == 1, from_right, from_left)
+    far_keys = flat_keys([two_away])
     guest_out, guest_lse = spatial_attention(
         guest_q.reshape(frames, lat_rows * columns, model_width),
-        flat_keys([guest_near, two_away]),
+        far_keys,
         expand_mask(guest_active, lat_rows),
         scale,
     )
@@ -239,12 +239,8 @@
     returned_lse = jnp.where(is_middle, masked_score, jnp.swapaxes(returned_lse, 2, 3))
     assert returned_lse.shape == lse_shape
 
-    far_active = window_mask(
-        own_cols, far_block * columns + column_ids, own_map, total_cols, lat_rows
-    ) & is_middle
-    far_part = spatial_attention(
-        query_flat, flat_keys([two_away]), expand_mask(far_active, lat_rows), scale
-    )
+    far_active = window_mask(own_cols, far_cols, own_map, total_cols, lat_rows)
+    far_part = spatial_attention(query_flat, far_keys, expand_mask(far_active, lat_rows), scale)
     return [near_part, far_part, (returned, returned_lse)]
 
 

time: 137 us -> 133 us (0.971)
  other arithmetic: 25.7 us -> 19.5 us
  starting transfers between devices: 23.1 us -> 27.3 us
  Pallas kernels: 26 us -> 24.4 us
    select_n x1, other arithmetic: 3.73 us -> 1.31 us  [spatial_line_of_four(): jnp.where(index <= 1, lax.ppermute(from_right, 'lon', [(2, 1), (1, 0)]),...]
    ppermute x1 -> x2, starting transfers between devices: 0.75 us -> 3.13 us  [the longest x1 1.83 us: spatial_line_of_four(): lax.ppermute(from_left, 'lon', [(1, 2), (2, 3)])]
    concatenate x2 -> x1, other arithmetic: 7.11 us -> 4.78 us  [flat_keys(): joined = jnp.concatenate(blocks, axis=3)]
    ppermute x1, starting transfers between devices: 7.44 us -> 9.25 us  [spatial_line_of_four(): guest_q = lax.ppermute(held_q, 'lon', [(0, 1), (3, 2)])]
    pallas_call x3, Pallas kernels: 20.6 us -> 19 us  [spatial_attention(): pl.pallas_call(functools.partial(spatial_kernel, scale=scale), grid=(fram...]
    unnamed x20 -> x14, local copies, waits for them, and re-layouts: 4.78 us -> 4.79 us
  transfers between devices with their start and end apart: 9 -> 10, of which waited for: 3 -> 3; matrix products, arithmetic and copies ran while one was open for 41% -> 40% of each run, Pallas kernels for 10% -> 10%
where the time goes in v7:
time: 133 us; the launch traced here: 132 us
  local copies, waits for them, and re-layouts  41.6 us (31%)
  starting transfers between devices  27.3 us (21%)
  Pallas kernels  24.4 us (18%)
  other arithmetic  19.5 us (15%)
  waiting for transfers between devices  19.1 us (14%)
    pallas_call x3, Pallas kernels, spatial_attention(): pl.pallas_call(functools.partial(spatial_kernel, scale=scale), grid=(fram...  19 us
    reshape x3, local copies, waits for them, and re-layouts, expand_mask(): return jnp.broadcast_to(active[None, :, None, :].astype(jnp.float32), (la...  14.1 us
    ppermute x2, waiting for transfers between devices, spatial_line_of_four(): lax.ppermute((guest_out.astype(jnp.bfloat16), jnp.swapaxes(guest_lse, 2,...  13 us
    ppermute x1, starting transfers between devices, spatial_line_of_four(): guest_q = lax.ppermute(held_q, 'lon', [(0, 1), (3, 2)])  9.25 us
    broadcast_in_dim x3, local copies, waits for them, and re-layouts, expand_mask(): jnp.broadcast_to(active[None, :, None, :].astype(jnp.float32), (lat_rows,...  7.35 us
    ppermute x1, starting transfers between devices, spatial_line_of_four(): from_left = lax.ppermute(key_value, 'lon', [(0, 1), (1, 2), (2, 3)])  6.77 us
    pallas_call x1, Pallas kernels, combine_partials(): pl.pallas_call(combine_kernel, grid=(frames, groups), in_specs=[big, smal...  5.36 us
    unnamed x14, local copies, waits for them, and re-layouts  4.79 us
  transfers between devices with their start and end apart: 10, of which 3 were waited for; matrix products, arithmetic and copies ran while one was open for 40% of the time, Pallas kernels for 10%

profile of v7, /device:TPU:0, one launch (start us, length us, event | category | flops | bytes accessed | tf_op | source)
XLA Modules:
  0.0 132.0 jit_solution(103944231825350782)
XLA Ops:
  0.0 2.1 %constant_dynamic-update-slice_fusion.1 = bf16[2,1,32,8,1536]{4,3,2,1,0:T(8,128)(2,1)} fusion(bf16[1,1,32,8,1536]{4,3,2,1,0:T(8,128)(2,1)} %param.6), kind=kLoop, calls=%fused_computation.27 | loop fusion | bytes 1572864
  2.1 0.0 copy-done.3
  2.2 1.0 constant_dynamic-update-slice_fusion
  3.1 1.3 collective-permute-start.1
  4.4 6.8 %collective-permute-start = (bf16[2,1,32,8,1536]{4,3,2,1,0:T(8,128)(2,1)}, bf16[2,1,32,8,1536]{4,3,2,1,0:T(8,128)(2,1)}, u32[]{:S(2)}, u32[]{:S(2)}) collective-permute-start(bf16[2,1,32,8,1536]{4,3,2,1,0:T(8,128)(2,1)} %constant_dynamic-update-slice_fusion), channel_id=1, source_target_pairs={{0,4},{4,8},{8,12},{1,5},{5,9},{9,13},{2,6},{6,10},{10,14},{3,7},{... | collective-permute-start | bytes 4718600 | tf_op jit(solution)/shard_map/ppermute | solution.py:191
  11.2 2.7 %collective-permute-start.5 = (s32[4,15]{1,0:T(4,128)S(1)}, s32[4,15]{1,0:T(4,128)S(1)}, u32[]{:S(2)}, u32[]{:S(2)}) collective-permute-start(s32[4,15]{1,0:T(4,128)S(1)} %copy-done.4), channel_id=1, source_target_pairs={{0,4},{12,8},{1,5},{13,9},{2,6},{14,10},{3,7},{15,11},{16,20},{28,... | collective-permute-start | bytes 728 | tf_op jit(solution)/shard_map/ppermute | solution.py:193
  13.9 2.9 %reshape.555 = bf16[2,1,256,12,128]{4,3,2,0,1:T(8,128)(2,1)S(1)} reshape(bf16[2,1,32,8,1536]{4,3,2,1,0:T(8,128)(2,1)} %constant_dynamic-update-slice_fusion) | data formatting | bytes 3145728 | tf_op jit(solution)/shard_map/reshape | solution.py:297
  16.8 1.6 %copy.12 = bf16[2,1,256,12,128]{4,2,3,1,0:T(8,128)(2,1)} copy(bf16[2,1,256,12,128]{4,3,2,0,1:T(8,128)(2,1)S(1)} %reshape.555) | data formatting | bytes 3145728 | tf_op jit(solution)/shard_map/reshape | solution.py:297
  18.4 1.5 %collective-permute-start.8 = (bf16[2,1,256,12,128]{4,2,3,1,0:T(8,128)(2,1)}, bf16[2,1,256,12,128]{4,2,3,1,0:T(8,128)(2,1)}, u32[]{:S(2)}, u32[]{:S(2)}) collective-permute-start(bf16[2,1,256,12,128]{4,2,3,1,0:T(8,128)(2,1)} %copy.12), channel_id=1, source_target_pairs={{0,2},{2,0},{1,3},{3,1},{4,6},{6,4},{5,7},{7,5},{8,10},{10,8},{9,1... | collective-permute-start | bytes 4718600 | tf_op jit(solution)/shard_map/ppermute | solution.py:21
  20.0 0.1 copy.11
  20.1 0.1 pad_add_fusion
  20.1 0.1 broadcast_in_dim.35
  20.2 0.1 and.236
  20.3 0.1 add_select_fusion.2
  20.4 0.1 fusion.6
  20.5 2.4 %broadcast_in_dim.36 = f32[32,8,32,24]{3,2,1,0:T(8,128)} broadcast(f32[8,24]{1,0:T(8,128)S(1)} %and_convert_fusion.1), dimensions={1,3} | broadcast | bytes 787200 | tf_op jit(solution)/shard_map/broadcast_in_dim | solution.py:169
  23.0 4.6 %reshape.550.m_ref = f32[256,768]{1,0:T(8,128)} reshape(f32[32,8,32,24]{3,2,1,0:T(8,128)} %broadcast_in_dim.36) | data formatting | bytes 1572864 | tf_op jit(solution)/shard_map/reshape | solution.py:171
  27.6 0.1 add_select_fusion
  27.7 0.3 fusion.8
  28.0 2.5 %broadcast_in_dim.37 = f32[32,8,32,8]{3,2,1,0:T(8,128)} broadcast(f32[8,8]{1,0:T(8,128)S(1)} %convert_element_type.72), dimensions={1,3} | broadcast | bytes 262400 | tf_op jit(solution)/shard_map/broadcast_in_dim | solution.py:169
  30.4 4.8 %reshape.552.m_ref = f32[256,256]{1,0:T(8,128)} reshape(f32[32,8,32,8]{3,2,1,0:T(8,128)} %broadcast_in_dim.37) | data formatting | bytes 524288 | tf_op jit(solution)/shard_map/reshape | solution.py:171
  35.2 1.8 %reshape.557 = f32[256,12,128]{2,1,0:T(8,128)} reshape(bf16[1,1,32,8,1536]{4,3,2,1,0:T(8,128)(2,1)S(1)} %copy-done.1) | data formatting | bytes 2359296 | tf_op jit(solution)/shard_map/convert_element_type | solution.py:128
  37.0 0.1 tile.10
  37.2 0.6 gather_fusion
  37.8 1.7 %constant_dynamic-update-slice_fusion.2 = bf16[2,2,256,12,128]{4,3,2,0,1:T(8,128)(2,1)} fusion(bf16[2,1,256,12,128]{4,3,2,0,1:T(8,128)(2,1)S(1)} %reshape.555), kind=kLoop, calls=%fused_computation.28 | loop fusion | bytes 3670016
  39.5 0.1 compare_or_fusion
  39.6 4.3 %collective-permute-done.5 = s32[4,15]{1,0:T(4,128)S(1)} collective-permute-done((s32[4,15]{1,0:T(4,128)S(1)}, s32[4,15]{1,0:T(4,128)S(1)}, u32[]{:S(2)}, u32[]{:S(2)}) %collective-permute-start.5) | collective-permute-done | bytes 272 | tf_op jit(solution)/shard_map/ppermute | solution.py:193
  44.0 0.3 fusion.10
  44.3 0.0 collective-permute-done.1
  44.3 1.3 collective-permute-start.2
  45.6 0.0 collective-permute-done
  45.6 1.8 %collective-permute-start.3 = (bf16[2,1,32,8,1536]{4,3,2,1,0:T(8,128)(2,1)}, bf16[2,1,32,8,1536]{4,3,2,1,0:T(8,128)(2,1)}, u32[]{:S(2)}, u32[]{:S(2)}) collective-permute-start(bf16[2,1,32,8,1536]{4,3,2,1,0:T(8,128)(2,1)} %collective-permute-done), channel_id=1, source_target_pairs={{4,8},{8,12},{5,9},{9,13},{6,10},{10,14},{7,11},{11,15},{20,24},{2... | collective-permute-start | bytes 4718600 | tf_op jit(solution)/shard_map/ppermute | solution.py:210
  47.4 2.5 %broadcast_in_dim.39 = f32[32,8,32,8]{3,2,1,0:T(8,128)} broadcast(f32[8,8]{1,0:T(8,128)S(1)} %and_convert_fusion), dimensions={1,3} | broadcast | bytes 262400 | tf_op jit(solution)/shard_map/broadcast_in_dim | solution.py:169
  49.9 4.7 %reshape.554.m_ref = f32[256,256]{1,0:T(8,128)} reshape(f32[32,8,32,8]{3,2,1,0:T(8,128)} %broadcast_in_dim.39) | data formatting | bytes 524288 | tf_op jit(solution)/shard_map/reshape | solution.py:171
  54.6 9.2 %collective-permute-start.4 = (bf16[1,32,8,1536]{3,2,1,0:T(8,128)(2,1)S(1)}, bf16[1,32,8,1536]{3,2,1,0:T(8,128)(2,1)}, u32[]{:S(2)}, u32[]{:S(2)}) collective-permute-start(bf16[1,32,8,1536]{3,2,1,0:T(8,128)(2,1)S(1)} %bitcast.35), channel_id=1, source_target_pairs={{0,4},{12,8},{1,5},{13,9},{2,6},{14,10},{3,7},{15,11},{16,20},{28,... | collective-permute-start | bytes 2359304 | tf_op jit(solution)/shard_map/ppermute | solution.py:213
  63.8 4.8 %pad_maximum_fusion = bf16[2,1,32,24,1536]{4,3,2,1,0:T(8,128)(2,1)} fusion(bf16[2,1,32,8,1536]{4,3,2,1,0:T(8,128)(2,1)} %collective-permute-done.1, bf16[2,1,32,8,1536]{4,3,2,1,0:T(8,128)(2,1)} %constant_dynamic-update-slice_fusion, bf16[2,1,32,8,1536]{4,3,2,1,0:T(8,128)(2,1)} %collective-permute-done), kind=kLoop, calls=%fused_computation.1 | loop fusion | flops 14155776 | bytes 9437184 | tf_op jit(solution)/shard_map/concatenate | solution.py:175
  68.6 8.4 %shard_map.55 = (f32[1,256,1536]{2,1,0:T(8,128)}, f32[1,3,256,4]{3,2,1,0:T(8,128)}) custom-call(bf16[1,256,1536]{2,1,0:T(8,128)(2,1)} %bitcast.33, bf16[2,1,768,1536]{3,2,1,0:T(8,128)(2,1)} %bitcast.27, bf16[2,1,768,1536]{3,2,1,0:T(8,128)(2,1)} %bitcast.28, f32[256,768]{1,0:T(8,128)} %reshape.550.m_ref), custom_call_target="tpu_custom_call" | custom-call | flops 1207959552 | bytes 7077888 | tf_op jit(solution)/shard_map/pallas_call | solution.py:65
  77.0 0.0 collective-permute-done.8
  77.0 4.0 %copy_dynamic-update-slice_fusion = bf16[2,2,256,12,128]{4,3,2,0,1:T(8,128)(2,1)} fusion(bf16[2,2,256,12,128]{4,3,2,0,1:T(8,128)(2,1)} %constant_dynamic-update-slice_fusion.2, bf16[2,1,256,12,128]{4,2,3,1,0:T(8,128)(2,1)} %collective-permute-done.8), kind=kLoop, calls=%fused_computation.4 | loop fusion | bytes 3670016 | tf_op jit(solution)/shard_map/concatenate | solution.py:301
  81.1 2.8 %multiply_reduce_fusion.1 = f32[2,256,12]{2,1,0:T(8,128)S(1)} fusion(bf16[2,2,256,12,128]{4,3,2,0,1:T(8,128)(2,1)} %copy_dynamic-update-slice_fusion, f32[256,12,128]{2,1,0:T(8,128)S(1)} %copy-done), kind=kLoop, calls=%fused_computation.3 | loop fusion | flops 2353152 | bytes 3170304 | tf_op jit(solution)/shard_map/reduce_sum | solution.py:130
  83.9 0.1 fusion.2
  84.0 0.1 fusion.3
  84.2 0.0 collective-permute-done.2
  84.2 0.0 collective-permute-done.3
  84.2 1.3 broadcast_select_fusion
  85.5 0.0 collective-permute-done.4
  85.5 5.3 %shard_map.57 = (f32[1,256,1536]{2,1,0:T(8,128)}, f32[1,3,256,4]{3,2,1,0:T(8,128)}) custom-call(bf16[1,256,1536]{2,1,0:T(8,128)(2,1)} %bitcast.7.q_ref, bf16[2,1,256,1536]{3,2,1,0:T(8,128)(2,1)} %bitcast.29, bf16[2,1,256,1536]{3,2,1,0:T(8,128)(2,1)} %bitcast.30, f32[256,256]{1,0:T(8,128)} %reshape.554.m_ref), custom_call_target="tpu_custom_call" | custom-call | flops 402653184 | bytes 3932160 | tf_op jit(solution)/shard_map/pallas_call | solution.py:65
  90.8 1.5 %convert_element_type.74 = bf16[1,256,1536]{2,1,0:T(8,128)(2,1)S(1)} convert(f32[1,256,1536]{2,1,0:T(8,128)} %get-tuple-element.25) | non-fusion elementwise | flops 393216 | bytes 2359296 | tf_op jit(solution)/shard_map/convert_element_type | solution.py:235
  92.3 1.3 collective-permute-start.6
  93.6 4.2 %multiply_reduce_fusion = f32[256,12,128]{2,1,0:T(8,128)S(1)} fusion(bf16[2,2,256,12,128]{4,3,2,0,1:T(8,128)(2,1)} %copy_dynamic-update-slice_fusion, f32[2,256,12]{2,1,0:T(8,128)S(1)} %get-tuple-element.28), kind=kLoop, calls=%fused_computation.2 | loop fusion | flops 1966080 | bytes 3170304 | tf_op jit(solution)/shard_map/reduce_sum | solution.py:138
  97.8 0.7 reduce-precision_convert_fusion
  98.6 0.9 copy.14
  99.4 1.2 copy.15.refs_6_
  100.6 1.3 collective-permute-start.7
  101.9 5.3 %shard_map.56 = (f32[1,256,1536]{2,1,0:T(8,128)}, f32[1,3,256,4]{3,2,1,0:T(8,128)}) custom-call(bf16[1,256,1536]{2,1,0:T(8,128)(2,1)} %bitcast.34, bf16[2,1,256,1536]{3,2,1,0:T(8,128)(2,1)} %bitcast.31, bf16[2,1,256,1536]{3,2,1,0:T(8,128)(2,1)} %bitcast.32, f32[256,256]{1,0:T(8,128)} %reshape.552.m_ref), custom_call_target="tpu_custom_call" | custom-call | flops 402653184 | bytes 3932160 | tf_op jit(solution)/shard_map/pallas_call | solution.py:65
  107.2 13.0 %collective-permute-done.7 = f32[1,3,4,256]{2,3,1,0:T(8,128)S(1)} collective-permute-done((f32[1,3,4,256]{2,3,1,0:T(8,128)}, f32[1,3,4,256]{2,3,1,0:T(8,128)S(1)}, u32[]{:S(2)}, u32[]{:S(2)}) %collective-permute-start.7) | collective-permute-done | bytes 12320 | tf_op jit(solution)/shard_map/ppermute | solution.py:234
  120.2 0.8 select_bitcast_fusion.refs_5_
  121.0 0.0 collective-permute-done.6.refs_4_
  121.0 0.9 copy-done.2
  121.9 5.4 %shard_map.58 = bf16[1,256,1536]{2,1,0:T(8,128)(2,1)} custom-call(f32[1,256,1536]{2,1,0:T(8,128)} %get-tuple-element.19.refs_0_, f32[1,3,256,4]{3,2,1,0:T(8,128)} %get-tuple-element.20.refs_1_, f32[1,256,1536]{2,1,0:T(8,128)} %get-tuple-element.22.refs_2_, f32[1,3,256,4]{3,2,1,0:T(8,128)} %get-tuple-element.23.refs_3_, bf16[1,256,1536]{2,1,0:T(8,128)(2,1)} %copy-done.2, ...), custom_call_target="tpu_custom_call" | custom-call | tf_op jit(solution)/shard_map/pallas_call | solution.py:118
  127.3 1.0 constant_dynamic-slice_fusion
  128.3 0.1 collective-permute-start.9
  128.4 1.7 %collective-permute-done.9 = bf16[1,32,8,768]{3,2,1,0:T(8,128)(2,1)S(1)} collective-permute-done((bf16[1,32,8,768]{3,2,1,0:T(8,128)(2,1)S(1)}, bf16[1,32,8,768]{3,2,1,0:T(8,128)(2,1)S(1)}, u32[]{:S(2)}, u32[]{:S(2)}) %collective-permute-start.9) | collective-permute-done | bytes 393248 | tf_op jit(solution)/shard_map/ppermute | solution.py:25
  130.1 1.9 %fusion.1 = bf16[1,32,8,768]{3,2,1,0:T(8,128)(2,1)} fusion(bf16[1,32,8,768]{3,2,1,0:T(8,128)(2,1)S(1)} %collective-permute-done.9, bf16[1,32,8,1536]{3,2,1,0:T(8,128)(2,1)} %bitcast.38, s32[]{:T(128)S(6)} %select_n.230, pred[]{:T(512)S(6)} %eq.73), kind=kLoop, calls=%fused_computation.10 | loop fusion | flops 1572864 | bytes 1179653 | tf_op jit(solution)/shard_map/convert_element_type | solution.py:324
  (27 shorter events, 0.2 us)
Async XLA Ops:
  0.0 2.2 %copy-start.3 = (bf16[1,1,32,8,1536]{4,3,2,1,0:T(8,128)(2,1)S(1)}, bf16[1,1,32,8,1536]{4,3,2,1,0:T(8,128)(2,1)}, u32[]{:S(2)}) copy-start(bf16[1,1,32,8,1536]{4,3,2,1,0:T(8,128)(2,1)} %param.7) | copy-start | bytes 2359300
  0.0 11.2 %copy-start.4 = (s32[4,15]{1,0:T(4,128)S(1)}, s32[4,15]{1,0:T(4,128)}, u32[]{:S(2)}) copy-start(s32[4,15]{1,0:T(4,128)} %param.8) | copy-start | bytes 724
  3.1 41.2 %collective-permute-start.1 = (bf16[2,1,32,8,1536]{4,3,2,1,0:T(8,128)(2,1)}, bf16[2,1,32,8,1536]{4,3,2,1,0:T(8,128)(2,1)}, u32[]{:S(2)}, u32[]{:S(2)}) collective-permute-start(bf16[2,1,32,8,1536]{4,3,2,1,0:T(8,128)(2,1)} %constant_dynamic-update-slice_fusion), channel_id=1, source_target_pairs={{12,8},{8,4},{4,0},{13,9},{9,5},{5,1},{14,10},{10,6},{6,2},{15,11}... | collective-permute-start | bytes 4718600 | tf_op jit(solution)/shard_map/ppermute | solution.py:192
  4.4 41.2 %collective-permute-start = (bf16[2,1,32,8,1536]{4,3,2,1,0:T(8,128)(2,1)}, bf16[2,1,32,8,1536]{4,3,2,1,0:T(8,128)(2,1)}, u32[]{:S(2)}, u32[]{:S(2)}) collective-permute-start(bf16[2,1,32,8,1536]{4,3,2,1,0:T(8,128)(2,1)} %constant_dynamic-update-slice_fusion), channel_id=1, source_target_pairs={{0,4},{4,8},{8,12},{1,5},{5,9},{9,13},{2,6},{6,10},{10,14},{3,7},{... | collective-permute-start | bytes 4718600 | tf_op jit(solution)/shard_map/ppermute | solution.py:191
  11.2 32.8 %collective-permute-start.5 = (s32[4,15]{1,0:T(4,128)S(1)}, s32[4,15]{1,0:T(4,128)S(1)}, u32[]{:S(2)}, u32[]{:S(2)}) collective-permute-start(s32[4,15]{1,0:T(4,128)S(1)} %copy-done.4), channel_id=1, source_target_pairs={{0,4},{12,8},{1,5},{13,9},{2,6},{14,10},{3,7},{15,11},{16,20},{28,... | collective-permute-start | bytes 728 | tf_op jit(solution)/shard_map/ppermute | solution.py:193
  18.4 58.6 %collective-permute-start.8 = (bf16[2,1,256,12,128]{4,2,3,1,0:T(8,128)(2,1)}, bf16[2,1,256,12,128]{4,2,3,1,0:T(8,128)(2,1)}, u32[]{:S(2)}, u32[]{:S(2)}) collective-permute-start(bf16[2,1,256,12,128]{4,2,3,1,0:T(8,128)(2,1)} %copy.12), channel_id=1, source_target_pairs={{0,2},{2,0},{1,3},{3,1},{4,6},{6,4},{5,7},{7,5},{8,10},{10,8},{9,1... | collective-permute-start | bytes 4718600 | tf_op jit(solution)/shard_map/ppermute | solution.py:21
  30.4 4.8 %copy-start.1 = (bf16[1,1,32,8,1536]{4,3,2,1,0:T(8,128)(2,1)S(1)}, bf16[1,1,32,8,1536]{4,3,2,1,0:T(8,128)(2,1)}, u32[]{:S(2)}) copy-start(bf16[1,1,32,8,1536]{4,3,2,1,0:T(8,128)(2,1)} %param.5) | copy-start | bytes 2359300
  35.2 1.8 %copy-start.5 = (s32[2,8]{1,0:T(2,128)S(1)}, s32[2,8]{1,0:T(2,128)}, u32[]{:S(2)}) copy-start(s32[2,8]{1,0:T(2,128)} %param.9) | copy-start | bytes 196
  44.3 39.9 %collective-permute-start.2 = (bf16[2,1,32,8,1536]{4,3,2,1,0:T(8,128)(2,1)}, bf16[2,1,32,8,1536]{4,3,2,1,0:T(8,128)(2,1)S(1)}, u32[]{:S(2)}, u32[]{:S(2)}) collective-permute-start(bf16[2,1,32,8,1536]{4,3,2,1,0:T(8,128)(2,1)} %collective-permute-done.1), channel_id=1, source_target_pairs={{8,4},{4,0},{9,5},{5,1},{10,6},{6,2},{11,7},{7,3},{24,20},{20,16},... | collective-permute-start | bytes 4718600 | tf_op jit(solution)/shard_map/ppermute | solution.py:209
  45.6 38.6 %collective-permute-start.3 = (bf16[2,1,32,8,1536]{4,3,2,1,0:T(8,128)(2,1)}, bf16[2,1,32,8,1536]{4,3,2,1,0:T(8,128)(2,1)}, u32[]{:S(2)}, u32[]{:S(2)}) collective-permute-start(bf16[2,1,32,8,1536]{4,3,2,1,0:T(8,128)(2,1)} %collective-permute-done), channel_id=1, source_target_pairs={{4,8},{8,12},{5,9},{9,13},{6,10},{10,14},{7,11},{11,15},{20,24},{2... | collective-permute-start | bytes 4718600 | tf_op jit(solution)/shard_map/ppermute | solution.py:210
  54.6 31.0 %collective-permute-start.4 = (bf16[1,32,8,1536]{3,2,1,0:T(8,128)(2,1)S(1)}, bf16[1,32,8,1536]{3,2,1,0:T(8,128)(2,1)}, u32[]{:S(2)}, u32[]{:S(2)}) collective-permute-start(bf16[1,32,8,1536]{3,2,1,0:T(8,128)(2,1)S(1)} %bitcast.35), channel_id=1, source_target_pairs={{0,4},{12,8},{1,5},{13,9},{2,6},{14,10},{3,7},{15,11},{16,20},{28,... | collective-permute-start | bytes 2359304 | tf_op jit(solution)/shard_map/ppermute | solution.py:213
  77.0 4.0 %copy-start = (f32[256,12,128]{2,1,0:T(8,128)S(1)}, f32[256,12,128]{2,1,0:T(8,128)}, u32[]{:S(2)}) copy-start(f32[256,12,128]{2,1,0:T(8,128)} %reshape.557) | copy-start | bytes 4718596
  92.3 28.7 %collective-permute-start.6 = (bf16[1,256,1536]{2,1,0:T(8,128)(2,1)S(1)}, bf16[1,256,1536]{2,1,0:T(8,128)(2,1)S(1)}, u32[]{:S(2)}, u32[]{:S(2)}) collective-permute-start(bf16[1,256,1536]{2,1,0:T(8,128)(2,1)S(1)} %convert_element_type.74), channel_id=1, source_target_pairs={{4,0},{8,12},{5,1},{9,13},{6,2},{10,14},{7,3},{11,15},{20,16},{24,... | collective-permute-start | bytes 2359304 | tf_op jit(solution)/shard_map/ppermute | solution.py:234
  100.6 19.6 %collective-permute-start.7 = (f32[1,3,4,256]{2,3,1,0:T(8,128)}, f32[1,3,4,256]{2,3,1,0:T(8,128)S(1)}, u32[]{:S(2)}, u32[]{:S(2)}) collective-permute-start(f32[1,3,4,256]{2,3,1,0:T(8,128)} %bitcast.40), channel_id=1, source_target_pairs={{4,0},{8,12},{5,1},{9,13},{6,2},{10,14},{7,3},{11,15},{20,16},{24,... | collective-permute-start | bytes 36872 | tf_op jit(solution)/shard_map/ppermute | solution.py:234
  121.0 0.9 copy-start.2
  128.3 1.8 %collective-permute-start.9 = (bf16[1,32,8,768]{3,2,1,0:T(8,128)(2,1)S(1)}, bf16[1,32,8,768]{3,2,1,0:T(8,128)(2,1)S(1)}, u32[]{:S(2)}, u32[]{:S(2)}) collective-permute-start(bf16[1,32,8,768]{3,2,1,0:T(8,128)(2,1)S(1)} %constant_dynamic-slice_fusion), channel_id=1, source_target_pairs={{0,1},{1,0},{2,3},{3,2},{4,5},{5,4},{6,7},{7,6},{8,9},{9,8},{10,11... | collective-permute-start | bytes 1179656 | tf_op jit(solution)/shard_map/ppermute | solution.py:25

commit v8 on v7

--- a/solution.py
+++ b/solution.py
@@ -4,6 +4,7 @@
 import jax.numpy as jnp
 from jax import lax
 from jax.experimental import pallas as pl
+from jax.experimental.pallas import tpu as pltpu
 from jax.sharding import PartitionSpec as P
 
 DH = 128
@@ -32,7 +33,8 @@
     return DH
 
 
-def spatial_kernel(q_ref, k_ref, v_ref, m_ref, o_ref, lse_ref, *, scale):
+def spatial_kernel(first_ref, q_ref, k_ref, v_ref, m_ref, o_ref, lse_ref, *, scale):
+    del first_ref
     allowed = m_ref[...] > 0
     for head in range(q_ref.shape[-1] // DH):
         lanes = slice(head * DH, (head + 1) * DH)
@@ -52,43 +54,52 @@
         result = jnp.dot(
             weights.astype(jnp.bfloat16), v_ref[:, lanes], preferred_element_type=jnp.float32
         )
-        o_ref[:, lanes] = result / totals
+        o_ref[:, lanes] = (result / totals).astype(o_ref.dtype)
         lse_ref[:, head : head + 1] = maxima + jnp.log(totals)
 
 
-def spatial_attention(query_flat, key_value_flat, mask, scale):
+def spatial_attention(
+    query_flat, key_value_flat, mask, scale, out_dtype=jnp.float32, first=None, count=None
+):
     frames, query_count, model_width = query_flat.shape
     key_count = key_value_flat.shape[2]
-    head_count = model_width // DH
-    width = group_width(model_width)
+    width = group_width(model_width // 2)
     groups = model_width // width
+    if first is None:
+        first, count = jnp.zeros((1,), jnp.int32), groups
+    grid_spec = pltpu.PrefetchScalarGridSpec(
+        num_scalar_prefetch=1,
+        grid=(frames, count),
+        in_specs=[
+            pl.BlockSpec((None, query_count, width), lambda f, g, s: (f, 0, s[0] + g)),
+            pl.BlockSpec((None, None, key_count, width), lambda f, g, s: (0, f, 0, s[0] + g)),
+            pl.BlockSpec((None, None, key_count, width), lambda f, g, s: (1, f, 0, s[0] + g)),
+            pl.BlockSpec((query_count, key_count), lambda f, g, s: (0, 0)),
+        ],
+        out_specs=[
+            pl.BlockSpec((None, query_count, width), lambda f, g, s: (f, 0, g)),
+            pl.BlockSpec((None, None, query_count, width // DH), lambda f, g, s: (f, g, 0, 0)),
+        ],
+    )
+    used = count * width
     return pl.pallas_call(
         functools.partial(spatial_kernel, scale=scale),
-        grid=(frames, groups),
-        in_specs=[
-            pl.BlockSpec((None, query_count, width), lambda f, g: (f, 0, g)),
-            pl.BlockSpec((None, None, key_count, width), lambda f, g: (0, f, 0, g)),
-            pl.BlockSpec((None, None, key_count, width), lambda f, g: (1, f, 0, g)),
-            pl.BlockSpec((query_count, key_count), lambda f, g: (0, 0)),
-        ],
-        out_specs=[
-            pl.BlockSpec((None, query_count, width), lambda f, g: (f, 0, g)),
-            pl.BlockSpec((None, None, query_count, width // DH), lambda f, g: (f, g, 0, 0)),
-        ],
+        grid_spec=grid_spec,
         out_shape=[
-            jax.ShapeDtypeStruct((frames, query_count, model_width), jnp.float32),
-            jax.ShapeDtypeStruct((frames, groups, query_count, width // DH), jnp.float32),
+            jax.ShapeDtypeStruct((frames, query_count, used), out_dtype),
+            jax.ShapeDtypeStruct((frames, count, query_count, width // DH), jnp.float32),
         ],
         cost_estimate=pl.CostEstimate(
-            flops=4 * frames * query_count * key_count * model_width,
-            transcendentals=frames * head_count * query_count * key_count,
-            bytes_accessed=2 * model_width * frames * (query_count + 2 * key_count)
-            + 4 * frames * query_count * model_width,
+            flops=4 * frames * query_count * key_count * used,
+            transcendentals=frames * (used // DH) * query_count * key_count,
+            bytes_accessed=2 * used * frames * (query_count + 2 * key_count)
+            + 4 * frames * query_count * used,
         ),
-    )(query_flat, key_value_flat, key_value_flat, mask)
-
-
-def combine_kernel(*refs):
+    )(first, query_flat, key_value_flat, key_value_flat, mask)
+
+
+def combine_kernel(first_ref, *refs):
+    del first_ref
     *parts, temporal_ref, mixed_ref = refs
     outs, lses = parts[0::2], parts[1::2]
     for head in range(mixed_ref.shape[-1] // DH):
@@ -106,22 +117,38 @@
         )
 
 
-def combine_partials(partials, temporal):
+def combine_partials(partials, temporal, first=None, count=None):
     frames, query_count, model_width = temporal.shape
-    width = group_width(model_width)
+    width = group_width(model_width // 2)
     groups = model_width // width
-    big = pl.BlockSpec((None, query_count, width), lambda f, g: (f, 0, g))
-    small = pl.BlockSpec((None, None, query_count, width // DH), lambda f, g: (f, g, 0, 0))
-    operands = []
-    for out, lse in partials:
+    if first is None:
+        first, count = jnp.zeros((1,), jnp.int32), groups
+    heads = width // DH
+    in_specs, operands = [], []
+    for out, lse, whole in partials:
+        if whole:
+            in_specs += [
+                pl.BlockSpec((None, query_count, width), lambda f, g, s: (f, 0, s[0] + g)),
+                pl.BlockSpec((None, None, query_count, heads), lambda f, g, s: (f, s[0] + g, 0, 0)),
+            ]
+        else:
+            in_specs += [
+                pl.BlockSpec((None, query_count, width), lambda f, g, s: (f, 0, g)),
+                pl.BlockSpec((None, None, query_count, heads), lambda f, g, s: (f, g, 0, 0)),
+            ]
         operands += [out, lse]
+    in_specs.append(pl.BlockSpec((None, query_count, width), lambda f, g, s: (f, 0, s[0] + g)))
+    grid_spec = pltpu.PrefetchScalarGridSpec(
+        num_scalar_prefetch=1,
+        grid=(frames, count),
+        in_specs=in_specs,
+        out_specs=pl.BlockSpec((None, query_count, width), lambda f, g, s: (f, 0, g)),
+    )
     return pl.pallas_call(
         combine_kernel,
-        grid=(frames, groups),
-        in_specs=[big, small] * len(partials) + [big],
-        out_specs=big,
-        out_shape=jax.ShapeDtypeStruct((frames, query_count, model_width), jnp.bfloat16),
-    )(*operands, temporal)
+        grid_spec=grid_spec,
+        out_shape=jax.ShapeDtypeStruct((frames, query_count, count * width), jnp.bfloat16),
+    )(first, *operands, temporal)
 
 
 def temporal_attention(own_q, all_k, all_v, valid, own_ids, all_ids, scale):
@@ -177,7 +204,7 @@
     return joined.reshape(two, frames, lat_rows * cols, model_width)
 
 
-def spatial_line_of_four(own_q, key_value, window_map, scale):
+def spatial_line_of_four(own_q, key_value, window_map, temporal, scale):
     frames, lat_rows, columns, model_width = own_q.shape
     count = 4
     total_cols = count * columns
@@ -224,24 +251,35 @@
         lat_rows,
     ) & is_middle
     far_keys = flat_keys([two_away])
-    guest_out, guest_lse = spatial_attention(
-        guest_q.reshape(frames, lat_rows * columns, model_width),
-        far_keys,
-        expand_mask(guest_active, lat_rows),
-        scale,
-    )
-    lse_shape = guest_lse.shape
-    returned, returned_lse = lax.ppermute(
-        (guest_out.astype(jnp.bfloat16), jnp.swapaxes(guest_lse, 2, 3)),
-        "lon",
-        [(1, 0), (2, 3)],
-    )
-    returned_lse = jnp.where(is_middle, masked_score, jnp.swapaxes(returned_lse, 2, 3))
-    assert returned_lse.shape == lse_shape
-
     far_active = window_mask(own_cols, far_cols, own_map, total_cols, lat_rows)
-    far_part = spatial_attention(query_flat, far_keys, expand_mask(far_active, lat_rows), scale)
-    return [near_part, far_part, (returned, returned_lse)]
+    guest_flat = guest_q.reshape(frames, lat_rows * columns, model_width)
+    guest_mask = expand_mask(guest_active, lat_rows)
+    branch_index = lax.axis_index("branch")
+    half_groups = (model_width // group_width(model_width // 2)) // 2
+    sends = []
+    for half_index in (1 - branch_index, branch_index):
+        first = jnp.reshape(half_index * half_groups, (1,)).astype(jnp.int32)
+        guest_out, guest_lse = spatial_attention(
+            guest_flat, far_keys, guest_mask, scale, jnp.bfloat16, first, half_groups
+        )
+        returned, returned_lse = lax.ppermute(
+            (guest_out, jnp.swapaxes(guest_lse, 2, 3)), "lon", [(1, 0), (2, 3)]
+        )
+        returned_lse = jnp.where(is_middle, masked_score, jnp.swapaxes(returned_lse, 2, 3))
+        sends.append((returned, returned_lse, first, guest_out))
+    far_query, _ = lax.optimization_barrier((query_flat, sends[-1][3]))
+    far_part = spatial_attention(far_query, far_keys, expand_mask(far_active, lat_rows), scale)
+    halves = []
+    for returned, returned_lse, first, _ in sends:
+        halves.append(
+            combine_partials(
+                [near_part + (True,), far_part + (True,), (returned, returned_lse, False)],
+                temporal,
+                first,
+                half_groups,
+            ).reshape(frames, lat_rows, columns, model_width // 2)
+        )
+    return halves
 
 
 def local(queries, keys, values, window_map, frame_valid):
@@ -258,10 +296,29 @@
     key_value = jnp.stack([own_k, own_v])
     column_ids = jnp.arange(columns, dtype=jnp.int32)
     per_column_map = jnp.repeat(window_map, BLK, axis=0)
+    token_count = lat_rows * columns
+    tm_count = lax.axis_size("tm")
+    tm_index = lax.axis_index("tm")
+    key_value_rows = key_value.reshape(2, frames, token_count, head_count, DH)
+    pieces = [key_value_rows]
+    for step_by in range(1, tm_count):
+        pieces.append(shifted(key_value_rows, "tm", step_by))
+    gathered = jnp.concatenate(pieces, axis=1)
+    piece_ids = jnp.arange(tm_count * frames, dtype=jnp.int32)
+    frame_ids = ((tm_index - piece_ids // frames) % tm_count) * frames + piece_ids % frames
+    valid_tokens = jnp.take(jnp.tile(frame_valid, (1, lat_rows)), frame_ids, axis=0)
+    temporal = temporal_attention(
+        own_q.reshape(frames, token_count, head_count, DH),
+        gathered[0],
+        gathered[1],
+        valid_tokens,
+        frame_ids[:frames],
+        frame_ids,
+        scale,
+    )
+    temporal = temporal.reshape(frames, token_count, model_width)
     full_ring = ext_count >= total_cols and WIN * BLK <= total_cols
-    if full_ring and lon_count == 4:
-        partials = spatial_line_of_four(own_q, key_value, window_map, scale)
-    else:
+    if not (full_ring and lon_count == 4):
         if full_ring:
             extended = jnp.concatenate(line_gather(key_value, "lon"), axis=3)
             key_cols = total_cols
@@ -291,32 +348,17 @@
             spatial_attention(query_flat, key_value_flat, expand_mask(active, lat_rows), scale)
         ]
 
-    token_count = lat_rows * columns
-    tm_count = lax.axis_size("tm")
-    tm_index = lax.axis_index("tm")
-    key_value_rows = key_value.reshape(2, frames, token_count, head_count, DH)
-    pieces = [key_value_rows]
-    for step_by in range(1, tm_count):
-        pieces.append(shifted(key_value_rows, "tm", step_by))
-    gathered = jnp.concatenate(pieces, axis=1)
-    piece_ids = jnp.arange(tm_count * frames, dtype=jnp.int32)
-    frame_ids = ((tm_index - piece_ids // frames) % tm_count) * frames + piece_ids % frames
-    valid_tokens = jnp.take(jnp.tile(frame_valid, (1, lat_rows)), frame_ids, axis=0)
-    temporal = temporal_attention(
-        own_q.reshape(frames, token_count, head_count, DH),
-        gathered[0],
-        gathered[1],
-        valid_tokens,
-        frame_ids[:frames],
-        frame_ids,
-        scale,
-    )
-    temporal = temporal.reshape(frames, token_count, model_width)
-    mixed = combine_partials(partials, temporal).reshape(frames, lat_rows, columns, model_width)
     half_width = model_width // 2
     branch_index = lax.axis_index("branch")
-    own_half = lax.dynamic_slice_in_dim(mixed, branch_index * half_width, half_width, 3)
-    other_half = lax.dynamic_slice_in_dim(mixed, (1 - branch_index) * half_width, half_width, 3)
+    if full_ring and lon_count == 4:
+        other_half, own_half = spatial_line_of_four(own_q, key_value, window_map, temporal, scale)
+    else:
+        mixed = combine_partials([partial + (True,) for partial in partials], temporal)
+        mixed = mixed.reshape(frames, lat_rows, columns, model_width)
+        own_half = lax.dynamic_slice_in_dim(mixed, branch_index * half_width, half_width, 3)
+        other_half = lax.dynamic_slice_in_dim(
+            mixed, (1 - branch_index) * half_width, half_width, 3
+        )
     partner = from_partner(other_half, "branch", 0)
     is_conditional = branch_index == 0
     conditional = jnp.where(is_conditional, own_half, partner).astype(jnp.float32)

time: 133 us -> 156 us (1.17)
  waiting for transfers between devices: 19.1 us -> 43.4 us
  Pallas kernels: 24.4 us -> 28.5 us
  local copies, waits for them, and re-layouts: 41.6 us -> 38.9 us
    ppermute x1, waiting for transfers between devices: 0.01 us -> 12.1 us  [spatial_line_of_four(): lax.ppermute(from_right, 'lon', [(2, 1), (1, 0)])]
    ppermute x1, waiting for transfers between devices: 4.33 us -> 13.1 us  [spatial_line_of_four(): guest_map = lax.ppermute(window_map, 'lon', [(0, 1), (3, 2)])]
    ppermute x2 -> x4, waiting for transfers between devices: 13 us -> 18.1 us  [spatial_line_of_four(): lax.ppermute((guest_out, jnp.swapaxes(guest_lse, 2, 3)), 'lon', [(1, 0),...]
    pallas_call x4 -> x6, Pallas kernels: 24.4 us -> 28.5 us  [the longest x4 21.9 us: spatial_attention(): pl.pallas_call(functools.partial(spatial_kernel, scale=scale), grid_spec=...]
    ppermute x1, starting transfers between devices: 9.25 us -> 5.26 us  [spatial_line_of_four(): guest_q = lax.ppermute(held_q, 'lon', [(0, 1), (3, 2)])]
    ppermute x2 -> x4, starting transfers between devices: 2.57 us -> 5.15 us  [spatial_line_of_four(): lax.ppermute((guest_out, jnp.swapaxes(guest_lse, 2, 3)), 'lon', [(1, 0),...]
    ppermute x1, waiting for transfers between devices: 1.7 us -> 0.01 us  [from_partner(): lax.ppermute(value, axis, [(i, i ^ 1 << bit) for i in range(lax.axis_size...]
    unnamed x14 -> x18, local copies, waits for them, and re-layouts: 4.79 us -> 4.67 us
  transfers between devices with their start and end apart: 10 -> 12, of which waited for: 3 -> 4; matrix products, arithmetic and copies ran while one was open for 40% -> 33% of each run, Pallas kernels for 10% -> 16%
where the time goes in v8:
time: 156 us
  waiting for transfers between devices  43.4 us (28%)
  local copies, waits for them, and re-layouts  38.9 us (25%)
  Pallas kernels  28.5 us (18%)
  starting transfers between devices  25.9 us (17%)
  other arithmetic  18.7 us (12%)
    pallas_call x4, Pallas kernels, spatial_attention(): pl.pallas_call(functools.partial(spatial_kernel, scale=scale), grid_spec=...  21.9 us
    ppermute x4, waiting for transfers between devices, spatial_line_of_four(): lax.ppermute((guest_out, jnp.swapaxes(guest_lse, 2, 3)), 'lon', [(1, 0),...  18.1 us
    reshape x3, local copies, waits for them, and re-layouts, expand_mask(): return jnp.broadcast_to(active[None, :, None, :].astype(jnp.float32), (la...  14.1 us
    ppermute x1, waiting for transfers between devices, spatial_line_of_four(): guest_map = lax.ppermute(window_map, 'lon', [(0, 1), (3, 2)])  13.1 us
    ppermute x1, waiting for transfers between devices, spatial_line_of_four(): lax.ppermute(from_right, 'lon', [(2, 1), (1, 0)])  12.1 us
    broadcast_in_dim x3, local copies, waits for them, and re-layouts, expand_mask(): jnp.broadcast_to(active[None, :, None, :].astype(jnp.float32), (lat_rows,...  7.37 us
    ppermute x1, starting transfers between devices, spatial_line_of_four(): from_left = lax.ppermute(key_value, 'lon', [(0, 1), (1, 2), (2, 3)])  6.71 us
    pallas_call x2, Pallas kernels, combine_partials(): pl.pallas_call(combine_kernel, grid_spec=grid_spec, out_shape=jax.ShapeDt...  6.61 us
  transfers between devices with their start and end apart: 12, of which 4 were waited for; matrix products, arithmetic and copies ran while one was open for 33% of the time, Pallas kernels for 16%

profile of v8, /device:TPU:0, one launch (start us, length us, event | category | flops | bytes accessed | tf_op | source)
XLA Modules:
  0.0 155.6 jit_solution(16836949131514801955)
XLA Ops:
  0.0 2.1 %constant_dynamic-update-slice_fusion.1 = bf16[2,1,32,8,1536]{4,3,2,1,0:T(8,128)(2,1)} fusion(bf16[1,1,32,8,1536]{4,3,2,1,0:T(8,128)(2,1)} %param.6), kind=kLoop, calls=%fused_computation.30 | loop fusion | bytes 1572864
  2.1 0.9 constant_dynamic-update-slice_fusion
  3.1 1.3 collective-permute-start.1
  4.4 6.7 %collective-permute-start = (bf16[2,1,32,8,1536]{4,3,2,1,0:T(8,128)(2,1)}, bf16[2,1,32,8,1536]{4,3,2,1,0:T(8,128)(2,1)}, u32[]{:S(2)}, u32[]{:S(2)}) collective-permute-start(bf16[2,1,32,8,1536]{4,3,2,1,0:T(8,128)(2,1)} %constant_dynamic-update-slice_fusion), channel_id=1, source_target_pairs={{0,4},{4,8},{8,12},{1,5},{5,9},{9,13},{2,6},{6,10},{10,14},{3,7},{... | collective-permute-start | bytes 4718600 | tf_op jit(solution)/shard_map/ppermute | solution.py:218
  11.1 2.8 %collective-permute-start.5 = (s32[4,15]{1,0:T(4,128)S(1)}, s32[4,15]{1,0:T(4,128)S(1)}, u32[]{:S(2)}, u32[]{:S(2)}) collective-permute-start(s32[4,15]{1,0:T(4,128)S(1)} %copy-done.4), channel_id=1, source_target_pairs={{0,4},{12,8},{1,5},{13,9},{2,6},{14,10},{3,7},{15,11},{16,20},{28,... | collective-permute-start | bytes 728 | tf_op jit(solution)/shard_map/ppermute | solution.py:220
  13.9 2.9 %reshape.566 = bf16[2,1,256,12,128]{4,3,2,0,1:T(8,128)(2,1)S(1)} reshape(bf16[2,1,32,8,1536]{4,3,2,1,0:T(8,128)(2,1)} %constant_dynamic-update-slice_fusion) | data formatting | bytes 3145728 | tf_op jit(solution)/shard_map/reshape | solution.py:302
  16.8 0.0 copy-start.5
  16.8 1.6 copy.14
  18.3 1.5 collective-permute-start.8
  20.0 0.1 add_select_fusion.2
  20.1 0.1 pad_add_fusion
  20.2 0.1 copy.13
  20.3 0.1 broadcast_in_dim.39
  20.4 0.1 and.236
  20.5 0.1 tile.10
  20.6 0.6 gather_fusion
  21.1 0.1 fusion.6
  21.2 1.7 %constant_dynamic-update-slice_fusion.2 = bf16[2,2,256,12,128]{4,3,2,0,1:T(8,128)(2,1)} fusion(bf16[2,1,256,12,128]{4,3,2,0,1:T(8,128)(2,1)S(1)} %reshape.566), kind=kLoop, calls=%fused_computation.31 | loop fusion | bytes 3670016
  23.0 0.1 compare_or_fusion
  23.1 0.1 add_select_fusion
  23.1 2.5 %broadcast_in_dim.40 = f32[32,8,32,24]{3,2,1,0:T(8,128)} broadcast(f32[8,24]{1,0:T(8,128)S(1)} %and_convert_fusion.1), dimensions={1,3} | broadcast | bytes 787200 | tf_op jit(solution)/shard_map/broadcast_in_dim | solution.py:196
  25.6 4.7 %reshape.560.m_ref = f32[256,768]{1,0:T(8,128)} reshape(f32[32,8,32,24]{3,2,1,0:T(8,128)} %broadcast_in_dim.40) | data formatting | bytes 1572864 | tf_op jit(solution)/shard_map/reshape | solution.py:198
  30.3 0.5 reshape.569
  30.8 13.1 %collective-permute-done.5 = s32[4,15]{1,0:T(4,128)S(1)} collective-permute-done((s32[4,15]{1,0:T(4,128)S(1)}, s32[4,15]{1,0:T(4,128)S(1)}, u32[]{:S(2)}, u32[]{:S(2)}) %collective-permute-start.5) | collective-permute-done | bytes 272 | tf_op jit(solution)/shard_map/ppermute | solution.py:220
  43.9 0.4 fusion.8
  44.4 2.5 %broadcast_in_dim.42 = f32[32,8,32,8]{3,2,1,0:T(8,128)} broadcast(f32[8,8]{1,0:T(8,128)S(1)} %and_convert_fusion), dimensions={1,3} | broadcast | bytes 262400 | tf_op jit(solution)/shard_map/broadcast_in_dim | solution.py:196
  46.8 4.7 %reshape.564.m_ref = f32[256,256]{1,0:T(8,128)} reshape(f32[32,8,32,8]{3,2,1,0:T(8,128)} %broadcast_in_dim.42) | data formatting | bytes 524288 | tf_op jit(solution)/shard_map/reshape | solution.py:198
  51.5 2.5 %broadcast_in_dim.43 = f32[32,8,32,8]{3,2,1,0:T(8,128)} broadcast(f32[8,8]{1,0:T(8,128)S(1)} %convert_element_type.70), dimensions={1,3} | broadcast | bytes 262400 | tf_op jit(solution)/shard_map/broadcast_in_dim | solution.py:196
  54.0 4.7 %reshape.565.m_ref = f32[256,256]{1,0:T(8,128)} reshape(f32[32,8,32,8]{3,2,1,0:T(8,128)} %broadcast_in_dim.43) | data formatting | bytes 524288 | tf_op jit(solution)/shard_map/reshape | solution.py:198
  58.6 0.0 collective-permute-done
  58.6 5.3 %collective-permute-start.4 = (bf16[1,32,8,1536]{3,2,1,0:T(8,128)(2,1)S(1)}, bf16[1,32,8,1536]{3,2,1,0:T(8,128)(2,1)}, u32[]{:S(2)}, u32[]{:S(2)}) collective-permute-start(bf16[1,32,8,1536]{3,2,1,0:T(8,128)(2,1)S(1)} %bitcast.49), channel_id=1, source_target_pairs={{0,4},{12,8},{1,5},{13,9},{2,6},{14,10},{3,7},{15,11},{16,20},{28,... | collective-permute-start | bytes 2359304 | tf_op jit(solution)/shard_map/ppermute | solution.py:240
  63.9 1.8 %collective-permute-start.3 = (bf16[2,1,32,8,1536]{4,3,2,1,0:T(8,128)(2,1)}, bf16[2,1,32,8,1536]{4,3,2,1,0:T(8,128)(2,1)}, u32[]{:S(2)}, u32[]{:S(2)}) collective-permute-start(bf16[2,1,32,8,1536]{4,3,2,1,0:T(8,128)(2,1)} %collective-permute-done), channel_id=1, source_target_pairs={{4,8},{8,12},{5,9},{9,13},{6,10},{10,14},{7,11},{11,15},{20,24},{2... | collective-permute-start | bytes 4718600 | tf_op jit(solution)/shard_map/ppermute | solution.py:237
  65.7 1.5 collective-permute-start.2
  67.2 0.0 collective-permute-done.8
  67.2 3.9 %copy_dynamic-update-slice_fusion = bf16[2,2,256,12,128]{4,3,2,0,1:T(8,128)(2,1)} fusion(bf16[2,2,256,12,128]{4,3,2,0,1:T(8,128)(2,1)} %constant_dynamic-update-slice_fusion.2, bf16[2,1,256,12,128]{4,2,3,1,0:T(8,128)(2,1)} %collective-permute-done.8), kind=kLoop, calls=%fused_computation.4 | loop fusion | bytes 3670016 | tf_op jit(solution)/shard_map/concatenate | solution.py:306
  71.1 2.8 %multiply_reduce_fusion.1 = f32[2,256,12]{2,1,0:T(8,128)S(1)} fusion(bf16[2,2,256,12,128]{4,3,2,0,1:T(8,128)(2,1)} %copy_dynamic-update-slice_fusion, f32[256,12,128]{2,1,0:T(8,128)S(1)} %reshape.569), kind=kLoop, calls=%fused_computation.3 | loop fusion | flops 2353152 | bytes 3170304 | tf_op jit(solution)/shard_map/reduce_sum | solution.py:157
  73.9 0.1 fusion.2
  74.0 0.1 fusion.3
  74.2 5.0 %pad_maximum_fusion = bf16[2,1,32,24,1536]{4,3,2,1,0:T(8,128)(2,1)} fusion(bf16[2,1,32,8,1536]{4,3,2,1,0:T(8,128)(2,1)} %collective-permute-done.1, bf16[2,1,32,8,1536]{4,3,2,1,0:T(8,128)(2,1)} %constant_dynamic-update-slice_fusion, bf16[2,1,32,8,1536]{4,3,2,1,0:T(8,128)(2,1)} %collective-permute-done), kind=kLoop, calls=%fused_computation.1 | loop fusion | flops 14155776 | bytes 9437184 | tf_op jit(solution)/shard_map/concatenate | solution.py:202
  79.1 2.9 %multiply_reduce_fusion = f32[256,12,128]{2,1,0:T(8,128)S(1)} fusion(bf16[2,2,256,12,128]{4,3,2,0,1:T(8,128)(2,1)S(1)} %copy-done, f32[2,256,12]{2,1,0:T(8,128)S(1)} %get-tuple-element.34), kind=kLoop, calls=%fused_computation.2 | loop fusion | flops 1966080 | bytes 3170304 | tf_op jit(solution)/shard_map/reduce_sum | solution.py:165
  82.1 8.7 %shard_map.55 = (f32[1,256,1536]{2,1,0:T(8,128)}, f32[1,4,256,3]{3,2,1,0:T(8,128)}) custom-call(s32[1]{0:T(128)} %constant.173.clone.1.first_ref, bf16[1,256,1536]{2,1,0:T(8,128)(2,1)} %bitcast.47, bf16[2,1,768,1536]{3,2,1,0:T(8,128)(2,1)} %bitcast.45, bf16[2,1,768,1536]{3,2,1,0:T(8,128)(2,1)} %bitcast.46, f32[256,768]{1,0:T(8,128)} %reshape.560.m_ref), custom_call_target="tpu_custom_call" | custom-call | flops 1207959552 | bytes 7077888 | tf_op jit(solution)/shard_map/pallas_call | solution.py:85
  90.8 12.1 %collective-permute-done.2 = bf16[2,1,32,8,1536]{4,3,2,1,0:T(8,128)(2,1)} collective-permute-done((bf16[2,1,32,8,1536]{4,3,2,1,0:T(8,128)(2,1)}, bf16[2,1,32,8,1536]{4,3,2,1,0:T(8,128)(2,1)}, u32[]{:S(2)}, u32[]{:S(2)}) %collective-permute-start.2) | collective-permute-done | bytes 1572896 | tf_op jit(solution)/shard_map/ppermute | solution.py:236
  102.9 0.0 collective-permute-done.3
  102.9 2.7 %broadcast_select_fusion = bf16[2,1,32,8,1536]{4,3,2,1,0:T(8,128)(2,1)} fusion(bf16[2,1,32,8,1536]{4,3,2,1,0:T(8,128)(2,1)} %collective-permute-done.2, bf16[2,1,32,8,1536]{4,3,2,1,0:T(8,128)(2,1)} %collective-permute-done.3, pred[]{:T(512)S(6)} %le.15), kind=kLoop, calls=%fused_computation.6 | loop fusion | flops 786432 | bytes 4718593 | tf_op jit(solution)/shard_map/jit(_where)/select_n | solution.py:234
  105.7 0.0 collective-permute-done.4
  105.7 3.6 %shard_map.58 = (bf16[1,256,768]{2,1,0:T(8,128)(2,1)}, f32[1,2,256,3]{3,2,1,0:T(8,128)}) custom-call(s32[1]{0:T(128)} %bitcast.first_ref, bf16[1,256,1536]{2,1,0:T(8,128)(2,1)} %bitcast.8.q_ref, bf16[2,1,256,1536]{3,2,1,0:T(8,128)(2,1)} %bitcast.39, bf16[2,1,256,1536]{3,2,1,0:T(8,128)(2,1)} %bitcast.40, f32[256,256]{1,0:T(8,128)} %reshape.564.m_ref), custom_call_target="tpu_custom_call" | custom-call | flops 201326592 | bytes 1966080 | tf_op jit(solution)/shard_map/pallas_call | solution.py:85
  109.3 1.3 collective-permute-start.6
  110.6 0.7 reduce-precision_convert_fusion
  111.3 0.9 copy.16
  112.2 1.2 copy.17.refs_6_
  113.3 3.7 %shard_map.56 = (bf16[1,256,768]{2,1,0:T(8,128)(2,1)}, f32[1,2,256,3]{3,2,1,0:T(8,128)}) custom-call(s32[1]{0:T(128)} %bitcast.7.first_ref, bf16[1,256,1536]{2,1,0:T(8,128)(2,1)} %bitcast.8.q_ref, bf16[2,1,256,1536]{3,2,1,0:T(8,128)(2,1)} %bitcast.41, bf16[2,1,256,1536]{3,2,1,0:T(8,128)(2,1)} %bitcast.42, f32[256,256]{1,0:T(8,128)} %reshape.564.m_ref), custom_call_target="tpu_custom_call" | custom-call | flops 201326592 | bytes 1966080 | tf_op jit(solution)/shard_map/pallas_call | solution.py:85
  117.0 1.3 collective-permute-start.10
  118.3 1.3 collective-permute-start.7
  119.6 5.8 %shard_map.57 = (f32[1,256,1536]{2,1,0:T(8,128)}, f32[1,4,256,3]{3,2,1,0:T(8,128)}) custom-call(s32[1]{0:T(128)} %constant.173.clone.1.first_ref, bf16[1,256,1536]{2,1,0:T(8,128)(2,1)} %bitcast.48, bf16[2,1,256,1536]{3,2,1,0:T(8,128)(2,1)} %bitcast.43, bf16[2,1,256,1536]{3,2,1,0:T(8,128)(2,1)} %bitcast.44, f32[256,256]{1,0:T(8,128)} %reshape.565.m_ref), custom_call_target="tpu_custom_call" | custom-call | flops 402653184 | bytes 3932160 | tf_op jit(solution)/shard_map/pallas_call | solution.py:85
  125.4 8.8 %collective-permute-done.7 = f32[1,2,3,256]{2,3,1,0:T(8,128)S(1)} collective-permute-done((f32[1,2,3,256]{2,3,1,0:T(8,128)S(1)}, f32[1,2,3,256]{2,3,1,0:T(8,128)S(1)}, u32[]{:S(2)}, u32[]{:S(2)}) %collective-permute-start.7) | collective-permute-done | bytes 6176 | tf_op jit(solution)/shard_map/ppermute | solution.py:265
  134.3 0.7 select_bitcast_fusion.1.refs_5_
  135.0 3.3 %shard_map.59 = bf16[1,256,768]{2,1,0:T(8,128)(2,1)} custom-call(s32[1]{0:T(128)} %bitcast.first_ref, f32[1,256,1536]{2,1,0:T(8,128)} %get-tuple-element.22.refs_0_, f32[1,4,256,3]{3,2,1,0:T(8,128)} %get-tuple-element.23.refs_1_, f32[1,256,1536]{2,1,0:T(8,128)} %get-tuple-element.28.refs_2_, f32[1,4,256,3]{3,2,1,0:T(8,128)} %get-tuple-element.29.refs_3_, ...), custom_call_target="tpu_custom_call" | custom-call | tf_op jit(solution)/shard_map/pallas_call | solution.py:147
  138.3 1.3 collective-permute-start.11
  139.6 9.3 %collective-permute-done.11 = f32[1,2,3,256]{2,3,1,0:T(8,128)S(1)} collective-permute-done((f32[1,2,3,256]{2,3,1,0:T(8,128)S(1)}, f32[1,2,3,256]{2,3,1,0:T(8,128)S(1)}, u32[]{:S(2)}, u32[]{:S(2)}) %collective-permute-start.11) | collective-permute-done | bytes 6176 | tf_op jit(solution)/shard_map/ppermute | solution.py:265
  148.9 0.7 select_bitcast_fusion.refs_5_
  149.7 0.8 copy-done.3
  150.4 3.3 %shard_map.60 = bf16[1,256,768]{2,1,0:T(8,128)(2,1)} custom-call(s32[1]{0:T(128)} %bitcast.7.first_ref, f32[1,256,1536]{2,1,0:T(8,128)} %get-tuple-element.22.refs_0_, f32[1,4,256,3]{3,2,1,0:T(8,128)} %get-tuple-element.23.refs_1_, f32[1,256,1536]{2,1,0:T(8,128)} %get-tuple-element.28.refs_2_, f32[1,4,256,3]{3,2,1,0:T(8,128)} %get-tuple-element.29.refs_3_, ...), custom_call_target="tpu_custom_call" | custom-call | tf_op jit(solution)/shard_map/pallas_call | solution.py:147
  153.7 0.0 collective-permute-done.9
  153.7 1.9 %fusion.1 = bf16[1,32,8,768]{3,2,1,0:T(8,128)(2,1)} fusion(bf16[1,32,8,768]{3,2,1,0:T(8,128)(2,1)S(1)} %collective-permute-done.9, bf16[1,256,768]{2,1,0:T(8,128)(2,1)} %shard_map.60, pred[]{:T(512)S(6)} %eq.73), kind=kLoop, calls=%fused_computation.10 | loop fusion | flops 1572864 | bytes 1179649 | tf_op jit(solution)/shard_map/convert_element_type | solution.py:366
  (36 shorter events, 0.2 us)
Async XLA Ops:
  0.0 2.1 %copy-start.2 = (bf16[1,1,32,8,1536]{4,3,2,1,0:T(8,128)(2,1)S(1)}, bf16[1,1,32,8,1536]{4,3,2,1,0:T(8,128)(2,1)}, u32[]{:S(2)}) copy-start(bf16[1,1,32,8,1536]{4,3,2,1,0:T(8,128)(2,1)} %param.7) | copy-start | bytes 2359300
  0.0 11.1 %copy-start.4 = (s32[4,15]{1,0:T(4,128)S(1)}, s32[4,15]{1,0:T(4,128)}, u32[]{:S(2)}) copy-start(s32[4,15]{1,0:T(4,128)} %param.8) | copy-start | bytes 724
  3.1 62.6 %collective-permute-start.1 = (bf16[2,1,32,8,1536]{4,3,2,1,0:T(8,128)(2,1)}, bf16[2,1,32,8,1536]{4,3,2,1,0:T(8,128)(2,1)}, u32[]{:S(2)}, u32[]{:S(2)}) collective-permute-start(bf16[2,1,32,8,1536]{4,3,2,1,0:T(8,128)(2,1)} %constant_dynamic-update-slice_fusion), channel_id=1, source_target_pairs={{12,8},{8,4},{4,0},{13,9},{9,5},{5,1},{14,10},{10,6},{6,2},{15,11}... | collective-permute-start | bytes 4718600 | tf_op jit(solution)/shard_map/ppermute | solution.py:219
  4.4 54.3 %collective-permute-start = (bf16[2,1,32,8,1536]{4,3,2,1,0:T(8,128)(2,1)}, bf16[2,1,32,8,1536]{4,3,2,1,0:T(8,128)(2,1)}, u32[]{:S(2)}, u32[]{:S(2)}) collective-permute-start(bf16[2,1,32,8,1536]{4,3,2,1,0:T(8,128)(2,1)} %constant_dynamic-update-slice_fusion), channel_id=1, source_target_pairs={{0,4},{4,8},{8,12},{1,5},{5,9},{9,13},{2,6},{6,10},{10,14},{3,7},{... | collective-permute-start | bytes 4718600 | tf_op jit(solution)/shard_map/ppermute | solution.py:218
  11.1 32.8 %collective-permute-start.5 = (s32[4,15]{1,0:T(4,128)S(1)}, s32[4,15]{1,0:T(4,128)S(1)}, u32[]{:S(2)}, u32[]{:S(2)}) collective-permute-start(s32[4,15]{1,0:T(4,128)S(1)} %copy-done.4), channel_id=1, source_target_pairs={{0,4},{12,8},{1,5},{13,9},{2,6},{14,10},{3,7},{15,11},{16,20},{28,... | collective-permute-start | bytes 728 | tf_op jit(solution)/shard_map/ppermute | solution.py:220
  16.8 3.7 %copy-start.5 = (s32[2,8]{1,0:T(2,128)S(1)}, s32[2,8]{1,0:T(2,128)}, u32[]{:S(2)}) copy-start(s32[2,8]{1,0:T(2,128)} %param.9) | copy-start | bytes 196
  18.3 48.8 %collective-permute-start.8 = (bf16[2,1,256,12,128]{4,2,3,1,0:T(8,128)(2,1)}, bf16[2,1,256,12,128]{4,2,3,1,0:T(8,128)(2,1)}, u32[]{:S(2)}, u32[]{:S(2)}) collective-permute-start(bf16[2,1,256,12,128]{4,2,3,1,0:T(8,128)(2,1)} %copy.14), channel_id=1, source_target_pairs={{0,2},{2,0},{1,3},{3,1},{4,6},{6,4},{5,7},{7,5},{8,10},{10,8},{9,1... | collective-permute-start | bytes 4718600 | tf_op jit(solution)/shard_map/ppermute | solution.py:22
  25.6 4.7 %copy-start.1 = (bf16[1,1,32,8,1536]{4,3,2,1,0:T(8,128)(2,1)S(1)}, bf16[1,1,32,8,1536]{4,3,2,1,0:T(8,128)(2,1)}, u32[]{:S(2)}) copy-start(bf16[1,1,32,8,1536]{4,3,2,1,0:T(8,128)(2,1)} %param.5) | copy-start | bytes 2359300
  58.6 47.0 %collective-permute-start.4 = (bf16[1,32,8,1536]{3,2,1,0:T(8,128)(2,1)S(1)}, bf16[1,32,8,1536]{3,2,1,0:T(8,128)(2,1)}, u32[]{:S(2)}, u32[]{:S(2)}) collective-permute-start(bf16[1,32,8,1536]{3,2,1,0:T(8,128)(2,1)S(1)} %bitcast.49), channel_id=1, source_target_pairs={{0,4},{12,8},{1,5},{13,9},{2,6},{14,10},{3,7},{15,11},{16,20},{28,... | collective-permute-start | bytes 2359304 | tf_op jit(solution)/shard_map/ppermute | solution.py:240
  63.9 39.0 %collective-permute-start.3 = (bf16[2,1,32,8,1536]{4,3,2,1,0:T(8,128)(2,1)}, bf16[2,1,32,8,1536]{4,3,2,1,0:T(8,128)(2,1)}, u32[]{:S(2)}, u32[]{:S(2)}) collective-permute-start(bf16[2,1,32,8,1536]{4,3,2,1,0:T(8,128)(2,1)} %collective-permute-done), channel_id=1, source_target_pairs={{4,8},{8,12},{5,9},{9,13},{6,10},{10,14},{7,11},{11,15},{20,24},{2... | collective-permute-start | bytes 4718600 | tf_op jit(solution)/shard_map/ppermute | solution.py:237
  65.7 37.2 %collective-permute-start.2 = (bf16[2,1,32,8,1536]{4,3,2,1,0:T(8,128)(2,1)}, bf16[2,1,32,8,1536]{4,3,2,1,0:T(8,128)(2,1)}, u32[]{:S(2)}, u32[]{:S(2)}) collective-permute-start(bf16[2,1,32,8,1536]{4,3,2,1,0:T(8,128)(2,1)} %collective-permute-done.1), channel_id=1, source_target_pairs={{8,4},{4,0},{9,5},{5,1},{10,6},{6,2},{11,7},{7,3},{24,20},{20,16},... | collective-permute-start | bytes 4718600 | tf_op jit(solution)/shard_map/ppermute | solution.py:236
  74.2 5.0 %copy-start = (bf16[2,2,256,12,128]{4,3,2,0,1:T(8,128)(2,1)S(1)}, bf16[2,2,256,12,128]{4,3,2,0,1:T(8,128)(2,1)}, u32[]{:S(2)}) copy-start(bf16[2,2,256,12,128]{4,3,2,0,1:T(8,128)(2,1)} %copy_dynamic-update-slice_fusion) | copy-start | bytes 9437188
  109.3 25.7 %collective-permute-start.6 = (bf16[1,256,768]{2,1,0:T(8,128)(2,1)}, bf16[1,256,768]{2,1,0:T(8,128)(2,1)}, u32[]{:S(2)}, u32[]{:S(2)}) collective-permute-start(bf16[1,256,768]{2,1,0:T(8,128)(2,1)} %get-tuple-element.30), channel_id=1, source_target_pairs={{4,0},{8,12},{5,1},{9,13},{6,2},{10,14},{7,3},{11,15},{20,16},{24,... | collective-permute-start | bytes 1179656 | tf_op jit(solution)/shard_map/ppermute | solution.py:265
  113.3 5.0 %copy-start.7 = (f32[1,2,256,3]{3,2,1,0:T(8,128)S(1)}, f32[1,2,256,3]{3,2,1,0:T(8,128)}, u32[]{:S(2)}) copy-start(f32[1,2,256,3]{3,2,1,0:T(8,128)} %get-tuple-element.31) | copy-start | bytes 18436
  117.0 32.6 %collective-permute-start.10 = (bf16[1,256,768]{2,1,0:T(8,128)(2,1)}, bf16[1,256,768]{2,1,0:T(8,128)(2,1)S(1)}, u32[]{:S(2)}, u32[]{:S(2)}) collective-permute-start(bf16[1,256,768]{2,1,0:T(8,128)(2,1)} %get-tuple-element.26), channel_id=1, source_target_pairs={{4,0},{8,12},{5,1},{9,13},{6,2},{10,14},{7,3},{11,15},{20,16},{24,... | collective-permute-start | bytes 1179656 | tf_op jit(solution)/shard_map/ppermute | solution.py:265
  118.3 15.9 %collective-permute-start.7 = (f32[1,2,3,256]{2,3,1,0:T(8,128)S(1)}, f32[1,2,3,256]{2,3,1,0:T(8,128)S(1)}, u32[]{:S(2)}, u32[]{:S(2)}) collective-permute-start(f32[1,2,3,256]{2,3,1,0:T(8,128)S(1)} %bitcast.54), channel_id=1, source_target_pairs={{4,0},{8,12},{5,1},{9,13},{6,2},{10,14},{7,3},{11,15},{20,16},{24,... | collective-permute-start | bytes 18440 | tf_op jit(solution)/shard_map/ppermute | solution.py:265
  135.0 3.3 %copy-start.6 = (f32[1,2,256,3]{3,2,1,0:T(8,128)S(1)}, f32[1,2,256,3]{3,2,1,0:T(8,128)}, u32[]{:S(2)}) copy-start(f32[1,2,256,3]{3,2,1,0:T(8,128)} %get-tuple-element.32) | copy-start | bytes 18436
  138.3 15.4 %collective-permute-start.9 = (bf16[1,32,8,768]{3,2,1,0:T(8,128)(2,1)}, bf16[1,32,8,768]{3,2,1,0:T(8,128)(2,1)S(1)}, u32[]{:S(2)}, u32[]{:S(2)}) collective-permute-start(bf16[1,32,8,768]{3,2,1,0:T(8,128)(2,1)} %bitcast.51), channel_id=1, source_target_pairs={{0,1},{1,0},{2,3},{3,2},{4,5},{5,4},{6,7},{7,6},{8,9},{9,8},{10,11... | collective-permute-start | bytes 1179656 | tf_op jit(solution)/shard_map/ppermute | solution.py:26
  138.3 10.6 %collective-permute-start.11 = (f32[1,2,3,256]{2,3,1,0:T(8,128)S(1)}, f32[1,2,3,256]{2,3,1,0:T(8,128)S(1)}, u32[]{:S(2)}, u32[]{:S(2)}) collective-permute-start(f32[1,2,3,256]{2,3,1,0:T(8,128)S(1)} %bitcast.53), channel_id=1, source_target_pairs={{4,0},{8,12},{5,1},{9,13},{6,2},{10,14},{7,3},{11,15},{20,16},{24,... | collective-permute-start | bytes 18440 | tf_op jit(solution)/shard_map/ppermute | solution.py:265
  149.7 0.8 copy-start.3

commit v9 on v7

--- a/solution.py
+++ b/solution.py
@@ -52,11 +52,11 @@
         result = jnp.dot(
             weights.astype(jnp.bfloat16), v_ref[:, lanes], preferred_element_type=jnp.float32
         )
-        o_ref[:, lanes] = result / totals
+        o_ref[:, lanes] = (result / totals).astype(o_ref.dtype)
         lse_ref[:, head : head + 1] = maxima + jnp.log(totals)
 
 
-def spatial_attention(query_flat, key_value_flat, mask, scale):
+def spatial_attention(query_flat, key_value_flat, mask, scale, out_dtype=jnp.float32):
     frames, query_count, model_width = query_flat.shape
     key_count = key_value_flat.shape[2]
     head_count = model_width // DH
@@ -76,7 +76,7 @@
             pl.BlockSpec((None, None, query_count, width // DH), lambda f, g: (f, g, 0, 0)),
         ],
         out_shape=[
-            jax.ShapeDtypeStruct((frames, query_count, model_width), jnp.float32),
+            jax.ShapeDtypeStruct((frames, query_count, model_width), out_dtype),
             jax.ShapeDtypeStruct((frames, groups, query_count, width // DH), jnp.float32),
         ],
         cost_estimate=pl.CostEstimate(
@@ -104,6 +104,42 @@
         mixed_ref[:, lanes] = (value / total + temporal_ref[:, lanes].astype(jnp.float32)).astype(
             mixed_ref.dtype
         )
+
+
+def merge_kernel(*refs):
+    *parts, out_ref, lse_ref = refs
+    outs, lses = parts[0::2], parts[1::2]
+    for head in range(out_ref.shape[-1] // DH):
+        lanes = slice(head * DH, (head + 1) * DH)
+        logs = [lse[:, head : head + 1] for lse in lses]
+        top = functools.reduce(jnp.maximum, logs)
+        weights = [jnp.exp(log - top) for log in logs]
+        total = functools.reduce(jnp.add, weights)
+        value = functools.reduce(jnp.add, [w * o[:, lanes] for w, o in zip(weights, outs)])
+        out_ref[:, lanes] = value / total
+        lse_ref[:, head : head + 1] = top + jnp.log(total)
+
+
+def merge_partials(partials):
+    out, lse = partials[0]
+    frames, query_count, model_width = out.shape
+    width = group_width(model_width)
+    groups = model_width // width
+    big = pl.BlockSpec((None, query_count, width), lambda f, g: (f, 0, g))
+    small = pl.BlockSpec((None, None, query_count, width // DH), lambda f, g: (f, g, 0, 0))
+    operands = []
+    for out, lse in partials:
+        operands += [out, lse]
+    return pl.pallas_call(
+        merge_kernel,
+        grid=(frames, groups),
+        in_specs=[big, small] * len(partials),
+        out_specs=[big, small],
+        out_shape=[
+            jax.ShapeDtypeStruct(out.shape, jnp.float32),
+            jax.ShapeDtypeStruct(lse.shape, jnp.float32),
+        ],
+    )(*operands)
 
 
 def combine_partials(partials, temporal):
@@ -229,10 +265,11 @@
         far_keys,
         expand_mask(guest_active, lat_rows),
         scale,
+        jnp.bfloat16,
     )
     lse_shape = guest_lse.shape
     returned, returned_lse = lax.ppermute(
-        (guest_out.astype(jnp.bfloat16), jnp.swapaxes(guest_lse, 2, 3)),
+        (guest_out, jnp.swapaxes(guest_lse, 2, 3)),
         "lon",
         [(1, 0), (2, 3)],
     )
@@ -241,7 +278,7 @@
 
     far_active = window_mask(own_cols, far_cols, own_map, total_cols, lat_rows)
     far_part = spatial_attention(query_flat, far_keys, expand_mask(far_active, lat_rows), scale)
-    return [near_part, far_part, (returned, returned_lse)]
+    return [merge_partials([near_part, far_part]), (returned, returned_lse)]
 
 
 def local(queries, keys, values, window_map, frame_valid):

time: 133 us -> 134 us (level)
  Pallas kernels: 24.4 us -> 28.2 us
  starting transfers between devices: 27.3 us -> 25.9 us
    ppermute x2, waiting for transfers between devices: 13 us -> 8 us  [spatial_line_of_four(): lax.ppermute((guest_out, jnp.swapaxes(guest_lse, 2, 3)), 'lon', [(1, 0),...]
    pallas_call x0 -> x1, Pallas kernels: none -> 4.85 us  [merge_partials(): pl.pallas_call(merge_kernel, grid=(frames, groups), in_specs=[big, small]...]
    ppermute x1, waiting for transfers between devices: 0.01 us -> 4.17 us  [spatial_line_of_four(): from_right = lax.ppermute(key_value, 'lon', [(3, 2), (2, 1), (1, 0)])]
    ppermute x1, waiting for transfers between devices: 4.33 us -> 1.18 us  [spatial_line_of_four(): guest_map = lax.ppermute(window_map, 'lon', [(0, 1), (3, 2)])]
    ppermute x1, waiting for transfers between devices: 0.01 us -> 2.88 us  [spatial_line_of_four(): lax.ppermute(from_right, 'lon', [(2, 1), (1, 0)])]
    ppermute x1, starting transfers between devices: 2.72 us -> 4.55 us  [spatial_line_of_four(): guest_map = lax.ppermute(window_map, 'lon', [(0, 1), (3, 2)])]
    convert_element_type x1 -> x0, other arithmetic: 1.49 us -> none  [spatial_line_of_four(): guest_out.astype(jnp.bfloat16)]
    ppermute x1, starting transfers between devices: 9.25 us -> 7.77 us  [spatial_line_of_four(): guest_q = lax.ppermute(held_q, 'lon', [(0, 1), (3, 2)])]
  transfers between devices with their start and end apart: 10 -> 10, of which waited for: 3 -> 5; matrix products, arithmetic and copies ran while one was open for 40% -> 41% of each run, Pallas kernels for 10% -> 14%
where the time goes in v9:
time: 134 us; the launch traced here: 133 us
  local copies, waits for them, and re-layouts  41.7 us (31%)
  Pallas kernels  28.2 us (21%)
  starting transfers between devices  25.9 us (19%)
  other arithmetic  19.4 us (14%)
  waiting for transfers between devices  17.9 us (13%)
    pallas_call x3, Pallas kernels, spatial_attention(): pl.pallas_call(functools.partial(spatial_kernel, scale=scale), grid=(fram...  18.8 us
    reshape x3, local copies, waits for them, and re-layouts, expand_mask(): return jnp.broadcast_to(active[None, :, None, :].astype(jnp.float32), (la...  14.1 us
    ppermute x2, waiting for transfers between devices, spatial_line_of_four(): lax.ppermute((guest_out, jnp.swapaxes(guest_lse, 2, 3)), 'lon', [(1, 0),...  8 us
    ppermute x1, starting transfers between devices, spatial_line_of_four(): guest_q = lax.ppermute(held_q, 'lon', [(0, 1), (3, 2)])  7.77 us
    broadcast_in_dim x3, local copies, waits for them, and re-layouts, expand_mask(): jnp.broadcast_to(active[None, :, None, :].astype(jnp.float32), (lat_rows,...  7.36 us
    ppermute x1, starting transfers between devices, spatial_line_of_four(): from_left = lax.ppermute(key_value, 'lon', [(0, 1), (1, 2), (2, 3)])  6.12 us
    pallas_call x1, Pallas kernels, merge_partials(): pl.pallas_call(merge_kernel, grid=(frames, groups), in_specs=[big, small]...  4.85 us
    unnamed x16, local copies, waits for them, and re-layouts  4.84 us
  transfers between devices with their start and end apart: 10, of which 5 were waited for; matrix products, arithmetic and copies ran while one was open for 41% of the time, Pallas kernels for 14%

profile of v9, /device:TPU:0, one launch (start us, length us, event | category | flops | bytes accessed | tf_op | source)
XLA Modules:
  0.0 133.3 jit_solution(8053623511023288898)
XLA Ops:
  0.0 2.2 %constant_dynamic-update-slice_fusion.1 = bf16[2,1,32,8,1536]{4,3,2,1,0:T(8,128)(2,1)} fusion(bf16[1,1,32,8,1536]{4,3,2,1,0:T(8,128)(2,1)} %param.6), kind=kLoop, calls=%fused_computation.27 | loop fusion | bytes 1572864
  2.2 0.0 copy-done.3
  2.2 1.0 constant_dynamic-update-slice_fusion
  3.1 6.1 %collective-permute-start = (bf16[2,1,32,8,1536]{4,3,2,1,0:T(8,128)(2,1)}, bf16[2,1,32,8,1536]{4,3,2,1,0:T(8,128)(2,1)}, u32[]{:S(2)}, u32[]{:S(2)}) collective-permute-start(bf16[2,1,32,8,1536]{4,3,2,1,0:T(8,128)(2,1)} %constant_dynamic-update-slice_fusion), channel_id=1, source_target_pairs={{0,4},{4,8},{8,12},{1,5},{5,9},{9,13},{2,6},{6,10},{10,14},{3,7},{... | collective-permute-start | bytes 4718600 | tf_op jit(solution)/shard_map/ppermute | solution.py:227
  9.3 1.3 collective-permute-start.1
  10.6 4.5 %collective-permute-start.5 = (s32[4,15]{1,0:T(4,128)S(1)}, s32[4,15]{1,0:T(4,128)S(1)}, u32[]{:S(2)}, u32[]{:S(2)}) collective-permute-start(s32[4,15]{1,0:T(4,128)S(1)} %copy-done.4), channel_id=1, source_target_pairs={{0,4},{12,8},{1,5},{13,9},{2,6},{14,10},{3,7},{15,11},{16,20},{28,... | collective-permute-start | bytes 728 | tf_op jit(solution)/shard_map/ppermute | solution.py:229
  15.1 2.9 %reshape.555 = bf16[2,1,256,12,128]{4,3,2,0,1:T(8,128)(2,1)S(1)} reshape(bf16[2,1,32,8,1536]{4,3,2,1,0:T(8,128)(2,1)} %constant_dynamic-update-slice_fusion) | data formatting | bytes 3145728 | tf_op jit(solution)/shard_map/reshape | solution.py:334
  18.0 1.6 %copy.12 = bf16[2,1,256,12,128]{4,2,3,1,0:T(8,128)(2,1)} copy(bf16[2,1,256,12,128]{4,3,2,0,1:T(8,128)(2,1)S(1)} %reshape.555) | data formatting | bytes 3145728 | tf_op jit(solution)/shard_map/reshape | solution.py:334
  19.6 1.5 %collective-permute-start.8 = (bf16[2,1,256,12,128]{4,2,3,1,0:T(8,128)(2,1)}, bf16[2,1,256,12,128]{4,2,3,1,0:T(8,128)(2,1)}, u32[]{:S(2)}, u32[]{:S(2)}) collective-permute-start(bf16[2,1,256,12,128]{4,2,3,1,0:T(8,128)(2,1)} %copy.12), channel_id=1, source_target_pairs={{0,2},{2,0},{1,3},{3,1},{4,6},{6,4},{5,7},{7,5},{8,10},{10,8},{9,1... | collective-permute-start | bytes 4718600 | tf_op jit(solution)/shard_map/ppermute | solution.py:21
  21.1 0.1 pad_add_fusion
  21.2 0.1 broadcast_in_dim.35
  21.3 0.1 and.236
  21.4 0.1 copy.11
  21.5 0.1 add_select_fusion.2
  21.6 0.1 fusion.6
  21.7 2.5 %broadcast_in_dim.36 = f32[32,8,32,24]{3,2,1,0:T(8,128)} broadcast(f32[8,24]{1,0:T(8,128)S(1)} %and_convert_fusion.1), dimensions={1,3} | broadcast | bytes 787200 | tf_op jit(solution)/shard_map/broadcast_in_dim | solution.py:205
  24.1 4.7 %reshape.550.m_ref = f32[256,768]{1,0:T(8,128)} reshape(f32[32,8,32,24]{3,2,1,0:T(8,128)} %broadcast_in_dim.36) | data formatting | bytes 1572864 | tf_op jit(solution)/shard_map/reshape | solution.py:207
  28.8 0.1 add_select_fusion
  28.9 0.3 fusion.8
  29.2 2.5 %broadcast_in_dim.37 = f32[32,8,32,8]{3,2,1,0:T(8,128)} broadcast(f32[8,8]{1,0:T(8,128)S(1)} %convert_element_type.69), dimensions={1,3} | broadcast | bytes 262400 | tf_op jit(solution)/shard_map/broadcast_in_dim | solution.py:205
  31.7 4.8 %reshape.552.m_ref = f32[256,256]{1,0:T(8,128)} reshape(f32[32,8,32,8]{3,2,1,0:T(8,128)} %broadcast_in_dim.37) | data formatting | bytes 524288 | tf_op jit(solution)/shard_map/reshape | solution.py:207
  36.4 0.1 tile.10
  36.5 1.9 %reshape.557 = f32[256,12,128]{2,1,0:T(8,128)} reshape(bf16[1,1,32,8,1536]{4,3,2,1,0:T(8,128)(2,1)S(1)} %copy-done.1) | data formatting | bytes 2359296 | tf_op jit(solution)/shard_map/convert_element_type | solution.py:164
  38.4 0.6 gather_fusion
  39.0 1.7 %constant_dynamic-update-slice_fusion.2 = bf16[2,2,256,12,128]{4,3,2,0,1:T(8,128)(2,1)} fusion(bf16[2,1,256,12,128]{4,3,2,0,1:T(8,128)(2,1)S(1)} %reshape.555), kind=kLoop, calls=%fused_computation.28 | loop fusion | bytes 3670016
  40.8 0.1 compare_or_fusion
  40.9 1.2 collective-permute-done.5
  42.1 0.3 fusion.10
  42.4 0.0 collective-permute-done
  42.4 0.8 collective-permute-start.3
  43.1 4.2 %collective-permute-done.1 = bf16[2,1,32,8,1536]{4,3,2,1,0:T(8,128)(2,1)} collective-permute-done((bf16[2,1,32,8,1536]{4,3,2,1,0:T(8,128)(2,1)}, bf16[2,1,32,8,1536]{4,3,2,1,0:T(8,128)(2,1)}, u32[]{:S(2)}, u32[]{:S(2)}) %collective-permute-start.1) | collective-permute-done | bytes 1572896 | tf_op jit(solution)/shard_map/ppermute | solution.py:228
  47.3 1.3 collective-permute-start.2
  48.6 2.5 %broadcast_in_dim.39 = f32[32,8,32,8]{3,2,1,0:T(8,128)} broadcast(f32[8,8]{1,0:T(8,128)S(1)} %and_convert_fusion), dimensions={1,3} | broadcast | bytes 262400 | tf_op jit(solution)/shard_map/broadcast_in_dim | solution.py:205
  51.1 4.7 %reshape.554.m_ref = f32[256,256]{1,0:T(8,128)} reshape(f32[32,8,32,8]{3,2,1,0:T(8,128)} %broadcast_in_dim.39) | data formatting | bytes 524288 | tf_op jit(solution)/shard_map/reshape | solution.py:207
  55.7 7.8 %collective-permute-start.4 = (bf16[1,32,8,1536]{3,2,1,0:T(8,128)(2,1)S(1)}, bf16[1,32,8,1536]{3,2,1,0:T(8,128)(2,1)}, u32[]{:S(2)}, u32[]{:S(2)}) collective-permute-start(bf16[1,32,8,1536]{3,2,1,0:T(8,128)(2,1)S(1)} %bitcast.35), channel_id=1, source_target_pairs={{0,4},{12,8},{1,5},{13,9},{2,6},{14,10},{3,7},{15,11},{16,20},{28,... | collective-permute-start | bytes 2359304 | tf_op jit(solution)/shard_map/ppermute | solution.py:249
  63.5 4.8 %pad_maximum_fusion = bf16[2,1,32,24,1536]{4,3,2,1,0:T(8,128)(2,1)} fusion(bf16[2,1,32,8,1536]{4,3,2,1,0:T(8,128)(2,1)} %collective-permute-done.1, bf16[2,1,32,8,1536]{4,3,2,1,0:T(8,128)(2,1)} %constant_dynamic-update-slice_fusion, bf16[2,1,32,8,1536]{4,3,2,1,0:T(8,128)(2,1)} %collective-permute-done), kind=kLoop, calls=%fused_computation.1 | loop fusion | flops 14155776 | bytes 9437184 | tf_op jit(solution)/shard_map/concatenate | solution.py:211
  68.3 8.5 %shard_map.55 = (f32[1,256,1536]{2,1,0:T(8,128)}, f32[1,3,256,4]{3,2,1,0:T(8,128)}) custom-call(bf16[1,256,1536]{2,1,0:T(8,128)(2,1)} %bitcast.33, bf16[2,1,768,1536]{3,2,1,0:T(8,128)(2,1)} %bitcast.27, bf16[2,1,768,1536]{3,2,1,0:T(8,128)(2,1)} %bitcast.28, f32[256,768]{1,0:T(8,128)} %reshape.550.m_ref), custom_call_target="tpu_custom_call" | custom-call | flops 1207959552 | bytes 7077888 | tf_op jit(solution)/shard_map/pallas_call | solution.py:65
  76.8 0.0 collective-permute-done.8
  76.8 4.0 %copy_dynamic-update-slice_fusion = bf16[2,2,256,12,128]{4,3,2,0,1:T(8,128)(2,1)} fusion(bf16[2,2,256,12,128]{4,3,2,0,1:T(8,128)(2,1)} %constant_dynamic-update-slice_fusion.2, bf16[2,1,256,12,128]{4,2,3,1,0:T(8,128)(2,1)} %collective-permute-done.8), kind=kLoop, calls=%fused_computation.4 | loop fusion | bytes 3670016 | tf_op jit(solution)/shard_map/concatenate | solution.py:338
  80.8 2.8 %multiply_reduce_fusion.1 = f32[2,256,12]{2,1,0:T(8,128)S(1)} fusion(bf16[2,2,256,12,128]{4,3,2,0,1:T(8,128)(2,1)} %copy_dynamic-update-slice_fusion, f32[256,12,128]{2,1,0:T(8,128)S(1)} %copy-done), kind=kLoop, calls=%fused_computation.3 | loop fusion | flops 2353152 | bytes 3170304 | tf_op jit(solution)/shard_map/reduce_sum | solution.py:166
  83.6 0.1 fusion.2
  83.8 0.1 fusion.3
  83.9 0.0 collective-permute-done.3
  83.9 2.9 %collective-permute-done.2 = bf16[2,1,32,8,1536]{4,3,2,1,0:T(8,128)(2,1)} collective-permute-done((bf16[2,1,32,8,1536]{4,3,2,1,0:T(8,128)(2,1)}, bf16[2,1,32,8,1536]{4,3,2,1,0:T(8,128)(2,1)}, u32[]{:S(2)}, u32[]{:S(2)}) %collective-permute-start.2) | collective-permute-done | bytes 1572896 | tf_op jit(solution)/shard_map/ppermute | solution.py:245
  86.8 2.7 %broadcast_select_fusion = bf16[2,1,32,8,1536]{4,3,2,1,0:T(8,128)(2,1)} fusion(bf16[2,1,32,8,1536]{4,3,2,1,0:T(8,128)(2,1)} %collective-permute-done.2, bf16[2,1,32,8,1536]{4,3,2,1,0:T(8,128)(2,1)S(1)} %collective-permute-done.3, pred[]{:T(512)S(6)} %le.15), kind=kLoop, calls=%fused_computation.6 | loop fusion | flops 786432 | bytes 4718593 | tf_op jit(solution)/shard_map/jit(_where)/select_n | solution.py:243
  89.5 0.0 collective-permute-done.4
  89.5 5.1 %shard_map.58 = (bf16[1,256,1536]{2,1,0:T(8,128)(2,1)}, f32[1,3,256,4]{3,2,1,0:T(8,128)}) custom-call(bf16[1,256,1536]{2,1,0:T(8,128)(2,1)} %bitcast.7.q_ref, bf16[2,1,256,1536]{3,2,1,0:T(8,128)(2,1)} %bitcast.29, bf16[2,1,256,1536]{3,2,1,0:T(8,128)(2,1)} %bitcast.30, f32[256,256]{1,0:T(8,128)} %reshape.554.m_ref), custom_call_target="tpu_custom_call" | custom-call | flops 402653184 | bytes 3932160 | tf_op jit(solution)/shard_map/pallas_call | solution.py:65
  94.6 1.3 collective-permute-start.6
  95.9 4.2 %multiply_reduce_fusion = f32[256,12,128]{2,1,0:T(8,128)S(1)} fusion(bf16[2,2,256,12,128]{4,3,2,0,1:T(8,128)(2,1)} %copy_dynamic-update-slice_fusion, f32[2,256,12]{2,1,0:T(8,128)S(1)} %get-tuple-element.32), kind=kLoop, calls=%fused_computation.2 | loop fusion | flops 1966080 | bytes 3170304 | tf_op jit(solution)/shard_map/reduce_sum | solution.py:174
  100.1 0.7 reduce-precision_convert_fusion
  100.9 0.9 copy.14
  101.8 1.2 copy.15.refs_4_
  102.9 1.3 collective-permute-start.7
  104.2 5.3 %shard_map.56 = (f32[1,256,1536]{2,1,0:T(8,128)}, f32[1,3,256,4]{3,2,1,0:T(8,128)}) custom-call(bf16[1,256,1536]{2,1,0:T(8,128)(2,1)} %bitcast.34, bf16[2,1,256,1536]{3,2,1,0:T(8,128)(2,1)} %bitcast.31, bf16[2,1,256,1536]{3,2,1,0:T(8,128)(2,1)} %bitcast.32, f32[256,256]{1,0:T(8,128)} %reshape.552.m_ref), custom_call_target="tpu_custom_call" | custom-call | flops 402653184 | bytes 3932160 | tf_op jit(solution)/shard_map/pallas_call | solution.py:65
  109.5 4.8 %shard_map.57 = (f32[1,256,1536]{2,1,0:T(8,128)}, f32[1,3,256,4]{3,2,1,0:T(8,128)}) custom-call(f32[1,256,1536]{2,1,0:T(8,128)} %get-tuple-element.21.refs_0_, f32[1,3,256,4]{3,2,1,0:T(8,128)} %get-tuple-element.22.refs_1_, f32[1,256,1536]{2,1,0:T(8,128)} %get-tuple-element.24.refs_2_, f32[1,3,256,4]{3,2,1,0:T(8,128)} %get-tuple-element.25.refs_3_), custom_call_target="tpu_custom_call" | custom-call | tf_op jit(solution)/shard_map/pallas_call | solution.py:133
  114.3 8.0 %collective-permute-done.7 = f32[1,3,4,256]{2,3,1,0:T(8,128)S(1)} collective-permute-done((f32[1,3,4,256]{2,3,1,0:T(8,128)S(1)}, f32[1,3,4,256]{2,3,1,0:T(8,128)S(1)}, u32[]{:S(2)}, u32[]{:S(2)}) %collective-permute-start.7) | collective-permute-done | bytes 12320 | tf_op jit(solution)/shard_map/ppermute | solution.py:271
  122.3 0.8 select_bitcast_fusion.refs_3_
  123.1 0.0 collective-permute-done.6.refs_2_
  123.1 0.9 copy-done.2
  124.0 4.5 %shard_map.59 = bf16[1,256,1536]{2,1,0:T(8,128)(2,1)} custom-call(f32[1,256,1536]{2,1,0:T(8,128)} %get-tuple-element.26.refs_0_, f32[1,3,256,4]{3,2,1,0:T(8,128)} %get-tuple-element.27.refs_1_, bf16[1,256,1536]{2,1,0:T(8,128)(2,1)} %copy-done.2, f32[1,3,256,4]{3,2,1,0:T(8,128)} %select_bitcast_fusion.refs_3_, bf16[1,256,1536]{2,1,0:T(8,128)(2,1)} %copy.15.refs_4_), custom_call_target="tpu_custom_call" | custom-call | tf_op jit(solution)/shard_map/pallas_call | solution.py:154
  128.5 1.0 constant_dynamic-slice_fusion
  129.6 0.1 collective-permute-start.9
  129.6 1.7 %collective-permute-done.9 = bf16[1,32,8,768]{3,2,1,0:T(8,128)(2,1)S(1)} collective-permute-done((bf16[1,32,8,768]{3,2,1,0:T(8,128)(2,1)S(1)}, bf16[1,32,8,768]{3,2,1,0:T(8,128)(2,1)S(1)}, u32[]{:S(2)}, u32[]{:S(2)}) %collective-permute-start.9) | collective-permute-done | bytes 393248 | tf_op jit(solution)/shard_map/ppermute | solution.py:25
  131.3 1.9 %fusion.1 = bf16[1,32,8,768]{3,2,1,0:T(8,128)(2,1)} fusion(bf16[1,32,8,768]{3,2,1,0:T(8,128)(2,1)S(1)} %collective-permute-done.9, bf16[1,32,8,1536]{3,2,1,0:T(8,128)(2,1)} %bitcast.38, s32[]{:T(128)S(6)} %select_n.230, pred[]{:T(512)S(6)} %eq.73), kind=kLoop, calls=%fused_computation.10 | loop fusion | flops 1572864 | bytes 1179653 | tf_op jit(solution)/shard_map/convert_element_type | solution.py:361
  (29 shorter events, 0.2 us)
Async XLA Ops:
  0.0 2.2 %copy-start.3 = (bf16[1,1,32,8,1536]{4,3,2,1,0:T(8,128)(2,1)S(1)}, bf16[1,1,32,8,1536]{4,3,2,1,0:T(8,128)(2,1)}, u32[]{:S(2)}) copy-start(bf16[1,1,32,8,1536]{4,3,2,1,0:T(8,128)(2,1)} %param.7) | copy-start | bytes 2359300
  0.0 10.5 %copy-start.4 = (s32[4,15]{1,0:T(4,128)S(1)}, s32[4,15]{1,0:T(4,128)}, u32[]{:S(2)}) copy-start(s32[4,15]{1,0:T(4,128)} %param.8) | copy-start | bytes 724
  3.1 39.2 %collective-permute-start = (bf16[2,1,32,8,1536]{4,3,2,1,0:T(8,128)(2,1)}, bf16[2,1,32,8,1536]{4,3,2,1,0:T(8,128)(2,1)}, u32[]{:S(2)}, u32[]{:S(2)}) collective-permute-start(bf16[2,1,32,8,1536]{4,3,2,1,0:T(8,128)(2,1)} %constant_dynamic-update-slice_fusion), channel_id=1, source_target_pairs={{0,4},{4,8},{8,12},{1,5},{5,9},{9,13},{2,6},{6,10},{10,14},{3,7},{... | collective-permute-start | bytes 4718600 | tf_op jit(solution)/shard_map/ppermute | solution.py:227
  9.3 38.1 %collective-permute-start.1 = (bf16[2,1,32,8,1536]{4,3,2,1,0:T(8,128)(2,1)}, bf16[2,1,32,8,1536]{4,3,2,1,0:T(8,128)(2,1)}, u32[]{:S(2)}, u32[]{:S(2)}) collective-permute-start(bf16[2,1,32,8,1536]{4,3,2,1,0:T(8,128)(2,1)} %constant_dynamic-update-slice_fusion), channel_id=1, source_target_pairs={{12,8},{8,4},{4,0},{13,9},{9,5},{5,1},{14,10},{10,6},{6,2},{15,11}... | collective-permute-start | bytes 4718600 | tf_op jit(solution)/shard_map/ppermute | solution.py:228
  10.6 31.5 %collective-permute-start.5 = (s32[4,15]{1,0:T(4,128)S(1)}, s32[4,15]{1,0:T(4,128)S(1)}, u32[]{:S(2)}, u32[]{:S(2)}) collective-permute-start(s32[4,15]{1,0:T(4,128)S(1)} %copy-done.4), channel_id=1, source_target_pairs={{0,4},{12,8},{1,5},{13,9},{2,6},{14,10},{3,7},{15,11},{16,20},{28,... | collective-permute-start | bytes 728 | tf_op jit(solution)/shard_map/ppermute | solution.py:229
  19.6 57.2 %collective-permute-start.8 = (bf16[2,1,256,12,128]{4,2,3,1,0:T(8,128)(2,1)}, bf16[2,1,256,12,128]{4,2,3,1,0:T(8,128)(2,1)}, u32[]{:S(2)}, u32[]{:S(2)}) collective-permute-start(bf16[2,1,256,12,128]{4,2,3,1,0:T(8,128)(2,1)} %copy.12), channel_id=1, source_target_pairs={{0,2},{2,0},{1,3},{3,1},{4,6},{6,4},{5,7},{7,5},{8,10},{10,8},{9,1... | collective-permute-start | bytes 4718600 | tf_op jit(solution)/shard_map/ppermute | solution.py:21
  31.7 4.8 %copy-start.5 = (s32[2,8]{1,0:T(2,128)S(1)}, s32[2,8]{1,0:T(2,128)}, u32[]{:S(2)}) copy-start(s32[2,8]{1,0:T(2,128)} %param.9) | copy-start | bytes 196
  31.7 4.9 %copy-start.1 = (bf16[1,1,32,8,1536]{4,3,2,1,0:T(8,128)(2,1)S(1)}, bf16[1,1,32,8,1536]{4,3,2,1,0:T(8,128)(2,1)}, u32[]{:S(2)}) copy-start(bf16[1,1,32,8,1536]{4,3,2,1,0:T(8,128)(2,1)} %param.5) | copy-start | bytes 2359300
  42.4 41.6 %collective-permute-start.3 = (bf16[2,1,32,8,1536]{4,3,2,1,0:T(8,128)(2,1)}, bf16[2,1,32,8,1536]{4,3,2,1,0:T(8,128)(2,1)S(1)}, u32[]{:S(2)}, u32[]{:S(2)}) collective-permute-start(bf16[2,1,32,8,1536]{4,3,2,1,0:T(8,128)(2,1)} %collective-permute-done), channel_id=1, source_target_pairs={{4,8},{8,12},{5,9},{9,13},{6,10},{10,14},{7,11},{11,15},{20,24},{2... | collective-permute-start | bytes 4718600 | tf_op jit(solution)/shard_map/ppermute | solution.py:246
  47.3 39.5 %collective-permute-start.2 = (bf16[2,1,32,8,1536]{4,3,2,1,0:T(8,128)(2,1)}, bf16[2,1,32,8,1536]{4,3,2,1,0:T(8,128)(2,1)}, u32[]{:S(2)}, u32[]{:S(2)}) collective-permute-start(bf16[2,1,32,8,1536]{4,3,2,1,0:T(8,128)(2,1)} %collective-permute-done.1), channel_id=1, source_target_pairs={{8,4},{4,0},{9,5},{5,1},{10,6},{6,2},{11,7},{7,3},{24,20},{20,16},... | collective-permute-start | bytes 4718600 | tf_op jit(solution)/shard_map/ppermute | solution.py:245
  55.7 33.8 %collective-permute-start.4 = (bf16[1,32,8,1536]{3,2,1,0:T(8,128)(2,1)S(1)}, bf16[1,32,8,1536]{3,2,1,0:T(8,128)(2,1)}, u32[]{:S(2)}, u32[]{:S(2)}) collective-permute-start(bf16[1,32,8,1536]{3,2,1,0:T(8,128)(2,1)S(1)} %bitcast.35), channel_id=1, source_target_pairs={{0,4},{12,8},{1,5},{13,9},{2,6},{14,10},{3,7},{15,11},{16,20},{28,... | collective-permute-start | bytes 2359304 | tf_op jit(solution)/shard_map/ppermute | solution.py:249
  76.8 4.1 %copy-start = (f32[256,12,128]{2,1,0:T(8,128)S(1)}, f32[256,12,128]{2,1,0:T(8,128)}, u32[]{:S(2)}) copy-start(f32[256,12,128]{2,1,0:T(8,128)} %reshape.557) | copy-start | bytes 4718596
  94.6 28.5 %collective-permute-start.6 = (bf16[1,256,1536]{2,1,0:T(8,128)(2,1)}, bf16[1,256,1536]{2,1,0:T(8,128)(2,1)S(1)}, u32[]{:S(2)}, u32[]{:S(2)}) collective-permute-start(bf16[1,256,1536]{2,1,0:T(8,128)(2,1)} %get-tuple-element.29), channel_id=1, source_target_pairs={{4,0},{8,12},{5,1},{9,13},{6,2},{10,14},{7,3},{11,15},{20,16},{24,... | collective-permute-start | bytes 2359304 | tf_op jit(solution)/shard_map/ppermute | solution.py:271
  100.9 2.1 %copy-start.6 = (f32[1,3,256,4]{3,2,1,0:T(8,128)S(1)}, f32[1,3,256,4]{3,2,1,0:T(8,128)}, u32[]{:S(2)}) copy-start(f32[1,3,256,4]{3,2,1,0:T(8,128)} %get-tuple-element.30) | copy-start | bytes 36868
  102.9 19.4 %collective-permute-start.7 = (f32[1,3,4,256]{2,3,1,0:T(8,128)S(1)}, f32[1,3,4,256]{2,3,1,0:T(8,128)S(1)}, u32[]{:S(2)}, u32[]{:S(2)}) collective-permute-start(f32[1,3,4,256]{2,3,1,0:T(8,128)S(1)} %bitcast.40), channel_id=1, source_target_pairs={{4,0},{8,12},{5,1},{9,13},{6,2},{10,14},{7,3},{11,15},{20,16},{24,... | collective-permute-start | bytes 36872 | tf_op jit(solution)/shard_map/ppermute | solution.py:271
  123.1 0.9 copy-start.2
  129.6 1.8 %collective-permute-start.9 = (bf16[1,32,8,768]{3,2,1,0:T(8,128)(2,1)S(1)}, bf16[1,32,8,768]{3,2,1,0:T(8,128)(2,1)S(1)}, u32[]{:S(2)}, u32[]{:S(2)}) collective-permute-start(bf16[1,32,8,768]{3,2,1,0:T(8,128)(2,1)S(1)} %constant_dynamic-slice_fusion), channel_id=1, source_target_pairs={{0,1},{1,0},{2,3},{3,2},{4,5},{5,4},{6,7},{7,6},{8,9},{9,8},{10,11... | collective-permute-start | bytes 1179656 | tf_op jit(solution)/shard_map/ppermute | solution.py:25

commit v10 on v7

--- a/solution.py
+++ b/solution.py
@@ -177,6 +177,16 @@
     return joined.reshape(two, frames, lat_rows * cols, model_width)
 
 
+def send_pair(pair, axis, pairs):
+    return tuple(lax.ppermute(part, axis, pairs) for part in pair)
+
+
+def flat_pairs(pairs):
+    joined = jnp.stack([jnp.concatenate([pair[i] for pair in pairs], axis=2) for i in (0, 1)])
+    two, frames, lat_rows, cols, model_width = joined.shape
+    return joined.reshape(two, frames, lat_rows * cols, model_width)
+
+
 def spatial_line_of_four(own_q, key_value, window_map, scale):
     frames, lat_rows, columns, model_width = own_q.shape
     count = 4
@@ -188,8 +198,8 @@
     own_cols = index * columns + column_ids
     query_flat = own_q.reshape(frames, lat_rows * columns, model_width)
 
-    from_left = lax.ppermute(key_value, "lon", [(0, 1), (1, 2), (2, 3)])
-    from_right = lax.ppermute(key_value, "lon", [(3, 2), (2, 1), (1, 0)])
+    from_left = send_pair(key_value, "lon", [(0, 1), (1, 2), (2, 3)])
+    from_right = send_pair(key_value, "lon", [(3, 2), (2, 1), (1, 0)])
     guest_map = lax.ppermute(window_map, "lon", [(0, 1), (3, 2)])
 
     near_cols = ((index - 1) * columns + jnp.arange(3 * columns, dtype=jnp.int32)) % total_cols
@@ -199,17 +209,15 @@
     )[None, :]
     near_part = spatial_attention(
         query_flat,
-        flat_keys([from_left, key_value, from_right]),
+        flat_pairs([from_left, key_value, from_right]),
         expand_mask(near_active, lat_rows),
         scale,
     )
 
-    two_away = jnp.where(
-        index <= 1,
-        lax.ppermute(from_right, "lon", [(2, 1), (1, 0)]),
-        lax.ppermute(from_left, "lon", [(1, 2), (2, 3)]),
-    )
-    held_q, _ = lax.optimization_barrier((own_q, from_left))
+    toward_left = send_pair(from_right, "lon", [(2, 1), (1, 0)])
+    toward_right = send_pair(from_left, "lon", [(1, 2), (2, 3)])
+    two_away = tuple(jnp.where(index <= 1, a, b) for a, b in zip(toward_left, toward_right))
+    held_q, _ = lax.optimization_barrier((own_q, from_left[0]))
     guest_q = lax.ppermute(held_q, "lon", [(0, 1), (3, 2)])
     near_part, two_away, guest_q = lax.optimization_barrier((near_part, two_away, guest_q))
 
@@ -223,7 +231,7 @@
         total_cols,
         lat_rows,
     ) & is_middle
-    far_keys = flat_keys([two_away])
+    far_keys = flat_pairs([two_away])
     guest_out, guest_lse = spatial_attention(
         guest_q.reshape(frames, lat_rows * columns, model_width),
         far_keys,
@@ -260,7 +268,7 @@
     per_column_map = jnp.repeat(window_map, BLK, axis=0)
     full_ring = ext_count >= total_cols and WIN * BLK <= total_cols
     if full_ring and lon_count == 4:
-        partials = spatial_line_of_four(own_q, key_value, window_map, scale)
+        partials = spatial_line_of_four(own_q, (own_k, own_v), window_map, scale)
     else:
         if full_ring:
             extended = jnp.concatenate(line_gather(key_value, "lon"), axis=3)

time: 133 us -> 146 us (1.098)
  starting transfers between devices: 27.3 us -> 34.4 us
  other arithmetic: 19.5 us -> 25.9 us
  local copies, waits for them, and re-layouts: 41.6 us -> 37.2 us
  waiting for transfers between devices: 19.1 us -> 22.4 us
    ppermute x4 -> x8, starting transfers between devices: 11.2 us -> 20.3 us  [send_pair(): return tuple((lax.ppermute(part, axis, pairs) for part in pair))]
    ppermute x4 -> x8, waiting for transfers between devices: 0.01 us -> 8.52 us  [send_pair(): return tuple((lax.ppermute(part, axis, pairs) for part in pair))]
    ppermute x2, waiting for transfers between devices: 13 us -> 6.03 us  [spatial_line_of_four(): lax.ppermute((guest_out.astype(jnp.bfloat16), jnp.swapaxes(guest_lse, 2,...]
    another operation x0 -> x3, other arithmetic: none -> 6.59 us  [the longest x2 3.92 us: flat_pairs(): jnp.stack([jnp.concatenate([pair[i] for pair in pairs], axis=2) for i in...]
    ppermute x1, waiting for transfers between devices: 0.01 us -> 6.18 us  [spatial_line_of_four(): guest_q = lax.ppermute(held_q, 'lon', [(0, 1), (3, 2)])]
    ppermute x1, waiting for transfers between devices: 4.33 us -> 0.01 us  [spatial_line_of_four(): guest_map = lax.ppermute(window_map, 'lon', [(0, 1), (3, 2)])]
    unnamed x14 -> x17, local copies, waits for them, and re-layouts: 4.79 us -> 2.87 us
    ppermute x1, starting transfers between devices: 9.25 us -> 7.34 us  [spatial_line_of_four(): guest_q = lax.ppermute(held_q, 'lon', [(0, 1), (3, 2)])]
  transfers between devices with their start and end apart: 10 -> 14, of which waited for: 3 -> 5; matrix products, arithmetic and copies ran while one was open for 40% -> 41% of each run, Pallas kernels for 10% -> 13%
where the time goes in v10:
time: 146 us; the launch traced here: 145 us
  local copies, waits for them, and re-layouts  37.2 us (25%)
  starting transfers between devices  34.4 us (24%)
  other arithmetic  25.9 us (18%)
  Pallas kernels  24.5 us (17%)
  waiting for transfers between devices  22.4 us (15%)
    ppermute x8, starting transfers between devices, send_pair(): return tuple((lax.ppermute(part, axis, pairs) for part in pair))  20.3 us
    pallas_call x3, Pallas kernels, spatial_attention(): pl.pallas_call(functools.partial(spatial_kernel, scale=scale), grid=(fram...  19.1 us
    reshape x3, local copies, waits for them, and re-layouts, expand_mask(): return jnp.broadcast_to(active[None, :, None, :].astype(jnp.float32), (la...  14.2 us
    ppermute x8, waiting for transfers between devices, send_pair(): return tuple((lax.ppermute(part, axis, pairs) for part in pair))  8.52 us
    broadcast_in_dim x3, local copies, waits for them, and re-layouts, expand_mask(): jnp.broadcast_to(active[None, :, None, :].astype(jnp.float32), (lat_rows,...  7.36 us
    ppermute x1, starting transfers between devices, spatial_line_of_four(): guest_q = lax.ppermute(held_q, 'lon', [(0, 1), (3, 2)])  7.34 us
    ppermute x1, waiting for transfers between devices, spatial_line_of_four(): guest_q = lax.ppermute(held_q, 'lon', [(0, 1), (3, 2)])  6.18 us
    ppermute x2, waiting for transfers between devices, spatial_line_of_four(): lax.ppermute((guest_out.astype(jnp.bfloat16), jnp.swapaxes(guest_lse, 2,...  6.03 us
  transfers between devices with their start and end apart: 14, of which 5 were waited for; matrix products, arithmetic and copies ran while one was open for 41% of the time, Pallas kernels for 13%

profile of v10, /device:TPU:0, one launch (start us, length us, event | category | flops | bytes accessed | tf_op | source)
XLA Modules:
  0.0 144.7 jit_solution(14281313094619509858)
XLA Ops:
  0.0 1.3 collective-permute-start.3
  1.3 6.5 %collective-permute-start.2 = (bf16[1,32,8,1536]{3,2,1,0:T(8,128)(2,1)}, bf16[1,32,8,1536]{3,2,1,0:T(8,128)(2,1)}, u32[]{:S(2)}, u32[]{:S(2)}) collective-permute-start(bf16[1,32,8,1536]{3,2,1,0:T(8,128)(2,1)} %bitcast.38), channel_id=1, source_target_pairs={{0,4},{4,8},{8,12},{1,5},{5,9},{9,13},{2,6},{6,10},{10,14},{3,7},{... | collective-permute-start | bytes 2359304 | tf_op jit(solution)/shard_map/ppermute | solution.py:181
  7.8 1.3 collective-permute-start.1
  9.1 5.5 %collective-permute-start = (bf16[1,32,8,1536]{3,2,1,0:T(8,128)(2,1)}, bf16[1,32,8,1536]{3,2,1,0:T(8,128)(2,1)}, u32[]{:S(2)}, u32[]{:S(2)}) collective-permute-start(bf16[1,32,8,1536]{3,2,1,0:T(8,128)(2,1)} %bitcast.41), channel_id=1, source_target_pairs={{0,4},{4,8},{8,12},{1,5},{5,9},{9,13},{2,6},{6,10},{10,14},{3,7},{... | collective-permute-start | bytes 2359304 | tf_op jit(solution)/shard_map/ppermute | solution.py:181
  14.5 2.6 %collective-permute-start.9 = (s32[4,15]{1,0:T(4,128)}, s32[4,15]{1,0:T(4,128)S(1)}, u32[]{:S(2)}, u32[]{:S(2)}) collective-permute-start(s32[4,15]{1,0:T(4,128)} %param.8), channel_id=1, source_target_pairs={{0,4},{12,8},{1,5},{13,9},{2,6},{14,10},{3,7},{15,11},{16,20},{28,... | collective-permute-start | bytes 728 | tf_op jit(solution)/shard_map/ppermute | solution.py:203
  17.1 0.7 broadcast_compare_fusion.1
  17.8 2.7 %pad_maximum_fusion.4 = bf16[2,1,32,8,1536]{4,3,2,1,0:T(8,128)(2,1)} fusion(bf16[1,1,32,8,1536]{4,3,2,1,0:T(8,128)(2,1)} %param.7, bf16[1,1,32,8,1536]{4,3,2,1,0:T(8,128)(2,1)} %param.6), kind=kLoop, calls=%fused_computation.9 | loop fusion | flops 786432 | bytes 3145728 | tf_op jit(solution)/shard_map/stack | solution.py:266
  20.5 2.9 %reshape.557 = bf16[2,1,256,12,128]{4,3,2,0,1:T(8,128)(2,1)S(1)} reshape(bf16[2,1,32,8,1536]{4,3,2,1,0:T(8,128)(2,1)} %pad_maximum_fusion.4) | data formatting | bytes 3145728 | tf_op jit(solution)/shard_map/reshape | solution.py:305
  23.4 1.7 %constant_dynamic-update-slice_fusion = bf16[2,2,256,12,128]{4,3,2,0,1:T(8,128)(2,1)} fusion(bf16[2,1,256,12,128]{4,3,2,0,1:T(8,128)(2,1)S(1)} %reshape.557), kind=kLoop, calls=%fused_computation.44 | loop fusion | bytes 3670016
  25.1 1.6 %copy.12 = bf16[2,1,256,12,128]{4,2,3,1,0:T(8,128)(2,1)} copy(bf16[2,1,256,12,128]{4,3,2,0,1:T(8,128)(2,1)S(1)} %reshape.557) | data formatting | bytes 3145728 | tf_op jit(solution)/shard_map/reshape | solution.py:305
  26.8 0.1 copy.11
  26.9 0.1 pad_add_fusion
  27.0 0.1 and.236
  27.1 0.1 add_select_fusion.2
  27.2 0.1 fusion.6
  27.3 2.5 %broadcast_in_dim.36 = f32[32,8,32,24]{3,2,1,0:T(8,128)} broadcast(f32[8,24]{1,0:T(8,128)S(1)} %and_convert_fusion.1), dimensions={1,3} | broadcast | bytes 787200 | tf_op jit(solution)/shard_map/broadcast_in_dim | solution.py:169
  29.8 4.6 %reshape.553.m_ref = f32[256,768]{1,0:T(8,128)} reshape(f32[32,8,32,24]{3,2,1,0:T(8,128)} %broadcast_in_dim.36) | data formatting | bytes 1572864 | tf_op jit(solution)/shard_map/reshape | solution.py:171
  34.4 0.1 add_select_fusion
  34.5 0.3 fusion.8
  34.8 2.5 %broadcast_in_dim.37 = f32[32,8,32,8]{3,2,1,0:T(8,128)} broadcast(f32[8,8]{1,0:T(8,128)S(1)} %convert_element_type.72), dimensions={1,3} | broadcast | bytes 262400 | tf_op jit(solution)/shard_map/broadcast_in_dim | solution.py:169
  37.3 4.8 %reshape.554.m_ref = f32[256,256]{1,0:T(8,128)} reshape(f32[32,8,32,8]{3,2,1,0:T(8,128)} %broadcast_in_dim.37) | data formatting | bytes 524288 | tf_op jit(solution)/shard_map/reshape | solution.py:171
  42.0 0.5 reshape.559
  42.5 0.2 copy-done.7
  42.7 0.1 tile.10
  42.9 0.6 gather_fusion
  43.5 1.5 %collective-permute-start.12 = (bf16[2,1,256,12,128]{4,2,3,1,0:T(8,128)(2,1)}, bf16[2,1,256,12,128]{4,2,3,1,0:T(8,128)(2,1)}, u32[]{:S(2)}, u32[]{:S(2)}) collective-permute-start(bf16[2,1,256,12,128]{4,2,3,1,0:T(8,128)(2,1)} %copy.12), channel_id=1, source_target_pairs={{0,2},{2,0},{1,3},{3,1},{4,6},{6,4},{5,7},{7,5},{8,10},{10,8},{9,1... | collective-permute-start | bytes 4718600 | tf_op jit(solution)/shard_map/ppermute | solution.py:21
  45.1 0.3 fusion.10
  45.4 2.5 %broadcast_in_dim.39 = f32[32,8,32,8]{3,2,1,0:T(8,128)} broadcast(f32[8,8]{1,0:T(8,128)S(1)} %and_convert_fusion), dimensions={1,3} | broadcast | bytes 262400 | tf_op jit(solution)/shard_map/broadcast_in_dim | solution.py:169
  47.8 4.8 %reshape.556.m_ref = f32[256,256]{1,0:T(8,128)} reshape(f32[32,8,32,8]{3,2,1,0:T(8,128)} %broadcast_in_dim.39) | data formatting | bytes 524288 | tf_op jit(solution)/shard_map/reshape | solution.py:171
  52.6 1.4 collective-permute-start.4
  54.0 1.3 collective-permute-start.6
  55.3 1.5 %collective-permute-start.7 = (bf16[1,32,8,1536]{3,2,1,0:T(8,128)(2,1)}, bf16[1,32,8,1536]{3,2,1,0:T(8,128)(2,1)}, u32[]{:S(2)}, u32[]{:S(2)}) collective-permute-start(bf16[1,32,8,1536]{3,2,1,0:T(8,128)(2,1)} %collective-permute-done.2), channel_id=1, source_target_pairs={{4,8},{8,12},{5,9},{9,13},{6,10},{10,14},{7,11},{11,15},{20,24},{2... | collective-permute-start | bytes 2359304 | tf_op jit(solution)/shard_map/ppermute | solution.py:181
  56.9 1.5 %pad_maximum_fusion.2 = bf16[1,32,24,1536]{3,2,1,0:T(8,128)(2,1)S(1)} fusion(bf16[1,32,8,1536]{3,2,1,0:T(8,128)(2,1)} %collective-permute-done.3, bf16[1,32,8,1536]{3,2,1,0:T(8,128)(2,1)S(1)} %bitcast.39, bf16[1,32,8,1536]{3,2,1,0:T(8,128)(2,1)} %collective-permute-done.2), kind=kLoop, calls=%fused_computation.5 | loop fusion | flops 7077888 | bytes 4718592 | tf_op jit(solution)/shard_map/concatenate | solution.py:185
  58.4 1.6 %collective-permute-start.5 = (bf16[1,32,8,1536]{3,2,1,0:T(8,128)(2,1)}, bf16[1,32,8,1536]{3,2,1,0:T(8,128)(2,1)}, u32[]{:S(2)}, u32[]{:S(2)}) collective-permute-start(bf16[1,32,8,1536]{3,2,1,0:T(8,128)(2,1)} %collective-permute-done), channel_id=1, source_target_pairs={{4,8},{8,12},{5,9},{9,13},{6,10},{10,14},{7,11},{11,15},{20,24},{2... | collective-permute-start | bytes 2359304 | tf_op jit(solution)/shard_map/ppermute | solution.py:181
  60.0 1.5 %pad_maximum_fusion.1 = bf16[1,32,24,1536]{3,2,1,0:T(8,128)(2,1)S(1)} fusion(bf16[1,32,8,1536]{3,2,1,0:T(8,128)(2,1)} %collective-permute-done.1, bf16[1,32,8,1536]{3,2,1,0:T(8,128)(2,1)S(1)} %bitcast.42, bf16[1,32,8,1536]{3,2,1,0:T(8,128)(2,1)} %collective-permute-done), kind=kLoop, calls=%fused_computation.4 | loop fusion | flops 7077888 | bytes 4718592 | tf_op jit(solution)/shard_map/concatenate | solution.py:185
  61.5 2.5 %pad_maximum_fusion.k_ref.v_ref = bf16[2,1,768,1536]{3,2,1,0:T(8,128)(2,1)} fusion(bf16[1,1,768,1536]{3,2,1,0:T(8,128)(2,1)S(1)} %bitcast.31, bf16[1,1,768,1536]{3,2,1,0:T(8,128)(2,1)S(1)} %bitcast.32), kind=kLoop, calls=%fused_computation.1 | loop fusion | flops 2359296 | bytes 9437184 | tf_op jit(solution)/shard_map/stack | solution.py:185
  64.0 8.5 %shard_map.55 = (f32[1,256,1536]{2,1,0:T(8,128)}, f32[1,3,256,4]{3,2,1,0:T(8,128)}) custom-call(bf16[1,256,1536]{2,1,0:T(8,128)(2,1)} %bitcast.33, bf16[2,1,768,1536]{3,2,1,0:T(8,128)(2,1)} %pad_maximum_fusion.k_ref.v_ref, bf16[2,1,768,1536]{3,2,1,0:T(8,128)(2,1)} %pad_maximum_fusion.k_ref.v_ref, f32[256,768]{1,0:T(8,128)} %reshape.553.m_ref), custom_call_target="tpu_custom_call" | custom-call | flops 1207959552 | bytes 7077888 | tf_op jit(solution)/shard_map/pallas_call | solution.py:65
  72.6 2.8 %collective-permute-done.4 = bf16[1,32,8,1536]{3,2,1,0:T(8,128)(2,1)} collective-permute-done((bf16[1,32,8,1536]{3,2,1,0:T(8,128)(2,1)}, bf16[1,32,8,1536]{3,2,1,0:T(8,128)(2,1)}, u32[]{:S(2)}, u32[]{:S(2)}) %collective-permute-start.4) | collective-permute-done | bytes 786464 | tf_op jit(solution)/shard_map/ppermute | solution.py:181
  75.4 7.3 %collective-permute-start.8 = (bf16[1,32,8,1536]{3,2,1,0:T(8,128)(2,1)S(1)}, bf16[1,32,8,1536]{3,2,1,0:T(8,128)(2,1)S(1)}, u32[]{:S(2)}, u32[]{:S(2)}) collective-permute-start(bf16[1,32,8,1536]{3,2,1,0:T(8,128)(2,1)S(1)} %bitcast.35), channel_id=1, source_target_pairs={{0,4},{12,8},{1,5},{13,9},{2,6},{14,10},{3,7},{15,11},{16,20},{28,... | collective-permute-start | bytes 2359304 | tf_op jit(solution)/shard_map/ppermute | solution.py:221
  82.8 1.2 broadcast_select_fusion.1
  84.0 5.7 %collective-permute-done.6 = bf16[1,32,8,1536]{3,2,1,0:T(8,128)(2,1)} collective-permute-done((bf16[1,32,8,1536]{3,2,1,0:T(8,128)(2,1)}, bf16[1,32,8,1536]{3,2,1,0:T(8,128)(2,1)}, u32[]{:S(2)}, u32[]{:S(2)}) %collective-permute-start.6) | collective-permute-done | bytes 786464 | tf_op jit(solution)/shard_map/ppermute | solution.py:181
  89.7 1.2 broadcast_select_fusion
  90.9 6.2 %collective-permute-done.8 = bf16[1,32,8,1536]{3,2,1,0:T(8,128)(2,1)S(1)} collective-permute-done((bf16[1,32,8,1536]{3,2,1,0:T(8,128)(2,1)S(1)}, bf16[1,32,8,1536]{3,2,1,0:T(8,128)(2,1)S(1)}, u32[]{:S(2)}, u32[]{:S(2)}) %collective-permute-start.8) | collective-permute-done | bytes 786464 | tf_op jit(solution)/shard_map/ppermute | solution.py:221
  97.1 1.4 pad_maximum_fusion.3.k_ref.v_ref
  98.5 5.3 %shard_map.57 = (f32[1,256,1536]{2,1,0:T(8,128)}, f32[1,3,256,4]{3,2,1,0:T(8,128)}) custom-call(bf16[1,256,1536]{2,1,0:T(8,128)(2,1)} %bitcast.47, bf16[2,1,256,1536]{3,2,1,0:T(8,128)(2,1)} %pad_maximum_fusion.3.k_ref.v_ref, bf16[2,1,256,1536]{3,2,1,0:T(8,128)(2,1)} %pad_maximum_fusion.3.k_ref.v_ref, f32[256,256]{1,0:T(8,128)} %reshape.556.m_ref), custom_call_target="tpu_custom_call" | custom-call | flops 402653184 | bytes 3932160 | tf_op jit(solution)/shard_map/pallas_call | solution.py:65
  103.7 2.4 %convert_element_type.74 = bf16[1,256,1536]{2,1,0:T(8,128)(2,1)} convert(f32[1,256,1536]{2,1,0:T(8,128)} %get-tuple-element.27) | non-fusion elementwise | flops 393216 | bytes 2359296 | tf_op jit(solution)/shard_map/convert_element_type | solution.py:243
  106.1 1.3 collective-permute-start.10
  107.4 1.3 collective-permute-start.11
  108.7 3.9 %copy_dynamic-update-slice_fusion = bf16[2,2,256,12,128]{4,3,2,0,1:T(8,128)(2,1)} fusion(bf16[2,2,256,12,128]{4,3,2,0,1:T(8,128)(2,1)} %constant_dynamic-update-slice_fusion, bf16[2,1,256,12,128]{4,2,3,1,0:T(8,128)(2,1)} %collective-permute-done.12), kind=kLoop, calls=%fused_computation.6 | loop fusion | bytes 3670016 | tf_op jit(solution)/shard_map/concatenate | solution.py:309
  112.6 2.9 %multiply_reduce_fusion.1 = f32[2,256,12]{2,1,0:T(8,128)S(1)} fusion(bf16[2,2,256,12,128]{4,3,2,0,1:T(8,128)(2,1)} %copy_dynamic-update-slice_fusion, f32[256,12,128]{2,1,0:T(8,128)S(1)} %reshape.559), kind=kLoop, calls=%fused_computation.3 | loop fusion | flops 2353152 | bytes 3170304 | tf_op jit(solution)/shard_map/reduce_sum | solution.py:130
  115.5 0.1 fusion.2
  115.7 0.1 fusion.3
  115.8 2.9 %multiply_reduce_fusion = f32[256,12,128]{2,1,0:T(8,128)S(1)} fusion(bf16[2,2,256,12,128]{4,3,2,0,1:T(8,128)(2,1)S(1)} %copy-done, f32[2,256,12]{2,1,0:T(8,128)S(1)} %get-tuple-element.30), kind=kLoop, calls=%fused_computation.2 | loop fusion | flops 1966080 | bytes 3170304 | tf_op jit(solution)/shard_map/reduce_sum | solution.py:138
  118.8 0.7 reduce-precision_convert_fusion
  119.5 5.3 %shard_map.56 = (f32[1,256,1536]{2,1,0:T(8,128)}, f32[1,3,256,4]{3,2,1,0:T(8,128)}) custom-call(bf16[1,256,1536]{2,1,0:T(8,128)(2,1)} %bitcast.34, bf16[2,1,256,1536]{3,2,1,0:T(8,128)(2,1)} %pad_maximum_fusion.3.k_ref.v_ref, bf16[2,1,256,1536]{3,2,1,0:T(8,128)(2,1)} %pad_maximum_fusion.3.k_ref.v_ref, f32[256,256]{1,0:T(8,128)} %reshape.554.m_ref), custom_call_target="tpu_custom_call" | custom-call | flops 402653184 | bytes 3932160 | tf_op jit(solution)/shard_map/pallas_call | solution.py:65
  124.8 0.8 copy.14
  125.7 1.2 copy.15.refs_6_
  126.8 6.0 %collective-permute-done.11 = f32[1,3,4,256]{2,3,1,0:T(8,128)S(1)} collective-permute-done((f32[1,3,4,256]{2,3,1,0:T(8,128)}, f32[1,3,4,256]{2,3,1,0:T(8,128)S(1)}, u32[]{:S(2)}, u32[]{:S(2)}) %collective-permute-start.11) | collective-permute-done | bytes 12320 | tf_op jit(solution)/shard_map/ppermute | solution.py:242
  132.9 0.8 select_bitcast_fusion.refs_5_
  133.6 0.9 copy-done.5
  134.5 5.4 %shard_map.58 = bf16[1,256,1536]{2,1,0:T(8,128)(2,1)} custom-call(f32[1,256,1536]{2,1,0:T(8,128)} %get-tuple-element.20.refs_0_, f32[1,3,256,4]{3,2,1,0:T(8,128)} %get-tuple-element.21.refs_1_, f32[1,256,1536]{2,1,0:T(8,128)} %get-tuple-element.24.refs_2_, f32[1,3,256,4]{3,2,1,0:T(8,128)} %get-tuple-element.25.refs_3_, bf16[1,256,1536]{2,1,0:T(8,128)(2,1)} %copy-done.5, ...), custom_call_target="tpu_custom_call" | custom-call | tf_op jit(solution)/shard_map/pallas_call | solution.py:118
  139.9 1.0 constant_dynamic-slice_fusion
  141.0 1.7 %collective-permute-done.13 = bf16[1,32,8,768]{3,2,1,0:T(8,128)(2,1)S(1)} collective-permute-done((bf16[1,32,8,768]{3,2,1,0:T(8,128)(2,1)S(1)}, bf16[1,32,8,768]{3,2,1,0:T(8,128)(2,1)S(1)}, u32[]{:S(2)}, u32[]{:S(2)}) %collective-permute-start.13) | collective-permute-done | bytes 393248 | tf_op jit(solution)/shard_map/ppermute | solution.py:25
  142.7 1.9 %fusion.1 = bf16[1,32,8,768]{3,2,1,0:T(8,128)(2,1)} fusion(bf16[1,32,8,768]{3,2,1,0:T(8,128)(2,1)S(1)} %collective-permute-done.13, bf16[1,32,8,1536]{3,2,1,0:T(8,128)(2,1)} %bitcast.44, s32[]{:T(128)S(6)} %select_n.235, pred[]{:T(512)S(6)} %eq.73), kind=kLoop, calls=%fused_computation.13 | loop fusion | flops 1572864 | bytes 1179653 | tf_op jit(solution)/shard_map/convert_element_type | solution.py:332
  (42 shorter events, 0.5 us)
Async XLA Ops:
  0.0 54.0 %collective-permute-start.3 = (bf16[1,32,8,1536]{3,2,1,0:T(8,128)(2,1)}, bf16[1,32,8,1536]{3,2,1,0:T(8,128)(2,1)}, u32[]{:S(2)}, u32[]{:S(2)}) collective-permute-start(bf16[1,32,8,1536]{3,2,1,0:T(8,128)(2,1)} %bitcast.37), channel_id=1, source_target_pairs={{12,8},{8,4},{4,0},{13,9},{9,5},{5,1},{14,10},{10,6},{6,2},{15,11}... | collective-permute-start | bytes 2359304 | tf_op jit(solution)/shard_map/ppermute | solution.py:181
  1.3 54.0 %collective-permute-start.2 = (bf16[1,32,8,1536]{3,2,1,0:T(8,128)(2,1)}, bf16[1,32,8,1536]{3,2,1,0:T(8,128)(2,1)}, u32[]{:S(2)}, u32[]{:S(2)}) collective-permute-start(bf16[1,32,8,1536]{3,2,1,0:T(8,128)(2,1)} %bitcast.38), channel_id=1, source_target_pairs={{0,4},{4,8},{8,12},{1,5},{5,9},{9,13},{2,6},{6,10},{10,14},{3,7},{... | collective-permute-start | bytes 2359304 | tf_op jit(solution)/shard_map/ppermute | solution.py:181
  7.8 44.8 %collective-permute-start.1 = (bf16[1,32,8,1536]{3,2,1,0:T(8,128)(2,1)}, bf16[1,32,8,1536]{3,2,1,0:T(8,128)(2,1)}, u32[]{:S(2)}, u32[]{:S(2)}) collective-permute-start(bf16[1,32,8,1536]{3,2,1,0:T(8,128)(2,1)} %bitcast.40), channel_id=1, source_target_pairs={{12,8},{8,4},{4,0},{13,9},{9,5},{5,1},{14,10},{10,6},{6,2},{15,11}... | collective-permute-start | bytes 2359304 | tf_op jit(solution)/shard_map/ppermute | solution.py:181
  9.1 49.4 %collective-permute-start = (bf16[1,32,8,1536]{3,2,1,0:T(8,128)(2,1)}, bf16[1,32,8,1536]{3,2,1,0:T(8,128)(2,1)}, u32[]{:S(2)}, u32[]{:S(2)}) collective-permute-start(bf16[1,32,8,1536]{3,2,1,0:T(8,128)(2,1)} %bitcast.41), channel_id=1, source_target_pairs={{0,4},{4,8},{8,12},{1,5},{5,9},{9,13},{2,6},{6,10},{10,14},{3,7},{... | collective-permute-start | bytes 2359304 | tf_op jit(solution)/shard_map/ppermute | solution.py:181
  14.5 29.0 %collective-permute-start.9 = (s32[4,15]{1,0:T(4,128)}, s32[4,15]{1,0:T(4,128)S(1)}, u32[]{:S(2)}, u32[]{:S(2)}) collective-permute-start(s32[4,15]{1,0:T(4,128)} %param.8), channel_id=1, source_target_pairs={{0,4},{12,8},{1,5},{13,9},{2,6},{14,10},{3,7},{15,11},{16,20},{28,... | collective-permute-start | bytes 728 | tf_op jit(solution)/shard_map/ppermute | solution.py:203
  37.3 4.8 %copy-start.1 = (bf16[1,1,32,8,1536]{4,3,2,1,0:T(8,128)(2,1)S(1)}, bf16[1,1,32,8,1536]{4,3,2,1,0:T(8,128)(2,1)}, u32[]{:S(2)}) copy-start(bf16[1,1,32,8,1536]{4,3,2,1,0:T(8,128)(2,1)} %param.5) | copy-start | bytes 2359300
  42.0 0.7 copy-start.7
  43.5 65.2 %collective-permute-start.12 = (bf16[2,1,256,12,128]{4,2,3,1,0:T(8,128)(2,1)}, bf16[2,1,256,12,128]{4,2,3,1,0:T(8,128)(2,1)}, u32[]{:S(2)}, u32[]{:S(2)}) collective-permute-start(bf16[2,1,256,12,128]{4,2,3,1,0:T(8,128)(2,1)} %copy.12), channel_id=1, source_target_pairs={{0,2},{2,0},{1,3},{3,1},{4,6},{6,4},{5,7},{7,5},{8,10},{10,8},{9,1... | collective-permute-start | bytes 4718600 | tf_op jit(solution)/shard_map/ppermute | solution.py:21
  47.8 9.0 %copy-start.3 = (bf16[1,1,32,8,1536]{4,3,2,1,0:T(8,128)(2,1)S(1)}, bf16[1,1,32,8,1536]{4,3,2,1,0:T(8,128)(2,1)}, u32[]{:S(2)}) copy-start(bf16[1,1,32,8,1536]{4,3,2,1,0:T(8,128)(2,1)} %param.7) | copy-start | bytes 2359300
  52.6 7.4 %copy-start.4 = (bf16[1,1,32,8,1536]{4,3,2,1,0:T(8,128)(2,1)S(1)}, bf16[1,1,32,8,1536]{4,3,2,1,0:T(8,128)(2,1)}, u32[]{:S(2)}) copy-start(bf16[1,1,32,8,1536]{4,3,2,1,0:T(8,128)(2,1)} %param.6) | copy-start | bytes 2359300
  52.6 22.8 %collective-permute-start.4 = (bf16[1,32,8,1536]{3,2,1,0:T(8,128)(2,1)}, bf16[1,32,8,1536]{3,2,1,0:T(8,128)(2,1)}, u32[]{:S(2)}, u32[]{:S(2)}) collective-permute-start(bf16[1,32,8,1536]{3,2,1,0:T(8,128)(2,1)} %collective-permute-done.1), channel_id=1, source_target_pairs={{8,4},{4,0},{9,5},{5,1},{10,6},{6,2},{11,7},{7,3},{24,20},{20,16},... | collective-permute-start | bytes 2359304 | tf_op jit(solution)/shard_map/ppermute | solution.py:181
  54.0 35.6 %collective-permute-start.6 = (bf16[1,32,8,1536]{3,2,1,0:T(8,128)(2,1)}, bf16[1,32,8,1536]{3,2,1,0:T(8,128)(2,1)}, u32[]{:S(2)}, u32[]{:S(2)}) collective-permute-start(bf16[1,32,8,1536]{3,2,1,0:T(8,128)(2,1)} %collective-permute-done.3), channel_id=1, source_target_pairs={{8,4},{4,0},{9,5},{5,1},{10,6},{6,2},{11,7},{7,3},{24,20},{20,16},... | collective-permute-start | bytes 2359304 | tf_op jit(solution)/shard_map/ppermute | solution.py:181
  55.3 34.3 %collective-permute-start.7 = (bf16[1,32,8,1536]{3,2,1,0:T(8,128)(2,1)}, bf16[1,32,8,1536]{3,2,1,0:T(8,128)(2,1)}, u32[]{:S(2)}, u32[]{:S(2)}) collective-permute-start(bf16[1,32,8,1536]{3,2,1,0:T(8,128)(2,1)} %collective-permute-done.2), channel_id=1, source_target_pairs={{4,8},{8,12},{5,9},{9,13},{6,10},{10,14},{7,11},{11,15},{20,24},{2... | collective-permute-start | bytes 2359304 | tf_op jit(solution)/shard_map/ppermute | solution.py:181
  58.4 24.3 %collective-permute-start.5 = (bf16[1,32,8,1536]{3,2,1,0:T(8,128)(2,1)}, bf16[1,32,8,1536]{3,2,1,0:T(8,128)(2,1)}, u32[]{:S(2)}, u32[]{:S(2)}) collective-permute-start(bf16[1,32,8,1536]{3,2,1,0:T(8,128)(2,1)} %collective-permute-done), channel_id=1, source_target_pairs={{4,8},{8,12},{5,9},{9,13},{6,10},{10,14},{7,11},{11,15},{20,24},{2... | collective-permute-start | bytes 2359304 | tf_op jit(solution)/shard_map/ppermute | solution.py:181
  64.0 11.4 %copy-start.2 = (bf16[1,1,32,8,1536]{4,3,2,1,0:T(8,128)(2,1)S(1)}, bf16[1,1,32,8,1536]{4,3,2,1,0:T(8,128)(2,1)}, u32[]{:S(2)}) copy-start(bf16[1,1,32,8,1536]{4,3,2,1,0:T(8,128)(2,1)} %param.5) | copy-start | bytes 2359300
  75.4 21.7 %collective-permute-start.8 = (bf16[1,32,8,1536]{3,2,1,0:T(8,128)(2,1)S(1)}, bf16[1,32,8,1536]{3,2,1,0:T(8,128)(2,1)S(1)}, u32[]{:S(2)}, u32[]{:S(2)}) collective-permute-start(bf16[1,32,8,1536]{3,2,1,0:T(8,128)(2,1)S(1)} %bitcast.35), channel_id=1, source_target_pairs={{0,4},{12,8},{1,5},{13,9},{2,6},{14,10},{3,7},{15,11},{16,20},{28,... | collective-permute-start | bytes 2359304 | tf_op jit(solution)/shard_map/ppermute | solution.py:221
  97.1 1.4 copy-start.6
  106.1 27.5 %collective-permute-start.10 = (bf16[1,256,1536]{2,1,0:T(8,128)(2,1)}, bf16[1,256,1536]{2,1,0:T(8,128)(2,1)S(1)}, u32[]{:S(2)}, u32[]{:S(2)}) collective-permute-start(bf16[1,256,1536]{2,1,0:T(8,128)(2,1)} %convert_element_type.74), channel_id=1, source_target_pairs={{4,0},{8,12},{5,1},{9,13},{6,2},{10,14},{7,3},{11,15},{20,16},{24,... | collective-permute-start | bytes 2359304 | tf_op jit(solution)/shard_map/ppermute | solution.py:242
  107.4 25.5 %collective-permute-start.11 = (f32[1,3,4,256]{2,3,1,0:T(8,128)}, f32[1,3,4,256]{2,3,1,0:T(8,128)S(1)}, u32[]{:S(2)}, u32[]{:S(2)}) collective-permute-start(f32[1,3,4,256]{2,3,1,0:T(8,128)} %bitcast.12), channel_id=1, source_target_pairs={{4,0},{8,12},{5,1},{9,13},{6,2},{10,14},{7,3},{11,15},{20,16},{24,... | collective-permute-start | bytes 36872 | tf_op jit(solution)/shard_map/ppermute | solution.py:242
  112.6 3.2 %copy-start = (bf16[2,2,256,12,128]{4,3,2,0,1:T(8,128)(2,1)S(1)}, bf16[2,2,256,12,128]{4,3,2,0,1:T(8,128)(2,1)}, u32[]{:S(2)}) copy-start(bf16[2,2,256,12,128]{4,3,2,0,1:T(8,128)(2,1)} %copy_dynamic-update-slice_fusion) | copy-start | bytes 9437188
  133.6 0.9 copy-start.5
  140.9 1.8 %collective-permute-start.13 = (bf16[1,32,8,768]{3,2,1,0:T(8,128)(2,1)S(1)}, bf16[1,32,8,768]{3,2,1,0:T(8,128)(2,1)S(1)}, u32[]{:S(2)}, u32[]{:S(2)}) collective-permute-start(bf16[1,32,8,768]{3,2,1,0:T(8,128)(2,1)S(1)} %constant_dynamic-slice_fusion), channel_id=1, source_target_pairs={{0,1},{1,0},{2,3},{3,2},{4,5},{5,4},{6,7},{7,6},{8,9},{9,8},{10,11... | collective-permute-start | bytes 1179656 | tf_op jit(solution)/shard_map/ppermute | solution.py:25

commit v11 on v7

--- a/solution.py
+++ b/solution.py
@@ -204,13 +204,15 @@
         scale,
     )
 
-    two_away = jnp.where(
-        index <= 1,
-        lax.ppermute(from_right, "lon", [(2, 1), (1, 0)]),
-        lax.ppermute(from_left, "lon", [(1, 2), (2, 3)]),
-    )
-    held_q, _ = lax.optimization_barrier((own_q, from_left))
-    guest_q = lax.ppermute(held_q, "lon", [(0, 1), (3, 2)])
+    own_q_pair = jnp.stack([own_q, own_q])
+    toward_left = lax.ppermute(
+        jnp.where(index == count - 1, own_q_pair, from_right), "lon", [(2, 1), (1, 0), (3, 2)]
+    )
+    toward_right = lax.ppermute(
+        jnp.where(index == 0, own_q_pair, from_left), "lon", [(1, 2), (2, 3), (0, 1)]
+    )
+    two_away = jnp.where(index <= 1, toward_left, toward_right)
+    guest_q = jnp.where(index == 1, toward_right[0], toward_left[0])
     near_part, two_away, guest_q = lax.optimization_barrier((near_part, two_away, guest_q))
 
     guest_device = jnp.where(index == 1, 0, count - 1)

time: 133 us -> 138 us (1.038)
  starting transfers between devices: 27.3 us -> 21.9 us
  waiting for transfers between devices: 19.1 us -> 24.4 us
  other arithmetic: 19.5 us -> 24.7 us
    ppermute x3 -> x2, starting transfers between devices: 12.4 us -> 7.04 us  [the longest x1 5.76 us: spatial_line_of_four(): lax.ppermute(jnp.where(index == 0, own_q_pair, from_left), 'lon', [(1, 2)...]
    ppermute x3 -> x2, waiting for transfers between devices: 0.01 us -> 5.28 us  [the longest x1 3.99 us: spatial_line_of_four(): lax.ppermute(jnp.where(index == count - 1, own_q_pair, from_right), 'lon'...]
    select_n x1 -> x3, other arithmetic: 1.31 us -> 5.63 us  [the longest x1 3.31 us: spatial_line_of_four(): jnp.where(index == 0, own_q_pair, from_left)]
    unnamed x14 -> x17, local copies, waits for them, and re-layouts: 4.79 us -> 4.83 us
  transfers between devices with their start and end apart: 10 -> 9, of which waited for: 3 -> 5; matrix products, arithmetic and copies ran while one was open for 40% -> 40% of each run, Pallas kernels for 10% -> 10%
where the time goes in v11:
time: 138 us; the launch traced here: 137 us
  local copies, waits for them, and re-layouts  41.6 us (30%)
  other arithmetic  24.7 us (18%)
  waiting for transfers between devices  24.4 us (18%)
  Pallas kernels  24.4 us (18%)
  starting transfers between devices  21.9 us (16%)
    pallas_call x3, Pallas kernels, spatial_attention(): pl.pallas_call(functools.partial(spatial_kernel, scale=scale), grid=(fram...  19 us
    reshape x3, local copies, waits for them, and re-layouts, expand_mask(): return jnp.broadcast_to(active[None, :, None, :].astype(jnp.float32), (la...  14.1 us
    ppermute x2, waiting for transfers between devices, spatial_line_of_four(): lax.ppermute((guest_out.astype(jnp.bfloat16), jnp.swapaxes(guest_lse, 2,...  13.1 us
    broadcast_in_dim x3, local copies, waits for them, and re-layouts, expand_mask(): jnp.broadcast_to(active[None, :, None, :].astype(jnp.float32), (lat_rows,...  7.37 us
    ppermute x1, starting transfers between devices, spatial_line_of_four(): from_left = lax.ppermute(key_value, 'lon', [(0, 1), (1, 2), (2, 3)])  6.7 us
    ppermute x1, starting transfers between devices, spatial_line_of_four(): lax.ppermute(jnp.where(index == 0, own_q_pair, from_left), 'lon', [(1, 2)...  5.76 us
    pallas_call x1, Pallas kernels, combine_partials(): pl.pallas_call(combine_kernel, grid=(frames, groups), in_specs=[big, smal...  5.36 us
    unnamed x17, local copies, waits for them, and re-layouts  4.83 us
  transfers between devices with their start and end apart: 9, of which 5 were waited for; matrix products, arithmetic and copies ran while one was open for 40% of the time, Pallas kernels for 10%

profile of v11, /device:TPU:0, one launch (start us, length us, event | category | flops | bytes accessed | tf_op | source)
XLA Modules:
  0.0 137.3 jit_solution(16674933539497066122)
XLA Ops:
  0.0 2.1 %constant_dynamic-update-slice_fusion.1 = bf16[2,1,32,8,1536]{4,3,2,1,0:T(8,128)(2,1)} fusion(bf16[1,1,32,8,1536]{4,3,2,1,0:T(8,128)(2,1)} %param.6), kind=kLoop, calls=%fused_computation.31 | loop fusion | bytes 1572864
  2.1 0.9 constant_dynamic-update-slice_fusion
  3.1 1.3 collective-permute-start.1
  4.4 6.7 %collective-permute-start = (bf16[2,1,32,8,1536]{4,3,2,1,0:T(8,128)(2,1)}, bf16[2,1,32,8,1536]{4,3,2,1,0:T(8,128)(2,1)}, u32[]{:S(2)}, u32[]{:S(2)}) collective-permute-start(bf16[2,1,32,8,1536]{4,3,2,1,0:T(8,128)(2,1)} %constant_dynamic-update-slice_fusion), channel_id=1, source_target_pairs={{0,4},{4,8},{8,12},{1,5},{5,9},{9,13},{2,6},{6,10},{10,14},{3,7},{... | collective-permute-start | bytes 4718600 | tf_op jit(solution)/shard_map/ppermute | solution.py:191
  11.1 2.8 %collective-permute-start.4 = (s32[4,15]{1,0:T(4,128)S(1)}, s32[4,15]{1,0:T(4,128)S(1)}, u32[]{:S(2)}, u32[]{:S(2)}) collective-permute-start(s32[4,15]{1,0:T(4,128)S(1)} %copy-done.4), channel_id=1, source_target_pairs={{0,4},{12,8},{1,5},{13,9},{2,6},{14,10},{3,7},{15,11},{16,20},{28,... | collective-permute-start | bytes 728 | tf_op jit(solution)/shard_map/ppermute | solution.py:193
  13.9 2.9 %reshape.577 = bf16[2,1,256,12,128]{4,3,2,0,1:T(8,128)(2,1)S(1)} reshape(bf16[2,1,32,8,1536]{4,3,2,1,0:T(8,128)(2,1)} %constant_dynamic-update-slice_fusion) | data formatting | bytes 3145728 | tf_op jit(solution)/shard_map/reshape | solution.py:299
  16.8 1.6 %copy.12 = bf16[2,1,256,12,128]{4,2,3,1,0:T(8,128)(2,1)} copy(bf16[2,1,256,12,128]{4,3,2,0,1:T(8,128)(2,1)S(1)} %reshape.577) | data formatting | bytes 3145728 | tf_op jit(solution)/shard_map/reshape | solution.py:299
  18.4 1.5 %collective-permute-start.7 = (bf16[2,1,256,12,128]{4,2,3,1,0:T(8,128)(2,1)}, bf16[2,1,256,12,128]{4,2,3,1,0:T(8,128)(2,1)}, u32[]{:S(2)}, u32[]{:S(2)}) collective-permute-start(bf16[2,1,256,12,128]{4,2,3,1,0:T(8,128)(2,1)} %copy.12), channel_id=1, source_target_pairs={{0,2},{2,0},{1,3},{3,1},{4,6},{6,4},{5,7},{7,5},{8,10},{10,8},{9,1... | collective-permute-start | bytes 4718600 | tf_op jit(solution)/shard_map/ppermute | solution.py:21
  19.9 0.1 copy.11
  20.0 0.1 pad_add_fusion
  20.1 0.1 broadcast_in_dim.35
  20.2 0.1 and.236
  20.3 0.1 add_select_fusion.2
  20.4 0.1 add_select_fusion
  20.4 0.3 fusion.9
  20.7 0.1 fusion.7
  20.9 2.5 %broadcast_in_dim.36 = f32[32,8,32,24]{3,2,1,0:T(8,128)} broadcast(f32[8,24]{1,0:T(8,128)S(1)} %and_convert_fusion.1), dimensions={1,3} | broadcast | bytes 787200 | tf_op jit(solution)/shard_map/broadcast_in_dim | solution.py:169
  23.3 4.6 %reshape.572.m_ref = f32[256,768]{1,0:T(8,128)} reshape(f32[32,8,32,24]{3,2,1,0:T(8,128)} %broadcast_in_dim.36) | data formatting | bytes 1572864 | tf_op jit(solution)/shard_map/reshape | solution.py:171
  28.0 2.5 %broadcast_in_dim.37 = f32[32,8,32,8]{3,2,1,0:T(8,128)} broadcast(f32[8,8]{1,0:T(8,128)S(1)} %convert_element_type.72), dimensions={1,3} | broadcast | bytes 262400 | tf_op jit(solution)/shard_map/broadcast_in_dim | solution.py:169
  30.4 4.8 %reshape.574.m_ref = f32[256,256]{1,0:T(8,128)} reshape(f32[32,8,32,8]{3,2,1,0:T(8,128)} %broadcast_in_dim.37) | data formatting | bytes 524288 | tf_op jit(solution)/shard_map/reshape | solution.py:171
  35.2 1.8 %reshape.579 = f32[256,12,128]{2,1,0:T(8,128)} reshape(bf16[1,1,32,8,1536]{4,3,2,1,0:T(8,128)(2,1)S(1)} %copy-done) | data formatting | bytes 2359296 | tf_op jit(solution)/shard_map/convert_element_type | solution.py:128
  37.0 0.1 tile.10
  37.1 0.6 gather_fusion
  37.8 1.7 %constant_dynamic-update-slice_fusion.4 = bf16[2,2,256,12,128]{4,3,2,0,1:T(8,128)(2,1)} fusion(bf16[2,1,256,12,128]{4,3,2,0,1:T(8,128)(2,1)S(1)} %reshape.577), kind=kLoop, calls=%fused_computation.34 | loop fusion | bytes 3670016
  39.5 0.1 compare_or_fusion
  39.6 0.1 constant_dynamic-update-slice_fusion.3
  39.6 0.1 constant_dynamic-update-slice_fusion.2
  39.7 4.2 %collective-permute-done.4 = s32[4,15]{1,0:T(4,128)S(1)} collective-permute-done((s32[4,15]{1,0:T(4,128)S(1)}, s32[4,15]{1,0:T(4,128)S(1)}, u32[]{:S(2)}, u32[]{:S(2)}) %collective-permute-start.4) | collective-permute-done | bytes 272 | tf_op jit(solution)/shard_map/ppermute | solution.py:193
  44.0 0.3 fusion.11
  44.2 0.0 collective-permute-done.1
  44.3 0.0 collective-permute-done
  44.3 3.3 %broadcast_select_fusion = (bf16[2,1,32,8,1536]{4,3,2,1,0:T(8,128)(2,1)}, bf16[2,1,32,8,1536]{4,3,2,1,0:T(8,128)(2,1)}) fusion(bf16[2,1,32,8,1536]{4,3,2,1,0:T(8,128)(2,1)S(1)} %constant_dynamic-update-slice_fusion.2, bf16[2,1,32,8,1536]{4,3,2,1,0:T(8,128)(2,1)} %collective-permute-done, pred[]{:T(512)S(6)} %eq.85, ...), kind=kLoop, calls=%fused_computation.6 | loop fusion | flops 1572864 | bytes 7864322 | tf_op jit(solution)/shard_map/jit(_where)/select_n | solution.py:212
  47.6 1.3 collective-permute-start.2
  48.9 5.8 %collective-permute-start.3 = (bf16[2,1,32,8,1536]{4,3,2,1,0:T(8,128)(2,1)}, bf16[2,1,32,8,1536]{4,3,2,1,0:T(8,128)(2,1)S(1)}, u32[]{:S(2)}, u32[]{:S(2)}) collective-permute-start(bf16[2,1,32,8,1536]{4,3,2,1,0:T(8,128)(2,1)} %get-tuple-element.25), channel_id=1, source_target_pairs={{4,8},{8,12},{0,4},{5,9},{9,13},{1,5},{6,10},{10,14},{2,6},{7,11},... | collective-permute-start | bytes 4718600 | tf_op jit(solution)/shard_map/ppermute | solution.py:211
  54.7 2.5 %broadcast_in_dim.39 = f32[32,8,32,8]{3,2,1,0:T(8,128)} broadcast(f32[8,8]{1,0:T(8,128)S(1)} %and_convert_fusion), dimensions={1,3} | broadcast | bytes 262400 | tf_op jit(solution)/shard_map/broadcast_in_dim | solution.py:169
  57.1 4.7 %reshape.576.m_ref = f32[256,256]{1,0:T(8,128)} reshape(f32[32,8,32,8]{3,2,1,0:T(8,128)} %broadcast_in_dim.39) | data formatting | bytes 524288 | tf_op jit(solution)/shard_map/reshape | solution.py:171
  61.8 4.8 %pad_maximum_fusion = bf16[2,1,32,24,1536]{4,3,2,1,0:T(8,128)(2,1)} fusion(bf16[2,1,32,8,1536]{4,3,2,1,0:T(8,128)(2,1)} %collective-permute-done.1, bf16[2,1,32,8,1536]{4,3,2,1,0:T(8,128)(2,1)} %constant_dynamic-update-slice_fusion, bf16[2,1,32,8,1536]{4,3,2,1,0:T(8,128)(2,1)} %collective-permute-done), kind=kLoop, calls=%fused_computation.1 | loop fusion | flops 14155776 | bytes 9437184 | tf_op jit(solution)/shard_map/concatenate | solution.py:175
  66.6 8.5 %shard_map.55 = (f32[1,256,1536]{2,1,0:T(8,128)}, f32[1,3,256,4]{3,2,1,0:T(8,128)}) custom-call(bf16[1,256,1536]{2,1,0:T(8,128)(2,1)} %bitcast.34, bf16[2,1,768,1536]{3,2,1,0:T(8,128)(2,1)} %bitcast.28, bf16[2,1,768,1536]{3,2,1,0:T(8,128)(2,1)} %bitcast.29, f32[256,768]{1,0:T(8,128)} %reshape.572.m_ref), custom_call_target="tpu_custom_call" | custom-call | flops 1207959552 | bytes 7077888 | tf_op jit(solution)/shard_map/pallas_call | solution.py:65
  75.0 0.0 collective-permute-done.7
  75.0 4.0 %copy_dynamic-update-slice_fusion = bf16[2,2,256,12,128]{4,3,2,0,1:T(8,128)(2,1)} fusion(bf16[2,2,256,12,128]{4,3,2,0,1:T(8,128)(2,1)} %constant_dynamic-update-slice_fusion.4, bf16[2,1,256,12,128]{4,2,3,1,0:T(8,128)(2,1)} %collective-permute-done.7), kind=kLoop, calls=%fused_computation.4 | loop fusion | bytes 3670016 | tf_op jit(solution)/shard_map/concatenate | solution.py:303
  79.1 2.8 %multiply_reduce_fusion.1 = f32[2,256,12]{2,1,0:T(8,128)S(1)} fusion(bf16[2,2,256,12,128]{4,3,2,0,1:T(8,128)(2,1)} %copy_dynamic-update-slice_fusion, f32[256,12,128]{2,1,0:T(8,128)S(1)} %copy-done.1), kind=kLoop, calls=%fused_computation.3 | loop fusion | flops 2353152 | bytes 3170304 | tf_op jit(solution)/shard_map/reduce_sum | solution.py:130
  81.9 0.1 fusion.3
  82.0 0.1 fusion.4
  82.2 4.0 %collective-permute-done.2 = bf16[2,1,32,8,1536]{4,3,2,1,0:T(8,128)(2,1)S(1)} collective-permute-done((bf16[2,1,32,8,1536]{4,3,2,1,0:T(8,128)(2,1)}, bf16[2,1,32,8,1536]{4,3,2,1,0:T(8,128)(2,1)S(1)}, u32[]{:S(2)}, u32[]{:S(2)}) %collective-permute-start.2) | collective-permute-done | bytes 1572896 | tf_op jit(solution)/shard_map/ppermute | solution.py:208
  86.2 1.3 collective-permute-done.3
  87.5 1.0 fusion.2
  88.4 1.3 broadcast_select_fusion.2
  89.8 5.3 %shard_map.57 = (f32[1,256,1536]{2,1,0:T(8,128)}, f32[1,3,256,4]{3,2,1,0:T(8,128)}) custom-call(bf16[1,256,1536]{2,1,0:T(8,128)(2,1)} %bitcast.36, bf16[2,1,256,1536]{3,2,1,0:T(8,128)(2,1)} %bitcast.30, bf16[2,1,256,1536]{3,2,1,0:T(8,128)(2,1)} %bitcast.31, f32[256,256]{1,0:T(8,128)} %reshape.576.m_ref), custom_call_target="tpu_custom_call" | custom-call | flops 402653184 | bytes 3932160 | tf_op jit(solution)/shard_map/pallas_call | solution.py:65
  95.1 2.4 %convert_element_type.74 = bf16[1,256,1536]{2,1,0:T(8,128)(2,1)} convert(f32[1,256,1536]{2,1,0:T(8,128)} %get-tuple-element.23) | non-fusion elementwise | flops 393216 | bytes 2359296 | tf_op jit(solution)/shard_map/convert_element_type | solution.py:237
  97.4 1.3 collective-permute-start.5
  98.7 4.2 %multiply_reduce_fusion = f32[256,12,128]{2,1,0:T(8,128)S(1)} fusion(bf16[2,2,256,12,128]{4,3,2,0,1:T(8,128)(2,1)} %copy_dynamic-update-slice_fusion, f32[2,256,12]{2,1,0:T(8,128)S(1)} %get-tuple-element.28), kind=kLoop, calls=%fused_computation.2 | loop fusion | flops 1966080 | bytes 3170304 | tf_op jit(solution)/shard_map/reduce_sum | solution.py:138
  102.9 0.7 reduce-precision_convert_fusion
  103.7 0.9 copy.14
  104.6 1.2 copy.15.refs_6_
  105.7 1.3 collective-permute-start.6
  107.0 5.3 %shard_map.56 = (f32[1,256,1536]{2,1,0:T(8,128)}, f32[1,3,256,4]{3,2,1,0:T(8,128)}) custom-call(bf16[1,256,1536]{2,1,0:T(8,128)(2,1)} %bitcast.35, bf16[2,1,256,1536]{3,2,1,0:T(8,128)(2,1)} %bitcast.32, bf16[2,1,256,1536]{3,2,1,0:T(8,128)(2,1)} %bitcast.33, f32[256,256]{1,0:T(8,128)} %reshape.574.m_ref), custom_call_target="tpu_custom_call" | custom-call | flops 402653184 | bytes 3932160 | tf_op jit(solution)/shard_map/pallas_call | solution.py:65
  112.3 13.1 %collective-permute-done.6 = f32[1,3,4,256]{2,3,1,0:T(8,128)S(1)} collective-permute-done((f32[1,3,4,256]{2,3,1,0:T(8,128)S(1)}, f32[1,3,4,256]{2,3,1,0:T(8,128)S(1)}, u32[]{:S(2)}, u32[]{:S(2)}) %collective-permute-start.6) | collective-permute-done | bytes 12320 | tf_op jit(solution)/shard_map/ppermute | solution.py:236
  125.5 0.8 select_bitcast_fusion.refs_5_
  126.3 0.9 copy-done.2
  127.2 5.4 %shard_map.58 = bf16[1,256,1536]{2,1,0:T(8,128)(2,1)} custom-call(f32[1,256,1536]{2,1,0:T(8,128)} %get-tuple-element.17.refs_0_, f32[1,3,256,4]{3,2,1,0:T(8,128)} %get-tuple-element.18.refs_1_, f32[1,256,1536]{2,1,0:T(8,128)} %get-tuple-element.20.refs_2_, f32[1,3,256,4]{3,2,1,0:T(8,128)} %get-tuple-element.21.refs_3_, bf16[1,256,1536]{2,1,0:T(8,128)(2,1)} %copy-done.2, ...), custom_call_target="tpu_custom_call" | custom-call | tf_op jit(solution)/shard_map/pallas_call | solution.py:118
  132.5 1.0 constant_dynamic-slice_fusion
  133.6 0.1 collective-permute-start.8
  133.6 1.7 %collective-permute-done.8 = bf16[1,32,8,768]{3,2,1,0:T(8,128)(2,1)S(1)} collective-permute-done((bf16[1,32,8,768]{3,2,1,0:T(8,128)(2,1)S(1)}, bf16[1,32,8,768]{3,2,1,0:T(8,128)(2,1)S(1)}, u32[]{:S(2)}, u32[]{:S(2)}) %collective-permute-start.8) | collective-permute-done | bytes 393248 | tf_op jit(solution)/shard_map/ppermute | solution.py:25
  135.3 1.9 %fusion.1 = bf16[1,32,8,768]{3,2,1,0:T(8,128)(2,1)} fusion(bf16[1,32,8,768]{3,2,1,0:T(8,128)(2,1)S(1)} %collective-permute-done.8, bf16[1,32,8,1536]{3,2,1,0:T(8,128)(2,1)} %bitcast.39, s32[]{:T(128)S(6)} %select_n.268, pred[]{:T(512)S(6)} %eq.80), kind=kLoop, calls=%fused_computation.12 | loop fusion | flops 1572864 | bytes 1179653 | tf_op jit(solution)/shard_map/convert_element_type | solution.py:326
  (31 shorter events, 0.2 us)
Async XLA Ops:
  0.0 2.1 %copy-start.3 = (bf16[1,1,32,8,1536]{4,3,2,1,0:T(8,128)(2,1)S(1)}, bf16[1,1,32,8,1536]{4,3,2,1,0:T(8,128)(2,1)}, u32[]{:S(2)}) copy-start(bf16[1,1,32,8,1536]{4,3,2,1,0:T(8,128)(2,1)} %param.7) | copy-start | bytes 2359300
  0.0 11.1 %copy-start.4 = (s32[4,15]{1,0:T(4,128)S(1)}, s32[4,15]{1,0:T(4,128)}, u32[]{:S(2)}) copy-start(s32[4,15]{1,0:T(4,128)} %param.8) | copy-start | bytes 724
  3.1 41.2 %collective-permute-start.1 = (bf16[2,1,32,8,1536]{4,3,2,1,0:T(8,128)(2,1)}, bf16[2,1,32,8,1536]{4,3,2,1,0:T(8,128)(2,1)}, u32[]{:S(2)}, u32[]{:S(2)}) collective-permute-start(bf16[2,1,32,8,1536]{4,3,2,1,0:T(8,128)(2,1)} %constant_dynamic-update-slice_fusion), channel_id=1, source_target_pairs={{12,8},{8,4},{4,0},{13,9},{9,5},{5,1},{14,10},{10,6},{6,2},{15,11}... | collective-permute-start | bytes 4718600 | tf_op jit(solution)/shard_map/ppermute | solution.py:192
  4.4 39.9 %collective-permute-start = (bf16[2,1,32,8,1536]{4,3,2,1,0:T(8,128)(2,1)}, bf16[2,1,32,8,1536]{4,3,2,1,0:T(8,128)(2,1)}, u32[]{:S(2)}, u32[]{:S(2)}) collective-permute-start(bf16[2,1,32,8,1536]{4,3,2,1,0:T(8,128)(2,1)} %constant_dynamic-update-slice_fusion), channel_id=1, source_target_pairs={{0,4},{4,8},{8,12},{1,5},{5,9},{9,13},{2,6},{6,10},{10,14},{3,7},{... | collective-permute-start | bytes 4718600 | tf_op jit(solution)/shard_map/ppermute | solution.py:191
  11.1 32.8 %collective-permute-start.4 = (s32[4,15]{1,0:T(4,128)S(1)}, s32[4,15]{1,0:T(4,128)S(1)}, u32[]{:S(2)}, u32[]{:S(2)}) collective-permute-start(s32[4,15]{1,0:T(4,128)S(1)} %copy-done.4), channel_id=1, source_target_pairs={{0,4},{12,8},{1,5},{13,9},{2,6},{14,10},{3,7},{15,11},{16,20},{28,... | collective-permute-start | bytes 728 | tf_op jit(solution)/shard_map/ppermute | solution.py:193
  18.4 56.7 %collective-permute-start.7 = (bf16[2,1,256,12,128]{4,2,3,1,0:T(8,128)(2,1)}, bf16[2,1,256,12,128]{4,2,3,1,0:T(8,128)(2,1)}, u32[]{:S(2)}, u32[]{:S(2)}) collective-permute-start(bf16[2,1,256,12,128]{4,2,3,1,0:T(8,128)(2,1)} %copy.12), channel_id=1, source_target_pairs={{0,2},{2,0},{1,3},{3,1},{4,6},{6,4},{5,7},{7,5},{8,10},{10,8},{9,1... | collective-permute-start | bytes 4718600 | tf_op jit(solution)/shard_map/ppermute | solution.py:21
  30.4 4.8 %copy-start = (bf16[1,1,32,8,1536]{4,3,2,1,0:T(8,128)(2,1)S(1)}, bf16[1,1,32,8,1536]{4,3,2,1,0:T(8,128)(2,1)}, u32[]{:S(2)}) copy-start(bf16[1,1,32,8,1536]{4,3,2,1,0:T(8,128)(2,1)} %param.5) | copy-start | bytes 2359300
  35.2 1.8 %copy-start.5 = (s32[2,8]{1,0:T(2,128)S(1)}, s32[2,8]{1,0:T(2,128)}, u32[]{:S(2)}) copy-start(s32[2,8]{1,0:T(2,128)} %param.9) | copy-start | bytes 196
  47.6 38.6 %collective-permute-start.2 = (bf16[2,1,32,8,1536]{4,3,2,1,0:T(8,128)(2,1)}, bf16[2,1,32,8,1536]{4,3,2,1,0:T(8,128)(2,1)S(1)}, u32[]{:S(2)}, u32[]{:S(2)}) collective-permute-start(bf16[2,1,32,8,1536]{4,3,2,1,0:T(8,128)(2,1)} %get-tuple-element.26), channel_id=1, source_target_pairs={{8,4},{4,0},{12,8},{9,5},{5,1},{13,9},{10,6},{6,2},{14,10},{11,7},... | collective-permute-start | bytes 4718600 | tf_op jit(solution)/shard_map/ppermute | solution.py:208
  48.9 38.6 %collective-permute-start.3 = (bf16[2,1,32,8,1536]{4,3,2,1,0:T(8,128)(2,1)}, bf16[2,1,32,8,1536]{4,3,2,1,0:T(8,128)(2,1)S(1)}, u32[]{:S(2)}, u32[]{:S(2)}) collective-permute-start(bf16[2,1,32,8,1536]{4,3,2,1,0:T(8,128)(2,1)} %get-tuple-element.25), channel_id=1, source_target_pairs={{4,8},{8,12},{0,4},{5,9},{9,13},{1,5},{6,10},{10,14},{2,6},{7,11},... | collective-permute-start | bytes 4718600 | tf_op jit(solution)/shard_map/ppermute | solution.py:211
  75.0 4.0 %copy-start.1 = (f32[256,12,128]{2,1,0:T(8,128)S(1)}, f32[256,12,128]{2,1,0:T(8,128)}, u32[]{:S(2)}) copy-start(f32[256,12,128]{2,1,0:T(8,128)} %reshape.579) | copy-start | bytes 4718596
  97.4 28.8 %collective-permute-start.5 = (bf16[1,256,1536]{2,1,0:T(8,128)(2,1)}, bf16[1,256,1536]{2,1,0:T(8,128)(2,1)S(1)}, u32[]{:S(2)}, u32[]{:S(2)}) collective-permute-start(bf16[1,256,1536]{2,1,0:T(8,128)(2,1)} %convert_element_type.74), channel_id=1, source_target_pairs={{4,0},{8,12},{5,1},{9,13},{6,2},{10,14},{7,3},{11,15},{20,16},{24,... | collective-permute-start | bytes 2359304 | tf_op jit(solution)/shard_map/ppermute | solution.py:236
  103.7 2.1 %copy-start.6 = (f32[1,3,256,4]{3,2,1,0:T(8,128)S(1)}, f32[1,3,256,4]{3,2,1,0:T(8,128)}, u32[]{:S(2)}) copy-start(f32[1,3,256,4]{3,2,1,0:T(8,128)} %get-tuple-element.24) | copy-start | bytes 36868
  105.7 19.7 %collective-permute-start.6 = (f32[1,3,4,256]{2,3,1,0:T(8,128)S(1)}, f32[1,3,4,256]{2,3,1,0:T(8,128)S(1)}, u32[]{:S(2)}, u32[]{:S(2)}) collective-permute-start(f32[1,3,4,256]{2,3,1,0:T(8,128)S(1)} %bitcast.41), channel_id=1, source_target_pairs={{4,0},{8,12},{5,1},{9,13},{6,2},{10,14},{7,3},{11,15},{20,16},{24,... | collective-permute-start | bytes 36872 | tf_op jit(solution)/shard_map/ppermute | solution.py:236
  126.3 0.9 copy-start.2
  133.6 1.8 %collective-permute-start.8 = (bf16[1,32,8,768]{3,2,1,0:T(8,128)(2,1)S(1)}, bf16[1,32,8,768]{3,2,1,0:T(8,128)(2,1)S(1)}, u32[]{:S(2)}, u32[]{:S(2)}) collective-permute-start(bf16[1,32,8,768]{3,2,1,0:T(8,128)(2,1)S(1)} %constant_dynamic-slice_fusion), channel_id=1, source_target_pairs={{0,1},{1,0},{2,3},{3,2},{4,5},{5,4},{6,7},{7,6},{8,9},{9,8},{10,11... | collective-permute-start | bytes 1179656 | tf_op jit(solution)/shard_map/ppermute | solution.py:25

commit v12 on v7

--- a/solution.py
+++ b/solution.py
@@ -52,11 +52,11 @@
         result = jnp.dot(
             weights.astype(jnp.bfloat16), v_ref[:, lanes], preferred_element_type=jnp.float32
         )
-        o_ref[:, lanes] = result / totals
+        o_ref[:, lanes] = (result / totals).astype(o_ref.dtype)
         lse_ref[:, head : head + 1] = maxima + jnp.log(totals)
 
 
-def spatial_attention(query_flat, key_value_flat, mask, scale):
+def spatial_attention(query_flat, key_value_flat, mask, scale, out_dtype=jnp.float32):
     frames, query_count, model_width = query_flat.shape
     key_count = key_value_flat.shape[2]
     head_count = model_width // DH
@@ -76,7 +76,7 @@
             pl.BlockSpec((None, None, query_count, width // DH), lambda f, g: (f, g, 0, 0)),
         ],
         out_shape=[
-            jax.ShapeDtypeStruct((frames, query_count, model_width), jnp.float32),
+            jax.ShapeDtypeStruct((frames, query_count, model_width), out_dtype),
             jax.ShapeDtypeStruct((frames, groups, query_count, width // DH), jnp.float32),
         ],
         cost_estimate=pl.CostEstimate(
@@ -229,10 +229,11 @@
         far_keys,
         expand_mask(guest_active, lat_rows),
         scale,
+        jnp.bfloat16,
     )
     lse_shape = guest_lse.shape
     returned, returned_lse = lax.ppermute(
-        (guest_out.astype(jnp.bfloat16), jnp.swapaxes(guest_lse, 2, 3)),
+        (guest_out, jnp.swapaxes(guest_lse, 2, 3)),
         "lon",
         [(1, 0), (2, 3)],
     )

time: 133 us -> 131 us (0.985)
  other arithmetic: 19.5 us -> 18 us
    convert_element_type x1 -> x0, other arithmetic: 1.49 us -> none  [spatial_line_of_four(): guest_out.astype(jnp.bfloat16)]
    unnamed x14 -> x16, local copies, waits for them, and re-layouts: 4.79 us -> 4.8 us
  transfers between devices with their start and end apart: 10 -> 10, of which waited for: 3 -> 3; matrix products, arithmetic and copies ran while one was open for 40% -> 40% of each run, Pallas kernels for 10% -> 11%
where the time goes in v12:
time: 131 us
  local copies, waits for them, and re-layouts  41.6 us (32%)
  starting transfers between devices  27.3 us (21%)
  Pallas kernels  24.2 us (18%)
  waiting for transfers between devices  19.3 us (15%)
  other arithmetic  18 us (14%)
    pallas_call x3, Pallas kernels, spatial_attention(): pl.pallas_call(functools.partial(spatial_kernel, scale=scale), grid=(fram...  18.8 us
    reshape x3, local copies, waits for them, and re-layouts, expand_mask(): return jnp.broadcast_to(active[None, :, None, :].astype(jnp.float32), (la...  14.1 us
    ppermute x2, waiting for transfers between devices, spatial_line_of_four(): lax.ppermute((guest_out, jnp.swapaxes(guest_lse, 2, 3)), 'lon', [(1, 0),...  13.2 us
    ppermute x1, starting transfers between devices, spatial_line_of_four(): guest_q = lax.ppermute(held_q, 'lon', [(0, 1), (3, 2)])  9.24 us
    broadcast_in_dim x3, local copies, waits for them, and re-layouts, expand_mask(): jnp.broadcast_to(active[None, :, None, :].astype(jnp.float32), (lat_rows,...  7.38 us
    ppermute x1, starting transfers between devices, spatial_line_of_four(): from_left = lax.ppermute(key_value, 'lon', [(0, 1), (1, 2), (2, 3)])  6.77 us
    pallas_call x1, Pallas kernels, combine_partials(): pl.pallas_call(combine_kernel, grid=(frames, groups), in_specs=[big, smal...  5.36 us
    unnamed x16, local copies, waits for them, and re-layouts  4.8 us
  transfers between devices with their start and end apart: 10, of which 3 were waited for; matrix products, arithmetic and copies ran while one was open for 40% of the time, Pallas kernels for 11%

profile of v12, /device:TPU:0, one launch (start us, length us, event | category | flops | bytes accessed | tf_op | source)
XLA Modules:
  0.0 130.6 jit_solution(17926003071899575974)
XLA Ops:
  0.0 2.1 %constant_dynamic-update-slice_fusion.1 = bf16[2,1,32,8,1536]{4,3,2,1,0:T(8,128)(2,1)} fusion(bf16[1,1,32,8,1536]{4,3,2,1,0:T(8,128)(2,1)} %param.6), kind=kLoop, calls=%fused_computation.27 | loop fusion | bytes 1572864
  2.1 1.0 constant_dynamic-update-slice_fusion
  3.1 1.3 collective-permute-start.1
  4.4 6.8 %collective-permute-start = (bf16[2,1,32,8,1536]{4,3,2,1,0:T(8,128)(2,1)}, bf16[2,1,32,8,1536]{4,3,2,1,0:T(8,128)(2,1)}, u32[]{:S(2)}, u32[]{:S(2)}) collective-permute-start(bf16[2,1,32,8,1536]{4,3,2,1,0:T(8,128)(2,1)} %constant_dynamic-update-slice_fusion), channel_id=1, source_target_pairs={{0,4},{4,8},{8,12},{1,5},{5,9},{9,13},{2,6},{6,10},{10,14},{3,7},{... | collective-permute-start | bytes 4718600 | tf_op jit(solution)/shard_map/ppermute | solution.py:191
  11.2 2.7 %collective-permute-start.5 = (s32[4,15]{1,0:T(4,128)S(1)}, s32[4,15]{1,0:T(4,128)S(1)}, u32[]{:S(2)}, u32[]{:S(2)}) collective-permute-start(s32[4,15]{1,0:T(4,128)S(1)} %copy-done.4), channel_id=1, source_target_pairs={{0,4},{12,8},{1,5},{13,9},{2,6},{14,10},{3,7},{15,11},{16,20},{28,... | collective-permute-start | bytes 728 | tf_op jit(solution)/shard_map/ppermute | solution.py:193
  13.9 2.9 %reshape.555 = bf16[2,1,256,12,128]{4,3,2,0,1:T(8,128)(2,1)S(1)} reshape(bf16[2,1,32,8,1536]{4,3,2,1,0:T(8,128)(2,1)} %constant_dynamic-update-slice_fusion) | data formatting | bytes 3145728 | tf_op jit(solution)/shard_map/reshape | solution.py:298
  16.8 1.6 %copy.12 = bf16[2,1,256,12,128]{4,2,3,1,0:T(8,128)(2,1)} copy(bf16[2,1,256,12,128]{4,3,2,0,1:T(8,128)(2,1)S(1)} %reshape.555) | data formatting | bytes 3145728 | tf_op jit(solution)/shard_map/reshape | solution.py:298
  18.4 1.5 %collective-permute-start.8 = (bf16[2,1,256,12,128]{4,2,3,1,0:T(8,128)(2,1)}, bf16[2,1,256,12,128]{4,2,3,1,0:T(8,128)(2,1)}, u32[]{:S(2)}, u32[]{:S(2)}) collective-permute-start(bf16[2,1,256,12,128]{4,2,3,1,0:T(8,128)(2,1)} %copy.12), channel_id=1, source_target_pairs={{0,2},{2,0},{1,3},{3,1},{4,6},{6,4},{5,7},{7,5},{8,10},{10,8},{9,1... | collective-permute-start | bytes 4718600 | tf_op jit(solution)/shard_map/ppermute | solution.py:21
  20.0 0.1 copy.11
  20.1 0.1 pad_add_fusion
  20.1 0.1 broadcast_in_dim.35
  20.2 0.1 and.236
  20.3 0.1 add_select_fusion.2
  20.4 0.1 fusion.6
  20.5 2.5 %broadcast_in_dim.36 = f32[32,8,32,24]{3,2,1,0:T(8,128)} broadcast(f32[8,24]{1,0:T(8,128)S(1)} %and_convert_fusion.1), dimensions={1,3} | broadcast | bytes 787200 | tf_op jit(solution)/shard_map/broadcast_in_dim | solution.py:169
  22.9 4.6 %reshape.550.m_ref = f32[256,768]{1,0:T(8,128)} reshape(f32[32,8,32,24]{3,2,1,0:T(8,128)} %broadcast_in_dim.36) | data formatting | bytes 1572864 | tf_op jit(solution)/shard_map/reshape | solution.py:171
  27.6 0.1 add_select_fusion
  27.7 0.3 fusion.8
  28.0 2.5 %broadcast_in_dim.37 = f32[32,8,32,8]{3,2,1,0:T(8,128)} broadcast(f32[8,8]{1,0:T(8,128)S(1)} %convert_element_type.69), dimensions={1,3} | broadcast | bytes 262400 | tf_op jit(solution)/shard_map/broadcast_in_dim | solution.py:169
  30.5 4.8 %reshape.552.m_ref = f32[256,256]{1,0:T(8,128)} reshape(f32[32,8,32,8]{3,2,1,0:T(8,128)} %broadcast_in_dim.37) | data formatting | bytes 524288 | tf_op jit(solution)/shard_map/reshape | solution.py:171
  35.2 1.8 %reshape.557 = f32[256,12,128]{2,1,0:T(8,128)} reshape(bf16[1,1,32,8,1536]{4,3,2,1,0:T(8,128)(2,1)S(1)} %copy-done.1) | data formatting | bytes 2359296 | tf_op jit(solution)/shard_map/convert_element_type | solution.py:128
  37.1 0.1 tile.10
  37.2 0.6 gather_fusion
  37.8 1.7 %constant_dynamic-update-slice_fusion.2 = bf16[2,2,256,12,128]{4,3,2,0,1:T(8,128)(2,1)} fusion(bf16[2,1,256,12,128]{4,3,2,0,1:T(8,128)(2,1)S(1)} %reshape.555), kind=kLoop, calls=%fused_computation.28 | loop fusion | bytes 3670016
  39.5 0.1 compare_or_fusion
  39.6 4.3 %collective-permute-done.5 = s32[4,15]{1,0:T(4,128)S(1)} collective-permute-done((s32[4,15]{1,0:T(4,128)S(1)}, s32[4,15]{1,0:T(4,128)S(1)}, u32[]{:S(2)}, u32[]{:S(2)}) %collective-permute-start.5) | collective-permute-done | bytes 272 | tf_op jit(solution)/shard_map/ppermute | solution.py:193
  44.0 0.3 fusion.10
  44.3 0.0 collective-permute-done.1
  44.3 1.3 collective-permute-start.2
  45.6 0.0 collective-permute-done
  45.6 1.8 %collective-permute-start.3 = (bf16[2,1,32,8,1536]{4,3,2,1,0:T(8,128)(2,1)}, bf16[2,1,32,8,1536]{4,3,2,1,0:T(8,128)(2,1)}, u32[]{:S(2)}, u32[]{:S(2)}) collective-permute-start(bf16[2,1,32,8,1536]{4,3,2,1,0:T(8,128)(2,1)} %collective-permute-done), channel_id=1, source_target_pairs={{4,8},{8,12},{5,9},{9,13},{6,10},{10,14},{7,11},{11,15},{20,24},{2... | collective-permute-start | bytes 4718600 | tf_op jit(solution)/shard_map/ppermute | solution.py:210
  47.4 2.5 %broadcast_in_dim.39 = f32[32,8,32,8]{3,2,1,0:T(8,128)} broadcast(f32[8,8]{1,0:T(8,128)S(1)} %and_convert_fusion), dimensions={1,3} | broadcast | bytes 262400 | tf_op jit(solution)/shard_map/broadcast_in_dim | solution.py:169
  49.9 4.7 %reshape.554.m_ref = f32[256,256]{1,0:T(8,128)} reshape(f32[32,8,32,8]{3,2,1,0:T(8,128)} %broadcast_in_dim.39) | data formatting | bytes 524288 | tf_op jit(solution)/shard_map/reshape | solution.py:171
  54.6 9.2 %collective-permute-start.4 = (bf16[1,32,8,1536]{3,2,1,0:T(8,128)(2,1)S(1)}, bf16[1,32,8,1536]{3,2,1,0:T(8,128)(2,1)}, u32[]{:S(2)}, u32[]{:S(2)}) collective-permute-start(bf16[1,32,8,1536]{3,2,1,0:T(8,128)(2,1)S(1)} %bitcast.35), channel_id=1, source_target_pairs={{0,4},{12,8},{1,5},{13,9},{2,6},{14,10},{3,7},{15,11},{16,20},{28,... | collective-permute-start | bytes 2359304 | tf_op jit(solution)/shard_map/ppermute | solution.py:213
  63.8 4.8 %pad_maximum_fusion = bf16[2,1,32,24,1536]{4,3,2,1,0:T(8,128)(2,1)} fusion(bf16[2,1,32,8,1536]{4,3,2,1,0:T(8,128)(2,1)} %collective-permute-done.1, bf16[2,1,32,8,1536]{4,3,2,1,0:T(8,128)(2,1)} %constant_dynamic-update-slice_fusion, bf16[2,1,32,8,1536]{4,3,2,1,0:T(8,128)(2,1)} %collective-permute-done), kind=kLoop, calls=%fused_computation.1 | loop fusion | flops 14155776 | bytes 9437184 | tf_op jit(solution)/shard_map/concatenate | solution.py:175
  68.6 8.5 %shard_map.55 = (f32[1,256,1536]{2,1,0:T(8,128)}, f32[1,3,256,4]{3,2,1,0:T(8,128)}) custom-call(bf16[1,256,1536]{2,1,0:T(8,128)(2,1)} %bitcast.33, bf16[2,1,768,1536]{3,2,1,0:T(8,128)(2,1)} %bitcast.27, bf16[2,1,768,1536]{3,2,1,0:T(8,128)(2,1)} %bitcast.28, f32[256,768]{1,0:T(8,128)} %reshape.550.m_ref), custom_call_target="tpu_custom_call" | custom-call | flops 1207959552 | bytes 7077888 | tf_op jit(solution)/shard_map/pallas_call | solution.py:65
  77.0 0.0 collective-permute-done.8
  77.1 4.0 %copy_dynamic-update-slice_fusion = bf16[2,2,256,12,128]{4,3,2,0,1:T(8,128)(2,1)} fusion(bf16[2,2,256,12,128]{4,3,2,0,1:T(8,128)(2,1)} %constant_dynamic-update-slice_fusion.2, bf16[2,1,256,12,128]{4,2,3,1,0:T(8,128)(2,1)} %collective-permute-done.8), kind=kLoop, calls=%fused_computation.4 | loop fusion | bytes 3670016 | tf_op jit(solution)/shard_map/concatenate | solution.py:302
  81.1 2.8 %multiply_reduce_fusion.1 = f32[2,256,12]{2,1,0:T(8,128)S(1)} fusion(bf16[2,2,256,12,128]{4,3,2,0,1:T(8,128)(2,1)} %copy_dynamic-update-slice_fusion, f32[256,12,128]{2,1,0:T(8,128)S(1)} %copy-done), kind=kLoop, calls=%fused_computation.3 | loop fusion | flops 2353152 | bytes 3170304 | tf_op jit(solution)/shard_map/reduce_sum | solution.py:130
  83.9 0.1 fusion.2
  84.1 0.1 fusion.3
  84.2 0.0 collective-permute-done.2
  84.2 0.0 collective-permute-done.3
  84.2 1.3 %broadcast_select_fusion = bf16[2,1,32,8,1536]{4,3,2,1,0:T(8,128)(2,1)} fusion(bf16[2,1,32,8,1536]{4,3,2,1,0:T(8,128)(2,1)S(1)} %collective-permute-done.2, bf16[2,1,32,8,1536]{4,3,2,1,0:T(8,128)(2,1)} %collective-permute-done.3, pred[]{:T(512)S(6)} %le.15), kind=kLoop, calls=%fused_computation.6 | loop fusion | flops 786432 | bytes 4718593 | tf_op jit(solution)/shard_map/jit(_where)/select_n | solution.py:207
  85.5 0.0 collective-permute-done.4
  85.5 5.1 %shard_map.57 = (bf16[1,256,1536]{2,1,0:T(8,128)(2,1)}, f32[1,3,256,4]{3,2,1,0:T(8,128)}) custom-call(bf16[1,256,1536]{2,1,0:T(8,128)(2,1)} %bitcast.7.q_ref, bf16[2,1,256,1536]{3,2,1,0:T(8,128)(2,1)} %bitcast.29, bf16[2,1,256,1536]{3,2,1,0:T(8,128)(2,1)} %bitcast.30, f32[256,256]{1,0:T(8,128)} %reshape.554.m_ref), custom_call_target="tpu_custom_call" | custom-call | flops 402653184 | bytes 3932160 | tf_op jit(solution)/shard_map/pallas_call | solution.py:65
  90.6 1.3 collective-permute-start.6
  91.9 4.2 %multiply_reduce_fusion = f32[256,12,128]{2,1,0:T(8,128)S(1)} fusion(bf16[2,2,256,12,128]{4,3,2,0,1:T(8,128)(2,1)} %copy_dynamic-update-slice_fusion, f32[2,256,12]{2,1,0:T(8,128)S(1)} %get-tuple-element.28), kind=kLoop, calls=%fused_computation.2 | loop fusion | flops 1966080 | bytes 3170304 | tf_op jit(solution)/shard_map/reduce_sum | solution.py:138
  96.1 0.7 reduce-precision_convert_fusion
  96.9 0.0 copy-start.6
  96.9 0.9 copy.14
  97.8 1.2 copy.15.refs_6_
  98.9 0.0 copy-done.6
  98.9 1.3 collective-permute-start.7
  100.2 5.3 %shard_map.56 = (f32[1,256,1536]{2,1,0:T(8,128)}, f32[1,3,256,4]{3,2,1,0:T(8,128)}) custom-call(bf16[1,256,1536]{2,1,0:T(8,128)(2,1)} %bitcast.34, bf16[2,1,256,1536]{3,2,1,0:T(8,128)(2,1)} %bitcast.31, bf16[2,1,256,1536]{3,2,1,0:T(8,128)(2,1)} %bitcast.32, f32[256,256]{1,0:T(8,128)} %reshape.552.m_ref), custom_call_target="tpu_custom_call" | custom-call | flops 402653184 | bytes 3932160 | tf_op jit(solution)/shard_map/pallas_call | solution.py:65
  105.5 13.2 %collective-permute-done.7 = f32[1,3,4,256]{2,3,1,0:T(8,128)S(1)} collective-permute-done((f32[1,3,4,256]{2,3,1,0:T(8,128)S(1)}, f32[1,3,4,256]{2,3,1,0:T(8,128)S(1)}, u32[]{:S(2)}, u32[]{:S(2)}) %collective-permute-start.7) | collective-permute-done | bytes 12320 | tf_op jit(solution)/shard_map/ppermute | solution.py:235
  118.8 0.8 select_bitcast_fusion.refs_5_
  119.5 0.0 collective-permute-done.6.refs_4_
  119.6 0.9 copy-done.2
  120.5 5.4 %shard_map.58 = bf16[1,256,1536]{2,1,0:T(8,128)(2,1)} custom-call(f32[1,256,1536]{2,1,0:T(8,128)} %get-tuple-element.19.refs_0_, f32[1,3,256,4]{3,2,1,0:T(8,128)} %get-tuple-element.20.refs_1_, f32[1,256,1536]{2,1,0:T(8,128)} %get-tuple-element.22.refs_2_, f32[1,3,256,4]{3,2,1,0:T(8,128)} %get-tuple-element.23.refs_3_, bf16[1,256,1536]{2,1,0:T(8,128)(2,1)} %copy-done.2, ...), custom_call_target="tpu_custom_call" | custom-call | tf_op jit(solution)/shard_map/pallas_call | solution.py:118
  125.8 1.0 constant_dynamic-slice_fusion
  126.8 0.1 collective-permute-start.9
  126.9 1.7 %collective-permute-done.9 = bf16[1,32,8,768]{3,2,1,0:T(8,128)(2,1)S(1)} collective-permute-done((bf16[1,32,8,768]{3,2,1,0:T(8,128)(2,1)S(1)}, bf16[1,32,8,768]{3,2,1,0:T(8,128)(2,1)S(1)}, u32[]{:S(2)}, u32[]{:S(2)}) %collective-permute-start.9) | collective-permute-done | bytes 393248 | tf_op jit(solution)/shard_map/ppermute | solution.py:25
  128.6 1.9 %fusion.1 = bf16[1,32,8,768]{3,2,1,0:T(8,128)(2,1)} fusion(bf16[1,32,8,768]{3,2,1,0:T(8,128)(2,1)S(1)} %collective-permute-done.9, bf16[1,32,8,1536]{3,2,1,0:T(8,128)(2,1)} %bitcast.38, s32[]{:T(128)S(6)} %select_n.230, pred[]{:T(512)S(6)} %eq.73), kind=kLoop, calls=%fused_computation.10 | loop fusion | flops 1572864 | bytes 1179653 | tf_op jit(solution)/shard_map/convert_element_type | solution.py:325
  (28 shorter events, 0.2 us)
Async XLA Ops:
  0.0 2.1 %copy-start.3 = (bf16[1,1,32,8,1536]{4,3,2,1,0:T(8,128)(2,1)S(1)}, bf16[1,1,32,8,1536]{4,3,2,1,0:T(8,128)(2,1)}, u32[]{:S(2)}) copy-start(bf16[1,1,32,8,1536]{4,3,2,1,0:T(8,128)(2,1)} %param.7) | copy-start | bytes 2359300
  0.0 11.2 %copy-start.4 = (s32[4,15]{1,0:T(4,128)S(1)}, s32[4,15]{1,0:T(4,128)}, u32[]{:S(2)}) copy-start(s32[4,15]{1,0:T(4,128)} %param.8) | copy-start | bytes 724
  3.1 41.2 %collective-permute-start.1 = (bf16[2,1,32,8,1536]{4,3,2,1,0:T(8,128)(2,1)}, bf16[2,1,32,8,1536]{4,3,2,1,0:T(8,128)(2,1)}, u32[]{:S(2)}, u32[]{:S(2)}) collective-permute-start(bf16[2,1,32,8,1536]{4,3,2,1,0:T(8,128)(2,1)} %constant_dynamic-update-slice_fusion), channel_id=1, source_target_pairs={{12,8},{8,4},{4,0},{13,9},{9,5},{5,1},{14,10},{10,6},{6,2},{15,11}... | collective-permute-start | bytes 4718600 | tf_op jit(solution)/shard_map/ppermute | solution.py:192
  4.4 41.2 %collective-permute-start = (bf16[2,1,32,8,1536]{4,3,2,1,0:T(8,128)(2,1)}, bf16[2,1,32,8,1536]{4,3,2,1,0:T(8,128)(2,1)}, u32[]{:S(2)}, u32[]{:S(2)}) collective-permute-start(bf16[2,1,32,8,1536]{4,3,2,1,0:T(8,128)(2,1)} %constant_dynamic-update-slice_fusion), channel_id=1, source_target_pairs={{0,4},{4,8},{8,12},{1,5},{5,9},{9,13},{2,6},{6,10},{10,14},{3,7},{... | collective-permute-start | bytes 4718600 | tf_op jit(solution)/shard_map/ppermute | solution.py:191
  11.2 32.8 %collective-permute-start.5 = (s32[4,15]{1,0:T(4,128)S(1)}, s32[4,15]{1,0:T(4,128)S(1)}, u32[]{:S(2)}, u32[]{:S(2)}) collective-permute-start(s32[4,15]{1,0:T(4,128)S(1)} %copy-done.4), channel_id=1, source_target_pairs={{0,4},{12,8},{1,5},{13,9},{2,6},{14,10},{3,7},{15,11},{16,20},{28,... | collective-permute-start | bytes 728 | tf_op jit(solution)/shard_map/ppermute | solution.py:193
  18.4 58.7 %collective-permute-start.8 = (bf16[2,1,256,12,128]{4,2,3,1,0:T(8,128)(2,1)}, bf16[2,1,256,12,128]{4,2,3,1,0:T(8,128)(2,1)}, u32[]{:S(2)}, u32[]{:S(2)}) collective-permute-start(bf16[2,1,256,12,128]{4,2,3,1,0:T(8,128)(2,1)} %copy.12), channel_id=1, source_target_pairs={{0,2},{2,0},{1,3},{3,1},{4,6},{6,4},{5,7},{7,5},{8,10},{10,8},{9,1... | collective-permute-start | bytes 4718600 | tf_op jit(solution)/shard_map/ppermute | solution.py:21
  30.4 4.8 %copy-start.1 = (bf16[1,1,32,8,1536]{4,3,2,1,0:T(8,128)(2,1)S(1)}, bf16[1,1,32,8,1536]{4,3,2,1,0:T(8,128)(2,1)}, u32[]{:S(2)}) copy-start(bf16[1,1,32,8,1536]{4,3,2,1,0:T(8,128)(2,1)} %param.5) | copy-start | bytes 2359300
  35.2 1.8 %copy-start.5 = (s32[2,8]{1,0:T(2,128)S(1)}, s32[2,8]{1,0:T(2,128)}, u32[]{:S(2)}) copy-start(s32[2,8]{1,0:T(2,128)} %param.9) | copy-start | bytes 196
  44.3 39.9 %collective-permute-start.2 = (bf16[2,1,32,8,1536]{4,3,2,1,0:T(8,128)(2,1)}, bf16[2,1,32,8,1536]{4,3,2,1,0:T(8,128)(2,1)S(1)}, u32[]{:S(2)}, u32[]{:S(2)}) collective-permute-start(bf16[2,1,32,8,1536]{4,3,2,1,0:T(8,128)(2,1)} %collective-permute-done.1), channel_id=1, source_target_pairs={{8,4},{4,0},{9,5},{5,1},{10,6},{6,2},{11,7},{7,3},{24,20},{20,16},... | collective-permute-start | bytes 4718600 | tf_op jit(solution)/shard_map/ppermute | solution.py:209
  45.6 38.6 %collective-permute-start.3 = (bf16[2,1,32,8,1536]{4,3,2,1,0:T(8,128)(2,1)}, bf16[2,1,32,8,1536]{4,3,2,1,0:T(8,128)(2,1)}, u32[]{:S(2)}, u32[]{:S(2)}) collective-permute-start(bf16[2,1,32,8,1536]{4,3,2,1,0:T(8,128)(2,1)} %collective-permute-done), channel_id=1, source_target_pairs={{4,8},{8,12},{5,9},{9,13},{6,10},{10,14},{7,11},{11,15},{20,24},{2... | collective-permute-start | bytes 4718600 | tf_op jit(solution)/shard_map/ppermute | solution.py:210
  54.6 31.0 %collective-permute-start.4 = (bf16[1,32,8,1536]{3,2,1,0:T(8,128)(2,1)S(1)}, bf16[1,32,8,1536]{3,2,1,0:T(8,128)(2,1)}, u32[]{:S(2)}, u32[]{:S(2)}) collective-permute-start(bf16[1,32,8,1536]{3,2,1,0:T(8,128)(2,1)S(1)} %bitcast.35), channel_id=1, source_target_pairs={{0,4},{12,8},{1,5},{13,9},{2,6},{14,10},{3,7},{15,11},{16,20},{28,... | collective-permute-start | bytes 2359304 | tf_op jit(solution)/shard_map/ppermute | solution.py:213
  77.0 4.0 %copy-start = (f32[256,12,128]{2,1,0:T(8,128)S(1)}, f32[256,12,128]{2,1,0:T(8,128)}, u32[]{:S(2)}) copy-start(f32[256,12,128]{2,1,0:T(8,128)} %reshape.557) | copy-start | bytes 4718596
  90.6 28.9 %collective-permute-start.6 = (bf16[1,256,1536]{2,1,0:T(8,128)(2,1)}, bf16[1,256,1536]{2,1,0:T(8,128)(2,1)S(1)}, u32[]{:S(2)}, u32[]{:S(2)}) collective-permute-start(bf16[1,256,1536]{2,1,0:T(8,128)(2,1)} %get-tuple-element.25), channel_id=1, source_target_pairs={{4,0},{8,12},{5,1},{9,13},{6,2},{10,14},{7,3},{11,15},{20,16},{24,... | collective-permute-start | bytes 2359304 | tf_op jit(solution)/shard_map/ppermute | solution.py:235
  96.9 2.1 %copy-start.6 = (f32[1,3,256,4]{3,2,1,0:T(8,128)S(1)}, f32[1,3,256,4]{3,2,1,0:T(8,128)}, u32[]{:S(2)}) copy-start(f32[1,3,256,4]{3,2,1,0:T(8,128)} %get-tuple-element.26) | copy-start | bytes 36868
  98.9 19.8 %collective-permute-start.7 = (f32[1,3,4,256]{2,3,1,0:T(8,128)S(1)}, f32[1,3,4,256]{2,3,1,0:T(8,128)S(1)}, u32[]{:S(2)}, u32[]{:S(2)}) collective-permute-start(f32[1,3,4,256]{2,3,1,0:T(8,128)S(1)} %bitcast.40), channel_id=1, source_target_pairs={{4,0},{8,12},{5,1},{9,13},{6,2},{10,14},{7,3},{11,15},{20,16},{24,... | collective-permute-start | bytes 36872 | tf_op jit(solution)/shard_map/ppermute | solution.py:235
  119.5 0.9 copy-start.2
  126.8 1.8 %collective-permute-start.9 = (bf16[1,32,8,768]{3,2,1,0:T(8,128)(2,1)S(1)}, bf16[1,32,8,768]{3,2,1,0:T(8,128)(2,1)S(1)}, u32[]{:S(2)}, u32[]{:S(2)}) collective-permute-start(bf16[1,32,8,768]{3,2,1,0:T(8,128)(2,1)S(1)} %constant_dynamic-slice_fusion), channel_id=1, source_target_pairs={{0,1},{1,0},{2,3},{3,2},{4,5},{5,4},{6,7},{7,6},{8,9},{9,8},{10,11... | collective-permute-start | bytes 1179656 | tf_op jit(solution)/shard_map/ppermute | solution.py:25

commit v13 on v12

--- a/solution.py
+++ b/solution.py
@@ -224,12 +224,20 @@
         lat_rows,
     ) & is_middle
     far_keys = flat_keys([two_away])
-    guest_out, guest_lse = spatial_attention(
+    def attend_guest(operands):
+        return tuple(spatial_attention(*operands, scale, jnp.bfloat16))
+
+    guest_operands = (
         guest_q.reshape(frames, lat_rows * columns, model_width),
         far_keys,
         expand_mask(guest_active, lat_rows),
-        scale,
-        jnp.bfloat16,
+    )
+    shapes = jax.eval_shape(attend_guest, guest_operands)
+    guest_out, guest_lse = lax.cond(
+        is_middle,
+        attend_guest,
+        lambda operands: tuple(jnp.zeros(shape.shape, shape.dtype) for shape in shapes),
+        guest_operands,
     )
     lse_shape = guest_lse.shape
     returned, returned_lse = lax.ppermute(

time: 131 us -> 141 us (1.076)
  waiting for transfers between devices: 19.3 us -> 41.9 us
  local copies, waits for them, and re-layouts: 41.6 us -> 33.7 us
  Pallas kernels: 24.2 us -> 18.6 us
    ppermute x1, waiting for transfers between devices: 0.01 us -> 19.5 us  [spatial_line_of_four(): from_right = lax.ppermute(key_value, 'lon', [(3, 2), (2, 1), (1, 0)])]
    ppermute x2, waiting for transfers between devices: 13.2 us -> 20.7 us  [spatial_line_of_four(): lax.ppermute((guest_out, jnp.swapaxes(guest_lse, 2, 3)), 'lon', [(1, 0),...]
    pallas_call x3 -> x2, Pallas kernels: 18.8 us -> 13.2 us  [spatial_attention(): pl.pallas_call(functools.partial(spatial_kernel, scale=scale), grid=(fram...]
    reshape x3 -> x2, local copies, waits for them, and re-layouts: 14.1 us -> 9.41 us  [expand_mask(): return jnp.broadcast_to(active[None, :, None, :].astype(jnp.float32), (la...]
    ppermute x1, waiting for transfers between devices: 4.32 us -> 0.01 us  [spatial_line_of_four(): guest_map = lax.ppermute(window_map, 'lon', [(0, 1), (3, 2)])]
    broadcast_in_dim x3 -> x2, local copies, waits for them, and re-layouts: 7.38 us -> 4.9 us  [expand_mask(): jnp.broadcast_to(active[None, :, None, :].astype(jnp.float32), (lat_rows,...]
    another operation x0 -> x3, local copies, waits for them, and re-layouts: none -> 1.7 us
    unnamed x16 -> x10, local copies, waits for them, and re-layouts: 4.8 us -> 3.93 us
  transfers between devices with their start and end apart: 10 -> 10, of which waited for: 3 -> 3; matrix products, arithmetic and copies ran while one was open for 40% -> 31% of each run, Pallas kernels for 11% -> 9%
where the time goes in v13:
time: 141 us; the launch traced here: 140 us
  waiting for transfers between devices  41.9 us (30%)
  local copies, waits for them, and re-layouts  33.7 us (24%)
  starting transfers between devices  27.6 us (20%)
  Pallas kernels  18.6 us (13%)
  other arithmetic  18 us (13%)
    ppermute x2, waiting for transfers between devices, spatial_line_of_four(): lax.ppermute((guest_out, jnp.swapaxes(guest_lse, 2, 3)), 'lon', [(1, 0),...  20.7 us
    ppermute x1, waiting for transfers between devices, spatial_line_of_four(): from_right = lax.ppermute(key_value, 'lon', [(3, 2), (2, 1), (1, 0)])  19.5 us
    pallas_call x2, Pallas kernels, spatial_attention(): pl.pallas_call(functools.partial(spatial_kernel, scale=scale), grid=(fram...  13.2 us
    ppermute x1, starting transfers between devices, spatial_line_of_four(): guest_q = lax.ppermute(held_q, 'lon', [(0, 1), (3, 2)])  9.55 us
    reshape x2, local copies, waits for them, and re-layouts, expand_mask(): return jnp.broadcast_to(active[None, :, None, :].astype(jnp.float32), (la...  9.41 us
    ppermute x1, starting transfers between devices, spatial_line_of_four(): from_left = lax.ppermute(key_value, 'lon', [(0, 1), (1, 2), (2, 3)])  6.8 us
    pallas_call x1, Pallas kernels, combine_partials(): pl.pallas_call(combine_kernel, grid=(frames, groups), in_specs=[big, smal...  5.37 us
    broadcast_in_dim x2, local copies, waits for them, and re-layouts, expand_mask(): jnp.broadcast_to(active[None, :, None, :].astype(jnp.float32), (lat_rows,...  4.9 us
  transfers between devices with their start and end apart: 10, of which 3 were waited for; matrix products, arithmetic and copies ran while one was open for 31% of the time, Pallas kernels for 9%

profile of v13, /device:TPU:0, one launch (start us, length us, event | category | flops | bytes accessed | tf_op | source)
XLA Modules:
  0.0 140.1 jit_solution(611760549029393106)
XLA Ops:
  0.0 2.2 %constant_dynamic-update-slice_fusion.1 = bf16[2,1,32,8,1536]{4,3,2,1,0:T(8,128)(2,1)} fusion(bf16[1,1,32,8,1536]{4,3,2,1,0:T(8,128)(2,1)} %param.8), kind=kLoop, calls=%fused_computation.30 | loop fusion | bytes 1572864
  2.2 0.9 constant_dynamic-update-slice_fusion
  3.1 1.3 collective-permute-start.1
  4.4 6.8 %collective-permute-start = (bf16[2,1,32,8,1536]{4,3,2,1,0:T(8,128)(2,1)}, bf16[2,1,32,8,1536]{4,3,2,1,0:T(8,128)(2,1)}, u32[]{:S(2)}, u32[]{:S(2)}) collective-permute-start(bf16[2,1,32,8,1536]{4,3,2,1,0:T(8,128)(2,1)} %constant_dynamic-update-slice_fusion), channel_id=1, source_target_pairs={{0,4},{4,8},{8,12},{1,5},{5,9},{9,13},{2,6},{6,10},{10,14},{3,7},{... | collective-permute-start | bytes 4718600 | tf_op jit(solution)/shard_map/ppermute | solution.py:191
  11.2 0.0 copy-done.2
  11.2 2.7 %collective-permute-start.5 = (s32[4,15]{1,0:T(4,128)S(1)}, s32[4,15]{1,0:T(4,128)S(1)}, u32[]{:S(2)}, u32[]{:S(2)}) collective-permute-start(s32[4,15]{1,0:T(4,128)S(1)} %copy-done.2), channel_id=1, source_target_pairs={{0,4},{12,8},{1,5},{13,9},{2,6},{14,10},{3,7},{15,11},{16,20},{28,... | collective-permute-start | bytes 728 | tf_op jit(solution)/shard_map/ppermute | solution.py:193
  13.9 2.9 %reshape.565 = bf16[2,1,256,12,128]{4,3,2,0,1:T(8,128)(2,1)S(1)} reshape(bf16[2,1,32,8,1536]{4,3,2,1,0:T(8,128)(2,1)} %constant_dynamic-update-slice_fusion) | data formatting | bytes 3145728 | tf_op jit(solution)/shard_map/reshape | solution.py:306
  16.8 1.6 %copy.12 = bf16[2,1,256,12,128]{4,2,3,1,0:T(8,128)(2,1)} copy(bf16[2,1,256,12,128]{4,3,2,0,1:T(8,128)(2,1)S(1)} %reshape.565) | data formatting | bytes 3145728 | tf_op jit(solution)/shard_map/reshape | solution.py:306
  18.4 1.5 %collective-permute-start.8 = (bf16[2,1,256,12,128]{4,2,3,1,0:T(8,128)(2,1)}, bf16[2,1,256,12,128]{4,2,3,1,0:T(8,128)(2,1)}, u32[]{:S(2)}, u32[]{:S(2)}) collective-permute-start(bf16[2,1,256,12,128]{4,2,3,1,0:T(8,128)(2,1)} %copy.12), channel_id=1, source_target_pairs={{0,2},{2,0},{1,3},{3,1},{4,6},{6,4},{5,7},{7,5},{8,10},{10,8},{9,1... | collective-permute-start | bytes 4718600 | tf_op jit(solution)/shard_map/ppermute | solution.py:21
  20.0 0.1 copy.11
  20.2 0.1 add_select_fusion.2
  20.2 0.1 fusion.7
  20.3 0.0 copy-start.3
  20.3 1.7 %constant_dynamic-update-slice_fusion.2 = bf16[2,2,256,12,128]{4,3,2,0,1:T(8,128)(2,1)} fusion(bf16[2,1,256,12,128]{4,3,2,0,1:T(8,128)(2,1)S(1)} %reshape.565), kind=kLoop, calls=%fused_computation.31 | loop fusion | bytes 3670016
  22.1 0.1 pad_add_fusion
  22.2 0.1 broadcast_in_dim.39
  22.2 0.1 and.240
  22.3 0.0 copy-done.3
  22.3 0.1 tile.10
  22.4 0.6 gather_fusion
  23.0 0.1 fusion.13
  23.1 0.1 compare_or_fusion
  23.1 0.1 fusion.12
  23.2 19.5 %collective-permute-done.1 = bf16[2,1,32,8,1536]{4,3,2,1,0:T(8,128)(2,1)} collective-permute-done((bf16[2,1,32,8,1536]{4,3,2,1,0:T(8,128)(2,1)}, bf16[2,1,32,8,1536]{4,3,2,1,0:T(8,128)(2,1)}, u32[]{:S(2)}, u32[]{:S(2)}) %collective-permute-start.1) | collective-permute-done | bytes 1572896 | tf_op jit(solution)/shard_map/ppermute | solution.py:192
  42.7 1.3 collective-permute-start.2
  44.0 0.0 collective-permute-done
  44.0 1.8 %collective-permute-start.3 = (bf16[2,1,32,8,1536]{4,3,2,1,0:T(8,128)(2,1)}, bf16[2,1,32,8,1536]{4,3,2,1,0:T(8,128)(2,1)}, u32[]{:S(2)}, u32[]{:S(2)}) collective-permute-start(bf16[2,1,32,8,1536]{4,3,2,1,0:T(8,128)(2,1)} %collective-permute-done), channel_id=1, source_target_pairs={{4,8},{8,12},{5,9},{9,13},{6,10},{10,14},{7,11},{11,15},{20,24},{2... | collective-permute-start | bytes 4718600 | tf_op jit(solution)/shard_map/ppermute | solution.py:210
  45.9 0.3 fusion.9
  46.2 2.4 %broadcast_in_dim.40 = f32[32,8,32,24]{3,2,1,0:T(8,128)} broadcast(f32[8,24]{1,0:T(8,128)S(1)} %and_convert_fusion.1), dimensions={1,3} | broadcast | bytes 787200 | tf_op jit(solution)/shard_map/broadcast_in_dim | solution.py:169
  48.6 4.7 %reshape.562.m_ref = f32[256,768]{1,0:T(8,128)} reshape(f32[32,8,32,24]{3,2,1,0:T(8,128)} %broadcast_in_dim.40) | data formatting | bytes 1572864 | tf_op jit(solution)/shard_map/reshape | solution.py:171
  53.3 2.5 %broadcast_in_dim.41 = f32[32,8,32,8]{3,2,1,0:T(8,128)} broadcast(f32[8,8]{1,0:T(8,128)S(1)} %convert_element_type.78), dimensions={1,3} | broadcast | bytes 262400 | tf_op jit(solution)/shard_map/broadcast_in_dim | solution.py:169
  55.7 4.8 %reshape.564.m_ref = f32[256,256]{1,0:T(8,128)} reshape(f32[32,8,32,8]{3,2,1,0:T(8,128)} %broadcast_in_dim.41) | data formatting | bytes 524288 | tf_op jit(solution)/shard_map/reshape | solution.py:171
  60.5 0.5 reshape.570
  61.0 9.5 %collective-permute-start.4 = (bf16[1,32,8,1536]{3,2,1,0:T(8,128)(2,1)S(1)}, bf16[1,32,8,1536]{3,2,1,0:T(8,128)(2,1)}, u32[]{:S(2)}, u32[]{:S(2)}) collective-permute-start(bf16[1,32,8,1536]{3,2,1,0:T(8,128)(2,1)S(1)} %bitcast.35), channel_id=1, source_target_pairs={{0,4},{12,8},{1,5},{13,9},{2,6},{14,10},{3,7},{15,11},{16,20},{28,... | collective-permute-start | bytes 2359304 | tf_op jit(solution)/shard_map/ppermute | solution.py:213
  70.5 4.8 %pad_maximum_fusion = bf16[2,1,32,24,1536]{4,3,2,1,0:T(8,128)(2,1)} fusion(bf16[2,1,32,8,1536]{4,3,2,1,0:T(8,128)(2,1)} %collective-permute-done.1, bf16[2,1,32,8,1536]{4,3,2,1,0:T(8,128)(2,1)} %constant_dynamic-update-slice_fusion, bf16[2,1,32,8,1536]{4,3,2,1,0:T(8,128)(2,1)} %collective-permute-done), kind=kLoop, calls=%fused_computation.7 | loop fusion | flops 14155776 | bytes 9437184 | tf_op jit(solution)/shard_map/concatenate | solution.py:175
  75.3 8.4 %shard_map.55 = (f32[1,256,1536]{2,1,0:T(8,128)}, f32[1,3,256,4]{3,2,1,0:T(8,128)}) custom-call(bf16[1,256,1536]{2,1,0:T(8,128)(2,1)} %bitcast.33, bf16[2,1,768,1536]{3,2,1,0:T(8,128)(2,1)} %bitcast.28, bf16[2,1,768,1536]{3,2,1,0:T(8,128)(2,1)} %bitcast.29, f32[256,768]{1,0:T(8,128)} %reshape.562.m_ref), custom_call_target="tpu_custom_call" | custom-call | flops 1207959552 | bytes 7077888 | tf_op jit(solution)/shard_map/pallas_call | solution.py:65
  83.7 0.0 collective-permute-done.8
  83.7 3.9 %copy_dynamic-update-slice_fusion = bf16[2,2,256,12,128]{4,3,2,0,1:T(8,128)(2,1)} fusion(bf16[2,2,256,12,128]{4,3,2,0,1:T(8,128)(2,1)} %constant_dynamic-update-slice_fusion.2, bf16[2,1,256,12,128]{4,2,3,1,0:T(8,128)(2,1)} %collective-permute-done.8), kind=kLoop, calls=%fused_computation.10 | loop fusion | bytes 3670016 | tf_op jit(solution)/shard_map/concatenate | solution.py:310
  87.6 2.8 %multiply_reduce_fusion.1 = f32[2,256,12]{2,1,0:T(8,128)S(1)} fusion(bf16[2,2,256,12,128]{4,3,2,0,1:T(8,128)(2,1)} %copy_dynamic-update-slice_fusion, f32[256,12,128]{2,1,0:T(8,128)S(1)} %reshape.570), kind=kLoop, calls=%fused_computation.9 | loop fusion | flops 2353152 | bytes 3170304 | tf_op jit(solution)/shard_map/reduce_sum | solution.py:130
  90.4 0.1 fusion.3
  90.5 0.1 fusion.4
  90.7 0.0 collective-permute-done.2
  90.7 0.0 collective-permute-done.3
  90.7 1.6 %broadcast_select_fusion = bf16[2,1,32,8,1536]{4,3,2,1,0:T(8,128)(2,1)S(1)} fusion(bf16[2,1,32,8,1536]{4,3,2,1,0:T(8,128)(2,1)} %collective-permute-done.2, bf16[2,1,32,8,1536]{4,3,2,1,0:T(8,128)(2,1)} %collective-permute-done.3, pred[]{:T(512)S(6)} %le.15), kind=kLoop, calls=%fused_computation.12 | loop fusion | flops 786432 | bytes 4718593 | tf_op jit(solution)/shard_map/jit(_where)/select_n | solution.py:207
  92.3 0.0 collective-permute-done.4
  92.3 0.0 collective-permute-done.5
  92.4 1.7 %conditional.1 = ((bf16[1,256,1536]{2,1,0:T(8,128)(2,1)}, f32[1,3,256,4]{3,2,1,0:T(8,128)})) conditional(s32[]{:T(128)} %convert_element_type.79, () %tuple.16, (bf16[1,32,8,1536]{3,2,1,0:T(8,128)(2,1)}, pred[8,8]{1,0:T(8,128)(4,1)S(1)}, bf16[2,1,256,1536]{3,2,1,0:T(8,128)(2,1)S(1)}, pred[]{:T(512)}, pred[]{:T(512)}, ...), branch_computations={%region_3.4_spmd, %region_4.5_spmd.clone.clone} | conditional | flops 402656640 | bytes 4725510 | solution.py:236
  92.4 0.9 broadcast.758
  93.3 0.8 broadcast.759
  94.1 1.3 collective-permute-start.6
  95.4 4.2 %multiply_reduce_fusion = f32[256,12,128]{2,1,0:T(8,128)S(1)} fusion(bf16[2,2,256,12,128]{4,3,2,0,1:T(8,128)(2,1)} %copy_dynamic-update-slice_fusion, f32[2,256,12]{2,1,0:T(8,128)S(1)} %get-tuple-element.124), kind=kLoop, calls=%fused_computation.8 | loop fusion | flops 1966080 | bytes 3170304 | tf_op jit(solution)/shard_map/reduce_sum | solution.py:138
  99.6 0.7 reduce-precision_convert_fusion
  100.3 0.9 copy.14
  101.2 1.2 copy.15.refs_6_
  102.4 1.3 collective-permute-start.7
  103.6 4.8 %shard_map.56 = (f32[1,256,1536]{2,1,0:T(8,128)}, f32[1,3,256,4]{3,2,1,0:T(8,128)}) custom-call(bf16[1,256,1536]{2,1,0:T(8,128)(2,1)} %bitcast.34, bf16[2,1,256,1536]{3,2,1,0:T(8,128)(2,1)S(1)} %bitcast.31, bf16[2,1,256,1536]{3,2,1,0:T(8,128)(2,1)S(1)} %bitcast.32, f32[256,256]{1,0:T(8,128)} %reshape.564.m_ref), custom_call_target="tpu_custom_call" | custom-call | flops 402653184 | bytes 3932160 | tf_op jit(solution)/shard_map/pallas_call | solution.py:65
  108.5 20.7 %collective-permute-done.7 = f32[1,3,4,256]{2,3,1,0:T(8,128)S(1)} collective-permute-done((f32[1,3,4,256]{2,3,1,0:T(8,128)}, f32[1,3,4,256]{2,3,1,0:T(8,128)S(1)}, u32[]{:S(2)}, u32[]{:S(2)}) %collective-permute-start.7) | collective-permute-done | bytes 12320 | tf_op jit(solution)/shard_map/ppermute | solution.py:243
  129.2 0.8 select_bitcast_fusion.refs_5_
  130.0 0.0 collective-permute-done.6.refs_4_
  130.0 5.4 %shard_map.57 = bf16[1,256,1536]{2,1,0:T(8,128)(2,1)} custom-call(f32[1,256,1536]{2,1,0:T(8,128)} %get-tuple-element.32.refs_0_, f32[1,3,256,4]{3,2,1,0:T(8,128)} %get-tuple-element.33.refs_1_, f32[1,256,1536]{2,1,0:T(8,128)} %get-tuple-element.35.refs_2_, f32[1,3,256,4]{3,2,1,0:T(8,128)} %get-tuple-element.36.refs_3_, ...), custom_call_target="tpu_custom_call" | custom-call | tf_op jit(solution)/shard_map/pallas_call | solution.py:118
  135.3 1.0 constant_dynamic-slice_fusion
  136.4 0.1 collective-permute-start.9
  136.4 1.7 %collective-permute-done.9 = bf16[1,32,8,768]{3,2,1,0:T(8,128)(2,1)S(1)} collective-permute-done((bf16[1,32,8,768]{3,2,1,0:T(8,128)(2,1)S(1)}, bf16[1,32,8,768]{3,2,1,0:T(8,128)(2,1)S(1)}, u32[]{:S(2)}, u32[]{:S(2)}) %collective-permute-start.9) | collective-permute-done | bytes 393248 | tf_op jit(solution)/shard_map/ppermute | solution.py:25
  138.1 1.9 %fusion.2 = bf16[1,32,8,768]{3,2,1,0:T(8,128)(2,1)} fusion(bf16[1,32,8,768]{3,2,1,0:T(8,128)(2,1)S(1)} %collective-permute-done.9, bf16[1,32,8,1536]{3,2,1,0:T(8,128)(2,1)} %bitcast.38, s32[]{:T(128)S(6)} %select_n.230, pred[]{:T(512)S(6)} %eq.73), kind=kLoop, calls=%fused_computation.16 | loop fusion | flops 1572864 | bytes 1179653 | tf_op jit(solution)/shard_map/convert_element_type | solution.py:333
  (21 shorter events, 0.2 us)
Async XLA Ops:
  0.0 2.2 %copy-start.1 = (bf16[1,1,32,8,1536]{4,3,2,1,0:T(8,128)(2,1)S(1)}, bf16[1,1,32,8,1536]{4,3,2,1,0:T(8,128)(2,1)}, u32[]{:S(2)}) copy-start(bf16[1,1,32,8,1536]{4,3,2,1,0:T(8,128)(2,1)} %param.9) | copy-start | bytes 2359300
  0.0 11.2 %copy-start.2 = (s32[4,15]{1,0:T(4,128)S(1)}, s32[4,15]{1,0:T(4,128)}, u32[]{:S(2)}) copy-start(s32[4,15]{1,0:T(4,128)} %param.10) | copy-start | bytes 724
  3.1 39.6 %collective-permute-start.1 = (bf16[2,1,32,8,1536]{4,3,2,1,0:T(8,128)(2,1)}, bf16[2,1,32,8,1536]{4,3,2,1,0:T(8,128)(2,1)}, u32[]{:S(2)}, u32[]{:S(2)}) collective-permute-start(bf16[2,1,32,8,1536]{4,3,2,1,0:T(8,128)(2,1)} %constant_dynamic-update-slice_fusion), channel_id=1, source_target_pairs={{12,8},{8,4},{4,0},{13,9},{9,5},{5,1},{14,10},{10,6},{6,2},{15,11}... | collective-permute-start | bytes 4718600 | tf_op jit(solution)/shard_map/ppermute | solution.py:192
  4.4 39.6 %collective-permute-start = (bf16[2,1,32,8,1536]{4,3,2,1,0:T(8,128)(2,1)}, bf16[2,1,32,8,1536]{4,3,2,1,0:T(8,128)(2,1)}, u32[]{:S(2)}, u32[]{:S(2)}) collective-permute-start(bf16[2,1,32,8,1536]{4,3,2,1,0:T(8,128)(2,1)} %constant_dynamic-update-slice_fusion), channel_id=1, source_target_pairs={{0,4},{4,8},{8,12},{1,5},{5,9},{9,13},{2,6},{6,10},{10,14},{3,7},{... | collective-permute-start | bytes 4718600 | tf_op jit(solution)/shard_map/ppermute | solution.py:191
  11.2 81.1 %collective-permute-start.5 = (s32[4,15]{1,0:T(4,128)S(1)}, s32[4,15]{1,0:T(4,128)S(1)}, u32[]{:S(2)}, u32[]{:S(2)}) collective-permute-start(s32[4,15]{1,0:T(4,128)S(1)} %copy-done.2), channel_id=1, source_target_pairs={{0,4},{12,8},{1,5},{13,9},{2,6},{14,10},{3,7},{15,11},{16,20},{28,... | collective-permute-start | bytes 728 | tf_op jit(solution)/shard_map/ppermute | solution.py:193
  18.4 65.4 %collective-permute-start.8 = (bf16[2,1,256,12,128]{4,2,3,1,0:T(8,128)(2,1)}, bf16[2,1,256,12,128]{4,2,3,1,0:T(8,128)(2,1)}, u32[]{:S(2)}, u32[]{:S(2)}) collective-permute-start(bf16[2,1,256,12,128]{4,2,3,1,0:T(8,128)(2,1)} %copy.12), channel_id=1, source_target_pairs={{0,2},{2,0},{1,3},{3,1},{4,6},{6,4},{5,7},{7,5},{8,10},{10,8},{9,1... | collective-permute-start | bytes 4718600 | tf_op jit(solution)/shard_map/ppermute | solution.py:21
  20.3 2.0 %copy-start.3 = (s32[2,8]{1,0:T(2,128)S(1)}, s32[2,8]{1,0:T(2,128)}, u32[]{:S(2)}) copy-start(s32[2,8]{1,0:T(2,128)} %param.11) | copy-start | bytes 196
  42.7 48.0 %collective-permute-start.2 = (bf16[2,1,32,8,1536]{4,3,2,1,0:T(8,128)(2,1)}, bf16[2,1,32,8,1536]{4,3,2,1,0:T(8,128)(2,1)}, u32[]{:S(2)}, u32[]{:S(2)}) collective-permute-start(bf16[2,1,32,8,1536]{4,3,2,1,0:T(8,128)(2,1)} %collective-permute-done.1), channel_id=1, source_target_pairs={{8,4},{4,0},{9,5},{5,1},{10,6},{6,2},{11,7},{7,3},{24,20},{20,16},... | collective-permute-start | bytes 4718600 | tf_op jit(solution)/shard_map/ppermute | solution.py:209
  44.0 46.7 %collective-permute-start.3 = (bf16[2,1,32,8,1536]{4,3,2,1,0:T(8,128)(2,1)}, bf16[2,1,32,8,1536]{4,3,2,1,0:T(8,128)(2,1)}, u32[]{:S(2)}, u32[]{:S(2)}) collective-permute-start(bf16[2,1,32,8,1536]{4,3,2,1,0:T(8,128)(2,1)} %collective-permute-done), channel_id=1, source_target_pairs={{4,8},{8,12},{5,9},{9,13},{6,10},{10,14},{7,11},{11,15},{20,24},{2... | collective-permute-start | bytes 4718600 | tf_op jit(solution)/shard_map/ppermute | solution.py:210
  55.7 4.8 %copy-start = (bf16[1,1,32,8,1536]{4,3,2,1,0:T(8,128)(2,1)S(1)}, bf16[1,1,32,8,1536]{4,3,2,1,0:T(8,128)(2,1)}, u32[]{:S(2)}) copy-start(bf16[1,1,32,8,1536]{4,3,2,1,0:T(8,128)(2,1)} %param.7) | copy-start | bytes 2359300
  61.0 31.3 %collective-permute-start.4 = (bf16[1,32,8,1536]{3,2,1,0:T(8,128)(2,1)S(1)}, bf16[1,32,8,1536]{3,2,1,0:T(8,128)(2,1)}, u32[]{:S(2)}, u32[]{:S(2)}) collective-permute-start(bf16[1,32,8,1536]{3,2,1,0:T(8,128)(2,1)S(1)} %bitcast.35), channel_id=1, source_target_pairs={{0,4},{12,8},{1,5},{13,9},{2,6},{14,10},{3,7},{15,11},{16,20},{28,... | collective-permute-start | bytes 2359304 | tf_op jit(solution)/shard_map/ppermute | solution.py:213
  94.1 35.9 %collective-permute-start.6 = (bf16[1,256,1536]{2,1,0:T(8,128)(2,1)}, bf16[1,256,1536]{2,1,0:T(8,128)(2,1)}, u32[]{:S(2)}, u32[]{:S(2)}) collective-permute-start(bf16[1,256,1536]{2,1,0:T(8,128)(2,1)} %get-tuple-element.38), channel_id=1, source_target_pairs={{4,0},{8,12},{5,1},{9,13},{6,2},{10,14},{7,3},{11,15},{20,16},{24,... | collective-permute-start | bytes 2359304 | tf_op jit(solution)/shard_map/ppermute | solution.py:243
  102.4 26.8 %collective-permute-start.7 = (f32[1,3,4,256]{2,3,1,0:T(8,128)}, f32[1,3,4,256]{2,3,1,0:T(8,128)S(1)}, u32[]{:S(2)}, u32[]{:S(2)}) collective-permute-start(f32[1,3,4,256]{2,3,1,0:T(8,128)} %bitcast.39), channel_id=1, source_target_pairs={{4,0},{8,12},{5,1},{9,13},{6,2},{10,14},{7,3},{11,15},{20,16},{24,... | collective-permute-start | bytes 36872 | tf_op jit(solution)/shard_map/ppermute | solution.py:243
  136.4 1.8 %collective-permute-start.9 = (bf16[1,32,8,768]{3,2,1,0:T(8,128)(2,1)S(1)}, bf16[1,32,8,768]{3,2,1,0:T(8,128)(2,1)S(1)}, u32[]{:S(2)}, u32[]{:S(2)}) collective-permute-start(bf16[1,32,8,768]{3,2,1,0:T(8,128)(2,1)S(1)} %constant_dynamic-slice_fusion), channel_id=1, source_target_pairs={{0,1},{1,0},{2,3},{3,2},{4,5},{5,4},{6,7},{7,6},{8,9},{9,8},{10,11... | collective-permute-start | bytes 1179656 | tf_op jit(solution)/shard_map/ppermute | solution.py:25

commit v14 on v6

--- a/solution.py
+++ b/solution.py
@@ -56,17 +56,20 @@
         lse_ref[:, head : head + 1] = maxima + jnp.log(totals)
 
 
-def spatial_attention(query_flat, key_value_flat, mask, scale, out_dtype=jnp.float32):
+def spatial_attention(
+    query_flat, key_value_flat, mask, scale, out_dtype=jnp.float32, query_first=0, count=None
+):
     frames, query_count, model_width = query_flat.shape
     key_count = key_value_flat.shape[2]
-    head_count = model_width // DH
     width = group_width(model_width)
-    groups = model_width // width
+    if count is None:
+        count = key_value_flat.shape[3] // width
+    used = count * width
     return pl.pallas_call(
         functools.partial(spatial_kernel, scale=scale),
-        grid=(frames, groups),
+        grid=(frames, count),
         in_specs=[
-            pl.BlockSpec((None, query_count, width), lambda f, g: (f, 0, g)),
+            pl.BlockSpec((None, query_count, width), lambda f, g: (f, 0, g + query_first)),
             pl.BlockSpec((None, None, key_count, width), lambda f, g: (0, f, 0, g)),
             pl.BlockSpec((None, None, key_count, width), lambda f, g: (1, f, 0, g)),
             pl.BlockSpec((query_count, key_count), lambda f, g: (0, 0)),
@@ -76,14 +79,14 @@
             pl.BlockSpec((None, None, query_count, width // DH), lambda f, g: (f, g, 0, 0)),
         ],
         out_shape=[
-            jax.ShapeDtypeStruct((frames, query_count, model_width), out_dtype),
-            jax.ShapeDtypeStruct((frames, groups, query_count, width // DH), jnp.float32),
+            jax.ShapeDtypeStruct((frames, query_count, used), out_dtype),
+            jax.ShapeDtypeStruct((frames, count, query_count, width // DH), jnp.float32),
         ],
         cost_estimate=pl.CostEstimate(
-            flops=4 * frames * query_count * key_count * model_width,
-            transcendentals=frames * head_count * query_count * key_count,
-            bytes_accessed=2 * model_width * frames * (query_count + 2 * key_count)
-            + 4 * frames * query_count * model_width,
+            flops=4 * frames * query_count * key_count * used,
+            transcendentals=frames * (used // DH) * query_count * key_count,
+            bytes_accessed=2 * used * frames * (query_count + 2 * key_count)
+            + 4 * frames * query_count * used,
         ),
     )(query_flat, key_value_flat, key_value_flat, mask)
 
@@ -106,21 +109,27 @@
         )
 
 
-def combine_partials(partials, temporal):
+def combine_partials(partials, temporal, first=0, count=None):
     frames, query_count, model_width = temporal.shape
     width = group_width(model_width)
-    groups = model_width // width
-    big = pl.BlockSpec((None, query_count, width), lambda f, g: (f, 0, g))
-    small = pl.BlockSpec((None, None, query_count, width // DH), lambda f, g: (f, g, 0, 0))
-    operands = []
-    for out, lse in partials:
-        operands += [out, lse]
+    if count is None:
+        count = model_width // width
+    heads = width // DH
+    whole_big = pl.BlockSpec((None, query_count, width), lambda f, g: (f, 0, g + first))
+    whole_small = pl.BlockSpec((None, None, query_count, heads), lambda f, g: (f, g + first, 0, 0))
+    part_big = pl.BlockSpec((None, query_count, width), lambda f, g: (f, 0, g))
+    part_small = pl.BlockSpec((None, None, query_count, heads), lambda f, g: (f, g, 0, 0))
+    in_specs, operands = [], []
+    for partial in partials:
+        whole = len(partial) == 2
+        in_specs += [whole_big, whole_small] if whole else [part_big, part_small]
+        operands += list(partial[:2])
     return pl.pallas_call(
         combine_kernel,
-        grid=(frames, groups),
-        in_specs=[big, small] * len(partials) + [big],
-        out_specs=big,
-        out_shape=jax.ShapeDtypeStruct((frames, query_count, model_width), jnp.bfloat16),
+        grid=(frames, count),
+        in_specs=in_specs + [whole_big],
+        out_specs=part_big,
+        out_shape=jax.ShapeDtypeStruct((frames, query_count, count * width), jnp.bfloat16),
     )(*operands, temporal)
 
 
@@ -181,32 +190,38 @@
     frames, lat_rows, columns, model_width = own_q.shape
     count = 4
     total_cols = count * columns
-    half = model_width // 2
     index = lax.axis_index("lon")
-    branch_index = lax.axis_index("branch")
     is_middle = (index >= 1) & (index <= count - 2)
     column_ids = jnp.arange(columns, dtype=jnp.int32)
     own_map = jnp.repeat(window_map, BLK, axis=0)
     own_cols = index * columns + column_ids
+    query_flat = own_q.reshape(frames, lat_rows * columns, model_width)
+
+    from_left = lax.ppermute(key_value, "lon", [(0, 1), (1, 2), (2, 3)])
+    from_right = lax.ppermute(key_value, "lon", [(3, 2), (2, 1), (1, 0)])
     guest_map = lax.ppermute(window_map, "lon", [(0, 1), (3, 2)])
 
     near_cols = ((index - 1) * columns + jnp.arange(3 * columns, dtype=jnp.int32)) % total_cols
     near_valid = jnp.stack([index >= 1, index >= 0, index <= count - 2])
-    near_mask = expand_mask(
-        window_mask(own_cols, near_cols, own_map, total_cols, lat_rows)
-        & jnp.repeat(near_valid, columns)[None, :],
-        lat_rows,
+    near_active = window_mask(own_cols, near_cols, own_map, total_cols, lat_rows) & jnp.repeat(
+        near_valid, columns
+    )[None, :]
+    near_part = spatial_attention(
+        query_flat,
+        flat_keys([from_left, key_value, from_right]),
+        expand_mask(near_active, lat_rows),
+        scale,
     )
+
+    held_q, _ = lax.optimization_barrier((own_q, from_left))
+    guest_q = lax.ppermute(held_q, "lon", [(0, 1), (3, 2)])
     guest_device = jnp.where(index == 1, 0, count - 1)
-    near_block = jnp.where(index == 1, index + 1, index - 1)
     far_block = (index + 2) % count
-    guest_key_cols = jnp.concatenate(
-        [near_block * columns + column_ids, far_block * columns + column_ids]
-    )
+    far_cols = far_block * columns + column_ids
     guest_mask = expand_mask(
         window_mask(
             guest_device * columns + column_ids,
-            guest_key_cols,
+            far_cols,
             jnp.repeat(guest_map, BLK, axis=0),
             total_cols,
             lat_rows,
@@ -214,55 +229,43 @@
         & is_middle,
         lat_rows,
     )
-    far_mask = expand_mask(
-        window_mask(own_cols, far_block * columns + column_ids, own_map, total_cols, lat_rows)
-        & is_middle,
-        lat_rows,
-    )
-
-    mixed = []
-    previous = None
-    for chunk in range(2):
-        start = jnp.where(chunk == 0, 1 - branch_index, branch_index) * half
-        chunk_q = lax.dynamic_slice_in_dim(own_q, start, half, 3)
-        chunk_kv = lax.dynamic_slice_in_dim(key_value, start, half, 4)
-        if previous is not None:
-            chunk_kv, _ = lax.optimization_barrier((chunk_kv, previous))
-        query_flat = chunk_q.reshape(frames, lat_rows * columns, half)
-        from_left = lax.ppermute(chunk_kv, "lon", [(0, 1), (1, 2), (2, 3)])
-        from_right = lax.ppermute(chunk_kv, "lon", [(3, 2), (2, 1), (1, 0)])
-        previous = (from_left, from_right)
-        near_part = spatial_attention(
-            query_flat, flat_keys([from_left, chunk_kv, from_right]), near_mask, scale
-        )
-        two_away = jnp.where(
-            index == 1,
-            lax.ppermute(from_right, "lon", [(2, 1)]),
-            lax.ppermute(from_left, "lon", [(1, 2)]),
-        )
-        held_q, _ = lax.optimization_barrier((chunk_q, from_left))
-        guest_q = lax.ppermute(held_q, "lon", [(0, 1), (3, 2)])
-        near_part, two_away, guest_q = lax.optimization_barrier((near_part, two_away, guest_q))
-        guest_near = jnp.where(index == 1, from_right, from_left)
+    far_mask = expand_mask(window_mask(own_cols, far_cols, own_map, total_cols, lat_rows), lat_rows)
+    guest_flat = guest_q.reshape(frames, lat_rows * columns, model_width)
+
+    width = group_width(model_width)
+    groups = model_width // width
+    chunks = [(0, groups - 1), (groups - 1, 1)] if groups > 1 else [(0, groups)]
+    mixed, landed = [], None
+    for first, size in chunks:
+        lanes = slice(first * width, (first + size) * width)
+        chunk_left, chunk_right = from_left[..., lanes], from_right[..., lanes]
+        if landed is not None:
+            chunk_left, chunk_right, _ = lax.optimization_barrier((chunk_left, chunk_right, landed))
+        toward_left = lax.ppermute(chunk_right, "lon", [(2, 1), (1, 0)])
+        toward_right = lax.ppermute(chunk_left, "lon", [(1, 2), (2, 3)])
+        landed = (toward_left, toward_right)
+        if first == 0:
+            near_part, toward_left, toward_right, guest_flat = lax.optimization_barrier(
+                (near_part, toward_left, toward_right, guest_flat)
+            )
+        far_keys = flat_keys([jnp.where(index <= 1, toward_left, toward_right)])
         guest_out, guest_lse = spatial_attention(
-            guest_q.reshape(frames, lat_rows * columns, half),
-            flat_keys([guest_near, two_away]),
-            guest_mask,
-            scale,
-            jnp.bfloat16,
+            guest_flat, far_keys, guest_mask, scale, jnp.bfloat16, first, size
         )
         returned, returned_lse = lax.ppermute(
             (guest_out, jnp.swapaxes(guest_lse, 2, 3)), "lon", [(1, 0), (2, 3)]
         )
         returned_lse = jnp.where(is_middle, masked_score, jnp.swapaxes(returned_lse, 2, 3))
-        far_part = spatial_attention(query_flat, flat_keys([two_away]), far_mask, scale)
-        chunk_temporal = lax.dynamic_slice_in_dim(temporal, start, half, 2)
+        far_part = spatial_attention(query_flat, far_keys, far_mask, scale, jnp.float32, first, size)
         mixed.append(
             combine_partials(
-                [near_part, far_part, (returned, returned_lse)], chunk_temporal
-            ).reshape(frames, lat_rows, columns, half)
-        )
-    return mixed
+                [near_part, far_part + (False,), (returned, returned_lse, False)],
+                temporal,
+                first,
+                size,
+            )
+        )
+    return jnp.concatenate(mixed, axis=2)
 
 
 def local(queries, keys, values, window_map, frame_valid):
@@ -331,18 +334,15 @@
             spatial_attention(query_flat, key_value_flat, expand_mask(active, lat_rows), scale)
         ]
 
+    if full_ring and lon_count == 4:
+        mixed = spatial_line_of_four(own_q, key_value, window_map, temporal, scale)
+    else:
+        mixed = combine_partials(partials, temporal)
+    mixed = mixed.reshape(frames, lat_rows, columns, model_width)
     half_width = model_width // 2
     branch_index = lax.axis_index("branch")
-    if full_ring and lon_count == 4:
-        other_half, own_half = spatial_line_of_four(own_q, key_value, window_map, temporal, scale)
-    else:
-        mixed = combine_partials(partials, temporal).reshape(
-            frames, lat_rows, columns, model_width
-        )
-        own_half = lax.dynamic_slice_in_dim(mixed, branch_index * half_width, half_width, 3)
-        other_half = lax.dynamic_slice_in_dim(
-            mixed, (1 - branch_index) * half_width, half_width, 3
-        )
+    own_half = lax.dynamic_slice_in_dim(mixed, branch_index * half_width, half_width, 3)
+    other_half = lax.dynamic_slice_in_dim(mixed, (1 - branch_index) * half_width, half_width, 3)
     partner = from_partner(other_half, "branch", 0)
     is_conditional = branch_index == 0
     conditional = jnp.where(is_conditional, own_half, partner).astype(jnp.float32)

time: 157 us -> 146 us (0.930)
  waiting for transfers between devices: 5.98 us -> 21.7 us
  starting transfers between devices: 46.2 us -> 32 us
  other arithmetic: 27.3 us -> 17.4 us
  Pallas kernels: 33.7 us -> 28.7 us
  local copies, waits for them, and re-layouts: 42.6 us -> 45.6 us
    ppermute x4, waiting for transfers between devices: 5.94 us -> 15.6 us  [spatial_line_of_four(): lax.ppermute((guest_out, jnp.swapaxes(guest_lse, 2, 3)), 'lon', [(1, 0),...]
    ppermute x2 -> x1, starting transfers between devices: 17.1 us -> 9.22 us  [spatial_line_of_four(): guest_q = lax.ppermute(held_q, 'lon', [(0, 1), (3, 2)])]
    ppermute x8 -> x6, starting transfers between devices: 19.1 us -> 13.2 us  [the longest x1 6.81 us: spatial_line_of_four(): from_left = lax.ppermute(key_value, 'lon', [(0, 1), (1, 2), (2, 3)])]
    select_n x4 -> x0, other arithmetic: 5.76 us -> none  [the longest x2 3.32 us: spatial_line_of_four(): guest_near = jnp.where(index == 1, from_right, from_left)]
    slice x0 -> x4, local copies, waits for them, and re-layouts: none -> 5.69 us  [spatial_line_of_four(): chunk_left, chunk_right = (from_left[..., lanes], from_right[..., lanes])]
    pallas_call x6 -> x5, Pallas kernels: 27.3 us -> 22 us  [spatial_attention(): pl.pallas_call(functools.partial(spatial_kernel, scale=scale), grid=(fram...]
    concatenate x4 -> x1, other arithmetic: 9.19 us -> 4.78 us  [flat_keys(): joined = jnp.concatenate(blocks, axis=3)]
    ppermute x1, waiting for transfers between devices: 0.01 us -> 4.36 us  [spatial_line_of_four(): guest_map = lax.ppermute(window_map, 'lon', [(0, 1), (3, 2)])]
  transfers between devices with their start and end apart: 17 -> 14, of which waited for: 1 -> 3; matrix products, arithmetic and copies ran while one was open for 40% -> 39% of each run, Pallas kernels for 22% -> 18%
where the time goes in v14:
time: 146 us
  local copies, waits for them, and re-layouts  45.6 us (31%)
  starting transfers between devices  32 us (22%)
  Pallas kernels  28.7 us (20%)
  waiting for transfers between devices  21.7 us (15%)
  other arithmetic  17.4 us (12%)
    pallas_call x5, Pallas kernels, spatial_attention(): pl.pallas_call(functools.partial(spatial_kernel, scale=scale), grid=(fram...  22 us
    ppermute x4, waiting for transfers between devices, spatial_line_of_four(): lax.ppermute((guest_out, jnp.swapaxes(guest_lse, 2, 3)), 'lon', [(1, 0),...  15.6 us
    reshape x3, local copies, waits for them, and re-layouts, expand_mask(): return jnp.broadcast_to(active[None, :, None, :].astype(jnp.float32), (la...  14.1 us
    ppermute x1, starting transfers between devices, spatial_line_of_four(): guest_q = lax.ppermute(held_q, 'lon', [(0, 1), (3, 2)])  9.22 us
    broadcast_in_dim x3, local copies, waits for them, and re-layouts, expand_mask(): jnp.broadcast_to(active[None, :, None, :].astype(jnp.float32), (lat_rows,...  7.43 us
    ppermute x1, starting transfers between devices, spatial_line_of_four(): from_left = lax.ppermute(key_value, 'lon', [(0, 1), (1, 2), (2, 3)])  6.81 us
    pallas_call x2, Pallas kernels, combine_partials(): pl.pallas_call(combine_kernel, grid=(frames, count), in_specs=in_specs +...  6.66 us
    slice x4, local copies, waits for them, and re-layouts, spatial_line_of_four(): chunk_left, chunk_right = (from_left[..., lanes], from_right[..., lanes])  5.69 us
  transfers between devices with their start and end apart: 14, of which 3 were waited for; matrix products, arithmetic and copies ran while one was open for 39% of the time, Pallas kernels for 18%

profile of v14, /device:TPU:0, one launch (start us, length us, event | category | flops | bytes accessed | tf_op | source)
XLA Modules:
  0.0 145.7 jit_solution(315707641765114935)
XLA Ops:
  0.0 2.2 %constant_dynamic-update-slice_fusion.1 = bf16[2,1,32,8,1536]{4,3,2,1,0:T(8,128)(2,1)} fusion(bf16[1,1,32,8,1536]{4,3,2,1,0:T(8,128)(2,1)} %param.6), kind=kLoop, calls=%fused_computation.30 | loop fusion | bytes 1572864
  2.2 1.0 constant_dynamic-update-slice_fusion
  3.1 1.3 collective-permute-start.1
  4.4 6.8 %collective-permute-start = (bf16[2,1,32,8,1536]{4,3,2,1,0:T(8,128)(2,1)}, bf16[2,1,32,8,1536]{4,3,2,1,0:T(8,128)(2,1)}, u32[]{:S(2)}, u32[]{:S(2)}) collective-permute-start(bf16[2,1,32,8,1536]{4,3,2,1,0:T(8,128)(2,1)} %constant_dynamic-update-slice_fusion), channel_id=1, source_target_pairs={{0,4},{4,8},{8,12},{1,5},{5,9},{9,13},{2,6},{6,10},{10,14},{3,7},{... | collective-permute-start | bytes 4718600 | tf_op jit(solution)/shard_map/ppermute | solution.py:200
  11.2 2.7 %collective-permute-start.5 = (s32[4,15]{1,0:T(4,128)S(1)}, s32[4,15]{1,0:T(4,128)S(1)}, u32[]{:S(2)}, u32[]{:S(2)}) collective-permute-start(s32[4,15]{1,0:T(4,128)S(1)} %copy-done.11), channel_id=1, source_target_pairs={{0,4},{12,8},{1,5},{13,9},{2,6},{14,10},{3,7},{15,11},{16,20},{28,... | collective-permute-start | bytes 728 | tf_op jit(solution)/shard_map/ppermute | solution.py:202
  13.9 2.9 %reshape.558 = bf16[2,1,256,12,128]{4,3,2,0,1:T(8,128)(2,1)S(1)} reshape(bf16[2,1,32,8,1536]{4,3,2,1,0:T(8,128)(2,1)} %constant_dynamic-update-slice_fusion) | data formatting | bytes 3145728 | tf_op jit(solution)/shard_map/reshape | solution.py:288
  16.8 1.5 %copy.14 = bf16[2,1,256,12,128]{4,2,3,1,0:T(8,128)(2,1)} copy(bf16[2,1,256,12,128]{4,3,2,0,1:T(8,128)(2,1)S(1)} %reshape.558) | data formatting | bytes 3145728 | tf_op jit(solution)/shard_map/reshape | solution.py:288
  18.4 1.5 %collective-permute-start.8 = (bf16[2,1,256,12,128]{4,2,3,1,0:T(8,128)(2,1)}, bf16[2,1,256,12,128]{4,2,3,1,0:T(8,128)(2,1)}, u32[]{:S(2)}, u32[]{:S(2)}) collective-permute-start(bf16[2,1,256,12,128]{4,2,3,1,0:T(8,128)(2,1)} %copy.14), channel_id=1, source_target_pairs={{0,2},{2,0},{1,3},{3,1},{4,6},{6,4},{5,7},{7,5},{8,10},{10,8},{9,1... | collective-permute-start | bytes 4718600 | tf_op jit(solution)/shard_map/ppermute | solution.py:21
  20.0 0.1 copy.13
  20.2 0.1 and.236
  20.4 0.1 fusion.6
  20.5 0.1 add_select_fusion
  20.6 2.5 %broadcast_in_dim.42 = f32[32,8,32,24]{3,2,1,0:T(8,128)} broadcast(f32[8,24]{1,0:T(8,128)S(1)} %and_convert_fusion.1), dimensions={1,3} | broadcast | bytes 787200 | tf_op jit(solution)/shard_map/broadcast_in_dim | solution.py:178
  23.1 4.6 %reshape.553.m_ref = f32[256,768]{1,0:T(8,128)} reshape(f32[32,8,32,24]{3,2,1,0:T(8,128)} %broadcast_in_dim.42) | data formatting | bytes 1572864 | tf_op jit(solution)/shard_map/reshape | solution.py:180
  27.7 0.3 fusion.8
  28.0 2.5 %broadcast_in_dim.43 = f32[32,8,32,8]{3,2,1,0:T(8,128)} broadcast(f32[8,8]{1,0:T(8,128)S(1)} %convert_element_type.69), dimensions={1,3} | broadcast | bytes 262400 | tf_op jit(solution)/shard_map/broadcast_in_dim | solution.py:178
  30.5 4.7 %reshape.556.m_ref = f32[256,256]{1,0:T(8,128)} reshape(f32[32,8,32,8]{3,2,1,0:T(8,128)} %broadcast_in_dim.43) | data formatting | bytes 524288 | tf_op jit(solution)/shard_map/reshape | solution.py:180
  35.2 1.8 %reshape.561 = f32[256,12,128]{2,1,0:T(8,128)} reshape(bf16[1,1,32,8,1536]{4,3,2,1,0:T(8,128)(2,1)S(1)} %copy-done) | data formatting | bytes 2359296 | tf_op jit(solution)/shard_map/convert_element_type | solution.py:137
  37.1 0.1 tile.10
  37.2 0.6 gather_fusion
  37.8 1.7 %constant_dynamic-update-slice_fusion.2 = bf16[2,2,256,12,128]{4,3,2,0,1:T(8,128)(2,1)} fusion(bf16[2,1,256,12,128]{4,3,2,0,1:T(8,128)(2,1)S(1)} %reshape.558), kind=kLoop, calls=%fused_computation.31 | loop fusion | bytes 3670016
  39.6 4.4 %collective-permute-done.5 = s32[4,15]{1,0:T(4,128)S(1)} collective-permute-done((s32[4,15]{1,0:T(4,128)S(1)}, s32[4,15]{1,0:T(4,128)S(1)}, u32[]{:S(2)}, u32[]{:S(2)}) %collective-permute-start.5) | collective-permute-done | bytes 272 | tf_op jit(solution)/shard_map/ppermute | solution.py:202
  44.0 0.3 fusion.10
  44.3 2.5 %broadcast_in_dim.45 = f32[32,8,32,8]{3,2,1,0:T(8,128)} broadcast(f32[8,8]{1,0:T(8,128)S(1)} %and_convert_fusion), dimensions={1,3} | broadcast | bytes 262400 | tf_op jit(solution)/shard_map/broadcast_in_dim | solution.py:178
  46.8 4.7 %reshape.557.m_ref = f32[256,256]{1,0:T(8,128)} reshape(f32[32,8,32,8]{3,2,1,0:T(8,128)} %broadcast_in_dim.45) | data formatting | bytes 524288 | tf_op jit(solution)/shard_map/reshape | solution.py:180
  51.5 1.4 slice.30
  52.9 1.4 collective-permute-start.2
  54.4 1.3 slice.31
  55.7 0.9 collective-permute-start.3
  56.5 9.2 %collective-permute-start.4 = (bf16[1,32,8,1536]{3,2,1,0:T(8,128)(2,1)S(1)}, bf16[1,32,8,1536]{3,2,1,0:T(8,128)(2,1)}, u32[]{:S(2)}, u32[]{:S(2)}) collective-permute-start(bf16[1,32,8,1536]{3,2,1,0:T(8,128)(2,1)S(1)} %bitcast.39), channel_id=1, source_target_pairs={{0,4},{12,8},{1,5},{13,9},{2,6},{14,10},{3,7},{15,11},{16,20},{28,... | collective-permute-start | bytes 2359304 | tf_op jit(solution)/shard_map/ppermute | solution.py:217
  65.8 2.6 %copy_dynamic-update-slice_fusion = bf16[2,2,256,12,128]{4,3,2,0,1:T(8,128)(2,1)S(1)} fusion(bf16[2,2,256,12,128]{4,3,2,0,1:T(8,128)(2,1)S(1)} %copy-done.1, bf16[2,1,256,12,128]{4,2,3,1,0:T(8,128)(2,1)} %collective-permute-done.8), kind=kLoop, calls=%fused_computation.4 | loop fusion | bytes 3670016 | tf_op jit(solution)/shard_map/concatenate | solution.py:292
  68.4 1.2 multiply_reduce_fusion.1
  69.6 1.1 slice.34
  70.7 1.9 %slice.35 = bf16[2,1,32,8,512]{4,3,2,1,0:T(8,128)(2,1)} slice(bf16[2,1,32,8,1536]{4,3,2,1,0:T(8,128)(2,1)} %collective-permute-done.1), slice={[0:2], [0:1], [0:32], [0:8], [1024:1536]} | slice | bytes 1048576 | tf_op jit(solution)/shard_map/slice | solution.py:241
  72.6 0.1 fusion.2
  72.7 0.1 fusion.3
  72.9 4.8 %pad_maximum_fusion = bf16[2,1,32,24,1536]{4,3,2,1,0:T(8,128)(2,1)} fusion(bf16[2,1,32,8,1536]{4,3,2,1,0:T(8,128)(2,1)} %collective-permute-done.1, bf16[2,1,32,8,1536]{4,3,2,1,0:T(8,128)(2,1)} %constant_dynamic-update-slice_fusion, bf16[2,1,32,8,1536]{4,3,2,1,0:T(8,128)(2,1)} %collective-permute-done), kind=kLoop, calls=%fused_computation.1 | loop fusion | flops 14155776 | bytes 9437184 | tf_op jit(solution)/shard_map/concatenate | solution.py:184
  77.7 2.9 %multiply_reduce_fusion = f32[256,12,128]{2,1,0:T(8,128)S(1)} fusion(bf16[2,2,256,12,128]{4,3,2,0,1:T(8,128)(2,1)S(1)} %copy_dynamic-update-slice_fusion, f32[2,256,12]{2,1,0:T(8,128)S(1)} %get-tuple-element.42), kind=kLoop, calls=%fused_computation.2 | loop fusion | flops 1966080 | bytes 3170304 | tf_op jit(solution)/shard_map/reduce_sum | solution.py:147
  80.7 1.3 collective-permute-start.9
  82.0 1.5 %collective-permute-start.10 = (bf16[2,1,32,8,512]{4,3,2,1,0:T(8,128)(2,1)S(1)}, bf16[2,1,32,8,512]{4,3,2,1,0:T(8,128)(2,1)}, u32[]{:S(2)}, u32[]{:S(2)}) collective-permute-start(bf16[2,1,32,8,512]{4,3,2,1,0:T(8,128)(2,1)S(1)} %slice.34), channel_id=1, source_target_pairs={{4,8},{8,12},{5,9},{9,13},{6,10},{10,14},{7,11},{11,15},{20,24},{2... | collective-permute-start | bytes 1572872 | tf_op jit(solution)/shard_map/ppermute | solution.py:245
  83.5 0.7 reduce-precision_convert_fusion
  84.2 0.9 copy.16
  85.0 1.2 copy.17.refs_6_
  86.3 8.6 %shard_map.55 = (f32[1,256,1536]{2,1,0:T(8,128)}, f32[1,3,256,4]{3,2,1,0:T(8,128)}) custom-call(bf16[1,256,1536]{2,1,0:T(8,128)(2,1)} %bitcast.36, bf16[2,1,768,1536]{3,2,1,0:T(8,128)(2,1)} %bitcast.34, bf16[2,1,768,1536]{3,2,1,0:T(8,128)(2,1)} %bitcast.35, f32[256,768]{1,0:T(8,128)} %reshape.553.m_ref), custom_call_target="tpu_custom_call" | custom-call | flops 1207959552 | bytes 7077888 | tf_op jit(solution)/shard_map/pallas_call | solution.py:68
  94.9 1.1 select_bitcast_fusion.k_ref.v_ref
  96.0 3.8 %shard_map.57 = (bf16[1,256,1024]{2,1,0:T(8,128)(2,1)}, f32[1,2,256,4]{3,2,1,0:T(8,128)}) custom-call(bf16[1,256,1536]{2,1,0:T(8,128)(2,1)} %bitcast.6.q_ref, bf16[2,1,256,1024]{3,2,1,0:T(8,128)(2,1)} %select_bitcast_fusion.k_ref.v_ref, bf16[2,1,256,1024]{3,2,1,0:T(8,128)(2,1)} %select_bitcast_fusion.k_ref.v_ref, f32[256,256]{1,0:T(8,128)} %reshape.557.m_ref), custom_call_target="tpu_custom_call" | custom-call | flops 268435456 | bytes 2621440 | tf_op jit(solution)/shard_map/pallas_call | solution.py:68
  99.8 1.3 collective-permute-start.6
  101.1 1.3 collective-permute-start.7
  102.4 3.9 %shard_map.56 = (f32[1,256,1024]{2,1,0:T(8,128)}, f32[1,2,256,4]{3,2,1,0:T(8,128)}) custom-call(bf16[1,256,1536]{2,1,0:T(8,128)(2,1)} %bitcast.37, bf16[2,1,256,1024]{3,2,1,0:T(8,128)(2,1)} %select_bitcast_fusion.k_ref.v_ref, bf16[2,1,256,1024]{3,2,1,0:T(8,128)(2,1)} %select_bitcast_fusion.k_ref.v_ref, f32[256,256]{1,0:T(8,128)} %reshape.556.m_ref), custom_call_target="tpu_custom_call" | custom-call | flops 268435456 | bytes 2621440 | tf_op jit(solution)/shard_map/pallas_call | solution.py:68
  106.4 1.9 %select_bitcast_fusion.1.k_ref.v_ref = bf16[2,1,256,512]{3,2,1,0:T(8,128)(2,1)} fusion(bf16[2,1,32,8,512]{4,3,2,1,0:T(8,128)(2,1)} %collective-permute-done.9, bf16[2,1,32,8,512]{4,3,2,1,0:T(8,128)(2,1)} %collective-permute-done.10, pred[]{:T(512)S(6)} %le.16), kind=kLoop, calls=%fused_computation.12 | loop fusion | flops 262144 | bytes 1572865 | tf_op jit(solution)/shard_map/reshape | solution.py:186
  108.3 2.8 %shard_map.60 = (bf16[1,256,512]{2,1,0:T(8,128)(2,1)}, f32[1,1,256,4]{3,2,1,0:T(8,128)}) custom-call(bf16[1,256,1536]{2,1,0:T(8,128)(2,1)} %bitcast.6.q_ref, bf16[2,1,256,512]{3,2,1,0:T(8,128)(2,1)} %select_bitcast_fusion.1.k_ref.v_ref, bf16[2,1,256,512]{3,2,1,0:T(8,128)(2,1)} %select_bitcast_fusion.1.k_ref.v_ref, f32[256,256]{1,0:T(8,128)} %reshape.557.m_ref), custom_call_target="tpu_custom_call" | custom-call | flops 134217728 | bytes 1310720 | tf_op jit(solution)/shard_map/pallas_call | solution.py:68
  111.1 1.3 collective-permute-start.11
  112.4 15.6 %collective-permute-done.7 = f32[1,2,4,256]{2,3,1,0:T(8,128)S(1)} collective-permute-done((f32[1,2,4,256]{2,3,1,0:T(8,128)}, f32[1,2,4,256]{2,3,1,0:T(8,128)S(1)}, u32[]{:S(2)}, u32[]{:S(2)}) %collective-permute-start.7) | collective-permute-done | bytes 8224 | tf_op jit(solution)/shard_map/ppermute | solution.py:255
  127.9 0.7 select_bitcast_fusion.2.refs_5_
  128.7 1.5 %collective-permute-start.12 = (f32[1,1,4,256]{2,3,1,0:T(8,128)}, f32[1,1,4,256]{2,3,1,0:T(8,128)S(1)}, u32[]{:S(2)}, u32[]{:S(2)}) collective-permute-start(f32[1,1,4,256]{2,3,1,0:T(8,128)} %bitcast.43), channel_id=1, source_target_pairs={{4,0},{8,12},{5,1},{9,13},{6,2},{10,14},{7,3},{11,15},{20,16},{24,... | collective-permute-start | bytes 12296 | tf_op jit(solution)/shard_map/ppermute | solution.py:255
  130.2 2.9 %shard_map.59 = (f32[1,256,512]{2,1,0:T(8,128)}, f32[1,1,256,4]{3,2,1,0:T(8,128)}) custom-call(bf16[1,256,1536]{2,1,0:T(8,128)(2,1)} %bitcast.38, bf16[2,1,256,512]{3,2,1,0:T(8,128)(2,1)} %select_bitcast_fusion.1.k_ref.v_ref, bf16[2,1,256,512]{3,2,1,0:T(8,128)(2,1)} %select_bitcast_fusion.1.k_ref.v_ref, f32[256,256]{1,0:T(8,128)} %reshape.556.m_ref), custom_call_target="tpu_custom_call" | custom-call | flops 134217728 | bytes 1310720 | tf_op jit(solution)/shard_map/pallas_call | solution.py:68
  133.1 0.8 copy-done.9
  133.9 3.7 %shard_map.58 = bf16[1,256,1024]{2,1,0:T(8,128)(2,1)} custom-call(f32[1,256,1536]{2,1,0:T(8,128)} %get-tuple-element.26.refs_0_, f32[1,3,256,4]{3,2,1,0:T(8,128)} %get-tuple-element.27.refs_1_, f32[1,256,1024]{2,1,0:T(8,128)} %get-tuple-element.30.refs_2_, f32[1,2,256,4]{3,2,1,0:T(8,128)} %get-tuple-element.31.refs_3_, bf16[1,256,1024]{2,1,0:T(8,128)(2,1)} %copy-done.9, ...), custom_call_target="tpu_custom_call" | custom-call | tf_op jit(solution)/shard_map/pallas_call | solution.py:127
  137.6 0.7 select_bitcast_fusion.3.refs_5_
  138.3 0.7 copy-done.10
  139.0 2.9 %shard_map.61 = bf16[1,256,512]{2,1,0:T(8,128)(2,1)} custom-call(f32[1,256,1536]{2,1,0:T(8,128)} %get-tuple-element.26.refs_0_, f32[1,3,256,4]{3,2,1,0:T(8,128)} %get-tuple-element.27.refs_1_, f32[1,256,512]{2,1,0:T(8,128)} %get-tuple-element.37.refs_2_, f32[1,1,256,4]{3,2,1,0:T(8,128)} %get-tuple-element.38.refs_3_, bf16[1,256,512]{2,1,0:T(8,128)(2,1)} %copy-done.10, ...), custom_call_target="tpu_custom_call" | custom-call | tf_op jit(solution)/shard_map/pallas_call | solution.py:127
  141.9 1.0 maximum_bitcast_fusion
  143.0 1.7 %collective-permute-done.13 = bf16[1,32,8,768]{3,2,1,0:T(8,128)(2,1)S(1)} collective-permute-done((bf16[1,32,8,768]{3,2,1,0:T(8,128)(2,1)S(1)}, bf16[1,32,8,768]{3,2,1,0:T(8,128)(2,1)S(1)}, u32[]{:S(2)}, u32[]{:S(2)}) %collective-permute-start.13) | collective-permute-done | bytes 393248 | tf_op jit(solution)/shard_map/ppermute | solution.py:25
  144.7 0.9 fusion.1
  (58 shorter events, 0.7 us)
Async XLA Ops:
  0.0 2.2 %copy-start.8 = (bf16[1,1,32,8,1536]{4,3,2,1,0:T(8,128)(2,1)S(1)}, bf16[1,1,32,8,1536]{4,3,2,1,0:T(8,128)(2,1)}, u32[]{:S(2)}) copy-start(bf16[1,1,32,8,1536]{4,3,2,1,0:T(8,128)(2,1)} %param.7) | copy-start | bytes 2359300
  0.0 11.2 %copy-start.11 = (s32[4,15]{1,0:T(4,128)S(1)}, s32[4,15]{1,0:T(4,128)}, u32[]{:S(2)}) copy-start(s32[4,15]{1,0:T(4,128)} %param.8) | copy-start | bytes 724
  3.1 48.3 %collective-permute-start.1 = (bf16[2,1,32,8,1536]{4,3,2,1,0:T(8,128)(2,1)}, bf16[2,1,32,8,1536]{4,3,2,1,0:T(8,128)(2,1)}, u32[]{:S(2)}, u32[]{:S(2)}) collective-permute-start(bf16[2,1,32,8,1536]{4,3,2,1,0:T(8,128)(2,1)} %constant_dynamic-update-slice_fusion), channel_id=1, source_target_pairs={{12,8},{8,4},{4,0},{13,9},{9,5},{5,1},{14,10},{10,6},{6,2},{15,11}... | collective-permute-start | bytes 4718600 | tf_op jit(solution)/shard_map/ppermute | solution.py:201
  4.4 49.9 %collective-permute-start = (bf16[2,1,32,8,1536]{4,3,2,1,0:T(8,128)(2,1)}, bf16[2,1,32,8,1536]{4,3,2,1,0:T(8,128)(2,1)}, u32[]{:S(2)}, u32[]{:S(2)}) collective-permute-start(bf16[2,1,32,8,1536]{4,3,2,1,0:T(8,128)(2,1)} %constant_dynamic-update-slice_fusion), channel_id=1, source_target_pairs={{0,4},{4,8},{8,12},{1,5},{5,9},{9,13},{2,6},{6,10},{10,14},{3,7},{... | collective-permute-start | bytes 4718600 | tf_op jit(solution)/shard_map/ppermute | solution.py:200
  11.2 32.7 %collective-permute-start.5 = (s32[4,15]{1,0:T(4,128)S(1)}, s32[4,15]{1,0:T(4,128)S(1)}, u32[]{:S(2)}, u32[]{:S(2)}) collective-permute-start(s32[4,15]{1,0:T(4,128)S(1)} %copy-done.11), channel_id=1, source_target_pairs={{0,4},{12,8},{1,5},{13,9},{2,6},{14,10},{3,7},{15,11},{16,20},{28,... | collective-permute-start | bytes 728 | tf_op jit(solution)/shard_map/ppermute | solution.py:202
  18.4 47.4 %collective-permute-start.8 = (bf16[2,1,256,12,128]{4,2,3,1,0:T(8,128)(2,1)}, bf16[2,1,256,12,128]{4,2,3,1,0:T(8,128)(2,1)}, u32[]{:S(2)}, u32[]{:S(2)}) collective-permute-start(bf16[2,1,256,12,128]{4,2,3,1,0:T(8,128)(2,1)} %copy.14), channel_id=1, source_target_pairs={{0,2},{2,0},{1,3},{3,1},{4,6},{6,4},{5,7},{7,5},{8,10},{10,8},{9,1... | collective-permute-start | bytes 4718600 | tf_op jit(solution)/shard_map/ppermute | solution.py:21
  30.5 4.8 %copy-start = (bf16[1,1,32,8,1536]{4,3,2,1,0:T(8,128)(2,1)S(1)}, bf16[1,1,32,8,1536]{4,3,2,1,0:T(8,128)(2,1)}, u32[]{:S(2)}) copy-start(bf16[1,1,32,8,1536]{4,3,2,1,0:T(8,128)(2,1)} %param.5) | copy-start | bytes 2359300
  35.2 1.8 %copy-start.12 = (s32[2,8]{1,0:T(2,128)S(1)}, s32[2,8]{1,0:T(2,128)}, u32[]{:S(2)}) copy-start(s32[2,8]{1,0:T(2,128)} %param.9) | copy-start | bytes 196
  51.5 14.3 %copy-start.1 = (bf16[2,2,256,12,128]{4,3,2,0,1:T(8,128)(2,1)S(1)}, bf16[2,2,256,12,128]{4,3,2,0,1:T(8,128)(2,1)}, u32[]{:S(2)}) copy-start(bf16[2,2,256,12,128]{4,3,2,0,1:T(8,128)(2,1)} %constant_dynamic-update-slice_fusion.2) | copy-start | bytes 9437188
  52.9 27.7 %collective-permute-start.2 = (bf16[2,1,32,8,1024]{4,3,2,1,0:T(8,128)(2,1)S(1)}, bf16[2,1,32,8,1024]{4,3,2,1,0:T(8,128)(2,1)S(1)}, u32[]{:S(2)}, u32[]{:S(2)}) collective-permute-start(bf16[2,1,32,8,1024]{4,3,2,1,0:T(8,128)(2,1)S(1)} %slice.30), channel_id=1, source_target_pairs={{8,4},{4,0},{9,5},{5,1},{10,6},{6,2},{11,7},{7,3},{24,20},{20,16},... | collective-permute-start | bytes 3145736 | tf_op jit(solution)/shard_map/ppermute | solution.py:244
  55.7 12.7 %copy-start.2 = (f32[256,12,128]{2,1,0:T(8,128)S(1)}, f32[256,12,128]{2,1,0:T(8,128)}, u32[]{:S(2)}) copy-start(f32[256,12,128]{2,1,0:T(8,128)} %reshape.561) | copy-start | bytes 4718596
  55.7 25.0 %collective-permute-start.3 = (bf16[2,1,32,8,1024]{4,3,2,1,0:T(8,128)(2,1)S(1)}, bf16[2,1,32,8,1024]{4,3,2,1,0:T(8,128)(2,1)S(1)}, u32[]{:S(2)}, u32[]{:S(2)}) collective-permute-start(bf16[2,1,32,8,1024]{4,3,2,1,0:T(8,128)(2,1)S(1)} %slice.31), channel_id=1, source_target_pairs={{4,8},{8,12},{5,9},{9,13},{6,10},{10,14},{7,11},{11,15},{20,24},{2... | collective-permute-start | bytes 3145736 | tf_op jit(solution)/shard_map/ppermute | solution.py:245
  56.5 38.4 %collective-permute-start.4 = (bf16[1,32,8,1536]{3,2,1,0:T(8,128)(2,1)S(1)}, bf16[1,32,8,1536]{3,2,1,0:T(8,128)(2,1)}, u32[]{:S(2)}, u32[]{:S(2)}) collective-permute-start(bf16[1,32,8,1536]{3,2,1,0:T(8,128)(2,1)S(1)} %bitcast.39), channel_id=1, source_target_pairs={{0,4},{12,8},{1,5},{13,9},{2,6},{14,10},{3,7},{15,11},{16,20},{28,... | collective-permute-start | bytes 2359304 | tf_op jit(solution)/shard_map/ppermute | solution.py:217
  80.6 2.8 %copy-start.4 = (bf16[2,1,32,8,1024]{4,3,2,1,0:T(8,128)(2,1)}, bf16[2,1,32,8,1024]{4,3,2,1,0:T(8,128)(2,1)S(1)}, u32[]{:S(2)}) copy-start(bf16[2,1,32,8,1024]{4,3,2,1,0:T(8,128)(2,1)S(1)} %collective-permute-done.2) | copy-start | bytes 3145732
  80.6 2.8 %copy-start.6 = (bf16[2,1,32,8,1024]{4,3,2,1,0:T(8,128)(2,1)}, bf16[2,1,32,8,1024]{4,3,2,1,0:T(8,128)(2,1)S(1)}, u32[]{:S(2)}) copy-start(bf16[2,1,32,8,1024]{4,3,2,1,0:T(8,128)(2,1)S(1)} %collective-permute-done.3) | copy-start | bytes 3145732
  80.7 25.7 %collective-permute-start.9 = (bf16[2,1,32,8,512]{4,3,2,1,0:T(8,128)(2,1)}, bf16[2,1,32,8,512]{4,3,2,1,0:T(8,128)(2,1)}, u32[]{:S(2)}, u32[]{:S(2)}) collective-permute-start(bf16[2,1,32,8,512]{4,3,2,1,0:T(8,128)(2,1)} %slice.35), channel_id=1, source_target_pairs={{8,4},{4,0},{9,5},{5,1},{10,6},{6,2},{11,7},{7,3},{24,20},{20,16},... | collective-permute-start | bytes 1572872 | tf_op jit(solution)/shard_map/ppermute | solution.py:244
  82.0 24.4 %collective-permute-start.10 = (bf16[2,1,32,8,512]{4,3,2,1,0:T(8,128)(2,1)S(1)}, bf16[2,1,32,8,512]{4,3,2,1,0:T(8,128)(2,1)}, u32[]{:S(2)}, u32[]{:S(2)}) collective-permute-start(bf16[2,1,32,8,512]{4,3,2,1,0:T(8,128)(2,1)S(1)} %slice.34), channel_id=1, source_target_pairs={{4,8},{8,12},{5,9},{9,13},{6,10},{10,14},{7,11},{11,15},{20,24},{2... | collective-permute-start | bytes 1572872 | tf_op jit(solution)/shard_map/ppermute | solution.py:245
  86.3 8.6 %copy-start.5 = (bf16[2,1,32,8,1024]{4,3,2,1,0:T(8,128)(2,1)S(1)}, bf16[2,1,32,8,1024]{4,3,2,1,0:T(8,128)(2,1)}, u32[]{:S(2)}) copy-start(bf16[2,1,32,8,1024]{4,3,2,1,0:T(8,128)(2,1)} %copy-done.4) | copy-start | bytes 3145732
  86.3 8.6 %copy-start.7 = (bf16[2,1,32,8,1024]{4,3,2,1,0:T(8,128)(2,1)S(1)}, bf16[2,1,32,8,1024]{4,3,2,1,0:T(8,128)(2,1)}, u32[]{:S(2)}) copy-start(bf16[2,1,32,8,1024]{4,3,2,1,0:T(8,128)(2,1)} %copy-done.6) | copy-start | bytes 3145732
  99.8 33.2 %collective-permute-start.6 = (bf16[1,256,1024]{2,1,0:T(8,128)(2,1)}, bf16[1,256,1024]{2,1,0:T(8,128)(2,1)S(1)}, u32[]{:S(2)}, u32[]{:S(2)}) collective-permute-start(bf16[1,256,1024]{2,1,0:T(8,128)(2,1)} %get-tuple-element.33), channel_id=1, source_target_pairs={{4,0},{8,12},{5,1},{9,13},{6,2},{10,14},{7,3},{11,15},{20,16},{24,... | collective-permute-start | bytes 1572872 | tf_op jit(solution)/shard_map/ppermute | solution.py:255
  101.1 26.8 %collective-permute-start.7 = (f32[1,2,4,256]{2,3,1,0:T(8,128)}, f32[1,2,4,256]{2,3,1,0:T(8,128)S(1)}, u32[]{:S(2)}, u32[]{:S(2)}) collective-permute-start(f32[1,2,4,256]{2,3,1,0:T(8,128)} %bitcast.42), channel_id=1, source_target_pairs={{4,0},{8,12},{5,1},{9,13},{6,2},{10,14},{7,3},{11,15},{20,16},{24,... | collective-permute-start | bytes 24584 | tf_op jit(solution)/shard_map/ppermute | solution.py:255
  111.1 27.2 %collective-permute-start.11 = (bf16[1,256,512]{2,1,0:T(8,128)(2,1)}, bf16[1,256,512]{2,1,0:T(8,128)(2,1)S(1)}, u32[]{:S(2)}, u32[]{:S(2)}) collective-permute-start(bf16[1,256,512]{2,1,0:T(8,128)(2,1)} %get-tuple-element.39), channel_id=1, source_target_pairs={{4,0},{8,12},{5,1},{9,13},{6,2},{10,14},{7,3},{11,15},{20,16},{24,... | collective-permute-start | bytes 786440 | tf_op jit(solution)/shard_map/ppermute | solution.py:255
  128.7 8.9 %collective-permute-start.12 = (f32[1,1,4,256]{2,3,1,0:T(8,128)}, f32[1,1,4,256]{2,3,1,0:T(8,128)S(1)}, u32[]{:S(2)}, u32[]{:S(2)}) collective-permute-start(f32[1,1,4,256]{2,3,1,0:T(8,128)} %bitcast.43), channel_id=1, source_target_pairs={{4,0},{8,12},{5,1},{9,13},{6,2},{10,14},{7,3},{11,15},{20,16},{24,... | collective-permute-start | bytes 12296 | tf_op jit(solution)/shard_map/ppermute | solution.py:255
  133.1 0.8 copy-start.9
  138.2 3.6 %copy-start.3 = (bf16[1,256,1024]{2,1,0:T(8,128)(2,1)S(1)}, bf16[1,256,1024]{2,1,0:T(8,128)(2,1)}, u32[]{:S(2)}) copy-start(bf16[1,256,1024]{2,1,0:T(8,128)(2,1)} %shard_map.58) | copy-start | bytes 1572868
  138.3 0.7 copy-start.10
  142.9 1.8 %collective-permute-start.13 = (bf16[1,32,8,768]{3,2,1,0:T(8,128)(2,1)S(1)}, bf16[1,32,8,768]{3,2,1,0:T(8,128)(2,1)S(1)}, u32[]{:S(2)}, u32[]{:S(2)}) collective-permute-start(bf16[1,32,8,768]{3,2,1,0:T(8,128)(2,1)S(1)} %constant_dynamic-slice_fusion), channel_id=1, source_target_pairs={{0,1},{1,0},{2,3},{3,2},{4,5},{5,4},{6,7},{7,6},{8,9},{9,8},{10,11... | collective-permute-start | bytes 1179656 | tf_op jit(solution)/shard_map/ppermute | solution.py:25

commit v15 on v12

--- a/solution.py
+++ b/solution.py
@@ -32,14 +32,22 @@
     return DH
 
 
-def spatial_kernel(q_ref, k_ref, v_ref, m_ref, o_ref, lse_ref, *, scale):
+def spatial_kernel(q_ref, k_ref, v_ref, *refs, scale):
+    if len(refs) == 5:
+        k2_ref, v2_ref, m_ref, o_ref, lse_ref = refs
+        read_k = lambda lanes: k_ref[:, lanes] + k2_ref[:, lanes]
+        read_v = lambda lanes: v_ref[:, lanes] + v2_ref[:, lanes]
+    else:
+        m_ref, o_ref, lse_ref = refs
+        read_k = lambda lanes: k_ref[:, lanes]
+        read_v = lambda lanes: v_ref[:, lanes]
     allowed = m_ref[...] > 0
     for head in range(q_ref.shape[-1] // DH):
         lanes = slice(head * DH, (head + 1) * DH)
         scores = (
             lax.dot_general(
                 q_ref[:, lanes],
-                k_ref[:, lanes],
+                read_k(lanes),
                 (((1,), (1,)), ((), ())),
                 preferred_element_type=jnp.float32,
             )
@@ -50,13 +58,13 @@
         weights = jnp.exp(limited - maxima)
         totals = jnp.sum(weights, axis=-1, keepdims=True)
         result = jnp.dot(
-            weights.astype(jnp.bfloat16), v_ref[:, lanes], preferred_element_type=jnp.float32
+            weights.astype(jnp.bfloat16), read_v(lanes), preferred_element_type=jnp.float32
         )
         o_ref[:, lanes] = (result / totals).astype(o_ref.dtype)
         lse_ref[:, head : head + 1] = maxima + jnp.log(totals)
 
 
-def spatial_attention(query_flat, key_value_flat, mask, scale, out_dtype=jnp.float32):
+def spatial_attention(query_flat, key_value_flat, mask, scale, out_dtype=jnp.float32, second=None):
     frames, query_count, model_width = query_flat.shape
     key_count = key_value_flat.shape[2]
     head_count = model_width // DH
@@ -69,6 +77,13 @@
             pl.BlockSpec((None, query_count, width), lambda f, g: (f, 0, g)),
             pl.BlockSpec((None, None, key_count, width), lambda f, g: (0, f, 0, g)),
             pl.BlockSpec((None, None, key_count, width), lambda f, g: (1, f, 0, g)),
+        ]
+        + [
+            pl.BlockSpec((None, None, key_count, width), lambda f, g: (0, f, 0, g)),
+            pl.BlockSpec((None, None, key_count, width), lambda f, g: (1, f, 0, g)),
+        ]
+        * (second is not None)
+        + [
             pl.BlockSpec((query_count, key_count), lambda f, g: (0, 0)),
         ],
         out_specs=[
@@ -85,7 +100,7 @@
             bytes_accessed=2 * model_width * frames * (query_count + 2 * key_count)
             + 4 * frames * query_count * model_width,
         ),
-    )(query_flat, key_value_flat, key_value_flat, mask)
+    )(query_flat, key_value_flat, key_value_flat, *([second, second] if second is not None else []), mask)
 
 
 def combine_kernel(*refs):
@@ -204,14 +219,14 @@
         scale,
     )
 
-    two_away = jnp.where(
-        index <= 1,
-        lax.ppermute(from_right, "lon", [(2, 1), (1, 0)]),
-        lax.ppermute(from_left, "lon", [(1, 2), (2, 3)]),
-    )
+    toward_left = lax.ppermute(from_right, "lon", [(2, 1), (1, 0)])
+    toward_right = lax.ppermute(from_left, "lon", [(1, 2), (2, 3)])
     held_q, _ = lax.optimization_barrier((own_q, from_left))
     guest_q = lax.ppermute(held_q, "lon", [(0, 1), (3, 2)])
-    near_part, two_away, guest_q = lax.optimization_barrier((near_part, two_away, guest_q))
+    near_part, toward_left, toward_right, guest_q = lax.optimization_barrier(
+        (near_part, toward_left, toward_right, guest_q)
+    )
+    two_away = jnp.where(index <= 1, toward_left, toward_right)
 
     guest_device = jnp.where(index == 1, 0, count - 1)
     far_block = (index + 2) % count
@@ -226,10 +241,11 @@
     far_keys = flat_keys([two_away])
     guest_out, guest_lse = spatial_attention(
         guest_q.reshape(frames, lat_rows * columns, model_width),
-        far_keys,
+        flat_keys([toward_left]),
         expand_mask(guest_active, lat_rows),
         scale,
         jnp.bfloat16,
+        flat_keys([toward_right]),
     )
     lse_shape = guest_lse.shape
     returned, returned_lse = lax.ppermute(

time: 131 us -> 142 us (1.084)
  waiting for transfers between devices: 19.3 us -> 28.4 us
  local copies, waits for them, and re-layouts: 41.6 us -> 46.6 us
  starting transfers between devices: 27.3 us -> 22.5 us
    ppermute x2, waiting for transfers between devices: 0.01 us -> 5.88 us  [the longest x1 5.88 us: spatial_line_of_four(): toward_left = lax.ppermute(from_right, 'lon', [(2, 1), (1, 0)])]
    ppermute x2, waiting for transfers between devices: 13.2 us -> 17.2 us  [spatial_line_of_four(): lax.ppermute((guest_out, jnp.swapaxes(guest_lse, 2, 3)), 'lon', [(1, 0),...]
    ppermute x1, starting transfers between devices: 9.24 us -> 5.41 us  [spatial_line_of_four(): guest_q = lax.ppermute(held_q, 'lon', [(0, 1), (3, 2)])]
    convert_element_type x2, local copies, waits for them, and re-layouts: 2.03 us -> 4.91 us  [temporal_attention(): return result.astype(jnp.bfloat16)]
    reshape x0 -> x1, other arithmetic: none -> 2.74 us  [flat_keys(): return joined.reshape(two, frames, lat_rows * cols, model_width)]
    unnamed x16 -> x18, local copies, waits for them, and re-layouts: 4.8 us -> 6.42 us
  transfers between devices with their start and end apart: 10 -> 10, of which waited for: 3 -> 4; matrix products, arithmetic and copies ran while one was open for 40% -> 40% of each run, Pallas kernels for 11% -> 10%
where the time goes in v15:
time: 142 us; the launch traced here: 141 us
  local copies, waits for them, and re-layouts  46.6 us (33%)
  waiting for transfers between devices  28.4 us (20%)
  Pallas kernels  24.6 us (17%)
  starting transfers between devices  22.5 us (16%)
  other arithmetic  19.1 us (13%)
    pallas_call x3, Pallas kernels, spatial_attention(): pl.pallas_call(functools.partial(spatial_kernel, scale=scale), grid=(fram...  19.3 us
    ppermute x2, waiting for transfers between devices, spatial_line_of_four(): lax.ppermute((guest_out, jnp.swapaxes(guest_lse, 2, 3)), 'lon', [(1, 0),...  17.2 us
    reshape x3, local copies, waits for them, and re-layouts, expand_mask(): return jnp.broadcast_to(active[None, :, None, :].astype(jnp.float32), (la...  14 us
    broadcast_in_dim x3, local copies, waits for them, and re-layouts, expand_mask(): jnp.broadcast_to(active[None, :, None, :].astype(jnp.float32), (lat_rows,...  7.4 us
    ppermute x1, starting transfers between devices, spatial_line_of_four(): from_left = lax.ppermute(key_value, 'lon', [(0, 1), (1, 2), (2, 3)])  6.71 us
    unnamed x18, local copies, waits for them, and re-layouts  6.42 us
    ppermute x1, waiting for transfers between devices, spatial_line_of_four(): toward_left = lax.ppermute(from_right, 'lon', [(2, 1), (1, 0)])  5.88 us
    ppermute x1, starting transfers between devices, spatial_line_of_four(): guest_q = lax.ppermute(held_q, 'lon', [(0, 1), (3, 2)])  5.41 us
  transfers between devices with their start and end apart: 10, of which 4 were waited for; matrix products, arithmetic and copies ran while one was open for 40% of the time, Pallas kernels for 10%

profile of v15, /device:TPU:0, one launch (start us, length us, event | category | flops | bytes accessed | tf_op | source)
XLA Modules:
  0.0 141.4 jit_solution(10414443910289866170)
XLA Ops:
  0.0 2.2 %constant_dynamic-update-slice_fusion.1 = bf16[2,1,32,8,1536]{4,3,2,1,0:T(8,128)(2,1)} fusion(bf16[1,1,32,8,1536]{4,3,2,1,0:T(8,128)(2,1)} %param.6), kind=kLoop, calls=%fused_computation.27 | loop fusion | bytes 1572864
  2.2 0.9 constant_dynamic-update-slice_fusion
  3.1 1.3 collective-permute-start.1
  4.4 6.7 %collective-permute-start = (bf16[2,1,32,8,1536]{4,3,2,1,0:T(8,128)(2,1)}, bf16[2,1,32,8,1536]{4,3,2,1,0:T(8,128)(2,1)}, u32[]{:S(2)}, u32[]{:S(2)}) collective-permute-start(bf16[2,1,32,8,1536]{4,3,2,1,0:T(8,128)(2,1)} %constant_dynamic-update-slice_fusion), channel_id=1, source_target_pairs={{0,4},{4,8},{8,12},{1,5},{5,9},{9,13},{2,6},{6,10},{10,14},{3,7},{... | collective-permute-start | bytes 4718600 | tf_op jit(solution)/shard_map/ppermute | solution.py:206
  11.1 2.8 %collective-permute-start.5 = (s32[4,15]{1,0:T(4,128)S(1)}, s32[4,15]{1,0:T(4,128)S(1)}, u32[]{:S(2)}, u32[]{:S(2)}) collective-permute-start(s32[4,15]{1,0:T(4,128)S(1)} %copy-done.6), channel_id=1, source_target_pairs={{0,4},{12,8},{1,5},{13,9},{2,6},{14,10},{3,7},{15,11},{16,20},{28,... | collective-permute-start | bytes 728 | tf_op jit(solution)/shard_map/ppermute | solution.py:208
  13.9 2.9 %reshape.563 = bf16[2,1,256,12,128]{4,3,2,0,1:T(8,128)(2,1)S(1)} reshape(bf16[2,1,32,8,1536]{4,3,2,1,0:T(8,128)(2,1)} %constant_dynamic-update-slice_fusion) | data formatting | bytes 3145728 | tf_op jit(solution)/shard_map/reshape | solution.py:314
  16.8 1.6 %copy.12 = bf16[2,1,256,12,128]{4,2,3,1,0:T(8,128)(2,1)} copy(bf16[2,1,256,12,128]{4,3,2,0,1:T(8,128)(2,1)S(1)} %reshape.563) | data formatting | bytes 3145728 | tf_op jit(solution)/shard_map/reshape | solution.py:314
  18.4 1.5 %collective-permute-start.8 = (bf16[2,1,256,12,128]{4,2,3,1,0:T(8,128)(2,1)}, bf16[2,1,256,12,128]{4,2,3,1,0:T(8,128)(2,1)}, u32[]{:S(2)}, u32[]{:S(2)}) collective-permute-start(bf16[2,1,256,12,128]{4,2,3,1,0:T(8,128)(2,1)} %copy.12), channel_id=1, source_target_pairs={{0,2},{2,0},{1,3},{3,1},{4,6},{6,4},{5,7},{7,5},{8,10},{10,8},{9,1... | collective-permute-start | bytes 4718600 | tf_op jit(solution)/shard_map/ppermute | solution.py:21
  19.9 0.1 copy.11
  20.0 0.1 pad_add_fusion
  20.1 0.1 broadcast_in_dim.35
  20.2 0.1 and.236
  20.3 0.1 add_select_fusion.2
  20.4 0.1 fusion.6
  20.5 0.1 add_select_fusion
  20.6 2.5 %broadcast_in_dim.36 = f32[32,8,32,24]{3,2,1,0:T(8,128)} broadcast(f32[8,24]{1,0:T(8,128)S(1)} %and_convert_fusion.1), dimensions={1,3} | broadcast | bytes 787200 | tf_op jit(solution)/shard_map/broadcast_in_dim | solution.py:184
  23.0 4.6 %reshape.556.refs_0_ = f32[256,768]{1,0:T(8,128)} reshape(f32[32,8,32,24]{3,2,1,0:T(8,128)} %broadcast_in_dim.36) | data formatting | bytes 1572864 | tf_op jit(solution)/shard_map/reshape | solution.py:186
  27.7 0.3 fusion.8
  28.0 2.5 %broadcast_in_dim.37 = f32[32,8,32,8]{3,2,1,0:T(8,128)} broadcast(f32[8,8]{1,0:T(8,128)S(1)} %convert_element_type.69), dimensions={1,3} | broadcast | bytes 262400 | tf_op jit(solution)/shard_map/broadcast_in_dim | solution.py:184
  30.4 4.7 %reshape.558.refs_0_ = f32[256,256]{1,0:T(8,128)} reshape(f32[32,8,32,8]{3,2,1,0:T(8,128)} %broadcast_in_dim.37) | data formatting | bytes 524288 | tf_op jit(solution)/shard_map/reshape | solution.py:186
  35.1 2.7 %reshape.565 = f32[256,12,128]{2,1,0:T(8,128)} reshape(bf16[1,1,32,8,1536]{4,3,2,1,0:T(8,128)(2,1)} %param.5) | data formatting | bytes 2359296 | tf_op jit(solution)/shard_map/convert_element_type | solution.py:143
  37.8 0.1 tile.10
  37.9 0.6 gather_fusion
  38.5 1.7 %constant_dynamic-update-slice_fusion.2 = bf16[2,2,256,12,128]{4,3,2,0,1:T(8,128)(2,1)} fusion(bf16[2,1,256,12,128]{4,3,2,0,1:T(8,128)(2,1)S(1)} %reshape.563), kind=kLoop, calls=%fused_computation.28 | loop fusion | bytes 3670016
  40.2 0.1 compare_or_fusion
  40.3 3.6 %collective-permute-done.5 = s32[4,15]{1,0:T(4,128)S(1)} collective-permute-done((s32[4,15]{1,0:T(4,128)S(1)}, s32[4,15]{1,0:T(4,128)S(1)}, u32[]{:S(2)}, u32[]{:S(2)}) %collective-permute-start.5) | collective-permute-done | bytes 272 | tf_op jit(solution)/shard_map/ppermute | solution.py:208
  44.0 0.3 fusion.10
  44.3 2.5 %broadcast_in_dim.39 = f32[32,8,32,8]{3,2,1,0:T(8,128)} broadcast(f32[8,8]{1,0:T(8,128)S(1)} %and_convert_fusion), dimensions={1,3} | broadcast | bytes 262400 | tf_op jit(solution)/shard_map/broadcast_in_dim | solution.py:184
  46.8 4.7 %reshape.562.refs_2_ = f32[256,256]{1,0:T(8,128)} reshape(f32[32,8,32,8]{3,2,1,0:T(8,128)} %broadcast_in_dim.39) | data formatting | bytes 524288 | tf_op jit(solution)/shard_map/reshape | solution.py:186
  51.4 0.0 collective-permute-done
  51.4 5.4 %collective-permute-start.4 = (bf16[1,32,8,1536]{3,2,1,0:T(8,128)(2,1)}, bf16[1,32,8,1536]{3,2,1,0:T(8,128)(2,1)}, u32[]{:S(2)}, u32[]{:S(2)}) collective-permute-start(bf16[1,32,8,1536]{3,2,1,0:T(8,128)(2,1)} %bitcast.5), channel_id=1, source_target_pairs={{0,4},{12,8},{1,5},{13,9},{2,6},{14,10},{3,7},{15,11},{16,20},{28,... | collective-permute-start | bytes 2359304 | tf_op jit(solution)/shard_map/ppermute | solution.py:225
  56.8 0.7 collective-permute-start.3
  57.6 0.0 collective-permute-done.1
  57.6 1.5 %collective-permute-start.2 = (bf16[2,1,32,8,1536]{4,3,2,1,0:T(8,128)(2,1)}, bf16[2,1,32,8,1536]{4,3,2,1,0:T(8,128)(2,1)S(1)}, u32[]{:S(2)}, u32[]{:S(2)}) collective-permute-start(bf16[2,1,32,8,1536]{4,3,2,1,0:T(8,128)(2,1)} %collective-permute-done.1), channel_id=1, source_target_pairs={{8,4},{4,0},{9,5},{5,1},{10,6},{6,2},{11,7},{7,3},{24,20},{20,16},... | collective-permute-start | bytes 4718600 | tf_op jit(solution)/shard_map/ppermute | solution.py:222
  59.1 0.0 collective-permute-done.8
  59.1 3.8 %copy_dynamic-update-slice_fusion = bf16[2,2,256,12,128]{4,3,2,0,1:T(8,128)(2,1)} fusion(bf16[2,2,256,12,128]{4,3,2,0,1:T(8,128)(2,1)} %constant_dynamic-update-slice_fusion.2, bf16[2,1,256,12,128]{4,2,3,1,0:T(8,128)(2,1)} %collective-permute-done.8), kind=kLoop, calls=%fused_computation.4 | loop fusion | bytes 3670016 | tf_op jit(solution)/shard_map/concatenate | solution.py:318
  62.9 3.0 %multiply_reduce_fusion.1 = f32[2,256,12]{2,1,0:T(8,128)S(1)} fusion(bf16[2,2,256,12,128]{4,3,2,0,1:T(8,128)(2,1)} %copy_dynamic-update-slice_fusion, f32[256,12,128]{2,1,0:T(8,128)S(1)} %copy-done.3), kind=kLoop, calls=%fused_computation.3 | loop fusion | flops 2353152 | bytes 3170304 | tf_op jit(solution)/shard_map/reduce_sum | solution.py:145
  65.9 0.1 fusion.2
  66.0 0.1 fusion.3
  66.2 2.9 %multiply_reduce_fusion = f32[256,12,128]{2,1,0:T(8,128)S(1)} fusion(bf16[2,2,256,12,128]{4,3,2,0,1:T(8,128)(2,1)S(1)} %copy-done.2, f32[2,256,12]{2,1,0:T(8,128)S(1)} %get-tuple-element.30), kind=kLoop, calls=%fused_computation.2 | loop fusion | flops 1966080 | bytes 3170304 | tf_op jit(solution)/shard_map/reduce_sum | solution.py:153
  69.1 1.5 %reduce-precision_convert_fusion = bf16[256,12,128]{2,1,0:T(8,128)(2,1)} fusion(f32[256,12,128]{2,1,0:T(8,128)S(1)} %multiply_reduce_fusion, f32[256,12]{1,0:T(8,128)S(1)} %get-tuple-element.29), kind=kLoop, calls=%fused_computation.5 | loop fusion | flops 1179648 | bytes 2371584 | tf_op jit(solution)/shard_map/convert_element_type | solution.py:155
  70.7 2.5 %copy.14 = bf16[256,12,128]{0,2,1:T(8,128)(2,1)} copy(bf16[256,12,128]{2,1,0:T(8,128)(2,1)} %reduce-precision_convert_fusion) | data formatting | bytes 1572864 | tf_op jit(solution)/shard_map/convert_element_type | solution.py:155
  73.2 2.4 %copy.15.refs_6_ = bf16[1,256,1536]{2,1,0:T(8,128)(2,1)} copy(bf16[1,256,1536]{1,2,0:T(8,128)(2,1)} %bitcast.36) | data formatting | bytes 1572864 | tf_op jit(solution)/shard_map/convert_element_type | solution.py:155
  75.6 4.8 %pad_maximum_fusion = bf16[2,1,32,24,1536]{4,3,2,1,0:T(8,128)(2,1)} fusion(bf16[2,1,32,8,1536]{4,3,2,1,0:T(8,128)(2,1)} %collective-permute-done.1, bf16[2,1,32,8,1536]{4,3,2,1,0:T(8,128)(2,1)} %constant_dynamic-update-slice_fusion, bf16[2,1,32,8,1536]{4,3,2,1,0:T(8,128)(2,1)} %collective-permute-done), kind=kLoop, calls=%fused_computation.1 | loop fusion | flops 14155776 | bytes 9437184 | tf_op jit(solution)/shard_map/concatenate | solution.py:190
  80.3 8.5 %shard_map.55 = (f32[1,256,1536]{2,1,0:T(8,128)}, f32[1,3,256,4]{3,2,1,0:T(8,128)}) custom-call(bf16[1,256,1536]{2,1,0:T(8,128)(2,1)} %bitcast.q_ref, bf16[2,1,768,1536]{3,2,1,0:T(8,128)(2,1)} %bitcast.30, bf16[2,1,768,1536]{3,2,1,0:T(8,128)(2,1)} %bitcast.31, f32[256,768]{1,0:T(8,128)} %reshape.556.refs_0_), custom_call_target="tpu_custom_call" | custom-call | flops 1207959552 | bytes 7077888 | tf_op jit(solution)/shard_map/pallas_call | solution.py:73
  88.8 0.0 collective-permute-done.4
  88.8 5.9 %collective-permute-done.2 = bf16[2,1,32,8,1536]{4,3,2,1,0:T(8,128)(2,1)S(1)} collective-permute-done((bf16[2,1,32,8,1536]{4,3,2,1,0:T(8,128)(2,1)}, bf16[2,1,32,8,1536]{4,3,2,1,0:T(8,128)(2,1)S(1)}, u32[]{:S(2)}, u32[]{:S(2)}) %collective-permute-start.2) | collective-permute-done | bytes 1572896 | tf_op jit(solution)/shard_map/ppermute | solution.py:222
  94.7 0.0 collective-permute-done.3
  94.7 1.1 copy-done.1
  95.9 0.6 copy-done
  96.4 5.5 %shard_map.57 = (bf16[1,256,1536]{2,1,0:T(8,128)(2,1)}, f32[1,3,256,4]{3,2,1,0:T(8,128)}) custom-call(bf16[1,256,1536]{2,1,0:T(8,128)(2,1)} %bitcast.7.q_ref, bf16[2,1,256,1536]{3,2,1,0:T(8,128)(2,1)} %bitcast.34, bf16[2,1,256,1536]{3,2,1,0:T(8,128)(2,1)} %bitcast.35, bf16[2,1,256,1536]{3,2,1,0:T(8,128)(2,1)} %bitcast.32, ...), custom_call_target="tpu_custom_call" | custom-call | flops 402653184 | bytes 3932160 | tf_op jit(solution)/shard_map/pallas_call | solution.py:73
  101.9 1.3 collective-permute-start.6
  103.2 1.3 collective-permute-start.7
  104.5 2.7 %select_bitcast_fusion.k_ref.v_ref = bf16[2,1,256,1536]{3,2,1,0:T(8,128)(2,1)} fusion(bf16[2,1,32,8,1536]{4,3,2,1,0:T(8,128)(2,1)} %copy-done.1, bf16[2,1,32,8,1536]{4,3,2,1,0:T(8,128)(2,1)} %copy-done, pred[]{:T(512)S(6)} %le.15), kind=kLoop, calls=%fused_computation.6 | loop fusion | flops 786432 | bytes 4718593 | tf_op jit(solution)/shard_map/reshape | solution.py:192
  107.2 5.3 %shard_map.56 = (f32[1,256,1536]{2,1,0:T(8,128)}, f32[1,3,256,4]{3,2,1,0:T(8,128)}) custom-call(bf16[1,256,1536]{2,1,0:T(8,128)(2,1)} %bitcast.q_ref, bf16[2,1,256,1536]{3,2,1,0:T(8,128)(2,1)} %select_bitcast_fusion.k_ref.v_ref, bf16[2,1,256,1536]{3,2,1,0:T(8,128)(2,1)} %select_bitcast_fusion.k_ref.v_ref, f32[256,256]{1,0:T(8,128)} %reshape.558.refs_0_), custom_call_target="tpu_custom_call" | custom-call | flops 402653184 | bytes 3932160 | tf_op jit(solution)/shard_map/pallas_call | solution.py:73
  112.5 17.2 %collective-permute-done.7 = f32[1,3,4,256]{2,3,1,0:T(8,128)S(1)} collective-permute-done((f32[1,3,4,256]{2,3,1,0:T(8,128)}, f32[1,3,4,256]{2,3,1,0:T(8,128)S(1)}, u32[]{:S(2)}, u32[]{:S(2)}) %collective-permute-start.7) | collective-permute-done | bytes 12320 | tf_op jit(solution)/shard_map/ppermute | solution.py:251
  129.7 0.8 select_bitcast_fusion.1.refs_5_
  130.5 0.0 collective-permute-done.6.refs_4_
  130.5 0.9 copy-done.4
  131.4 5.3 %shard_map.58 = bf16[1,256,1536]{2,1,0:T(8,128)(2,1)} custom-call(f32[1,256,1536]{2,1,0:T(8,128)} %get-tuple-element.20.refs_0_, f32[1,3,256,4]{3,2,1,0:T(8,128)} %get-tuple-element.21.refs_1_, f32[1,256,1536]{2,1,0:T(8,128)} %get-tuple-element.24.refs_2_, f32[1,3,256,4]{3,2,1,0:T(8,128)} %get-tuple-element.25.refs_3_, bf16[1,256,1536]{2,1,0:T(8,128)(2,1)} %copy-done.4, ...), custom_call_target="tpu_custom_call" | custom-call | tf_op jit(solution)/shard_map/pallas_call | solution.py:133
  136.7 1.0 constant_dynamic-slice_fusion
  137.7 0.1 collective-permute-start.9
  137.8 1.7 %collective-permute-done.9 = bf16[1,32,8,768]{3,2,1,0:T(8,128)(2,1)S(1)} collective-permute-done((bf16[1,32,8,768]{3,2,1,0:T(8,128)(2,1)S(1)}, bf16[1,32,8,768]{3,2,1,0:T(8,128)(2,1)S(1)}, u32[]{:S(2)}, u32[]{:S(2)}) %collective-permute-start.9) | collective-permute-done | bytes 393248 | tf_op jit(solution)/shard_map/ppermute | solution.py:25
  139.5 1.9 %fusion.1 = bf16[1,32,8,768]{3,2,1,0:T(8,128)(2,1)} fusion(bf16[1,32,8,768]{3,2,1,0:T(8,128)(2,1)S(1)} %collective-permute-done.9, bf16[1,32,8,1536]{3,2,1,0:T(8,128)(2,1)} %bitcast.38, s32[]{:T(128)S(6)} %select_n.230, pred[]{:T(512)S(6)} %eq.73), kind=kLoop, calls=%fused_computation.10 | loop fusion | flops 1572864 | bytes 1179653 | tf_op jit(solution)/shard_map/convert_element_type | solution.py:341
  (30 shorter events, 0.2 us)
Async XLA Ops:
  0.0 2.2 %copy-start.5 = (bf16[1,1,32,8,1536]{4,3,2,1,0:T(8,128)(2,1)S(1)}, bf16[1,1,32,8,1536]{4,3,2,1,0:T(8,128)(2,1)}, u32[]{:S(2)}) copy-start(bf16[1,1,32,8,1536]{4,3,2,1,0:T(8,128)(2,1)} %param.7) | copy-start | bytes 2359300
  0.0 11.1 %copy-start.6 = (s32[4,15]{1,0:T(4,128)S(1)}, s32[4,15]{1,0:T(4,128)}, u32[]{:S(2)}) copy-start(s32[4,15]{1,0:T(4,128)} %param.8) | copy-start | bytes 724
  3.1 54.5 %collective-permute-start.1 = (bf16[2,1,32,8,1536]{4,3,2,1,0:T(8,128)(2,1)}, bf16[2,1,32,8,1536]{4,3,2,1,0:T(8,128)(2,1)}, u32[]{:S(2)}, u32[]{:S(2)}) collective-permute-start(bf16[2,1,32,8,1536]{4,3,2,1,0:T(8,128)(2,1)} %constant_dynamic-update-slice_fusion), channel_id=1, source_target_pairs={{12,8},{8,4},{4,0},{13,9},{9,5},{5,1},{14,10},{10,6},{6,2},{15,11}... | collective-permute-start | bytes 4718600 | tf_op jit(solution)/shard_map/ppermute | solution.py:207
  4.4 47.0 %collective-permute-start = (bf16[2,1,32,8,1536]{4,3,2,1,0:T(8,128)(2,1)}, bf16[2,1,32,8,1536]{4,3,2,1,0:T(8,128)(2,1)}, u32[]{:S(2)}, u32[]{:S(2)}) collective-permute-start(bf16[2,1,32,8,1536]{4,3,2,1,0:T(8,128)(2,1)} %constant_dynamic-update-slice_fusion), channel_id=1, source_target_pairs={{0,4},{4,8},{8,12},{1,5},{5,9},{9,13},{2,6},{6,10},{10,14},{3,7},{... | collective-permute-start | bytes 4718600 | tf_op jit(solution)/shard_map/ppermute | solution.py:206
  11.1 32.8 %collective-permute-start.5 = (s32[4,15]{1,0:T(4,128)S(1)}, s32[4,15]{1,0:T(4,128)S(1)}, u32[]{:S(2)}, u32[]{:S(2)}) collective-permute-start(s32[4,15]{1,0:T(4,128)S(1)} %copy-done.6), channel_id=1, source_target_pairs={{0,4},{12,8},{1,5},{13,9},{2,6},{14,10},{3,7},{15,11},{16,20},{28,... | collective-permute-start | bytes 728 | tf_op jit(solution)/shard_map/ppermute | solution.py:208
  18.4 40.7 %collective-permute-start.8 = (bf16[2,1,256,12,128]{4,2,3,1,0:T(8,128)(2,1)}, bf16[2,1,256,12,128]{4,2,3,1,0:T(8,128)(2,1)}, u32[]{:S(2)}, u32[]{:S(2)}) collective-permute-start(bf16[2,1,256,12,128]{4,2,3,1,0:T(8,128)(2,1)} %copy.12), channel_id=1, source_target_pairs={{0,2},{2,0},{1,3},{3,1},{4,6},{6,4},{5,7},{7,5},{8,10},{10,8},{9,1... | collective-permute-start | bytes 4718600 | tf_op jit(solution)/shard_map/ppermute | solution.py:21
  35.1 2.7 %copy-start.7 = (s32[2,8]{1,0:T(2,128)S(1)}, s32[2,8]{1,0:T(2,128)}, u32[]{:S(2)}) copy-start(s32[2,8]{1,0:T(2,128)} %param.9) | copy-start | bytes 196
  51.4 11.5 %copy-start.3 = (f32[256,12,128]{2,1,0:T(8,128)S(1)}, f32[256,12,128]{2,1,0:T(8,128)}, u32[]{:S(2)}) copy-start(f32[256,12,128]{2,1,0:T(8,128)} %reshape.565) | copy-start | bytes 4718596
  51.4 37.4 %collective-permute-start.4 = (bf16[1,32,8,1536]{3,2,1,0:T(8,128)(2,1)}, bf16[1,32,8,1536]{3,2,1,0:T(8,128)(2,1)}, u32[]{:S(2)}, u32[]{:S(2)}) collective-permute-start(bf16[1,32,8,1536]{3,2,1,0:T(8,128)(2,1)} %bitcast.5), channel_id=1, source_target_pairs={{0,4},{12,8},{1,5},{13,9},{2,6},{14,10},{3,7},{15,11},{16,20},{28,... | collective-permute-start | bytes 2359304 | tf_op jit(solution)/shard_map/ppermute | solution.py:225
  56.8 37.9 %collective-permute-start.3 = (bf16[2,1,32,8,1536]{4,3,2,1,0:T(8,128)(2,1)}, bf16[2,1,32,8,1536]{4,3,2,1,0:T(8,128)(2,1)S(1)}, u32[]{:S(2)}, u32[]{:S(2)}) collective-permute-start(bf16[2,1,32,8,1536]{4,3,2,1,0:T(8,128)(2,1)} %collective-permute-done), channel_id=1, source_target_pairs={{4,8},{8,12},{5,9},{9,13},{6,10},{10,14},{7,11},{11,15},{20,24},{2... | collective-permute-start | bytes 4718600 | tf_op jit(solution)/shard_map/ppermute | solution.py:223
  57.6 37.1 %collective-permute-start.2 = (bf16[2,1,32,8,1536]{4,3,2,1,0:T(8,128)(2,1)}, bf16[2,1,32,8,1536]{4,3,2,1,0:T(8,128)(2,1)S(1)}, u32[]{:S(2)}, u32[]{:S(2)}) collective-permute-start(bf16[2,1,32,8,1536]{4,3,2,1,0:T(8,128)(2,1)} %collective-permute-done.1), channel_id=1, source_target_pairs={{8,4},{4,0},{9,5},{5,1},{10,6},{6,2},{11,7},{7,3},{24,20},{20,16},... | collective-permute-start | bytes 4718600 | tf_op jit(solution)/shard_map/ppermute | solution.py:222
  62.9 3.3 %copy-start.2 = (bf16[2,2,256,12,128]{4,3,2,0,1:T(8,128)(2,1)S(1)}, bf16[2,2,256,12,128]{4,3,2,0,1:T(8,128)(2,1)}, u32[]{:S(2)}) copy-start(bf16[2,2,256,12,128]{4,3,2,0,1:T(8,128)(2,1)} %copy_dynamic-update-slice_fusion) | copy-start | bytes 9437188
  94.7 1.1 copy-start.1
  94.7 1.7 %copy-start = (bf16[2,1,32,8,1536]{4,3,2,1,0:T(8,128)(2,1)}, bf16[2,1,32,8,1536]{4,3,2,1,0:T(8,128)(2,1)S(1)}, u32[]{:S(2)}) copy-start(bf16[2,1,32,8,1536]{4,3,2,1,0:T(8,128)(2,1)S(1)} %collective-permute-done.3) | copy-start | bytes 4718596
  101.9 28.6 %collective-permute-start.6 = (bf16[1,256,1536]{2,1,0:T(8,128)(2,1)}, bf16[1,256,1536]{2,1,0:T(8,128)(2,1)S(1)}, u32[]{:S(2)}, u32[]{:S(2)}) collective-permute-start(bf16[1,256,1536]{2,1,0:T(8,128)(2,1)} %get-tuple-element.27), channel_id=1, source_target_pairs={{4,0},{8,12},{5,1},{9,13},{6,2},{10,14},{7,3},{11,15},{20,16},{24,... | collective-permute-start | bytes 2359304 | tf_op jit(solution)/shard_map/ppermute | solution.py:251
  103.2 26.5 %collective-permute-start.7 = (f32[1,3,4,256]{2,3,1,0:T(8,128)}, f32[1,3,4,256]{2,3,1,0:T(8,128)S(1)}, u32[]{:S(2)}, u32[]{:S(2)}) collective-permute-start(f32[1,3,4,256]{2,3,1,0:T(8,128)} %bitcast.40), channel_id=1, source_target_pairs={{4,0},{8,12},{5,1},{9,13},{6,2},{10,14},{7,3},{11,15},{20,16},{24,... | collective-permute-start | bytes 36872 | tf_op jit(solution)/shard_map/ppermute | solution.py:251
  130.5 0.9 copy-start.4
  137.7 1.8 %collective-permute-start.9 = (bf16[1,32,8,768]{3,2,1,0:T(8,128)(2,1)S(1)}, bf16[1,32,8,768]{3,2,1,0:T(8,128)(2,1)S(1)}, u32[]{:S(2)}, u32[]{:S(2)}) collective-permute-start(bf16[1,32,8,768]{3,2,1,0:T(8,128)(2,1)S(1)} %constant_dynamic-slice_fusion), channel_id=1, source_target_pairs={{0,1},{1,0},{2,3},{3,2},{4,5},{5,4},{6,7},{7,6},{8,9},{9,8},{10,11... | collective-permute-start | bytes 1179656 | tf_op jit(solution)/shard_map/ppermute | solution.py:25

commit v16 on v12

--- a/solution.py
+++ b/solution.py
@@ -242,7 +242,7 @@
 
     far_active = window_mask(own_cols, far_cols, own_map, total_cols, lat_rows)
     far_part = spatial_attention(query_flat, far_keys, expand_mask(far_active, lat_rows), scale)
-    return [near_part, far_part, (returned, returned_lse)]
+    return [near_part, far_part, (returned, returned_lse)], from_left
 
 
 def local(queries, keys, values, window_map, frame_valid):
@@ -261,7 +261,7 @@
     per_column_map = jnp.repeat(window_map, BLK, axis=0)
     full_ring = ext_count >= total_cols and WIN * BLK <= total_cols
     if full_ring and lon_count == 4:
-        partials = spatial_line_of_four(own_q, key_value, window_map, scale)
+        partials, first_hop = spatial_line_of_four(own_q, key_value, window_map, scale)
     else:
         if full_ring:
             extended = jnp.concatenate(line_gather(key_value, "lon"), axis=3)
@@ -296,6 +296,8 @@
     tm_count = lax.axis_size("tm")
     tm_index = lax.axis_index("tm")
     key_value_rows = key_value.reshape(2, frames, token_count, head_count, DH)
+    if full_ring and lon_count == 4:
+        key_value_rows, _ = lax.optimization_barrier((key_value_rows, first_hop))
     pieces = [key_value_rows]
     for step_by in range(1, tm_count):
         pieces.append(shifted(key_value_rows, "tm", step_by))

time: 131 us -> 145 us (1.11)
  waiting for transfers between devices: 19.3 us -> 37.5 us
  local copies, waits for them, and re-layouts: 41.6 us -> 38.4 us
  starting transfers between devices: 27.3 us -> 24.8 us
    ppermute x1, waiting for transfers between devices: 0.01 us -> 12.6 us  [spatial_line_of_four(): lax.ppermute(from_right, 'lon', [(2, 1), (1, 0)])]
    ppermute x1, waiting for transfers between devices: 0.01 us -> 6.16 us  [spatial_line_of_four(): from_left = lax.ppermute(key_value, 'lon', [(0, 1), (1, 2), (2, 3)])]
    ppermute x1, waiting for transfers between devices: 4.32 us -> 0.01 us  [spatial_line_of_four(): guest_map = lax.ppermute(window_map, 'lon', [(0, 1), (3, 2)])]
    ppermute x1, waiting for transfers between devices: 0.01 us -> 4.31 us  [shifted(): lax.ppermute(value, axis, [(i, (i + by) % count) for i in range(count)])]
    ppermute x1, starting transfers between devices: 9.24 us -> 5.29 us  [spatial_line_of_four(): guest_q = lax.ppermute(held_q, 'lon', [(0, 1), (3, 2)])]
    ppermute x1, starting transfers between devices: 2.73 us -> 4.55 us  [spatial_line_of_four(): guest_map = lax.ppermute(window_map, 'lon', [(0, 1), (3, 2)])]
    reduce_sum x1, other arithmetic: 2.82 us -> 1.23 us  [temporal_attention(): scores = jnp.sum(q32[:, None] * k32[None], axis=-1) * scale]
    reshape x2 -> x1, local copies, waits for them, and re-layouts: 4.48 us -> 2.9 us  [local(): key_value_rows = key_value.reshape(2, frames, token_count, head_count, DH)]
  transfers between devices with their start and end apart: 10 -> 10, of which waited for: 3 -> 5; matrix products, arithmetic and copies ran while one was open for 40% -> 35% of each run, Pallas kernels for 11% -> 10%
where the time goes in v16:
time: 145 us; the launch traced here: 144 us
  local copies, waits for them, and re-layouts  38.4 us (26%)
  waiting for transfers between devices  37.5 us (26%)
  starting transfers between devices  24.8 us (17%)
  Pallas kernels  24.3 us (17%)
  other arithmetic  18.9 us (13%)
    pallas_call x3, Pallas kernels, spatial_attention(): pl.pallas_call(functools.partial(spatial_kernel, scale=scale), grid=(fram...  18.9 us
    reshape x3, local copies, waits for them, and re-layouts, expand_mask(): return jnp.broadcast_to(active[None, :, None, :].astype(jnp.float32), (la...  14 us
    ppermute x2, waiting for transfers between devices, spatial_line_of_four(): lax.ppermute((guest_out, jnp.swapaxes(guest_lse, 2, 3)), 'lon', [(1, 0),...  12.7 us
    ppermute x1, waiting for transfers between devices, spatial_line_of_four(): lax.ppermute(from_right, 'lon', [(2, 1), (1, 0)])  12.6 us
    broadcast_in_dim x3, local copies, waits for them, and re-layouts, expand_mask(): jnp.broadcast_to(active[None, :, None, :].astype(jnp.float32), (lat_rows,...  7.36 us
    ppermute x1, starting transfers between devices, spatial_line_of_four(): from_left = lax.ppermute(key_value, 'lon', [(0, 1), (1, 2), (2, 3)])  6.29 us
    ppermute x1, waiting for transfers between devices, spatial_line_of_four(): from_left = lax.ppermute(key_value, 'lon', [(0, 1), (1, 2), (2, 3)])  6.16 us
    pallas_call x1, Pallas kernels, combine_partials(): pl.pallas_call(combine_kernel, grid=(frames, groups), in_specs=[big, smal...  5.39 us
  transfers between devices with their start and end apart: 10, of which 5 were waited for; matrix products, arithmetic and copies ran while one was open for 35% of the time, Pallas kernels for 10%

profile of v16, /device:TPU:0, one launch (start us, length us, event | category | flops | bytes accessed | tf_op | source)
XLA Modules:
  0.0 144.2 jit_solution(12270739698155950675)
XLA Ops:
  0.0 2.1 %constant_dynamic-update-slice_fusion.1 = bf16[2,1,32,8,1536]{4,3,2,1,0:T(8,128)(2,1)} fusion(bf16[1,1,32,8,1536]{4,3,2,1,0:T(8,128)(2,1)} %param.6), kind=kLoop, calls=%fused_computation.27 | loop fusion | bytes 1572864
  2.2 0.0 copy-done.3
  2.2 0.9 constant_dynamic-update-slice_fusion
  3.1 6.3 %collective-permute-start = (bf16[2,1,32,8,1536]{4,3,2,1,0:T(8,128)(2,1)}, bf16[2,1,32,8,1536]{4,3,2,1,0:T(8,128)(2,1)}, u32[]{:S(2)}, u32[]{:S(2)}) collective-permute-start(bf16[2,1,32,8,1536]{4,3,2,1,0:T(8,128)(2,1)} %constant_dynamic-update-slice_fusion), channel_id=1, source_target_pairs={{0,4},{4,8},{8,12},{1,5},{5,9},{9,13},{2,6},{6,10},{10,14},{3,7},{... | collective-permute-start | bytes 4718600 | tf_op jit(solution)/shard_map/ppermute | solution.py:191
  9.4 1.3 collective-permute-start.1
  10.7 0.0 copy-done.4
  10.7 4.5 %collective-permute-start.5 = (s32[4,15]{1,0:T(4,128)S(1)}, s32[4,15]{1,0:T(4,128)S(1)}, u32[]{:S(2)}, u32[]{:S(2)}) collective-permute-start(s32[4,15]{1,0:T(4,128)S(1)} %copy-done.4), channel_id=1, source_target_pairs={{0,4},{12,8},{1,5},{13,9},{2,6},{14,10},{3,7},{15,11},{16,20},{28,... | collective-permute-start | bytes 728 | tf_op jit(solution)/shard_map/ppermute | solution.py:193
  15.3 2.9 %reshape.555 = bf16[2,1,256,12,128]{4,3,2,0,1:T(8,128)(2,1)S(1)} reshape(bf16[2,1,32,8,1536]{4,3,2,1,0:T(8,128)(2,1)} %constant_dynamic-update-slice_fusion) | data formatting | bytes 3145728 | tf_op jit(solution)/shard_map/reshape | solution.py:298
  18.2 0.1 tile.10
  18.3 1.8 %reshape.557 = f32[256,12,128]{2,1,0:T(8,128)} reshape(bf16[1,1,32,8,1536]{4,3,2,1,0:T(8,128)(2,1)S(1)} %copy-done.2) | data formatting | bytes 2359296 | tf_op jit(solution)/shard_map/convert_element_type | solution.py:128
  20.2 0.1 pad_add_fusion
  20.3 0.1 broadcast_in_dim.35
  20.3 0.1 and.236
  20.4 0.1 copy.11
  20.6 0.1 add_select_fusion.2
  20.7 0.1 fusion.6
  20.8 2.4 %broadcast_in_dim.36 = f32[32,8,32,24]{3,2,1,0:T(8,128)} broadcast(f32[8,24]{1,0:T(8,128)S(1)} %and_convert_fusion.1), dimensions={1,3} | broadcast | bytes 787200 | tf_op jit(solution)/shard_map/broadcast_in_dim | solution.py:169
  23.2 4.6 %reshape.550.m_ref = f32[256,768]{1,0:T(8,128)} reshape(f32[32,8,32,24]{3,2,1,0:T(8,128)} %broadcast_in_dim.36) | data formatting | bytes 1572864 | tf_op jit(solution)/shard_map/reshape | solution.py:171
  27.9 0.1 add_select_fusion
  27.9 0.3 fusion.8
  28.2 2.5 %broadcast_in_dim.37 = f32[32,8,32,8]{3,2,1,0:T(8,128)} broadcast(f32[8,8]{1,0:T(8,128)S(1)} %convert_element_type.69), dimensions={1,3} | broadcast | bytes 262400 | tf_op jit(solution)/shard_map/broadcast_in_dim | solution.py:169
  30.7 4.7 %reshape.552.m_ref = f32[256,256]{1,0:T(8,128)} reshape(f32[32,8,32,8]{3,2,1,0:T(8,128)} %broadcast_in_dim.37) | data formatting | bytes 524288 | tf_op jit(solution)/shard_map/reshape | solution.py:171
  35.4 0.6 gather_fusion
  36.0 6.2 %collective-permute-done = bf16[2,1,32,8,1536]{4,3,2,1,0:T(8,128)(2,1)} collective-permute-done((bf16[2,1,32,8,1536]{4,3,2,1,0:T(8,128)(2,1)}, bf16[2,1,32,8,1536]{4,3,2,1,0:T(8,128)(2,1)}, u32[]{:S(2)}, u32[]{:S(2)}) %collective-permute-start) | collective-permute-done | bytes 1572896 | tf_op jit(solution)/shard_map/ppermute | solution.py:191
  42.1 1.6 %copy.12 = bf16[2,1,256,12,128]{4,2,3,1,0:T(8,128)(2,1)} copy(bf16[2,1,256,12,128]{4,3,2,0,1:T(8,128)(2,1)S(1)} %reshape.555) | data formatting | bytes 3145728 | tf_op jit(solution)/shard_map/optimization_barrier | solution.py:300
  43.7 1.5 %collective-permute-start.8 = (bf16[2,1,256,12,128]{4,2,3,1,0:T(8,128)(2,1)}, bf16[2,1,256,12,128]{4,2,3,1,0:T(8,128)(2,1)}, u32[]{:S(2)}, u32[]{:S(2)}) collective-permute-start(bf16[2,1,256,12,128]{4,2,3,1,0:T(8,128)(2,1)} %copy.12), channel_id=1, source_target_pairs={{0,2},{2,0},{1,3},{3,1},{4,6},{6,4},{5,7},{7,5},{8,10},{10,8},{9,1... | collective-permute-start | bytes 4718600 | tf_op jit(solution)/shard_map/ppermute | solution.py:21
  45.3 0.1 compare_or_fusion
  45.3 0.0 collective-permute-done.5
  45.4 0.3 fusion.10
  45.7 2.5 %broadcast_in_dim.39 = f32[32,8,32,8]{3,2,1,0:T(8,128)} broadcast(f32[8,8]{1,0:T(8,128)S(1)} %and_convert_fusion), dimensions={1,3} | broadcast | bytes 262400 | tf_op jit(solution)/shard_map/broadcast_in_dim | solution.py:169
  48.1 4.7 %reshape.554.m_ref = f32[256,256]{1,0:T(8,128)} reshape(f32[32,8,32,8]{3,2,1,0:T(8,128)} %broadcast_in_dim.39) | data formatting | bytes 524288 | tf_op jit(solution)/shard_map/reshape | solution.py:171
  52.8 5.3 %collective-permute-start.4 = (bf16[1,32,8,1536]{3,2,1,0:T(8,128)(2,1)S(1)}, bf16[1,32,8,1536]{3,2,1,0:T(8,128)(2,1)}, u32[]{:S(2)}, u32[]{:S(2)}) collective-permute-start(bf16[1,32,8,1536]{3,2,1,0:T(8,128)(2,1)S(1)} %bitcast.35), channel_id=1, source_target_pairs={{0,4},{12,8},{1,5},{13,9},{2,6},{14,10},{3,7},{15,11},{16,20},{28,... | collective-permute-start | bytes 2359304 | tf_op jit(solution)/shard_map/ppermute | solution.py:213
  58.1 1.8 %collective-permute-start.3 = (bf16[2,1,32,8,1536]{4,3,2,1,0:T(8,128)(2,1)}, bf16[2,1,32,8,1536]{4,3,2,1,0:T(8,128)(2,1)}, u32[]{:S(2)}, u32[]{:S(2)}) collective-permute-start(bf16[2,1,32,8,1536]{4,3,2,1,0:T(8,128)(2,1)} %collective-permute-done), channel_id=1, source_target_pairs={{4,8},{8,12},{5,9},{9,13},{6,10},{10,14},{7,11},{11,15},{20,24},{2... | collective-permute-start | bytes 4718600 | tf_op jit(solution)/shard_map/ppermute | solution.py:210
  59.9 0.0 collective-permute-done.1
  59.9 1.5 %collective-permute-start.2 = (bf16[2,1,32,8,1536]{4,3,2,1,0:T(8,128)(2,1)}, bf16[2,1,32,8,1536]{4,3,2,1,0:T(8,128)(2,1)}, u32[]{:S(2)}, u32[]{:S(2)}) collective-permute-start(bf16[2,1,32,8,1536]{4,3,2,1,0:T(8,128)(2,1)} %collective-permute-done.1), channel_id=1, source_target_pairs={{8,4},{4,0},{9,5},{5,1},{10,6},{6,2},{11,7},{7,3},{24,20},{20,16},... | collective-permute-start | bytes 4718600 | tf_op jit(solution)/shard_map/ppermute | solution.py:209
  61.4 4.8 %pad_maximum_fusion = bf16[2,1,32,24,1536]{4,3,2,1,0:T(8,128)(2,1)} fusion(bf16[2,1,32,8,1536]{4,3,2,1,0:T(8,128)(2,1)} %collective-permute-done.1, bf16[2,1,32,8,1536]{4,3,2,1,0:T(8,128)(2,1)} %constant_dynamic-update-slice_fusion, bf16[2,1,32,8,1536]{4,3,2,1,0:T(8,128)(2,1)} %collective-permute-done), kind=kLoop, calls=%fused_computation.1 | loop fusion | flops 14155776 | bytes 9437184 | tf_op jit(solution)/shard_map/concatenate | solution.py:175
  66.2 8.4 %shard_map.55 = (f32[1,256,1536]{2,1,0:T(8,128)}, f32[1,3,256,4]{3,2,1,0:T(8,128)}) custom-call(bf16[1,256,1536]{2,1,0:T(8,128)(2,1)} %bitcast.33, bf16[2,1,768,1536]{3,2,1,0:T(8,128)(2,1)} %bitcast.27, bf16[2,1,768,1536]{3,2,1,0:T(8,128)(2,1)} %bitcast.28, f32[256,768]{1,0:T(8,128)} %reshape.550.m_ref), custom_call_target="tpu_custom_call" | custom-call | flops 1207959552 | bytes 7077888 | tf_op jit(solution)/shard_map/pallas_call | solution.py:65
  74.6 0.4 constant_dynamic-update-slice_fusion.2
  75.0 4.3 %collective-permute-done.8 = bf16[2,1,256,12,128]{4,2,3,1,0:T(8,128)(2,1)} collective-permute-done((bf16[2,1,256,12,128]{4,2,3,1,0:T(8,128)(2,1)}, bf16[2,1,256,12,128]{4,2,3,1,0:T(8,128)(2,1)}, u32[]{:S(2)}, u32[]{:S(2)}) %collective-permute-start.8) | collective-permute-done | bytes 1572896 | tf_op jit(solution)/shard_map/ppermute | solution.py:21
  79.3 2.6 %copy_dynamic-update-slice_fusion = bf16[2,2,256,12,128]{4,3,2,0,1:T(8,128)(2,1)S(1)} fusion(bf16[2,2,256,12,128]{4,3,2,0,1:T(8,128)(2,1)S(1)} %constant_dynamic-update-slice_fusion.2, bf16[2,1,256,12,128]{4,2,3,1,0:T(8,128)(2,1)} %collective-permute-done.8), kind=kLoop, calls=%fused_computation.4 | loop fusion | bytes 3670016 | tf_op jit(solution)/shard_map/concatenate | solution.py:304
  81.9 1.2 multiply_reduce_fusion.1
  83.1 0.7 copy-done
  83.8 0.1 fusion.2
  84.0 0.1 fusion.3
  84.1 0.0 collective-permute-done.3
  84.1 12.6 %collective-permute-done.2 = bf16[2,1,32,8,1536]{4,3,2,1,0:T(8,128)(2,1)} collective-permute-done((bf16[2,1,32,8,1536]{4,3,2,1,0:T(8,128)(2,1)}, bf16[2,1,32,8,1536]{4,3,2,1,0:T(8,128)(2,1)}, u32[]{:S(2)}, u32[]{:S(2)}) %collective-permute-start.2) | collective-permute-done | bytes 1572896 | tf_op jit(solution)/shard_map/ppermute | solution.py:209
  96.8 2.8 %broadcast_select_fusion = bf16[2,1,32,8,1536]{4,3,2,1,0:T(8,128)(2,1)} fusion(bf16[2,1,32,8,1536]{4,3,2,1,0:T(8,128)(2,1)} %collective-permute-done.2, bf16[2,1,32,8,1536]{4,3,2,1,0:T(8,128)(2,1)} %collective-permute-done.3, pred[]{:T(512)S(6)} %le.15), kind=kLoop, calls=%fused_computation.6 | loop fusion | flops 786432 | bytes 4718593 | tf_op jit(solution)/shard_map/jit(_where)/select_n | solution.py:207
  99.6 0.0 collective-permute-done.4
  99.6 5.2 %shard_map.57 = (bf16[1,256,1536]{2,1,0:T(8,128)(2,1)}, f32[1,3,256,4]{3,2,1,0:T(8,128)}) custom-call(bf16[1,256,1536]{2,1,0:T(8,128)(2,1)} %bitcast.7.q_ref, bf16[2,1,256,1536]{3,2,1,0:T(8,128)(2,1)} %bitcast.29, bf16[2,1,256,1536]{3,2,1,0:T(8,128)(2,1)} %bitcast.30, f32[256,256]{1,0:T(8,128)} %reshape.554.m_ref), custom_call_target="tpu_custom_call" | custom-call | flops 402653184 | bytes 3932160 | tf_op jit(solution)/shard_map/pallas_call | solution.py:65
  104.7 1.3 collective-permute-start.6
  106.0 4.2 %multiply_reduce_fusion = f32[256,12,128]{2,1,0:T(8,128)S(1)} fusion(bf16[2,2,256,12,128]{4,3,2,0,1:T(8,128)(2,1)} %copy-done, f32[2,256,12]{2,1,0:T(8,128)S(1)} %get-tuple-element.30), kind=kLoop, calls=%fused_computation.2 | loop fusion | flops 1966080 | bytes 3170304 | tf_op jit(solution)/shard_map/reduce_sum | solution.py:138
  110.2 1.3 collective-permute-start.7
  111.5 0.7 reduce-precision_convert_fusion
  112.3 5.3 %shard_map.56 = (f32[1,256,1536]{2,1,0:T(8,128)}, f32[1,3,256,4]{3,2,1,0:T(8,128)}) custom-call(bf16[1,256,1536]{2,1,0:T(8,128)(2,1)} %bitcast.34, bf16[2,1,256,1536]{3,2,1,0:T(8,128)(2,1)} %bitcast.31, bf16[2,1,256,1536]{3,2,1,0:T(8,128)(2,1)} %bitcast.32, f32[256,256]{1,0:T(8,128)} %reshape.552.m_ref), custom_call_target="tpu_custom_call" | custom-call | flops 402653184 | bytes 3932160 | tf_op jit(solution)/shard_map/pallas_call | solution.py:65
  117.6 0.8 copy.14
  118.4 1.2 copy.15.refs_6_
  119.6 12.7 %collective-permute-done.7 = f32[1,3,4,256]{2,3,1,0:T(8,128)} collective-permute-done((f32[1,3,4,256]{2,3,1,0:T(8,128)}, f32[1,3,4,256]{2,3,1,0:T(8,128)}, u32[]{:S(2)}, u32[]{:S(2)}) %collective-permute-start.7) | collective-permute-done | bytes 12320 | tf_op jit(solution)/shard_map/ppermute | solution.py:235
  132.2 1.8 %select_bitcast_fusion.refs_5_ = f32[1,3,256,4]{3,2,1,0:T(8,128)} fusion(f32[1,3,4,256]{2,3,1,0:T(8,128)} %collective-permute-done.7, pred[]{:T(512)S(6)} %and.248), kind=kLoop, calls=%fused_computation.11 | loop fusion | flops 3072 | bytes 24577 | tf_op jit(solution)/shard_map/jit(_where)/select_n | solution.py:240
  134.0 0.0 collective-permute-done.6.refs_4_
  134.0 5.4 %shard_map.58 = bf16[1,256,1536]{2,1,0:T(8,128)(2,1)} custom-call(f32[1,256,1536]{2,1,0:T(8,128)} %get-tuple-element.20.refs_0_, f32[1,3,256,4]{3,2,1,0:T(8,128)} %get-tuple-element.21.refs_1_, f32[1,256,1536]{2,1,0:T(8,128)} %get-tuple-element.23.refs_2_, f32[1,3,256,4]{3,2,1,0:T(8,128)} %get-tuple-element.24.refs_3_, ...), custom_call_target="tpu_custom_call" | custom-call | tf_op jit(solution)/shard_map/pallas_call | solution.py:118
  139.4 1.0 constant_dynamic-slice_fusion
  140.5 0.1 collective-permute-start.9
  140.5 1.7 %collective-permute-done.9 = bf16[1,32,8,768]{3,2,1,0:T(8,128)(2,1)S(1)} collective-permute-done((bf16[1,32,8,768]{3,2,1,0:T(8,128)(2,1)S(1)}, bf16[1,32,8,768]{3,2,1,0:T(8,128)(2,1)S(1)}, u32[]{:S(2)}, u32[]{:S(2)}) %collective-permute-start.9) | collective-permute-done | bytes 393248 | tf_op jit(solution)/shard_map/ppermute | solution.py:25
  142.3 1.9 %fusion.1 = bf16[1,32,8,768]{3,2,1,0:T(8,128)(2,1)} fusion(bf16[1,32,8,768]{3,2,1,0:T(8,128)(2,1)S(1)} %collective-permute-done.9, bf16[1,32,8,1536]{3,2,1,0:T(8,128)(2,1)} %bitcast.38, s32[]{:T(128)S(6)} %select_n.230, pred[]{:T(512)S(6)} %eq.73), kind=kLoop, calls=%fused_computation.10 | loop fusion | flops 1572864 | bytes 1179653 | tf_op jit(solution)/shard_map/convert_element_type | solution.py:327
  (26 shorter events, 0.2 us)
Async XLA Ops:
  0.0 2.2 %copy-start.3 = (bf16[1,1,32,8,1536]{4,3,2,1,0:T(8,128)(2,1)S(1)}, bf16[1,1,32,8,1536]{4,3,2,1,0:T(8,128)(2,1)}, u32[]{:S(2)}) copy-start(bf16[1,1,32,8,1536]{4,3,2,1,0:T(8,128)(2,1)} %param.7) | copy-start | bytes 2359300
  0.0 10.7 %copy-start.4 = (s32[4,15]{1,0:T(4,128)S(1)}, s32[4,15]{1,0:T(4,128)}, u32[]{:S(2)}) copy-start(s32[4,15]{1,0:T(4,128)} %param.8) | copy-start | bytes 724
  3.1 15.1 %copy-start.5 = (s32[2,8]{1,0:T(2,128)S(1)}, s32[2,8]{1,0:T(2,128)}, u32[]{:S(2)}) copy-start(s32[2,8]{1,0:T(2,128)} %param.9) | copy-start | bytes 196
  3.1 15.2 %copy-start.2 = (bf16[1,1,32,8,1536]{4,3,2,1,0:T(8,128)(2,1)S(1)}, bf16[1,1,32,8,1536]{4,3,2,1,0:T(8,128)(2,1)}, u32[]{:S(2)}) copy-start(bf16[1,1,32,8,1536]{4,3,2,1,0:T(8,128)(2,1)} %param.5) | copy-start | bytes 2359300
  3.1 39.0 %collective-permute-start = (bf16[2,1,32,8,1536]{4,3,2,1,0:T(8,128)(2,1)}, bf16[2,1,32,8,1536]{4,3,2,1,0:T(8,128)(2,1)}, u32[]{:S(2)}, u32[]{:S(2)}) collective-permute-start(bf16[2,1,32,8,1536]{4,3,2,1,0:T(8,128)(2,1)} %constant_dynamic-update-slice_fusion), channel_id=1, source_target_pairs={{0,4},{4,8},{8,12},{1,5},{5,9},{9,13},{2,6},{6,10},{10,14},{3,7},{... | collective-permute-start | bytes 4718600 | tf_op jit(solution)/shard_map/ppermute | solution.py:191
  9.4 50.5 %collective-permute-start.1 = (bf16[2,1,32,8,1536]{4,3,2,1,0:T(8,128)(2,1)}, bf16[2,1,32,8,1536]{4,3,2,1,0:T(8,128)(2,1)}, u32[]{:S(2)}, u32[]{:S(2)}) collective-permute-start(bf16[2,1,32,8,1536]{4,3,2,1,0:T(8,128)(2,1)} %constant_dynamic-update-slice_fusion), channel_id=1, source_target_pairs={{12,8},{8,4},{4,0},{13,9},{9,5},{5,1},{14,10},{10,6},{6,2},{15,11}... | collective-permute-start | bytes 4718600 | tf_op jit(solution)/shard_map/ppermute | solution.py:192
  10.7 34.6 %collective-permute-start.5 = (s32[4,15]{1,0:T(4,128)S(1)}, s32[4,15]{1,0:T(4,128)S(1)}, u32[]{:S(2)}, u32[]{:S(2)}) collective-permute-start(s32[4,15]{1,0:T(4,128)S(1)} %copy-done.4), channel_id=1, source_target_pairs={{0,4},{12,8},{1,5},{13,9},{2,6},{14,10},{3,7},{15,11},{16,20},{28,... | collective-permute-start | bytes 728 | tf_op jit(solution)/shard_map/ppermute | solution.py:193
  43.7 35.6 %collective-permute-start.8 = (bf16[2,1,256,12,128]{4,2,3,1,0:T(8,128)(2,1)}, bf16[2,1,256,12,128]{4,2,3,1,0:T(8,128)(2,1)}, u32[]{:S(2)}, u32[]{:S(2)}) collective-permute-start(bf16[2,1,256,12,128]{4,2,3,1,0:T(8,128)(2,1)} %copy.12), channel_id=1, source_target_pairs={{0,2},{2,0},{1,3},{3,1},{4,6},{6,4},{5,7},{7,5},{8,10},{10,8},{9,1... | collective-permute-start | bytes 4718600 | tf_op jit(solution)/shard_map/ppermute | solution.py:21
  52.8 46.8 %collective-permute-start.4 = (bf16[1,32,8,1536]{3,2,1,0:T(8,128)(2,1)S(1)}, bf16[1,32,8,1536]{3,2,1,0:T(8,128)(2,1)}, u32[]{:S(2)}, u32[]{:S(2)}) collective-permute-start(bf16[1,32,8,1536]{3,2,1,0:T(8,128)(2,1)S(1)} %bitcast.35), channel_id=1, source_target_pairs={{0,4},{12,8},{1,5},{13,9},{2,6},{14,10},{3,7},{15,11},{16,20},{28,... | collective-permute-start | bytes 2359304 | tf_op jit(solution)/shard_map/ppermute | solution.py:213
  58.1 26.0 %collective-permute-start.3 = (bf16[2,1,32,8,1536]{4,3,2,1,0:T(8,128)(2,1)}, bf16[2,1,32,8,1536]{4,3,2,1,0:T(8,128)(2,1)}, u32[]{:S(2)}, u32[]{:S(2)}) collective-permute-start(bf16[2,1,32,8,1536]{4,3,2,1,0:T(8,128)(2,1)} %collective-permute-done), channel_id=1, source_target_pairs={{4,8},{8,12},{5,9},{9,13},{6,10},{10,14},{7,11},{11,15},{20,24},{2... | collective-permute-start | bytes 4718600 | tf_op jit(solution)/shard_map/ppermute | solution.py:210
  59.9 36.9 %collective-permute-start.2 = (bf16[2,1,32,8,1536]{4,3,2,1,0:T(8,128)(2,1)}, bf16[2,1,32,8,1536]{4,3,2,1,0:T(8,128)(2,1)}, u32[]{:S(2)}, u32[]{:S(2)}) collective-permute-start(bf16[2,1,32,8,1536]{4,3,2,1,0:T(8,128)(2,1)} %collective-permute-done.1), channel_id=1, source_target_pairs={{8,4},{4,0},{9,5},{5,1},{10,6},{6,2},{11,7},{7,3},{24,20},{20,16},... | collective-permute-start | bytes 4718600 | tf_op jit(solution)/shard_map/ppermute | solution.py:209
  75.0 6.9 %copy-start.1 = (f32[256,12,128]{2,1,0:T(8,128)S(1)}, f32[256,12,128]{2,1,0:T(8,128)}, u32[]{:S(2)}) copy-start(f32[256,12,128]{2,1,0:T(8,128)} %reshape.557) | copy-start | bytes 4718596
  81.9 1.9 %copy-start = (bf16[2,2,256,12,128]{4,3,2,0,1:T(8,128)(2,1)}, bf16[2,2,256,12,128]{4,3,2,0,1:T(8,128)(2,1)S(1)}, u32[]{:S(2)}) copy-start(bf16[2,2,256,12,128]{4,3,2,0,1:T(8,128)(2,1)S(1)} %copy_dynamic-update-slice_fusion) | copy-start | bytes 9437188
  104.7 29.3 %collective-permute-start.6 = (bf16[1,256,1536]{2,1,0:T(8,128)(2,1)}, bf16[1,256,1536]{2,1,0:T(8,128)(2,1)}, u32[]{:S(2)}, u32[]{:S(2)}) collective-permute-start(bf16[1,256,1536]{2,1,0:T(8,128)(2,1)} %get-tuple-element.26), channel_id=1, source_target_pairs={{4,0},{8,12},{5,1},{9,13},{6,2},{10,14},{7,3},{11,15},{20,16},{24,... | collective-permute-start | bytes 2359304 | tf_op jit(solution)/shard_map/ppermute | solution.py:235
  110.2 22.0 %collective-permute-start.7 = (f32[1,3,4,256]{2,3,1,0:T(8,128)}, f32[1,3,4,256]{2,3,1,0:T(8,128)}, u32[]{:S(2)}, u32[]{:S(2)}) collective-permute-start(f32[1,3,4,256]{2,3,1,0:T(8,128)} %bitcast.8), channel_id=1, source_target_pairs={{4,0},{8,12},{5,1},{9,13},{6,2},{10,14},{7,3},{11,15},{20,16},{24,... | collective-permute-start | bytes 36872 | tf_op jit(solution)/shard_map/ppermute | solution.py:235
  140.5 1.8 %collective-permute-start.9 = (bf16[1,32,8,768]{3,2,1,0:T(8,128)(2,1)S(1)}, bf16[1,32,8,768]{3,2,1,0:T(8,128)(2,1)S(1)}, u32[]{:S(2)}, u32[]{:S(2)}) collective-permute-start(bf16[1,32,8,768]{3,2,1,0:T(8,128)(2,1)S(1)} %constant_dynamic-slice_fusion), channel_id=1, source_target_pairs={{0,1},{1,0},{2,3},{3,2},{4,5},{5,4},{6,7},{7,6},{8,9},{9,8},{10,11... | collective-permute-start | bytes 1179656 | tf_op jit(solution)/shard_map/ppermute | solution.py:25

commit v17 on v12

--- a/solution.py
+++ b/solution.py
@@ -26,7 +26,7 @@
 
 
 def group_width(model_width):
-    for width in (512, 384, 256):
+    for width in (768, 512, 384, 256):
         if model_width % width == 0:
             return width
     return DH

time: 131 us -> 127 us (0.969)
  waiting for transfers between devices: 19.3 us -> 17.2 us
  Pallas kernels: 24.2 us -> 22.4 us
    ppermute x2, waiting for transfers between devices: 13.2 us -> 11.2 us  [spatial_line_of_four(): lax.ppermute((guest_out, jnp.swapaxes(guest_lse, 2, 3)), 'lon', [(1, 0),...]
  transfers between devices with their start and end apart: 10 -> 10, of which waited for: 3 -> 3; matrix products, arithmetic and copies ran while one was open for 40% -> 41% of each run, Pallas kernels for 11% -> 11%
where the time goes in v17:
time: 127 us
  local copies, waits for them, and re-layouts  41.6 us (33%)
  starting transfers between devices  27.3 us (21%)
  Pallas kernels  22.4 us (18%)
  other arithmetic  17.9 us (14%)
  waiting for transfers between devices  17.2 us (14%)
    pallas_call x3, Pallas kernels, spatial_attention(): pl.pallas_call(functools.partial(spatial_kernel, scale=scale), grid=(fram...  17.7 us
    reshape x3, local copies, waits for them, and re-layouts, expand_mask(): return jnp.broadcast_to(active[None, :, None, :].astype(jnp.float32), (la...  14.1 us
    ppermute x2, waiting for transfers between devices, spatial_line_of_four(): lax.ppermute((guest_out, jnp.swapaxes(guest_lse, 2, 3)), 'lon', [(1, 0),...  11.2 us
    ppermute x1, starting transfers between devices, spatial_line_of_four(): guest_q = lax.ppermute(held_q, 'lon', [(0, 1), (3, 2)])  9.24 us
    broadcast_in_dim x3, local copies, waits for them, and re-layouts, expand_mask(): jnp.broadcast_to(active[None, :, None, :].astype(jnp.float32), (lat_rows,...  7.38 us
    ppermute x1, starting transfers between devices, spatial_line_of_four(): from_left = lax.ppermute(key_value, 'lon', [(0, 1), (1, 2), (2, 3)])  6.77 us
    unnamed x16, local copies, waits for them, and re-layouts  4.8 us
    concatenate x1, other arithmetic, flat_keys(): joined = jnp.concatenate(blocks, axis=3)  4.78 us
  transfers between devices with their start and end apart: 10, of which 3 were waited for; matrix products, arithmetic and copies ran while one was open for 41% of the time, Pallas kernels for 11%

profile of v17, /device:TPU:0, one launch (start us, length us, event | category | flops | bytes accessed | tf_op | source)
XLA Modules:
  0.0 126.6 jit_solution(257133610730889856)
XLA Ops:
  0.0 2.1 %constant_dynamic-update-slice_fusion.1 = bf16[2,1,32,8,1536]{4,3,2,1,0:T(8,128)(2,1)} fusion(bf16[1,1,32,8,1536]{4,3,2,1,0:T(8,128)(2,1)} %param.6), kind=kLoop, calls=%fused_computation.27 | loop fusion | bytes 1572864
  2.1 1.0 constant_dynamic-update-slice_fusion
  3.1 1.3 %collective-permute-start.1 = (bf16[2,1,32,8,1536]{4,3,2,1,0:T(8,128)(2,1)}, bf16[2,1,32,8,1536]{4,3,2,1,0:T(8,128)(2,1)}, u32[]{:S(2)}, u32[]{:S(2)}) collective-permute-start(bf16[2,1,32,8,1536]{4,3,2,1,0:T(8,128)(2,1)} %constant_dynamic-update-slice_fusion), channel_id=1, source_target_pairs={{12,8},{8,4},{4,0},{13,9},{9,5},{5,1},{14,10},{10,6},{6,2},{15,11}... | collective-permute-start | bytes 4718600 | tf_op jit(solution)/shard_map/ppermute | solution.py:192
  4.4 6.8 %collective-permute-start = (bf16[2,1,32,8,1536]{4,3,2,1,0:T(8,128)(2,1)}, bf16[2,1,32,8,1536]{4,3,2,1,0:T(8,128)(2,1)}, u32[]{:S(2)}, u32[]{:S(2)}) collective-permute-start(bf16[2,1,32,8,1536]{4,3,2,1,0:T(8,128)(2,1)} %constant_dynamic-update-slice_fusion), channel_id=1, source_target_pairs={{0,4},{4,8},{8,12},{1,5},{5,9},{9,13},{2,6},{6,10},{10,14},{3,7},{... | collective-permute-start | bytes 4718600 | tf_op jit(solution)/shard_map/ppermute | solution.py:191
  11.2 0.0 copy-done.4
  11.2 2.7 %collective-permute-start.5 = (s32[4,15]{1,0:T(4,128)S(1)}, s32[4,15]{1,0:T(4,128)S(1)}, u32[]{:S(2)}, u32[]{:S(2)}) collective-permute-start(s32[4,15]{1,0:T(4,128)S(1)} %copy-done.4), channel_id=1, source_target_pairs={{0,4},{12,8},{1,5},{13,9},{2,6},{14,10},{3,7},{15,11},{16,20},{28,... | collective-permute-start | bytes 728 | tf_op jit(solution)/shard_map/ppermute | solution.py:193
  13.9 2.9 %reshape.555 = bf16[2,1,256,12,128]{4,3,2,0,1:T(8,128)(2,1)S(1)} reshape(bf16[2,1,32,8,1536]{4,3,2,1,0:T(8,128)(2,1)} %constant_dynamic-update-slice_fusion) | data formatting | bytes 3145728 | tf_op jit(solution)/shard_map/reshape | solution.py:298
  16.8 1.6 %copy.12 = bf16[2,1,256,12,128]{4,2,3,1,0:T(8,128)(2,1)} copy(bf16[2,1,256,12,128]{4,3,2,0,1:T(8,128)(2,1)S(1)} %reshape.555) | data formatting | bytes 3145728 | tf_op jit(solution)/shard_map/reshape | solution.py:298
  18.4 1.5 %collective-permute-start.8 = (bf16[2,1,256,12,128]{4,2,3,1,0:T(8,128)(2,1)}, bf16[2,1,256,12,128]{4,2,3,1,0:T(8,128)(2,1)}, u32[]{:S(2)}, u32[]{:S(2)}) collective-permute-start(bf16[2,1,256,12,128]{4,2,3,1,0:T(8,128)(2,1)} %copy.12), channel_id=1, source_target_pairs={{0,2},{2,0},{1,3},{3,1},{4,6},{6,4},{5,7},{7,5},{8,10},{10,8},{9,1... | collective-permute-start | bytes 4718600 | tf_op jit(solution)/shard_map/ppermute | solution.py:21
  20.0 0.1 copy.11
  20.1 0.1 pad_add_fusion
  20.1 0.1 broadcast_in_dim.35
  20.2 0.1 and.236
  20.3 0.1 add_select_fusion.2
  20.4 0.1 fusion.6
  20.5 2.5 %broadcast_in_dim.36 = f32[32,8,32,24]{3,2,1,0:T(8,128)} broadcast(f32[8,24]{1,0:T(8,128)S(1)} %and_convert_fusion.1), dimensions={1,3} | broadcast | bytes 787200 | tf_op jit(solution)/shard_map/broadcast_in_dim | solution.py:169
  22.9 4.6 %reshape.550.m_ref = f32[256,768]{1,0:T(8,128)} reshape(f32[32,8,32,24]{3,2,1,0:T(8,128)} %broadcast_in_dim.36) | data formatting | bytes 1572864 | tf_op jit(solution)/shard_map/reshape | solution.py:171
  27.6 0.1 add_select_fusion
  27.7 0.3 fusion.8
  28.0 2.5 %broadcast_in_dim.37 = f32[32,8,32,8]{3,2,1,0:T(8,128)} broadcast(f32[8,8]{1,0:T(8,128)S(1)} %convert_element_type.69), dimensions={1,3} | broadcast | bytes 262400 | tf_op jit(solution)/shard_map/broadcast_in_dim | solution.py:169
  30.5 4.8 %reshape.552.m_ref = f32[256,256]{1,0:T(8,128)} reshape(f32[32,8,32,8]{3,2,1,0:T(8,128)} %broadcast_in_dim.37) | data formatting | bytes 524288 | tf_op jit(solution)/shard_map/reshape | solution.py:171
  35.2 1.8 %reshape.557 = f32[256,12,128]{2,1,0:T(8,128)} reshape(bf16[1,1,32,8,1536]{4,3,2,1,0:T(8,128)(2,1)S(1)} %copy-done.1) | data formatting | bytes 2359296 | tf_op jit(solution)/shard_map/convert_element_type | solution.py:128
  37.1 0.1 tile.10
  37.2 0.6 gather_fusion
  37.8 1.7 %constant_dynamic-update-slice_fusion.2 = bf16[2,2,256,12,128]{4,3,2,0,1:T(8,128)(2,1)} fusion(bf16[2,1,256,12,128]{4,3,2,0,1:T(8,128)(2,1)S(1)} %reshape.555), kind=kLoop, calls=%fused_computation.28 | loop fusion | bytes 3670016
  39.5 0.1 compare_or_fusion
  39.6 4.3 %collective-permute-done.5 = s32[4,15]{1,0:T(4,128)S(1)} collective-permute-done((s32[4,15]{1,0:T(4,128)S(1)}, s32[4,15]{1,0:T(4,128)S(1)}, u32[]{:S(2)}, u32[]{:S(2)}) %collective-permute-start.5) | collective-permute-done | bytes 272 | tf_op jit(solution)/shard_map/ppermute | solution.py:193
  44.0 0.3 fusion.10
  44.3 0.0 collective-permute-done.1
  44.3 1.3 %collective-permute-start.2 = (bf16[2,1,32,8,1536]{4,3,2,1,0:T(8,128)(2,1)}, bf16[2,1,32,8,1536]{4,3,2,1,0:T(8,128)(2,1)S(1)}, u32[]{:S(2)}, u32[]{:S(2)}) collective-permute-start(bf16[2,1,32,8,1536]{4,3,2,1,0:T(8,128)(2,1)} %collective-permute-done.1), channel_id=1, source_target_pairs={{8,4},{4,0},{9,5},{5,1},{10,6},{6,2},{11,7},{7,3},{24,20},{20,16},... | collective-permute-start | bytes 4718600 | tf_op jit(solution)/shard_map/ppermute | solution.py:209
  45.6 0.0 collective-permute-done
  45.6 1.8 %collective-permute-start.3 = (bf16[2,1,32,8,1536]{4,3,2,1,0:T(8,128)(2,1)}, bf16[2,1,32,8,1536]{4,3,2,1,0:T(8,128)(2,1)}, u32[]{:S(2)}, u32[]{:S(2)}) collective-permute-start(bf16[2,1,32,8,1536]{4,3,2,1,0:T(8,128)(2,1)} %collective-permute-done), channel_id=1, source_target_pairs={{4,8},{8,12},{5,9},{9,13},{6,10},{10,14},{7,11},{11,15},{20,24},{2... | collective-permute-start | bytes 4718600 | tf_op jit(solution)/shard_map/ppermute | solution.py:210
  47.4 2.5 %broadcast_in_dim.39 = f32[32,8,32,8]{3,2,1,0:T(8,128)} broadcast(f32[8,8]{1,0:T(8,128)S(1)} %and_convert_fusion), dimensions={1,3} | broadcast | bytes 262400 | tf_op jit(solution)/shard_map/broadcast_in_dim | solution.py:169
  49.9 4.7 %reshape.554.m_ref = f32[256,256]{1,0:T(8,128)} reshape(f32[32,8,32,8]{3,2,1,0:T(8,128)} %broadcast_in_dim.39) | data formatting | bytes 524288 | tf_op jit(solution)/shard_map/reshape | solution.py:171
  54.6 9.2 %collective-permute-start.4 = (bf16[1,32,8,1536]{3,2,1,0:T(8,128)(2,1)S(1)}, bf16[1,32,8,1536]{3,2,1,0:T(8,128)(2,1)}, u32[]{:S(2)}, u32[]{:S(2)}) collective-permute-start(bf16[1,32,8,1536]{3,2,1,0:T(8,128)(2,1)S(1)} %bitcast.35), channel_id=1, source_target_pairs={{0,4},{12,8},{1,5},{13,9},{2,6},{14,10},{3,7},{15,11},{16,20},{28,... | collective-permute-start | bytes 2359304 | tf_op jit(solution)/shard_map/ppermute | solution.py:213
  63.8 4.8 %pad_maximum_fusion = bf16[2,1,32,24,1536]{4,3,2,1,0:T(8,128)(2,1)} fusion(bf16[2,1,32,8,1536]{4,3,2,1,0:T(8,128)(2,1)} %collective-permute-done.1, bf16[2,1,32,8,1536]{4,3,2,1,0:T(8,128)(2,1)} %constant_dynamic-update-slice_fusion, bf16[2,1,32,8,1536]{4,3,2,1,0:T(8,128)(2,1)} %collective-permute-done), kind=kLoop, calls=%fused_computation.1 | loop fusion | flops 14155776 | bytes 9437184 | tf_op jit(solution)/shard_map/concatenate | solution.py:175
  68.6 8.8 %shard_map.55 = (f32[1,256,1536]{2,1,0:T(8,128)}, f32[1,2,256,6]{3,2,1,0:T(8,128)}) custom-call(bf16[1,256,1536]{2,1,0:T(8,128)(2,1)} %bitcast.33, bf16[2,1,768,1536]{3,2,1,0:T(8,128)(2,1)} %bitcast.27, bf16[2,1,768,1536]{3,2,1,0:T(8,128)(2,1)} %bitcast.28, f32[256,768]{1,0:T(8,128)} %reshape.550.m_ref), custom_call_target="tpu_custom_call" | custom-call | flops 1207959552 | bytes 7077888 | tf_op jit(solution)/shard_map/pallas_call | solution.py:65
  77.4 0.0 collective-permute-done.8
  77.4 4.0 %copy_dynamic-update-slice_fusion = bf16[2,2,256,12,128]{4,3,2,0,1:T(8,128)(2,1)} fusion(bf16[2,2,256,12,128]{4,3,2,0,1:T(8,128)(2,1)} %constant_dynamic-update-slice_fusion.2, bf16[2,1,256,12,128]{4,2,3,1,0:T(8,128)(2,1)} %collective-permute-done.8), kind=kLoop, calls=%fused_computation.4 | loop fusion | bytes 3670016 | tf_op jit(solution)/shard_map/concatenate | solution.py:302
  81.4 0.0 copy-done
  81.4 2.8 %multiply_reduce_fusion.1 = f32[2,256,12]{2,1,0:T(8,128)S(1)} fusion(bf16[2,2,256,12,128]{4,3,2,0,1:T(8,128)(2,1)} %copy_dynamic-update-slice_fusion, f32[256,12,128]{2,1,0:T(8,128)S(1)} %copy-done), kind=kLoop, calls=%fused_computation.3 | loop fusion | flops 2353152 | bytes 3170304 | tf_op jit(solution)/shard_map/reduce_sum | solution.py:130
  84.2 0.1 fusion.2
  84.4 0.1 fusion.3
  84.5 0.0 collective-permute-done.2
  84.5 0.0 collective-permute-done.3
  84.6 1.3 %broadcast_select_fusion = bf16[2,1,32,8,1536]{4,3,2,1,0:T(8,128)(2,1)} fusion(bf16[2,1,32,8,1536]{4,3,2,1,0:T(8,128)(2,1)S(1)} %collective-permute-done.2, bf16[2,1,32,8,1536]{4,3,2,1,0:T(8,128)(2,1)} %collective-permute-done.3, pred[]{:T(512)S(6)} %le.15), kind=kLoop, calls=%fused_computation.6 | loop fusion | flops 786432 | bytes 4718593 | tf_op jit(solution)/shard_map/jit(_where)/select_n | solution.py:207
  85.9 0.0 collective-permute-done.4
  85.9 4.4 %shard_map.57 = (bf16[1,256,1536]{2,1,0:T(8,128)(2,1)}, f32[1,2,256,6]{3,2,1,0:T(8,128)}) custom-call(bf16[1,256,1536]{2,1,0:T(8,128)(2,1)} %bitcast.7.q_ref, bf16[2,1,256,1536]{3,2,1,0:T(8,128)(2,1)} %bitcast.29, bf16[2,1,256,1536]{3,2,1,0:T(8,128)(2,1)} %bitcast.30, f32[256,256]{1,0:T(8,128)} %reshape.554.m_ref), custom_call_target="tpu_custom_call" | custom-call | flops 402653184 | bytes 3932160 | tf_op jit(solution)/shard_map/pallas_call | solution.py:65
  90.3 1.3 %collective-permute-start.6 = (bf16[1,256,1536]{2,1,0:T(8,128)(2,1)}, bf16[1,256,1536]{2,1,0:T(8,128)(2,1)S(1)}, u32[]{:S(2)}, u32[]{:S(2)}) collective-permute-start(bf16[1,256,1536]{2,1,0:T(8,128)(2,1)} %get-tuple-element.25), channel_id=1, source_target_pairs={{4,0},{8,12},{5,1},{9,13},{6,2},{10,14},{7,3},{11,15},{20,16},{24,... | collective-permute-start | bytes 2359304 | tf_op jit(solution)/shard_map/ppermute | solution.py:235
  91.6 4.2 %multiply_reduce_fusion = f32[256,12,128]{2,1,0:T(8,128)S(1)} fusion(bf16[2,2,256,12,128]{4,3,2,0,1:T(8,128)(2,1)} %copy_dynamic-update-slice_fusion, f32[2,256,12]{2,1,0:T(8,128)S(1)} %get-tuple-element.28), kind=kLoop, calls=%fused_computation.2 | loop fusion | flops 1966080 | bytes 3170304 | tf_op jit(solution)/shard_map/reduce_sum | solution.py:138
  95.8 0.7 reduce-precision_convert_fusion
  96.5 0.9 copy.14
  97.4 1.2 copy.15.refs_6_
  98.6 1.3 %collective-permute-start.7 = (f32[1,2,6,256]{2,3,1,0:T(8,128)S(1)}, f32[1,2,6,256]{2,3,1,0:T(8,128)S(1)}, u32[]{:S(2)}, u32[]{:S(2)}) collective-permute-start(f32[1,2,6,256]{2,3,1,0:T(8,128)S(1)} %bitcast.40), channel_id=1, source_target_pairs={{4,0},{8,12},{5,1},{9,13},{6,2},{10,14},{7,3},{11,15},{20,16},{24,... | collective-permute-start | bytes 36872 | tf_op jit(solution)/shard_map/ppermute | solution.py:235
  99.9 4.5 %shard_map.56 = (f32[1,256,1536]{2,1,0:T(8,128)}, f32[1,2,256,6]{3,2,1,0:T(8,128)}) custom-call(bf16[1,256,1536]{2,1,0:T(8,128)(2,1)} %bitcast.34, bf16[2,1,256,1536]{3,2,1,0:T(8,128)(2,1)} %bitcast.31, bf16[2,1,256,1536]{3,2,1,0:T(8,128)(2,1)} %bitcast.32, f32[256,256]{1,0:T(8,128)} %reshape.552.m_ref), custom_call_target="tpu_custom_call" | custom-call | flops 402653184 | bytes 3932160 | tf_op jit(solution)/shard_map/pallas_call | solution.py:65
  104.4 11.2 %collective-permute-done.7 = f32[1,2,6,256]{2,3,1,0:T(8,128)S(1)} collective-permute-done((f32[1,2,6,256]{2,3,1,0:T(8,128)S(1)}, f32[1,2,6,256]{2,3,1,0:T(8,128)S(1)}, u32[]{:S(2)}, u32[]{:S(2)}) %collective-permute-start.7) | collective-permute-done | bytes 12320 | tf_op jit(solution)/shard_map/ppermute | solution.py:235
  115.6 0.7 select_bitcast_fusion.refs_5_
  116.3 0.0 collective-permute-done.6.refs_4_
  116.3 0.9 copy-done.2
  117.2 4.6 %shard_map.58 = bf16[1,256,1536]{2,1,0:T(8,128)(2,1)} custom-call(f32[1,256,1536]{2,1,0:T(8,128)} %get-tuple-element.19.refs_0_, f32[1,2,256,6]{3,2,1,0:T(8,128)} %get-tuple-element.20.refs_1_, f32[1,256,1536]{2,1,0:T(8,128)} %get-tuple-element.22.refs_2_, f32[1,2,256,6]{3,2,1,0:T(8,128)} %get-tuple-element.23.refs_3_, bf16[1,256,1536]{2,1,0:T(8,128)(2,1)} %copy-done.2, ...), custom_call_target="tpu_custom_call" | custom-call | tf_op jit(solution)/shard_map/pallas_call | solution.py:118
  121.9 1.0 constant_dynamic-slice_fusion
  122.9 0.1 collective-permute-start.9
  123.0 1.7 %collective-permute-done.9 = bf16[1,32,8,768]{3,2,1,0:T(8,128)(2,1)S(1)} collective-permute-done((bf16[1,32,8,768]{3,2,1,0:T(8,128)(2,1)S(1)}, bf16[1,32,8,768]{3,2,1,0:T(8,128)(2,1)S(1)}, u32[]{:S(2)}, u32[]{:S(2)}) %collective-permute-start.9) | collective-permute-done | bytes 393248 | tf_op jit(solution)/shard_map/ppermute | solution.py:25
  124.7 1.9 %fusion.1 = bf16[1,32,8,768]{3,2,1,0:T(8,128)(2,1)} fusion(bf16[1,32,8,768]{3,2,1,0:T(8,128)(2,1)S(1)} %collective-permute-done.9, bf16[1,32,8,1536]{3,2,1,0:T(8,128)(2,1)} %bitcast.38, s32[]{:T(128)S(6)} %select_n.230, pred[]{:T(512)S(6)} %eq.73), kind=kLoop, calls=%fused_computation.10 | loop fusion | flops 1572864 | bytes 1179653 | tf_op jit(solution)/shard_map/convert_element_type | solution.py:325
  (28 shorter events, 0.2 us)
Async XLA Ops:
  0.0 2.1 %copy-start.3 = (bf16[1,1,32,8,1536]{4,3,2,1,0:T(8,128)(2,1)S(1)}, bf16[1,1,32,8,1536]{4,3,2,1,0:T(8,128)(2,1)}, u32[]{:S(2)}) copy-start(bf16[1,1,32,8,1536]{4,3,2,1,0:T(8,128)(2,1)} %param.7) | copy-start | bytes 2359300
  0.0 11.2 %copy-start.4 = (s32[4,15]{1,0:T(4,128)S(1)}, s32[4,15]{1,0:T(4,128)}, u32[]{:S(2)}) copy-start(s32[4,15]{1,0:T(4,128)} %param.8) | copy-start | bytes 724
  3.1 41.2 %collective-permute-start.1 = (bf16[2,1,32,8,1536]{4,3,2,1,0:T(8,128)(2,1)}, bf16[2,1,32,8,1536]{4,3,2,1,0:T(8,128)(2,1)}, u32[]{:S(2)}, u32[]{:S(2)}) collective-permute-start(bf16[2,1,32,8,1536]{4,3,2,1,0:T(8,128)(2,1)} %constant_dynamic-update-slice_fusion), channel_id=1, source_target_pairs={{12,8},{8,4},{4,0},{13,9},{9,5},{5,1},{14,10},{10,6},{6,2},{15,11}... | collective-permute-start | bytes 4718600 | tf_op jit(solution)/shard_map/ppermute | solution.py:192
  4.4 41.2 %collective-permute-start = (bf16[2,1,32,8,1536]{4,3,2,1,0:T(8,128)(2,1)}, bf16[2,1,32,8,1536]{4,3,2,1,0:T(8,128)(2,1)}, u32[]{:S(2)}, u32[]{:S(2)}) collective-permute-start(bf16[2,1,32,8,1536]{4,3,2,1,0:T(8,128)(2,1)} %constant_dynamic-update-slice_fusion), channel_id=1, source_target_pairs={{0,4},{4,8},{8,12},{1,5},{5,9},{9,13},{2,6},{6,10},{10,14},{3,7},{... | collective-permute-start | bytes 4718600 | tf_op jit(solution)/shard_map/ppermute | solution.py:191
  11.2 32.8 %collective-permute-start.5 = (s32[4,15]{1,0:T(4,128)S(1)}, s32[4,15]{1,0:T(4,128)S(1)}, u32[]{:S(2)}, u32[]{:S(2)}) collective-permute-start(s32[4,15]{1,0:T(4,128)S(1)} %copy-done.4), channel_id=1, source_target_pairs={{0,4},{12,8},{1,5},{13,9},{2,6},{14,10},{3,7},{15,11},{16,20},{28,... | collective-permute-start | bytes 728 | tf_op jit(solution)/shard_map/ppermute | solution.py:193
  18.4 59.0 %collective-permute-start.8 = (bf16[2,1,256,12,128]{4,2,3,1,0:T(8,128)(2,1)}, bf16[2,1,256,12,128]{4,2,3,1,0:T(8,128)(2,1)}, u32[]{:S(2)}, u32[]{:S(2)}) collective-permute-start(bf16[2,1,256,12,128]{4,2,3,1,0:T(8,128)(2,1)} %copy.12), channel_id=1, source_target_pairs={{0,2},{2,0},{1,3},{3,1},{4,6},{6,4},{5,7},{7,5},{8,10},{10,8},{9,1... | collective-permute-start | bytes 4718600 | tf_op jit(solution)/shard_map/ppermute | solution.py:21
  30.4 4.8 %copy-start.1 = (bf16[1,1,32,8,1536]{4,3,2,1,0:T(8,128)(2,1)S(1)}, bf16[1,1,32,8,1536]{4,3,2,1,0:T(8,128)(2,1)}, u32[]{:S(2)}) copy-start(bf16[1,1,32,8,1536]{4,3,2,1,0:T(8,128)(2,1)} %param.5) | copy-start | bytes 2359300
  35.2 1.8 %copy-start.5 = (s32[2,8]{1,0:T(2,128)S(1)}, s32[2,8]{1,0:T(2,128)}, u32[]{:S(2)}) copy-start(s32[2,8]{1,0:T(2,128)} %param.9) | copy-start | bytes 196
  44.3 40.3 %collective-permute-start.2 = (bf16[2,1,32,8,1536]{4,3,2,1,0:T(8,128)(2,1)}, bf16[2,1,32,8,1536]{4,3,2,1,0:T(8,128)(2,1)S(1)}, u32[]{:S(2)}, u32[]{:S(2)}) collective-permute-start(bf16[2,1,32,8,1536]{4,3,2,1,0:T(8,128)(2,1)} %collective-permute-done.1), channel_id=1, source_target_pairs={{8,4},{4,0},{9,5},{5,1},{10,6},{6,2},{11,7},{7,3},{24,20},{20,16},... | collective-permute-start | bytes 4718600 | tf_op jit(solution)/shard_map/ppermute | solution.py:209
  45.6 39.0 %collective-permute-start.3 = (bf16[2,1,32,8,1536]{4,3,2,1,0:T(8,128)(2,1)}, bf16[2,1,32,8,1536]{4,3,2,1,0:T(8,128)(2,1)}, u32[]{:S(2)}, u32[]{:S(2)}) collective-permute-start(bf16[2,1,32,8,1536]{4,3,2,1,0:T(8,128)(2,1)} %collective-permute-done), channel_id=1, source_target_pairs={{4,8},{8,12},{5,9},{9,13},{6,10},{10,14},{7,11},{11,15},{20,24},{2... | collective-permute-start | bytes 4718600 | tf_op jit(solution)/shard_map/ppermute | solution.py:210
  54.6 31.3 %collective-permute-start.4 = (bf16[1,32,8,1536]{3,2,1,0:T(8,128)(2,1)S(1)}, bf16[1,32,8,1536]{3,2,1,0:T(8,128)(2,1)}, u32[]{:S(2)}, u32[]{:S(2)}) collective-permute-start(bf16[1,32,8,1536]{3,2,1,0:T(8,128)(2,1)S(1)} %bitcast.35), channel_id=1, source_target_pairs={{0,4},{12,8},{1,5},{13,9},{2,6},{14,10},{3,7},{15,11},{16,20},{28,... | collective-permute-start | bytes 2359304 | tf_op jit(solution)/shard_map/ppermute | solution.py:213
  77.4 4.0 %copy-start = (f32[256,12,128]{2,1,0:T(8,128)S(1)}, f32[256,12,128]{2,1,0:T(8,128)}, u32[]{:S(2)}) copy-start(f32[256,12,128]{2,1,0:T(8,128)} %reshape.557) | copy-start | bytes 4718596
  90.3 26.0 %collective-permute-start.6 = (bf16[1,256,1536]{2,1,0:T(8,128)(2,1)}, bf16[1,256,1536]{2,1,0:T(8,128)(2,1)S(1)}, u32[]{:S(2)}, u32[]{:S(2)}) collective-permute-start(bf16[1,256,1536]{2,1,0:T(8,128)(2,1)} %get-tuple-element.25), channel_id=1, source_target_pairs={{4,0},{8,12},{5,1},{9,13},{6,2},{10,14},{7,3},{11,15},{20,16},{24,... | collective-permute-start | bytes 2359304 | tf_op jit(solution)/shard_map/ppermute | solution.py:235
  96.5 2.1 %copy-start.6 = (f32[1,2,256,6]{3,2,1,0:T(8,128)S(1)}, f32[1,2,256,6]{3,2,1,0:T(8,128)}, u32[]{:S(2)}) copy-start(f32[1,2,256,6]{3,2,1,0:T(8,128)} %get-tuple-element.26) | copy-start | bytes 36868
  98.6 17.0 %collective-permute-start.7 = (f32[1,2,6,256]{2,3,1,0:T(8,128)S(1)}, f32[1,2,6,256]{2,3,1,0:T(8,128)S(1)}, u32[]{:S(2)}, u32[]{:S(2)}) collective-permute-start(f32[1,2,6,256]{2,3,1,0:T(8,128)S(1)} %bitcast.40), channel_id=1, source_target_pairs={{4,0},{8,12},{5,1},{9,13},{6,2},{10,14},{7,3},{11,15},{20,16},{24,... | collective-permute-start | bytes 36872 | tf_op jit(solution)/shard_map/ppermute | solution.py:235
  116.3 0.9 copy-start.2
  122.9 1.8 %collective-permute-start.9 = (bf16[1,32,8,768]{3,2,1,0:T(8,128)(2,1)S(1)}, bf16[1,32,8,768]{3,2,1,0:T(8,128)(2,1)S(1)}, u32[]{:S(2)}, u32[]{:S(2)}) collective-permute-start(bf16[1,32,8,768]{3,2,1,0:T(8,128)(2,1)S(1)} %constant_dynamic-slice_fusion), channel_id=1, source_target_pairs={{0,1},{1,0},{2,3},{3,2},{4,5},{5,4},{6,7},{7,6},{8,9},{9,8},{10,11... | collective-permute-start | bytes 1179656 | tf_op jit(solution)/shard_map/ppermute | solution.py:25

commit v18 on v17

--- a/solution.py
+++ b/solution.py
@@ -26,7 +26,7 @@
 
 
 def group_width(model_width):
-    for width in (768, 512, 384, 256):
+    for width in (1536, 768, 512, 384, 256):
         if model_width % width == 0:
             return width
     return DH

time: 127 us -> 128 us (level)
  other arithmetic: 17.9 us -> 19.3 us
    ppermute x1, waiting for transfers between devices: 0.01 us -> 4.18 us  [spatial_line_of_four(): from_right = lax.ppermute(key_value, 'lon', [(3, 2), (2, 1), (1, 0)])]
    ppermute x2, waiting for transfers between devices: 11.2 us -> 7.65 us  [spatial_line_of_four(): lax.ppermute((guest_out, jnp.swapaxes(guest_lse, 2, 3)), 'lon', [(1, 0),...]
    ppermute x1, waiting for transfers between devices: 4.32 us -> 1.2 us  [spatial_line_of_four(): guest_map = lax.ppermute(window_map, 'lon', [(0, 1), (3, 2)])]
    ppermute x1, waiting for transfers between devices: 0.01 us -> 2.17 us  [spatial_line_of_four(): lax.ppermute(from_right, 'lon', [(2, 1), (1, 0)])]
    ppermute x1, starting transfers between devices: 2.73 us -> 4.55 us  [spatial_line_of_four(): guest_map = lax.ppermute(window_map, 'lon', [(0, 1), (3, 2)])]
    ppermute x1, starting transfers between devices: 9.24 us -> 7.77 us  [spatial_line_of_four(): guest_q = lax.ppermute(held_q, 'lon', [(0, 1), (3, 2)])]
    select_n x1, other arithmetic: 1.31 us -> 2.7 us  [spatial_line_of_four(): jnp.where(index <= 1, lax.ppermute(from_right, 'lon', [(2, 1), (1, 0)]),...]
  transfers between devices with their start and end apart: 10 -> 10, of which waited for: 3 -> 5; matrix products, arithmetic and copies ran while one was open for 41% -> 42% of each run, Pallas kernels for 11% -> 11%
where the time goes in v18:
time: 128 us
  local copies, waits for them, and re-layouts  41.6 us (32%)
  starting transfers between devices  26.1 us (20%)
  Pallas kernels  23.6 us (18%)
  other arithmetic  19.3 us (15%)
  waiting for transfers between devices  16.9 us (13%)
    pallas_call x3, Pallas kernels, spatial_attention(): pl.pallas_call(functools.partial(spatial_kernel, scale=scale), grid=(fram...  18.2 us
    reshape x3, local copies, waits for them, and re-layouts, expand_mask(): return jnp.broadcast_to(active[None, :, None, :].astype(jnp.float32), (la...  14.1 us
    ppermute x1, starting transfers between devices, spatial_line_of_four(): guest_q = lax.ppermute(held_q, 'lon', [(0, 1), (3, 2)])  7.77 us
    ppermute x2, waiting for transfers between devices, spatial_line_of_four(): lax.ppermute((guest_out, jnp.swapaxes(guest_lse, 2, 3)), 'lon', [(1, 0),...  7.65 us
    broadcast_in_dim x3, local copies, waits for them, and re-layouts, expand_mask(): jnp.broadcast_to(active[None, :, None, :].astype(jnp.float32), (lat_rows,...  7.38 us
    ppermute x1, starting transfers between devices, spatial_line_of_four(): from_left = lax.ppermute(key_value, 'lon', [(0, 1), (1, 2), (2, 3)])  6.12 us
    pallas_call x1, Pallas kernels, combine_partials(): pl.pallas_call(combine_kernel, grid=(frames, groups), in_specs=[big, smal...  5.42 us
    unnamed x16, local copies, waits for them, and re-layouts  4.79 us
  transfers between devices with their start and end apart: 10, of which 5 were waited for; matrix products, arithmetic and copies ran while one was open for 42% of the time, Pallas kernels for 11%

profile of v18, /device:TPU:0, one launch (start us, length us, event | category | flops | bytes accessed | tf_op | source)
XLA Modules:
  0.0 127.7 jit_solution(16848264291376047422)
XLA Ops:
  0.0 2.1 %constant_dynamic-update-slice_fusion.1 = bf16[2,1,32,8,1536]{4,3,2,1,0:T(8,128)(2,1)} fusion(bf16[1,1,32,8,1536]{4,3,2,1,0:T(8,128)(2,1)} %param.6), kind=kLoop, calls=%fused_computation.27 | loop fusion | bytes 1572864
  2.1 1.0 constant_dynamic-update-slice_fusion
  3.1 6.1 %collective-permute-start = (bf16[2,1,32,8,1536]{4,3,2,1,0:T(8,128)(2,1)}, bf16[2,1,32,8,1536]{4,3,2,1,0:T(8,128)(2,1)}, u32[]{:S(2)}, u32[]{:S(2)}) collective-permute-start(bf16[2,1,32,8,1536]{4,3,2,1,0:T(8,128)(2,1)} %constant_dynamic-update-slice_fusion), channel_id=1, source_target_pairs={{0,4},{4,8},{8,12},{1,5},{5,9},{9,13},{2,6},{6,10},{10,14},{3,7},{... | collective-permute-start | bytes 4718600 | tf_op jit(solution)/shard_map/ppermute | solution.py:191
  9.2 1.3 %collective-permute-start.1 = (bf16[2,1,32,8,1536]{4,3,2,1,0:T(8,128)(2,1)}, bf16[2,1,32,8,1536]{4,3,2,1,0:T(8,128)(2,1)}, u32[]{:S(2)}, u32[]{:S(2)}) collective-permute-start(bf16[2,1,32,8,1536]{4,3,2,1,0:T(8,128)(2,1)} %constant_dynamic-update-slice_fusion), channel_id=1, source_target_pairs={{12,8},{8,4},{4,0},{13,9},{9,5},{5,1},{14,10},{10,6},{6,2},{15,11}... | collective-permute-start | bytes 4718600 | tf_op jit(solution)/shard_map/ppermute | solution.py:192
  10.5 4.5 %collective-permute-start.5 = (s32[4,15]{1,0:T(4,128)S(1)}, s32[4,15]{1,0:T(4,128)S(1)}, u32[]{:S(2)}, u32[]{:S(2)}) collective-permute-start(s32[4,15]{1,0:T(4,128)S(1)} %copy-done.4), channel_id=1, source_target_pairs={{0,4},{12,8},{1,5},{13,9},{2,6},{14,10},{3,7},{15,11},{16,20},{28,... | collective-permute-start | bytes 728 | tf_op jit(solution)/shard_map/ppermute | solution.py:193
  15.1 2.9 %reshape.555 = bf16[2,1,256,12,128]{4,3,2,0,1:T(8,128)(2,1)S(1)} reshape(bf16[2,1,32,8,1536]{4,3,2,1,0:T(8,128)(2,1)} %constant_dynamic-update-slice_fusion) | data formatting | bytes 3145728 | tf_op jit(solution)/shard_map/reshape | solution.py:298
  18.0 1.6 %copy.12 = bf16[2,1,256,12,128]{4,2,3,1,0:T(8,128)(2,1)} copy(bf16[2,1,256,12,128]{4,3,2,0,1:T(8,128)(2,1)S(1)} %reshape.555) | data formatting | bytes 3145728 | tf_op jit(solution)/shard_map/reshape | solution.py:298
  19.6 1.5 %collective-permute-start.8 = (bf16[2,1,256,12,128]{4,2,3,1,0:T(8,128)(2,1)}, bf16[2,1,256,12,128]{4,2,3,1,0:T(8,128)(2,1)}, u32[]{:S(2)}, u32[]{:S(2)}) collective-permute-start(bf16[2,1,256,12,128]{4,2,3,1,0:T(8,128)(2,1)} %copy.12), channel_id=1, source_target_pairs={{0,2},{2,0},{1,3},{3,1},{4,6},{6,4},{5,7},{7,5},{8,10},{10,8},{9,1... | collective-permute-start | bytes 4718600 | tf_op jit(solution)/shard_map/ppermute | solution.py:21
  21.1 0.1 pad_add_fusion
  21.2 0.1 broadcast_in_dim.35
  21.2 0.1 and.236
  21.4 0.1 copy.11
  21.5 0.1 add_select_fusion.2
  21.6 0.1 fusion.6
  21.7 2.5 %broadcast_in_dim.36 = f32[32,8,32,24]{3,2,1,0:T(8,128)} broadcast(f32[8,24]{1,0:T(8,128)S(1)} %and_convert_fusion.1), dimensions={1,3} | broadcast | bytes 787200 | tf_op jit(solution)/shard_map/broadcast_in_dim | solution.py:169
  24.1 4.6 %reshape.550.m_ref = f32[256,768]{1,0:T(8,128)} reshape(f32[32,8,32,24]{3,2,1,0:T(8,128)} %broadcast_in_dim.36) | data formatting | bytes 1572864 | tf_op jit(solution)/shard_map/reshape | solution.py:171
  28.8 0.1 add_select_fusion
  28.9 0.3 fusion.8
  29.2 2.5 %broadcast_in_dim.37 = f32[32,8,32,8]{3,2,1,0:T(8,128)} broadcast(f32[8,8]{1,0:T(8,128)S(1)} %convert_element_type.69), dimensions={1,3} | broadcast | bytes 262400 | tf_op jit(solution)/shard_map/broadcast_in_dim | solution.py:169
  31.6 4.8 %reshape.552.m_ref = f32[256,256]{1,0:T(8,128)} reshape(f32[32,8,32,8]{3,2,1,0:T(8,128)} %broadcast_in_dim.37) | data formatting | bytes 524288 | tf_op jit(solution)/shard_map/reshape | solution.py:171
  36.4 0.1 tile.10
  36.5 0.0 copy-done.1
  36.5 1.8 %reshape.557 = f32[256,12,128]{2,1,0:T(8,128)} reshape(bf16[1,1,32,8,1536]{4,3,2,1,0:T(8,128)(2,1)S(1)} %copy-done.1) | data formatting | bytes 2359296 | tf_op jit(solution)/shard_map/convert_element_type | solution.py:128
  38.4 0.6 gather_fusion
  39.0 1.7 %constant_dynamic-update-slice_fusion.2 = bf16[2,2,256,12,128]{4,3,2,0,1:T(8,128)(2,1)} fusion(bf16[2,1,256,12,128]{4,3,2,0,1:T(8,128)(2,1)S(1)} %reshape.555), kind=kLoop, calls=%fused_computation.28 | loop fusion | bytes 3670016
  40.7 0.1 compare_or_fusion
  40.8 1.2 collective-permute-done.5
  42.0 0.3 fusion.10
  42.3 0.0 collective-permute-done
  42.3 0.8 collective-permute-start.3
  43.1 4.2 %collective-permute-done.1 = bf16[2,1,32,8,1536]{4,3,2,1,0:T(8,128)(2,1)} collective-permute-done((bf16[2,1,32,8,1536]{4,3,2,1,0:T(8,128)(2,1)}, bf16[2,1,32,8,1536]{4,3,2,1,0:T(8,128)(2,1)}, u32[]{:S(2)}, u32[]{:S(2)}) %collective-permute-start.1) | collective-permute-done | bytes 1572896 | tf_op jit(solution)/shard_map/ppermute | solution.py:192
  47.3 1.3 %collective-permute-start.2 = (bf16[2,1,32,8,1536]{4,3,2,1,0:T(8,128)(2,1)}, bf16[2,1,32,8,1536]{4,3,2,1,0:T(8,128)(2,1)}, u32[]{:S(2)}, u32[]{:S(2)}) collective-permute-start(bf16[2,1,32,8,1536]{4,3,2,1,0:T(8,128)(2,1)} %collective-permute-done.1), channel_id=1, source_target_pairs={{8,4},{4,0},{9,5},{5,1},{10,6},{6,2},{11,7},{7,3},{24,20},{20,16},... | collective-permute-start | bytes 4718600 | tf_op jit(solution)/shard_map/ppermute | solution.py:209
  48.6 2.5 %broadcast_in_dim.39 = f32[32,8,32,8]{3,2,1,0:T(8,128)} broadcast(f32[8,8]{1,0:T(8,128)S(1)} %and_convert_fusion), dimensions={1,3} | broadcast | bytes 262400 | tf_op jit(solution)/shard_map/broadcast_in_dim | solution.py:169
  51.0 4.7 %reshape.554.m_ref = f32[256,256]{1,0:T(8,128)} reshape(f32[32,8,32,8]{3,2,1,0:T(8,128)} %broadcast_in_dim.39) | data formatting | bytes 524288 | tf_op jit(solution)/shard_map/reshape | solution.py:171
  55.7 7.8 %collective-permute-start.4 = (bf16[1,32,8,1536]{3,2,1,0:T(8,128)(2,1)S(1)}, bf16[1,32,8,1536]{3,2,1,0:T(8,128)(2,1)}, u32[]{:S(2)}, u32[]{:S(2)}) collective-permute-start(bf16[1,32,8,1536]{3,2,1,0:T(8,128)(2,1)S(1)} %bitcast.35), channel_id=1, source_target_pairs={{0,4},{12,8},{1,5},{13,9},{2,6},{14,10},{3,7},{15,11},{16,20},{28,... | collective-permute-start | bytes 2359304 | tf_op jit(solution)/shard_map/ppermute | solution.py:213
  63.5 4.8 %pad_maximum_fusion = bf16[2,1,32,24,1536]{4,3,2,1,0:T(8,128)(2,1)} fusion(bf16[2,1,32,8,1536]{4,3,2,1,0:T(8,128)(2,1)} %collective-permute-done.1, bf16[2,1,32,8,1536]{4,3,2,1,0:T(8,128)(2,1)} %constant_dynamic-update-slice_fusion, bf16[2,1,32,8,1536]{4,3,2,1,0:T(8,128)(2,1)} %collective-permute-done), kind=kLoop, calls=%fused_computation.1 | loop fusion | flops 14155776 | bytes 9437184 | tf_op jit(solution)/shard_map/concatenate | solution.py:175
  68.3 9.2 %shard_map.55 = (f32[1,256,1536]{2,1,0:T(8,128)}, f32[1,1,256,12]{3,2,1,0:T(8,128)}) custom-call(bf16[1,256,1536]{2,1,0:T(8,128)(2,1)} %bitcast.33, bf16[2,1,768,1536]{3,2,1,0:T(8,128)(2,1)} %bitcast.27, bf16[2,1,768,1536]{3,2,1,0:T(8,128)(2,1)} %bitcast.28, f32[256,768]{1,0:T(8,128)} %reshape.550.m_ref), custom_call_target="tpu_custom_call" | custom-call | flops 1207959552 | bytes 7077888 | tf_op jit(solution)/shard_map/pallas_call | solution.py:65
  77.4 0.0 collective-permute-done.8
  77.5 4.0 %copy_dynamic-update-slice_fusion = bf16[2,2,256,12,128]{4,3,2,0,1:T(8,128)(2,1)} fusion(bf16[2,2,256,12,128]{4,3,2,0,1:T(8,128)(2,1)} %constant_dynamic-update-slice_fusion.2, bf16[2,1,256,12,128]{4,2,3,1,0:T(8,128)(2,1)} %collective-permute-done.8), kind=kLoop, calls=%fused_computation.4 | loop fusion | bytes 3670016 | tf_op jit(solution)/shard_map/concatenate | solution.py:302
  81.5 2.8 %multiply_reduce_fusion.1 = f32[2,256,12]{2,1,0:T(8,128)S(1)} fusion(bf16[2,2,256,12,128]{4,3,2,0,1:T(8,128)(2,1)} %copy_dynamic-update-slice_fusion, f32[256,12,128]{2,1,0:T(8,128)S(1)} %copy-done), kind=kLoop, calls=%fused_computation.3 | loop fusion | flops 2353152 | bytes 3170304 | tf_op jit(solution)/shard_map/reduce_sum | solution.py:130
  84.3 0.1 fusion.2
  84.5 0.1 fusion.3
  84.6 0.0 collective-permute-done.3
  84.6 2.2 %collective-permute-done.2 = bf16[2,1,32,8,1536]{4,3,2,1,0:T(8,128)(2,1)} collective-permute-done((bf16[2,1,32,8,1536]{4,3,2,1,0:T(8,128)(2,1)}, bf16[2,1,32,8,1536]{4,3,2,1,0:T(8,128)(2,1)}, u32[]{:S(2)}, u32[]{:S(2)}) %collective-permute-start.2) | collective-permute-done | bytes 1572896 | tf_op jit(solution)/shard_map/ppermute | solution.py:209
  86.8 2.7 %broadcast_select_fusion = bf16[2,1,32,8,1536]{4,3,2,1,0:T(8,128)(2,1)} fusion(bf16[2,1,32,8,1536]{4,3,2,1,0:T(8,128)(2,1)} %collective-permute-done.2, bf16[2,1,32,8,1536]{4,3,2,1,0:T(8,128)(2,1)S(1)} %collective-permute-done.3, pred[]{:T(512)S(6)} %le.15), kind=kLoop, calls=%fused_computation.6 | loop fusion | flops 786432 | bytes 4718593 | tf_op jit(solution)/shard_map/jit(_where)/select_n | solution.py:207
  89.5 0.0 collective-permute-done.4
  89.5 4.4 %shard_map.57 = (bf16[1,256,1536]{2,1,0:T(8,128)(2,1)}, f32[1,1,256,12]{3,2,1,0:T(8,128)}) custom-call(bf16[1,256,1536]{2,1,0:T(8,128)(2,1)} %bitcast.7.q_ref, bf16[2,1,256,1536]{3,2,1,0:T(8,128)(2,1)} %bitcast.29, bf16[2,1,256,1536]{3,2,1,0:T(8,128)(2,1)} %bitcast.30, f32[256,256]{1,0:T(8,128)} %reshape.554.m_ref), custom_call_target="tpu_custom_call" | custom-call | flops 402653184 | bytes 3932160 | tf_op jit(solution)/shard_map/pallas_call | solution.py:65
  93.9 1.5 %collective-permute-start.6 = (bf16[1,256,1536]{2,1,0:T(8,128)(2,1)}, bf16[1,256,1536]{2,1,0:T(8,128)(2,1)S(1)}, u32[]{:S(2)}, u32[]{:S(2)}) collective-permute-start(bf16[1,256,1536]{2,1,0:T(8,128)(2,1)} %get-tuple-element.25), channel_id=1, source_target_pairs={{4,0},{8,12},{5,1},{9,13},{6,2},{10,14},{7,3},{11,15},{20,16},{24,... | collective-permute-start | bytes 2359304 | tf_op jit(solution)/shard_map/ppermute | solution.py:235
  95.4 4.2 %multiply_reduce_fusion = f32[256,12,128]{2,1,0:T(8,128)S(1)} fusion(bf16[2,2,256,12,128]{4,3,2,0,1:T(8,128)(2,1)} %copy_dynamic-update-slice_fusion, f32[2,256,12]{2,1,0:T(8,128)S(1)} %get-tuple-element.28), kind=kLoop, calls=%fused_computation.2 | loop fusion | flops 1966080 | bytes 3170304 | tf_op jit(solution)/shard_map/reduce_sum | solution.py:138
  99.6 0.7 reduce-precision_convert_fusion
  100.4 0.0 copy-start.6
  100.4 0.9 copy.14
  101.2 1.2 copy.15.refs_6_
  102.4 1.3 %collective-permute-start.7 = (f32[1,1,12,256]{2,3,1,0:T(8,128)S(1)}, f32[1,1,12,256]{2,3,1,0:T(8,128)S(1)}, u32[]{:S(2)}, u32[]{:S(2)}) collective-permute-start(f32[1,1,12,256]{2,3,1,0:T(8,128)S(1)} %bitcast.40), channel_id=1, source_target_pairs={{4,0},{8,12},{5,1},{9,13},{6,2},{10,14},{7,3},{11,15},{20,16},{24,... | collective-permute-start | bytes 36872 | tf_op jit(solution)/shard_map/ppermute | solution.py:235
  103.7 4.6 %shard_map.56 = (f32[1,256,1536]{2,1,0:T(8,128)}, f32[1,1,256,12]{3,2,1,0:T(8,128)}) custom-call(bf16[1,256,1536]{2,1,0:T(8,128)(2,1)} %bitcast.34, bf16[2,1,256,1536]{3,2,1,0:T(8,128)(2,1)} %bitcast.31, bf16[2,1,256,1536]{3,2,1,0:T(8,128)(2,1)} %bitcast.32, f32[256,256]{1,0:T(8,128)} %reshape.552.m_ref), custom_call_target="tpu_custom_call" | custom-call | flops 402653184 | bytes 3932160 | tf_op jit(solution)/shard_map/pallas_call | solution.py:65
  108.3 7.7 %collective-permute-done.7 = f32[1,1,12,256]{2,3,1,0:T(8,128)S(1)} collective-permute-done((f32[1,1,12,256]{2,3,1,0:T(8,128)S(1)}, f32[1,1,12,256]{2,3,1,0:T(8,128)S(1)}, u32[]{:S(2)}, u32[]{:S(2)}) %collective-permute-start.7) | collective-permute-done | bytes 12320 | tf_op jit(solution)/shard_map/ppermute | solution.py:235
  116.0 0.7 select_bitcast_fusion.refs_5_
  116.7 0.0 collective-permute-done.6.refs_4_
  116.7 0.9 copy-done.3
  117.5 5.4 %shard_map.58 = bf16[1,256,1536]{2,1,0:T(8,128)(2,1)} custom-call(f32[1,256,1536]{2,1,0:T(8,128)} %get-tuple-element.19.refs_0_, f32[1,1,256,12]{3,2,1,0:T(8,128)} %get-tuple-element.20.refs_1_, f32[1,256,1536]{2,1,0:T(8,128)} %get-tuple-element.22.refs_2_, f32[1,1,256,12]{3,2,1,0:T(8,128)} %get-tuple-element.23.refs_3_, bf16[1,256,1536]{2,1,0:T(8,128)(2,1)} %copy-done.3, ...), custom_call_target="tpu_custom_call" | custom-call | tf_op jit(solution)/shard_map/pallas_call | solution.py:118
  123.0 1.0 constant_dynamic-slice_fusion
  124.0 0.1 collective-permute-start.9
  124.1 1.7 %collective-permute-done.9 = bf16[1,32,8,768]{3,2,1,0:T(8,128)(2,1)S(1)} collective-permute-done((bf16[1,32,8,768]{3,2,1,0:T(8,128)(2,1)S(1)}, bf16[1,32,8,768]{3,2,1,0:T(8,128)(2,1)S(1)}, u32[]{:S(2)}, u32[]{:S(2)}) %collective-permute-start.9) | collective-permute-done | bytes 393248 | tf_op jit(solution)/shard_map/ppermute | solution.py:25
  125.8 1.9 %fusion.1 = bf16[1,32,8,768]{3,2,1,0:T(8,128)(2,1)} fusion(bf16[1,32,8,768]{3,2,1,0:T(8,128)(2,1)S(1)} %collective-permute-done.9, bf16[1,32,8,1536]{3,2,1,0:T(8,128)(2,1)} %bitcast.38, s32[]{:T(128)S(6)} %select_n.230, pred[]{:T(512)S(6)} %eq.73), kind=kLoop, calls=%fused_computation.10 | loop fusion | flops 1572864 | bytes 1179653 | tf_op jit(solution)/shard_map/convert_element_type | solution.py:325
  (28 shorter events, 0.2 us)
Async XLA Ops:
  0.0 2.1 %copy-start.2 = (bf16[1,1,32,8,1536]{4,3,2,1,0:T(8,128)(2,1)S(1)}, bf16[1,1,32,8,1536]{4,3,2,1,0:T(8,128)(2,1)}, u32[]{:S(2)}) copy-start(bf16[1,1,32,8,1536]{4,3,2,1,0:T(8,128)(2,1)} %param.7) | copy-start | bytes 2359300
  0.0 10.5 %copy-start.4 = (s32[4,15]{1,0:T(4,128)S(1)}, s32[4,15]{1,0:T(4,128)}, u32[]{:S(2)}) copy-start(s32[4,15]{1,0:T(4,128)} %param.8) | copy-start | bytes 724
  3.1 39.2 %collective-permute-start = (bf16[2,1,32,8,1536]{4,3,2,1,0:T(8,128)(2,1)}, bf16[2,1,32,8,1536]{4,3,2,1,0:T(8,128)(2,1)}, u32[]{:S(2)}, u32[]{:S(2)}) collective-permute-start(bf16[2,1,32,8,1536]{4,3,2,1,0:T(8,128)(2,1)} %constant_dynamic-update-slice_fusion), channel_id=1, source_target_pairs={{0,4},{4,8},{8,12},{1,5},{5,9},{9,13},{2,6},{6,10},{10,14},{3,7},{... | collective-permute-start | bytes 4718600 | tf_op jit(solution)/shard_map/ppermute | solution.py:191
  9.2 38.1 %collective-permute-start.1 = (bf16[2,1,32,8,1536]{4,3,2,1,0:T(8,128)(2,1)}, bf16[2,1,32,8,1536]{4,3,2,1,0:T(8,128)(2,1)}, u32[]{:S(2)}, u32[]{:S(2)}) collective-permute-start(bf16[2,1,32,8,1536]{4,3,2,1,0:T(8,128)(2,1)} %constant_dynamic-update-slice_fusion), channel_id=1, source_target_pairs={{12,8},{8,4},{4,0},{13,9},{9,5},{5,1},{14,10},{10,6},{6,2},{15,11}... | collective-permute-start | bytes 4718600 | tf_op jit(solution)/shard_map/ppermute | solution.py:192
  10.5 31.5 %collective-permute-start.5 = (s32[4,15]{1,0:T(4,128)S(1)}, s32[4,15]{1,0:T(4,128)S(1)}, u32[]{:S(2)}, u32[]{:S(2)}) collective-permute-start(s32[4,15]{1,0:T(4,128)S(1)} %copy-done.4), channel_id=1, source_target_pairs={{0,4},{12,8},{1,5},{13,9},{2,6},{14,10},{3,7},{15,11},{16,20},{28,... | collective-permute-start | bytes 728 | tf_op jit(solution)/shard_map/ppermute | solution.py:193
  19.6 57.9 %collective-permute-start.8 = (bf16[2,1,256,12,128]{4,2,3,1,0:T(8,128)(2,1)}, bf16[2,1,256,12,128]{4,2,3,1,0:T(8,128)(2,1)}, u32[]{:S(2)}, u32[]{:S(2)}) collective-permute-start(bf16[2,1,256,12,128]{4,2,3,1,0:T(8,128)(2,1)} %copy.12), channel_id=1, source_target_pairs={{0,2},{2,0},{1,3},{3,1},{4,6},{6,4},{5,7},{7,5},{8,10},{10,8},{9,1... | collective-permute-start | bytes 4718600 | tf_op jit(solution)/shard_map/ppermute | solution.py:21
  31.6 4.8 %copy-start.5 = (s32[2,8]{1,0:T(2,128)S(1)}, s32[2,8]{1,0:T(2,128)}, u32[]{:S(2)}) copy-start(s32[2,8]{1,0:T(2,128)} %param.9) | copy-start | bytes 196
  31.6 4.9 %copy-start.1 = (bf16[1,1,32,8,1536]{4,3,2,1,0:T(8,128)(2,1)S(1)}, bf16[1,1,32,8,1536]{4,3,2,1,0:T(8,128)(2,1)}, u32[]{:S(2)}) copy-start(bf16[1,1,32,8,1536]{4,3,2,1,0:T(8,128)(2,1)} %param.5) | copy-start | bytes 2359300
  42.3 42.3 %collective-permute-start.3 = (bf16[2,1,32,8,1536]{4,3,2,1,0:T(8,128)(2,1)}, bf16[2,1,32,8,1536]{4,3,2,1,0:T(8,128)(2,1)S(1)}, u32[]{:S(2)}, u32[]{:S(2)}) collective-permute-start(bf16[2,1,32,8,1536]{4,3,2,1,0:T(8,128)(2,1)} %collective-permute-done), channel_id=1, source_target_pairs={{4,8},{8,12},{5,9},{9,13},{6,10},{10,14},{7,11},{11,15},{20,24},{2... | collective-permute-start | bytes 4718600 | tf_op jit(solution)/shard_map/ppermute | solution.py:210
  47.3 39.5 %collective-permute-start.2 = (bf16[2,1,32,8,1536]{4,3,2,1,0:T(8,128)(2,1)}, bf16[2,1,32,8,1536]{4,3,2,1,0:T(8,128)(2,1)}, u32[]{:S(2)}, u32[]{:S(2)}) collective-permute-start(bf16[2,1,32,8,1536]{4,3,2,1,0:T(8,128)(2,1)} %collective-permute-done.1), channel_id=1, source_target_pairs={{8,4},{4,0},{9,5},{5,1},{10,6},{6,2},{11,7},{7,3},{24,20},{20,16},... | collective-permute-start | bytes 4718600 | tf_op jit(solution)/shard_map/ppermute | solution.py:209
  55.7 33.8 %collective-permute-start.4 = (bf16[1,32,8,1536]{3,2,1,0:T(8,128)(2,1)S(1)}, bf16[1,32,8,1536]{3,2,1,0:T(8,128)(2,1)}, u32[]{:S(2)}, u32[]{:S(2)}) collective-permute-start(bf16[1,32,8,1536]{3,2,1,0:T(8,128)(2,1)S(1)} %bitcast.35), channel_id=1, source_target_pairs={{0,4},{12,8},{1,5},{13,9},{2,6},{14,10},{3,7},{15,11},{16,20},{28,... | collective-permute-start | bytes 2359304 | tf_op jit(solution)/shard_map/ppermute | solution.py:213
  77.4 4.0 %copy-start = (f32[256,12,128]{2,1,0:T(8,128)S(1)}, f32[256,12,128]{2,1,0:T(8,128)}, u32[]{:S(2)}) copy-start(f32[256,12,128]{2,1,0:T(8,128)} %reshape.557) | copy-start | bytes 4718596
  93.9 22.8 %collective-permute-start.6 = (bf16[1,256,1536]{2,1,0:T(8,128)(2,1)}, bf16[1,256,1536]{2,1,0:T(8,128)(2,1)S(1)}, u32[]{:S(2)}, u32[]{:S(2)}) collective-permute-start(bf16[1,256,1536]{2,1,0:T(8,128)(2,1)} %get-tuple-element.25), channel_id=1, source_target_pairs={{4,0},{8,12},{5,1},{9,13},{6,2},{10,14},{7,3},{11,15},{20,16},{24,... | collective-permute-start | bytes 2359304 | tf_op jit(solution)/shard_map/ppermute | solution.py:235
  100.4 2.1 %copy-start.6 = (f32[1,1,256,12]{3,2,1,0:T(8,128)S(1)}, f32[1,1,256,12]{3,2,1,0:T(8,128)}, u32[]{:S(2)}) copy-start(f32[1,1,256,12]{3,2,1,0:T(8,128)} %get-tuple-element.26) | copy-start | bytes 36868
  102.4 13.6 %collective-permute-start.7 = (f32[1,1,12,256]{2,3,1,0:T(8,128)S(1)}, f32[1,1,12,256]{2,3,1,0:T(8,128)S(1)}, u32[]{:S(2)}, u32[]{:S(2)}) collective-permute-start(f32[1,1,12,256]{2,3,1,0:T(8,128)S(1)} %bitcast.40), channel_id=1, source_target_pairs={{4,0},{8,12},{5,1},{9,13},{6,2},{10,14},{7,3},{11,15},{20,16},{24,... | collective-permute-start | bytes 36872 | tf_op jit(solution)/shard_map/ppermute | solution.py:235
  116.7 0.9 copy-start.3
  124.0 1.8 %collective-permute-start.9 = (bf16[1,32,8,768]{3,2,1,0:T(8,128)(2,1)S(1)}, bf16[1,32,8,768]{3,2,1,0:T(8,128)(2,1)S(1)}, u32[]{:S(2)}, u32[]{:S(2)}) collective-permute-start(bf16[1,32,8,768]{3,2,1,0:T(8,128)(2,1)S(1)} %constant_dynamic-slice_fusion), channel_id=1, source_target_pairs={{0,1},{1,0},{2,3},{3,2},{4,5},{5,4},{6,7},{7,6},{8,9},{9,8},{10,11... | collective-permute-start | bytes 1179656 | tf_op jit(solution)/shard_map/ppermute | solution.py:25

commit v19 on v17

--- a/solution.py
+++ b/solution.py
@@ -167,7 +167,7 @@
 def expand_mask(active, lat_rows):
     query_cols, key_cols = active.shape
     return jnp.broadcast_to(
-        active[None, :, None, :].astype(jnp.float32), (lat_rows, query_cols, lat_rows, key_cols)
+        active[None, :, None, :].astype(jnp.bfloat16), (lat_rows, query_cols, lat_rows, key_cols)
     ).reshape(lat_rows * query_cols, lat_rows * key_cols)
 
 

time: 127 us -> 129 us (1.016)
  waiting for transfers between devices: 17.2 us -> 21 us
  local copies, waits for them, and re-layouts: 41.6 us -> 37.9 us
  other arithmetic: 17.9 us -> 19.3 us
    broadcast_in_dim x3, local copies, waits for them, and re-layouts: 7.38 us -> 4.13 us  [expand_mask(): jnp.broadcast_to(active[None, :, None, :].astype(jnp.bfloat16), (lat_rows...]
    ppermute x2, waiting for transfers between devices: 11.2 us -> 12.6 us  [spatial_line_of_four(): lax.ppermute((guest_out, jnp.swapaxes(guest_lse, 2, 3)), 'lon', [(1, 0),...]
    ppermute x1, waiting for transfers between devices: 4.32 us -> 5.74 us  [spatial_line_of_four(): guest_map = lax.ppermute(window_map, 'lon', [(0, 1), (3, 2)])]
    select_n x1, other arithmetic: 1.31 us -> 2.71 us  [spatial_line_of_four(): jnp.where(index <= 1, lax.ppermute(from_right, 'lon', [(2, 1), (1, 0)]),...]
    reshape x3, local copies, waits for them, and re-layouts: 14.1 us -> 12.7 us  [expand_mask(): return jnp.broadcast_to(active[None, :, None, :].astype(jnp.bfloat16), (l...]
    unnamed x16 -> x18, local copies, waits for them, and re-layouts: 4.8 us -> 5.7 us
  transfers between devices with their start and end apart: 10 -> 10, of which waited for: 3 -> 4; matrix products, arithmetic and copies ran while one was open for 41% -> 39% of each run, Pallas kernels for 11% -> 10%
where the time goes in v19:
time: 129 us; the launch traced here: 128 us
  local copies, waits for them, and re-layouts  37.9 us (29%)
  starting transfers between devices  27.6 us (21%)
  Pallas kernels  21.9 us (17%)
  waiting for transfers between devices  21 us (16%)
  other arithmetic  19.3 us (15%)
    pallas_call x3, Pallas kernels, spatial_attention(): pl.pallas_call(functools.partial(spatial_kernel, scale=scale), grid=(fram...  17.2 us
    reshape x3, local copies, waits for them, and re-layouts, expand_mask(): return jnp.broadcast_to(active[None, :, None, :].astype(jnp.bfloat16), (l...  12.7 us
    ppermute x2, waiting for transfers between devices, spatial_line_of_four(): lax.ppermute((guest_out, jnp.swapaxes(guest_lse, 2, 3)), 'lon', [(1, 0),...  12.6 us
    ppermute x1, starting transfers between devices, spatial_line_of_four(): guest_q = lax.ppermute(held_q, 'lon', [(0, 1), (3, 2)])  9.62 us
    ppermute x1, starting transfers between devices, spatial_line_of_four(): from_left = lax.ppermute(key_value, 'lon', [(0, 1), (1, 2), (2, 3)])  6.76 us
    ppermute x1, waiting for transfers between devices, spatial_line_of_four(): guest_map = lax.ppermute(window_map, 'lon', [(0, 1), (3, 2)])  5.74 us
    unnamed x18, local copies, waits for them, and re-layouts  5.7 us
    concatenate x1, other arithmetic, flat_keys(): joined = jnp.concatenate(blocks, axis=3)  4.78 us
  transfers between devices with their start and end apart: 10, of which 4 were waited for; matrix products, arithmetic and copies ran while one was open for 39% of the time, Pallas kernels for 10%

profile of v19, /device:TPU:0, one launch (start us, length us, event | category | flops | bytes accessed | tf_op | source)
XLA Modules:
  0.0 128.0 jit_solution(13361293109455978550)
XLA Ops:
  0.0 2.2 %constant_dynamic-update-slice_fusion.1 = bf16[2,1,32,8,1536]{4,3,2,1,0:T(8,128)(2,1)} fusion(bf16[1,1,32,8,1536]{4,3,2,1,0:T(8,128)(2,1)} %param.6), kind=kLoop, calls=%fused_computation.27 | loop fusion | bytes 1572864
  2.2 1.0 constant_dynamic-update-slice_fusion
  3.1 1.3 collective-permute-start.1
  4.4 6.8 %collective-permute-start = (bf16[2,1,32,8,1536]{4,3,2,1,0:T(8,128)(2,1)}, bf16[2,1,32,8,1536]{4,3,2,1,0:T(8,128)(2,1)}, u32[]{:S(2)}, u32[]{:S(2)}) collective-permute-start(bf16[2,1,32,8,1536]{4,3,2,1,0:T(8,128)(2,1)} %constant_dynamic-update-slice_fusion), channel_id=1, source_target_pairs={{0,4},{4,8},{8,12},{1,5},{5,9},{9,13},{2,6},{6,10},{10,14},{3,7},{... | collective-permute-start | bytes 4718600 | tf_op jit(solution)/shard_map/ppermute | solution.py:191
  11.2 2.7 %collective-permute-start.5 = (s32[4,15]{1,0:T(4,128)S(1)}, s32[4,15]{1,0:T(4,128)S(1)}, u32[]{:S(2)}, u32[]{:S(2)}) collective-permute-start(s32[4,15]{1,0:T(4,128)S(1)} %copy-done.5), channel_id=1, source_target_pairs={{0,4},{12,8},{1,5},{13,9},{2,6},{14,10},{3,7},{15,11},{16,20},{28,... | collective-permute-start | bytes 728 | tf_op jit(solution)/shard_map/ppermute | solution.py:193
  13.9 2.9 %reshape.555 = bf16[2,1,256,12,128]{4,3,2,0,1:T(8,128)(2,1)S(1)} reshape(bf16[2,1,32,8,1536]{4,3,2,1,0:T(8,128)(2,1)} %constant_dynamic-update-slice_fusion) | data formatting | bytes 3145728 | tf_op jit(solution)/shard_map/reshape | solution.py:298
  16.8 1.6 %copy.12 = bf16[2,1,256,12,128]{4,2,3,1,0:T(8,128)(2,1)} copy(bf16[2,1,256,12,128]{4,3,2,0,1:T(8,128)(2,1)S(1)} %reshape.555) | data formatting | bytes 3145728 | tf_op jit(solution)/shard_map/reshape | solution.py:298
  18.4 1.5 %collective-permute-start.8 = (bf16[2,1,256,12,128]{4,2,3,1,0:T(8,128)(2,1)}, bf16[2,1,256,12,128]{4,2,3,1,0:T(8,128)(2,1)}, u32[]{:S(2)}, u32[]{:S(2)}) collective-permute-start(bf16[2,1,256,12,128]{4,2,3,1,0:T(8,128)(2,1)} %copy.12), channel_id=1, source_target_pairs={{0,2},{2,0},{1,3},{3,1},{4,6},{6,4},{5,7},{7,5},{8,10},{10,8},{9,1... | collective-permute-start | bytes 4718600 | tf_op jit(solution)/shard_map/ppermute | solution.py:21
  20.0 0.1 copy.11
  20.1 0.1 pad_add_fusion
  20.2 0.1 broadcast_in_dim.35
  20.2 0.1 and.236
  20.3 0.1 add_select_fusion.2
  20.4 0.1 fusion.6
  20.5 1.8 %broadcast_in_dim.36 = bf16[32,8,32,24]{3,2,1,0:T(8,128)(2,1)} broadcast(bf16[8,24]{1,0:T(8,128)(2,1)S(1)} %and_convert_fusion.1), dimensions={1,3} | broadcast | bytes 393600 | tf_op jit(solution)/shard_map/broadcast_in_dim | solution.py:169
  22.3 4.5 %reshape.550.m_ref = bf16[256,768]{1,0:T(8,128)(2,1)} reshape(bf16[32,8,32,24]{3,2,1,0:T(8,128)(2,1)} %broadcast_in_dim.36) | data formatting | bytes 786432 | tf_op jit(solution)/shard_map/reshape | solution.py:171
  26.9 0.1 add_select_fusion
  27.0 0.3 fusion.8
  27.3 0.0 copy-start.1
  27.3 1.8 %broadcast_in_dim.37 = bf16[32,8,32,8]{3,2,1,0:T(8,128)(2,1)} broadcast(bf16[8,8]{1,0:T(8,128)(2,1)S(1)} %convert_element_type.69), dimensions={1,3} | broadcast | bytes 131200 | tf_op jit(solution)/shard_map/broadcast_in_dim | solution.py:169
  29.1 4.7 %reshape.552.m_ref = bf16[256,256]{1,0:T(8,128)(2,1)} reshape(bf16[32,8,32,8]{3,2,1,0:T(8,128)(2,1)} %broadcast_in_dim.37) | data formatting | bytes 262144 | tf_op jit(solution)/shard_map/reshape | solution.py:171
  33.8 1.9 %reshape.557 = f32[256,12,128]{2,1,0:T(8,128)} reshape(bf16[1,1,32,8,1536]{4,3,2,1,0:T(8,128)(2,1)S(1)} %copy-done.1) | data formatting | bytes 2359296 | tf_op jit(solution)/shard_map/convert_element_type | solution.py:128
  35.6 0.1 tile.10
  35.8 0.6 gather_fusion
  36.4 1.7 %constant_dynamic-update-slice_fusion.2 = bf16[2,2,256,12,128]{4,3,2,0,1:T(8,128)(2,1)} fusion(bf16[2,1,256,12,128]{4,3,2,0,1:T(8,128)(2,1)S(1)} %reshape.555), kind=kLoop, calls=%fused_computation.28 | loop fusion | bytes 3670016
  38.2 0.1 compare_or_fusion
  38.2 5.7 %collective-permute-done.5 = s32[4,15]{1,0:T(4,128)S(1)} collective-permute-done((s32[4,15]{1,0:T(4,128)S(1)}, s32[4,15]{1,0:T(4,128)S(1)}, u32[]{:S(2)}, u32[]{:S(2)}) %collective-permute-start.5) | collective-permute-done | bytes 272 | tf_op jit(solution)/shard_map/ppermute | solution.py:193
  44.0 0.3 fusion.10
  44.3 0.0 collective-permute-done.1
  44.3 1.3 %collective-permute-start.2 = (bf16[2,1,32,8,1536]{4,3,2,1,0:T(8,128)(2,1)}, bf16[2,1,32,8,1536]{4,3,2,1,0:T(8,128)(2,1)}, u32[]{:S(2)}, u32[]{:S(2)}) collective-permute-start(bf16[2,1,32,8,1536]{4,3,2,1,0:T(8,128)(2,1)} %collective-permute-done.1), channel_id=1, source_target_pairs={{8,4},{4,0},{9,5},{5,1},{10,6},{6,2},{11,7},{7,3},{24,20},{20,16},... | collective-permute-start | bytes 4718600 | tf_op jit(solution)/shard_map/ppermute | solution.py:209
  45.6 0.0 collective-permute-done
  45.6 1.8 %collective-permute-start.3 = (bf16[2,1,32,8,1536]{4,3,2,1,0:T(8,128)(2,1)}, bf16[2,1,32,8,1536]{4,3,2,1,0:T(8,128)(2,1)}, u32[]{:S(2)}, u32[]{:S(2)}) collective-permute-start(bf16[2,1,32,8,1536]{4,3,2,1,0:T(8,128)(2,1)} %collective-permute-done), channel_id=1, source_target_pairs={{4,8},{8,12},{5,9},{9,13},{6,10},{10,14},{7,11},{11,15},{20,24},{2... | collective-permute-start | bytes 4718600 | tf_op jit(solution)/shard_map/ppermute | solution.py:210
  47.4 0.5 broadcast_in_dim.39
  47.9 3.5 %reshape.554.m_ref = bf16[256,256]{1,0:T(8,128)(2,1)} reshape(bf16[32,8,32,8]{3,2,1,0:T(8,128)(2,1)S(1)} %broadcast_in_dim.39) | data formatting | bytes 262144 | tf_op jit(solution)/shard_map/reshape | solution.py:171
  51.4 9.6 %collective-permute-start.4 = (bf16[1,32,8,1536]{3,2,1,0:T(8,128)(2,1)S(1)}, bf16[1,32,8,1536]{3,2,1,0:T(8,128)(2,1)S(1)}, u32[]{:S(2)}, u32[]{:S(2)}) collective-permute-start(bf16[1,32,8,1536]{3,2,1,0:T(8,128)(2,1)S(1)} %bitcast.35), channel_id=1, source_target_pairs={{0,4},{12,8},{1,5},{13,9},{2,6},{14,10},{3,7},{15,11},{16,20},{28,... | collective-permute-start | bytes 2359304 | tf_op jit(solution)/shard_map/ppermute | solution.py:213
  61.1 4.8 %pad_maximum_fusion = bf16[2,1,32,24,1536]{4,3,2,1,0:T(8,128)(2,1)} fusion(bf16[2,1,32,8,1536]{4,3,2,1,0:T(8,128)(2,1)} %collective-permute-done.1, bf16[2,1,32,8,1536]{4,3,2,1,0:T(8,128)(2,1)} %constant_dynamic-update-slice_fusion, bf16[2,1,32,8,1536]{4,3,2,1,0:T(8,128)(2,1)} %collective-permute-done), kind=kLoop, calls=%fused_computation.1 | loop fusion | flops 14155776 | bytes 9437184 | tf_op jit(solution)/shard_map/concatenate | solution.py:175
  65.9 8.6 %shard_map.55 = (f32[1,256,1536]{2,1,0:T(8,128)}, f32[1,2,256,6]{3,2,1,0:T(8,128)}) custom-call(bf16[1,256,1536]{2,1,0:T(8,128)(2,1)} %bitcast.33, bf16[2,1,768,1536]{3,2,1,0:T(8,128)(2,1)} %bitcast.27, bf16[2,1,768,1536]{3,2,1,0:T(8,128)(2,1)} %bitcast.28, bf16[256,768]{1,0:T(8,128)(2,1)} %reshape.550.m_ref), custom_call_target="tpu_custom_call" | custom-call | flops 1207959552 | bytes 7077888 | tf_op jit(solution)/shard_map/pallas_call | solution.py:65
  74.5 0.0 collective-permute-done.8
  74.5 4.0 %copy_dynamic-update-slice_fusion = bf16[2,2,256,12,128]{4,3,2,0,1:T(8,128)(2,1)} fusion(bf16[2,2,256,12,128]{4,3,2,0,1:T(8,128)(2,1)} %constant_dynamic-update-slice_fusion.2, bf16[2,1,256,12,128]{4,2,3,1,0:T(8,128)(2,1)} %collective-permute-done.8), kind=kLoop, calls=%fused_computation.4 | loop fusion | bytes 3670016 | tf_op jit(solution)/shard_map/concatenate | solution.py:302
  78.5 2.8 %multiply_reduce_fusion.1 = f32[2,256,12]{2,1,0:T(8,128)S(1)} fusion(bf16[2,2,256,12,128]{4,3,2,0,1:T(8,128)(2,1)} %copy_dynamic-update-slice_fusion, f32[256,12,128]{2,1,0:T(8,128)S(1)} %copy-done), kind=kLoop, calls=%fused_computation.3 | loop fusion | flops 2353152 | bytes 3170304 | tf_op jit(solution)/shard_map/reduce_sum | solution.py:130
  81.3 0.1 fusion.2
  81.5 0.1 fusion.3
  81.6 0.9 collective-permute-done.2
  82.5 0.0 collective-permute-done.3
  82.5 2.7 %broadcast_select_fusion = bf16[2,1,32,8,1536]{4,3,2,1,0:T(8,128)(2,1)} fusion(bf16[2,1,32,8,1536]{4,3,2,1,0:T(8,128)(2,1)} %collective-permute-done.2, bf16[2,1,32,8,1536]{4,3,2,1,0:T(8,128)(2,1)} %collective-permute-done.3, pred[]{:T(512)S(6)} %le.15), kind=kLoop, calls=%fused_computation.6 | loop fusion | flops 786432 | bytes 4718593 | tf_op jit(solution)/shard_map/jit(_where)/select_n | solution.py:207
  85.3 0.9 copy-done.4
  86.1 4.3 %shard_map.57 = (bf16[1,256,1536]{2,1,0:T(8,128)(2,1)}, f32[1,2,256,6]{3,2,1,0:T(8,128)}) custom-call(bf16[1,256,1536]{2,1,0:T(8,128)(2,1)} %bitcast.39, bf16[2,1,256,1536]{3,2,1,0:T(8,128)(2,1)} %bitcast.29, bf16[2,1,256,1536]{3,2,1,0:T(8,128)(2,1)} %bitcast.30, bf16[256,256]{1,0:T(8,128)(2,1)} %reshape.554.m_ref), custom_call_target="tpu_custom_call" | custom-call | flops 402653184 | bytes 3932160 | tf_op jit(solution)/shard_map/pallas_call | solution.py:65
  90.4 1.3 collective-permute-start.6
  91.7 4.2 %multiply_reduce_fusion = f32[256,12,128]{2,1,0:T(8,128)S(1)} fusion(bf16[2,2,256,12,128]{4,3,2,0,1:T(8,128)(2,1)} %copy_dynamic-update-slice_fusion, f32[2,256,12]{2,1,0:T(8,128)S(1)} %get-tuple-element.28), kind=kLoop, calls=%fused_computation.2 | loop fusion | flops 1966080 | bytes 3170304 | tf_op jit(solution)/shard_map/reduce_sum | solution.py:138
  95.9 0.7 reduce-precision_convert_fusion
  96.6 0.0 copy-start.7
  96.7 0.9 copy.14
  97.5 1.2 copy.15.refs_6_
  98.7 1.3 %collective-permute-start.7 = (f32[1,2,6,256]{2,3,1,0:T(8,128)S(1)}, f32[1,2,6,256]{2,3,1,0:T(8,128)S(1)}, u32[]{:S(2)}, u32[]{:S(2)}) collective-permute-start(f32[1,2,6,256]{2,3,1,0:T(8,128)S(1)} %bitcast.41), channel_id=1, source_target_pairs={{4,0},{8,12},{5,1},{9,13},{6,2},{10,14},{7,3},{11,15},{20,16},{24,... | collective-permute-start | bytes 36872 | tf_op jit(solution)/shard_map/ppermute | solution.py:235
  100.0 4.4 %shard_map.56 = (f32[1,256,1536]{2,1,0:T(8,128)}, f32[1,2,256,6]{3,2,1,0:T(8,128)}) custom-call(bf16[1,256,1536]{2,1,0:T(8,128)(2,1)} %bitcast.34, bf16[2,1,256,1536]{3,2,1,0:T(8,128)(2,1)} %bitcast.31, bf16[2,1,256,1536]{3,2,1,0:T(8,128)(2,1)} %bitcast.32, bf16[256,256]{1,0:T(8,128)(2,1)} %reshape.552.m_ref), custom_call_target="tpu_custom_call" | custom-call | flops 402653184 | bytes 3932160 | tf_op jit(solution)/shard_map/pallas_call | solution.py:65
  104.4 12.6 %collective-permute-done.7 = f32[1,2,6,256]{2,3,1,0:T(8,128)S(1)} collective-permute-done((f32[1,2,6,256]{2,3,1,0:T(8,128)S(1)}, f32[1,2,6,256]{2,3,1,0:T(8,128)S(1)}, u32[]{:S(2)}, u32[]{:S(2)}) %collective-permute-start.7) | collective-permute-done | bytes 12320 | tf_op jit(solution)/shard_map/ppermute | solution.py:235
  117.0 0.7 select_bitcast_fusion.refs_5_
  117.8 0.0 collective-permute-done.6.refs_4_
  117.8 0.9 copy-done.2
  118.6 4.6 %shard_map.58 = bf16[1,256,1536]{2,1,0:T(8,128)(2,1)} custom-call(f32[1,256,1536]{2,1,0:T(8,128)} %get-tuple-element.19.refs_0_, f32[1,2,256,6]{3,2,1,0:T(8,128)} %get-tuple-element.20.refs_1_, f32[1,256,1536]{2,1,0:T(8,128)} %get-tuple-element.22.refs_2_, f32[1,2,256,6]{3,2,1,0:T(8,128)} %get-tuple-element.23.refs_3_, bf16[1,256,1536]{2,1,0:T(8,128)(2,1)} %copy-done.2, ...), custom_call_target="tpu_custom_call" | custom-call | tf_op jit(solution)/shard_map/pallas_call | solution.py:118
  123.3 1.0 constant_dynamic-slice_fusion
  124.3 0.1 collective-permute-start.9
  124.4 1.7 %collective-permute-done.9 = bf16[1,32,8,768]{3,2,1,0:T(8,128)(2,1)S(1)} collective-permute-done((bf16[1,32,8,768]{3,2,1,0:T(8,128)(2,1)S(1)}, bf16[1,32,8,768]{3,2,1,0:T(8,128)(2,1)S(1)}, u32[]{:S(2)}, u32[]{:S(2)}) %collective-permute-start.9) | collective-permute-done | bytes 393248 | tf_op jit(solution)/shard_map/ppermute | solution.py:25
  126.1 1.9 %fusion.1 = bf16[1,32,8,768]{3,2,1,0:T(8,128)(2,1)} fusion(bf16[1,32,8,768]{3,2,1,0:T(8,128)(2,1)S(1)} %collective-permute-done.9, bf16[1,32,8,1536]{3,2,1,0:T(8,128)(2,1)} %bitcast.38, s32[]{:T(128)S(6)} %select_n.230, pred[]{:T(512)S(6)} %eq.73), kind=kLoop, calls=%fused_computation.10 | loop fusion | flops 1572864 | bytes 1179653 | tf_op jit(solution)/shard_map/convert_element_type | solution.py:325
  (30 shorter events, 0.2 us)
Async XLA Ops:
  0.0 2.2 %copy-start.3 = (bf16[1,1,32,8,1536]{4,3,2,1,0:T(8,128)(2,1)S(1)}, bf16[1,1,32,8,1536]{4,3,2,1,0:T(8,128)(2,1)}, u32[]{:S(2)}) copy-start(bf16[1,1,32,8,1536]{4,3,2,1,0:T(8,128)(2,1)} %param.7) | copy-start | bytes 2359300
  0.0 11.2 %copy-start.5 = (s32[4,15]{1,0:T(4,128)S(1)}, s32[4,15]{1,0:T(4,128)}, u32[]{:S(2)}) copy-start(s32[4,15]{1,0:T(4,128)} %param.8) | copy-start | bytes 724
  3.1 41.2 %collective-permute-start.1 = (bf16[2,1,32,8,1536]{4,3,2,1,0:T(8,128)(2,1)}, bf16[2,1,32,8,1536]{4,3,2,1,0:T(8,128)(2,1)}, u32[]{:S(2)}, u32[]{:S(2)}) collective-permute-start(bf16[2,1,32,8,1536]{4,3,2,1,0:T(8,128)(2,1)} %constant_dynamic-update-slice_fusion), channel_id=1, source_target_pairs={{12,8},{8,4},{4,0},{13,9},{9,5},{5,1},{14,10},{10,6},{6,2},{15,11}... | collective-permute-start | bytes 4718600 | tf_op jit(solution)/shard_map/ppermute | solution.py:192
  4.4 41.2 %collective-permute-start = (bf16[2,1,32,8,1536]{4,3,2,1,0:T(8,128)(2,1)}, bf16[2,1,32,8,1536]{4,3,2,1,0:T(8,128)(2,1)}, u32[]{:S(2)}, u32[]{:S(2)}) collective-permute-start(bf16[2,1,32,8,1536]{4,3,2,1,0:T(8,128)(2,1)} %constant_dynamic-update-slice_fusion), channel_id=1, source_target_pairs={{0,4},{4,8},{8,12},{1,5},{5,9},{9,13},{2,6},{6,10},{10,14},{3,7},{... | collective-permute-start | bytes 4718600 | tf_op jit(solution)/shard_map/ppermute | solution.py:191
  11.2 32.8 %collective-permute-start.5 = (s32[4,15]{1,0:T(4,128)S(1)}, s32[4,15]{1,0:T(4,128)S(1)}, u32[]{:S(2)}, u32[]{:S(2)}) collective-permute-start(s32[4,15]{1,0:T(4,128)S(1)} %copy-done.5), channel_id=1, source_target_pairs={{0,4},{12,8},{1,5},{13,9},{2,6},{14,10},{3,7},{15,11},{16,20},{28,... | collective-permute-start | bytes 728 | tf_op jit(solution)/shard_map/ppermute | solution.py:193
  18.4 56.0 %collective-permute-start.8 = (bf16[2,1,256,12,128]{4,2,3,1,0:T(8,128)(2,1)}, bf16[2,1,256,12,128]{4,2,3,1,0:T(8,128)(2,1)}, u32[]{:S(2)}, u32[]{:S(2)}) collective-permute-start(bf16[2,1,256,12,128]{4,2,3,1,0:T(8,128)(2,1)} %copy.12), channel_id=1, source_target_pairs={{0,2},{2,0},{1,3},{3,1},{4,6},{6,4},{5,7},{7,5},{8,10},{10,8},{9,1... | collective-permute-start | bytes 4718600 | tf_op jit(solution)/shard_map/ppermute | solution.py:21
  27.3 6.5 %copy-start.1 = (bf16[1,1,32,8,1536]{4,3,2,1,0:T(8,128)(2,1)S(1)}, bf16[1,1,32,8,1536]{4,3,2,1,0:T(8,128)(2,1)}, u32[]{:S(2)}) copy-start(bf16[1,1,32,8,1536]{4,3,2,1,0:T(8,128)(2,1)} %param.5) | copy-start | bytes 2359300
  29.1 6.6 %copy-start.6 = (s32[2,8]{1,0:T(2,128)S(1)}, s32[2,8]{1,0:T(2,128)}, u32[]{:S(2)}) copy-start(s32[2,8]{1,0:T(2,128)} %param.9) | copy-start | bytes 196
  44.3 38.2 %collective-permute-start.2 = (bf16[2,1,32,8,1536]{4,3,2,1,0:T(8,128)(2,1)}, bf16[2,1,32,8,1536]{4,3,2,1,0:T(8,128)(2,1)}, u32[]{:S(2)}, u32[]{:S(2)}) collective-permute-start(bf16[2,1,32,8,1536]{4,3,2,1,0:T(8,128)(2,1)} %collective-permute-done.1), channel_id=1, source_target_pairs={{8,4},{4,0},{9,5},{5,1},{10,6},{6,2},{11,7},{7,3},{24,20},{20,16},... | collective-permute-start | bytes 4718600 | tf_op jit(solution)/shard_map/ppermute | solution.py:209
  45.6 36.9 %collective-permute-start.3 = (bf16[2,1,32,8,1536]{4,3,2,1,0:T(8,128)(2,1)}, bf16[2,1,32,8,1536]{4,3,2,1,0:T(8,128)(2,1)}, u32[]{:S(2)}, u32[]{:S(2)}) collective-permute-start(bf16[2,1,32,8,1536]{4,3,2,1,0:T(8,128)(2,1)} %collective-permute-done), channel_id=1, source_target_pairs={{4,8},{8,12},{5,9},{9,13},{6,10},{10,14},{7,11},{11,15},{20,24},{2... | collective-permute-start | bytes 4718600 | tf_op jit(solution)/shard_map/ppermute | solution.py:210
  51.4 33.8 %collective-permute-start.4 = (bf16[1,32,8,1536]{3,2,1,0:T(8,128)(2,1)S(1)}, bf16[1,32,8,1536]{3,2,1,0:T(8,128)(2,1)S(1)}, u32[]{:S(2)}, u32[]{:S(2)}) collective-permute-start(bf16[1,32,8,1536]{3,2,1,0:T(8,128)(2,1)S(1)} %bitcast.35), channel_id=1, source_target_pairs={{0,4},{12,8},{1,5},{13,9},{2,6},{14,10},{3,7},{15,11},{16,20},{28,... | collective-permute-start | bytes 2359304 | tf_op jit(solution)/shard_map/ppermute | solution.py:213
  74.5 4.1 %copy-start = (f32[256,12,128]{2,1,0:T(8,128)S(1)}, f32[256,12,128]{2,1,0:T(8,128)}, u32[]{:S(2)}) copy-start(f32[256,12,128]{2,1,0:T(8,128)} %reshape.557) | copy-start | bytes 4718596
  85.3 0.9 copy-start.4
  90.4 27.4 %collective-permute-start.6 = (bf16[1,256,1536]{2,1,0:T(8,128)(2,1)}, bf16[1,256,1536]{2,1,0:T(8,128)(2,1)S(1)}, u32[]{:S(2)}, u32[]{:S(2)}) collective-permute-start(bf16[1,256,1536]{2,1,0:T(8,128)(2,1)} %get-tuple-element.25), channel_id=1, source_target_pairs={{4,0},{8,12},{5,1},{9,13},{6,2},{10,14},{7,3},{11,15},{20,16},{24,... | collective-permute-start | bytes 2359304 | tf_op jit(solution)/shard_map/ppermute | solution.py:235
  96.6 2.1 %copy-start.7 = (f32[1,2,256,6]{3,2,1,0:T(8,128)S(1)}, f32[1,2,256,6]{3,2,1,0:T(8,128)}, u32[]{:S(2)}) copy-start(f32[1,2,256,6]{3,2,1,0:T(8,128)} %get-tuple-element.26) | copy-start | bytes 36868
  98.7 18.3 %collective-permute-start.7 = (f32[1,2,6,256]{2,3,1,0:T(8,128)S(1)}, f32[1,2,6,256]{2,3,1,0:T(8,128)S(1)}, u32[]{:S(2)}, u32[]{:S(2)}) collective-permute-start(f32[1,2,6,256]{2,3,1,0:T(8,128)S(1)} %bitcast.41), channel_id=1, source_target_pairs={{4,0},{8,12},{5,1},{9,13},{6,2},{10,14},{7,3},{11,15},{20,16},{24,... | collective-permute-start | bytes 36872 | tf_op jit(solution)/shard_map/ppermute | solution.py:235
  117.8 0.9 copy-start.2
  124.3 1.8 %collective-permute-start.9 = (bf16[1,32,8,768]{3,2,1,0:T(8,128)(2,1)S(1)}, bf16[1,32,8,768]{3,2,1,0:T(8,128)(2,1)S(1)}, u32[]{:S(2)}, u32[]{:S(2)}) collective-permute-start(bf16[1,32,8,768]{3,2,1,0:T(8,128)(2,1)S(1)} %constant_dynamic-slice_fusion), channel_id=1, source_target_pairs={{0,1},{1,0},{2,3},{3,2},{4,5},{5,4},{6,7},{7,6},{8,9},{9,8},{10,11... | collective-permute-start | bytes 1179656 | tf_op jit(solution)/shard_map/ppermute | solution.py:25

commit v20 on v9

--- a/solution.py
+++ b/solution.py
@@ -26,7 +26,7 @@
 
 
 def group_width(model_width):
-    for width in (512, 384, 256):
+    for width in (768, 512, 384, 256):
         if model_width % width == 0:
             return width
     return DH

time: 134 us -> 130 us (0.970)
  Pallas kernels: 28.2 us -> 25.1 us
  transfers between devices with their start and end apart: 10 -> 10, of which waited for: 5 -> 5; matrix products, arithmetic and copies ran while one was open for 41% -> 42% of each run, Pallas kernels for 14% -> 13%
where the time goes in v20:
time: 130 us; the launch traced here: 129 us
  local copies, waits for them, and re-layouts  41.7 us (32%)
  starting transfers between devices  25.9 us (20%)
  Pallas kernels  25.1 us (19%)
  other arithmetic  19.3 us (15%)
  waiting for transfers between devices  16.7 us (13%)
    pallas_call x3, Pallas kernels, spatial_attention(): pl.pallas_call(functools.partial(spatial_kernel, scale=scale), grid=(fram...  17.6 us
    reshape x3, local copies, waits for them, and re-layouts, expand_mask(): return jnp.broadcast_to(active[None, :, None, :].astype(jnp.float32), (la...  14.1 us
    ppermute x1, starting transfers between devices, spatial_line_of_four(): guest_q = lax.ppermute(held_q, 'lon', [(0, 1), (3, 2)])  7.77 us
    broadcast_in_dim x3, local copies, waits for them, and re-layouts, expand_mask(): jnp.broadcast_to(active[None, :, None, :].astype(jnp.float32), (lat_rows,...  7.36 us
    ppermute x2, waiting for transfers between devices, spatial_line_of_four(): lax.ppermute((guest_out, jnp.swapaxes(guest_lse, 2, 3)), 'lon', [(1, 0),...  7.02 us
    ppermute x1, starting transfers between devices, spatial_line_of_four(): from_left = lax.ppermute(key_value, 'lon', [(0, 1), (1, 2), (2, 3)])  6.12 us
    unnamed x16, local copies, waits for them, and re-layouts  4.84 us
    concatenate x1, other arithmetic, flat_keys(): joined = jnp.concatenate(blocks, axis=3)  4.78 us
  transfers between devices with their start and end apart: 10, of which 5 were waited for; matrix products, arithmetic and copies ran while one was open for 42% of the time, Pallas kernels for 13%

profile of v20, /device:TPU:0, one launch (start us, length us, event | category | flops | bytes accessed | tf_op | source)
XLA Modules:
  0.0 128.9 jit_solution(12288565188731415541)
XLA Ops:
  0.0 2.2 %constant_dynamic-update-slice_fusion.1 = bf16[2,1,32,8,1536]{4,3,2,1,0:T(8,128)(2,1)} fusion(bf16[1,1,32,8,1536]{4,3,2,1,0:T(8,128)(2,1)} %param.6), kind=kLoop, calls=%fused_computation.27 | loop fusion | bytes 1572864
  2.2 1.0 constant_dynamic-update-slice_fusion
  3.1 6.1 %collective-permute-start = (bf16[2,1,32,8,1536]{4,3,2,1,0:T(8,128)(2,1)}, bf16[2,1,32,8,1536]{4,3,2,1,0:T(8,128)(2,1)}, u32[]{:S(2)}, u32[]{:S(2)}) collective-permute-start(bf16[2,1,32,8,1536]{4,3,2,1,0:T(8,128)(2,1)} %constant_dynamic-update-slice_fusion), channel_id=1, source_target_pairs={{0,4},{4,8},{8,12},{1,5},{5,9},{9,13},{2,6},{6,10},{10,14},{3,7},{... | collective-permute-start | bytes 4718600 | tf_op jit(solution)/shard_map/ppermute | solution.py:227
  9.3 1.3 collective-permute-start.1
  10.6 4.5 %collective-permute-start.5 = (s32[4,15]{1,0:T(4,128)S(1)}, s32[4,15]{1,0:T(4,128)S(1)}, u32[]{:S(2)}, u32[]{:S(2)}) collective-permute-start(s32[4,15]{1,0:T(4,128)S(1)} %copy-done.4), channel_id=1, source_target_pairs={{0,4},{12,8},{1,5},{13,9},{2,6},{14,10},{3,7},{15,11},{16,20},{28,... | collective-permute-start | bytes 728 | tf_op jit(solution)/shard_map/ppermute | solution.py:229
  15.1 2.9 %reshape.555 = bf16[2,1,256,12,128]{4,3,2,0,1:T(8,128)(2,1)S(1)} reshape(bf16[2,1,32,8,1536]{4,3,2,1,0:T(8,128)(2,1)} %constant_dynamic-update-slice_fusion) | data formatting | bytes 3145728 | tf_op jit(solution)/shard_map/reshape | solution.py:334
  18.0 1.6 %copy.12 = bf16[2,1,256,12,128]{4,2,3,1,0:T(8,128)(2,1)} copy(bf16[2,1,256,12,128]{4,3,2,0,1:T(8,128)(2,1)S(1)} %reshape.555) | data formatting | bytes 3145728 | tf_op jit(solution)/shard_map/reshape | solution.py:334
  19.6 1.5 %collective-permute-start.8 = (bf16[2,1,256,12,128]{4,2,3,1,0:T(8,128)(2,1)}, bf16[2,1,256,12,128]{4,2,3,1,0:T(8,128)(2,1)}, u32[]{:S(2)}, u32[]{:S(2)}) collective-permute-start(bf16[2,1,256,12,128]{4,2,3,1,0:T(8,128)(2,1)} %copy.12), channel_id=1, source_target_pairs={{0,2},{2,0},{1,3},{3,1},{4,6},{6,4},{5,7},{7,5},{8,10},{10,8},{9,1... | collective-permute-start | bytes 4718600 | tf_op jit(solution)/shard_map/ppermute | solution.py:21
  21.1 0.1 pad_add_fusion
  21.2 0.1 broadcast_in_dim.35
  21.3 0.1 and.236
  21.4 0.1 copy.11
  21.5 0.1 add_select_fusion.2
  21.6 0.1 fusion.6
  21.7 2.5 %broadcast_in_dim.36 = f32[32,8,32,24]{3,2,1,0:T(8,128)} broadcast(f32[8,24]{1,0:T(8,128)S(1)} %and_convert_fusion.1), dimensions={1,3} | broadcast | bytes 787200 | tf_op jit(solution)/shard_map/broadcast_in_dim | solution.py:205
  24.1 4.7 %reshape.550.m_ref = f32[256,768]{1,0:T(8,128)} reshape(f32[32,8,32,24]{3,2,1,0:T(8,128)} %broadcast_in_dim.36) | data formatting | bytes 1572864 | tf_op jit(solution)/shard_map/reshape | solution.py:207
  28.8 0.1 add_select_fusion
  28.9 0.3 fusion.8
  29.2 2.5 %broadcast_in_dim.37 = f32[32,8,32,8]{3,2,1,0:T(8,128)} broadcast(f32[8,8]{1,0:T(8,128)S(1)} %convert_element_type.69), dimensions={1,3} | broadcast | bytes 262400 | tf_op jit(solution)/shard_map/broadcast_in_dim | solution.py:205
  31.7 4.8 %reshape.552.m_ref = f32[256,256]{1,0:T(8,128)} reshape(f32[32,8,32,8]{3,2,1,0:T(8,128)} %broadcast_in_dim.37) | data formatting | bytes 524288 | tf_op jit(solution)/shard_map/reshape | solution.py:207
  36.4 0.1 tile.10
  36.5 0.0 copy-done.1
  36.5 1.9 %reshape.557 = f32[256,12,128]{2,1,0:T(8,128)} reshape(bf16[1,1,32,8,1536]{4,3,2,1,0:T(8,128)(2,1)S(1)} %copy-done.1) | data formatting | bytes 2359296 | tf_op jit(solution)/shard_map/convert_element_type | solution.py:164
  38.4 0.6 gather_fusion
  39.0 1.7 %constant_dynamic-update-slice_fusion.2 = bf16[2,2,256,12,128]{4,3,2,0,1:T(8,128)(2,1)} fusion(bf16[2,1,256,12,128]{4,3,2,0,1:T(8,128)(2,1)S(1)} %reshape.555), kind=kLoop, calls=%fused_computation.28 | loop fusion | bytes 3670016
  40.8 0.1 compare_or_fusion
  40.9 1.2 collective-permute-done.5
  42.1 0.3 fusion.10
  42.4 0.0 collective-permute-done
  42.4 0.8 collective-permute-start.3
  43.1 4.2 %collective-permute-done.1 = bf16[2,1,32,8,1536]{4,3,2,1,0:T(8,128)(2,1)} collective-permute-done((bf16[2,1,32,8,1536]{4,3,2,1,0:T(8,128)(2,1)}, bf16[2,1,32,8,1536]{4,3,2,1,0:T(8,128)(2,1)}, u32[]{:S(2)}, u32[]{:S(2)}) %collective-permute-start.1) | collective-permute-done | bytes 1572896 | tf_op jit(solution)/shard_map/ppermute | solution.py:228
  47.3 1.3 collective-permute-start.2
  48.6 2.5 %broadcast_in_dim.39 = f32[32,8,32,8]{3,2,1,0:T(8,128)} broadcast(f32[8,8]{1,0:T(8,128)S(1)} %and_convert_fusion), dimensions={1,3} | broadcast | bytes 262400 | tf_op jit(solution)/shard_map/broadcast_in_dim | solution.py:205
  51.1 4.7 %reshape.554.m_ref = f32[256,256]{1,0:T(8,128)} reshape(f32[32,8,32,8]{3,2,1,0:T(8,128)} %broadcast_in_dim.39) | data formatting | bytes 524288 | tf_op jit(solution)/shard_map/reshape | solution.py:207
  55.7 7.8 %collective-permute-start.4 = (bf16[1,32,8,1536]{3,2,1,0:T(8,128)(2,1)S(1)}, bf16[1,32,8,1536]{3,2,1,0:T(8,128)(2,1)}, u32[]{:S(2)}, u32[]{:S(2)}) collective-permute-start(bf16[1,32,8,1536]{3,2,1,0:T(8,128)(2,1)S(1)} %bitcast.35), channel_id=1, source_target_pairs={{0,4},{12,8},{1,5},{13,9},{2,6},{14,10},{3,7},{15,11},{16,20},{28,... | collective-permute-start | bytes 2359304 | tf_op jit(solution)/shard_map/ppermute | solution.py:249
  63.5 4.8 %pad_maximum_fusion = bf16[2,1,32,24,1536]{4,3,2,1,0:T(8,128)(2,1)} fusion(bf16[2,1,32,8,1536]{4,3,2,1,0:T(8,128)(2,1)} %collective-permute-done.1, bf16[2,1,32,8,1536]{4,3,2,1,0:T(8,128)(2,1)} %constant_dynamic-update-slice_fusion, bf16[2,1,32,8,1536]{4,3,2,1,0:T(8,128)(2,1)} %collective-permute-done), kind=kLoop, calls=%fused_computation.1 | loop fusion | flops 14155776 | bytes 9437184 | tf_op jit(solution)/shard_map/concatenate | solution.py:211
  68.3 8.7 %shard_map.55 = (f32[1,256,1536]{2,1,0:T(8,128)}, f32[1,2,256,6]{3,2,1,0:T(8,128)}) custom-call(bf16[1,256,1536]{2,1,0:T(8,128)(2,1)} %bitcast.33, bf16[2,1,768,1536]{3,2,1,0:T(8,128)(2,1)} %bitcast.27, bf16[2,1,768,1536]{3,2,1,0:T(8,128)(2,1)} %bitcast.28, f32[256,768]{1,0:T(8,128)} %reshape.550.m_ref), custom_call_target="tpu_custom_call" | custom-call | flops 1207959552 | bytes 7077888 | tf_op jit(solution)/shard_map/pallas_call | solution.py:65
  77.1 0.0 collective-permute-done.8
  77.1 4.0 %copy_dynamic-update-slice_fusion = bf16[2,2,256,12,128]{4,3,2,0,1:T(8,128)(2,1)} fusion(bf16[2,2,256,12,128]{4,3,2,0,1:T(8,128)(2,1)} %constant_dynamic-update-slice_fusion.2, bf16[2,1,256,12,128]{4,2,3,1,0:T(8,128)(2,1)} %collective-permute-done.8), kind=kLoop, calls=%fused_computation.4 | loop fusion | bytes 3670016 | tf_op jit(solution)/shard_map/concatenate | solution.py:338
  81.1 2.8 %multiply_reduce_fusion.1 = f32[2,256,12]{2,1,0:T(8,128)S(1)} fusion(bf16[2,2,256,12,128]{4,3,2,0,1:T(8,128)(2,1)} %copy_dynamic-update-slice_fusion, f32[256,12,128]{2,1,0:T(8,128)S(1)} %copy-done), kind=kLoop, calls=%fused_computation.3 | loop fusion | flops 2353152 | bytes 3170304 | tf_op jit(solution)/shard_map/reduce_sum | solution.py:166
  83.9 0.1 fusion.2
  84.1 0.1 fusion.3
  84.2 0.0 collective-permute-done.3
  84.2 2.6 %collective-permute-done.2 = bf16[2,1,32,8,1536]{4,3,2,1,0:T(8,128)(2,1)} collective-permute-done((bf16[2,1,32,8,1536]{4,3,2,1,0:T(8,128)(2,1)}, bf16[2,1,32,8,1536]{4,3,2,1,0:T(8,128)(2,1)}, u32[]{:S(2)}, u32[]{:S(2)}) %collective-permute-start.2) | collective-permute-done | bytes 1572896 | tf_op jit(solution)/shard_map/ppermute | solution.py:245
  86.8 2.7 %broadcast_select_fusion = bf16[2,1,32,8,1536]{4,3,2,1,0:T(8,128)(2,1)} fusion(bf16[2,1,32,8,1536]{4,3,2,1,0:T(8,128)(2,1)} %collective-permute-done.2, bf16[2,1,32,8,1536]{4,3,2,1,0:T(8,128)(2,1)S(1)} %collective-permute-done.3, pred[]{:T(512)S(6)} %le.15), kind=kLoop, calls=%fused_computation.6 | loop fusion | flops 786432 | bytes 4718593 | tf_op jit(solution)/shard_map/jit(_where)/select_n | solution.py:243
  89.5 0.0 collective-permute-done.4
  89.5 4.4 %shard_map.58 = (bf16[1,256,1536]{2,1,0:T(8,128)(2,1)}, f32[1,2,256,6]{3,2,1,0:T(8,128)}) custom-call(bf16[1,256,1536]{2,1,0:T(8,128)(2,1)} %bitcast.7.q_ref, bf16[2,1,256,1536]{3,2,1,0:T(8,128)(2,1)} %bitcast.29, bf16[2,1,256,1536]{3,2,1,0:T(8,128)(2,1)} %bitcast.30, f32[256,256]{1,0:T(8,128)} %reshape.554.m_ref), custom_call_target="tpu_custom_call" | custom-call | flops 402653184 | bytes 3932160 | tf_op jit(solution)/shard_map/pallas_call | solution.py:65
  93.9 1.3 collective-permute-start.6
  95.2 4.2 %multiply_reduce_fusion = f32[256,12,128]{2,1,0:T(8,128)S(1)} fusion(bf16[2,2,256,12,128]{4,3,2,0,1:T(8,128)(2,1)} %copy_dynamic-update-slice_fusion, f32[2,256,12]{2,1,0:T(8,128)S(1)} %get-tuple-element.32), kind=kLoop, calls=%fused_computation.2 | loop fusion | flops 1966080 | bytes 3170304 | tf_op jit(solution)/shard_map/reduce_sum | solution.py:174
  99.4 0.7 reduce-precision_convert_fusion
  100.2 0.9 copy.14
  101.0 1.2 copy.15.refs_4_
  102.2 1.3 collective-permute-start.7
  103.5 4.5 %shard_map.56 = (f32[1,256,1536]{2,1,0:T(8,128)}, f32[1,2,256,6]{3,2,1,0:T(8,128)}) custom-call(bf16[1,256,1536]{2,1,0:T(8,128)(2,1)} %bitcast.34, bf16[2,1,256,1536]{3,2,1,0:T(8,128)(2,1)} %bitcast.31, bf16[2,1,256,1536]{3,2,1,0:T(8,128)(2,1)} %bitcast.32, f32[256,256]{1,0:T(8,128)} %reshape.552.m_ref), custom_call_target="tpu_custom_call" | custom-call | flops 402653184 | bytes 3932160 | tf_op jit(solution)/shard_map/pallas_call | solution.py:65
  108.0 3.8 %shard_map.57 = (f32[1,256,1536]{2,1,0:T(8,128)}, f32[1,2,256,6]{3,2,1,0:T(8,128)}) custom-call(f32[1,256,1536]{2,1,0:T(8,128)} %get-tuple-element.21.refs_0_, f32[1,2,256,6]{3,2,1,0:T(8,128)} %get-tuple-element.22.refs_1_, f32[1,256,1536]{2,1,0:T(8,128)} %get-tuple-element.24.refs_2_, f32[1,2,256,6]{3,2,1,0:T(8,128)} %get-tuple-element.25.refs_3_), custom_call_target="tpu_custom_call" | custom-call | tf_op jit(solution)/shard_map/pallas_call | solution.py:133
  111.8 7.0 %collective-permute-done.7 = f32[1,2,6,256]{2,3,1,0:T(8,128)S(1)} collective-permute-done((f32[1,2,6,256]{2,3,1,0:T(8,128)S(1)}, f32[1,2,6,256]{2,3,1,0:T(8,128)S(1)}, u32[]{:S(2)}, u32[]{:S(2)}) %collective-permute-start.7) | collective-permute-done | bytes 12320 | tf_op jit(solution)/shard_map/ppermute | solution.py:271
  118.8 0.7 select_bitcast_fusion.refs_3_
  119.5 0.0 collective-permute-done.6.refs_2_
  119.5 0.9 copy-done.3
  120.4 3.7 %shard_map.59 = bf16[1,256,1536]{2,1,0:T(8,128)(2,1)} custom-call(f32[1,256,1536]{2,1,0:T(8,128)} %get-tuple-element.26.refs_0_, f32[1,2,256,6]{3,2,1,0:T(8,128)} %get-tuple-element.27.refs_1_, bf16[1,256,1536]{2,1,0:T(8,128)(2,1)} %copy-done.3, f32[1,2,256,6]{3,2,1,0:T(8,128)} %select_bitcast_fusion.refs_3_, bf16[1,256,1536]{2,1,0:T(8,128)(2,1)} %copy.15.refs_4_), custom_call_target="tpu_custom_call" | custom-call | tf_op jit(solution)/shard_map/pallas_call | solution.py:154
  124.1 1.0 constant_dynamic-slice_fusion
  125.2 0.1 collective-permute-start.9
  125.3 1.7 %collective-permute-done.9 = bf16[1,32,8,768]{3,2,1,0:T(8,128)(2,1)S(1)} collective-permute-done((bf16[1,32,8,768]{3,2,1,0:T(8,128)(2,1)S(1)}, bf16[1,32,8,768]{3,2,1,0:T(8,128)(2,1)S(1)}, u32[]{:S(2)}, u32[]{:S(2)}) %collective-permute-start.9) | collective-permute-done | bytes 393248 | tf_op jit(solution)/shard_map/ppermute | solution.py:25
  127.0 1.9 %fusion.1 = bf16[1,32,8,768]{3,2,1,0:T(8,128)(2,1)} fusion(bf16[1,32,8,768]{3,2,1,0:T(8,128)(2,1)S(1)} %collective-permute-done.9, bf16[1,32,8,1536]{3,2,1,0:T(8,128)(2,1)} %bitcast.38, s32[]{:T(128)S(6)} %select_n.230, pred[]{:T(512)S(6)} %eq.73), kind=kLoop, calls=%fused_computation.10 | loop fusion | flops 1572864 | bytes 1179653 | tf_op jit(solution)/shard_map/convert_element_type | solution.py:361
  (29 shorter events, 0.2 us)
Async XLA Ops:
  0.0 2.2 %copy-start.2 = (bf16[1,1,32,8,1536]{4,3,2,1,0:T(8,128)(2,1)S(1)}, bf16[1,1,32,8,1536]{4,3,2,1,0:T(8,128)(2,1)}, u32[]{:S(2)}) copy-start(bf16[1,1,32,8,1536]{4,3,2,1,0:T(8,128)(2,1)} %param.7) | copy-start | bytes 2359300
  0.0 10.5 %copy-start.4 = (s32[4,15]{1,0:T(4,128)S(1)}, s32[4,15]{1,0:T(4,128)}, u32[]{:S(2)}) copy-start(s32[4,15]{1,0:T(4,128)} %param.8) | copy-start | bytes 724
  3.1 39.2 %collective-permute-start = (bf16[2,1,32,8,1536]{4,3,2,1,0:T(8,128)(2,1)}, bf16[2,1,32,8,1536]{4,3,2,1,0:T(8,128)(2,1)}, u32[]{:S(2)}, u32[]{:S(2)}) collective-permute-start(bf16[2,1,32,8,1536]{4,3,2,1,0:T(8,128)(2,1)} %constant_dynamic-update-slice_fusion), channel_id=1, source_target_pairs={{0,4},{4,8},{8,12},{1,5},{5,9},{9,13},{2,6},{6,10},{10,14},{3,7},{... | collective-permute-start | bytes 4718600 | tf_op jit(solution)/shard_map/ppermute | solution.py:227
  9.3 38.1 %collective-permute-start.1 = (bf16[2,1,32,8,1536]{4,3,2,1,0:T(8,128)(2,1)}, bf16[2,1,32,8,1536]{4,3,2,1,0:T(8,128)(2,1)}, u32[]{:S(2)}, u32[]{:S(2)}) collective-permute-start(bf16[2,1,32,8,1536]{4,3,2,1,0:T(8,128)(2,1)} %constant_dynamic-update-slice_fusion), channel_id=1, source_target_pairs={{12,8},{8,4},{4,0},{13,9},{9,5},{5,1},{14,10},{10,6},{6,2},{15,11}... | collective-permute-start | bytes 4718600 | tf_op jit(solution)/shard_map/ppermute | solution.py:228
  10.6 31.5 %collective-permute-start.5 = (s32[4,15]{1,0:T(4,128)S(1)}, s32[4,15]{1,0:T(4,128)S(1)}, u32[]{:S(2)}, u32[]{:S(2)}) collective-permute-start(s32[4,15]{1,0:T(4,128)S(1)} %copy-done.4), channel_id=1, source_target_pairs={{0,4},{12,8},{1,5},{13,9},{2,6},{14,10},{3,7},{15,11},{16,20},{28,... | collective-permute-start | bytes 728 | tf_op jit(solution)/shard_map/ppermute | solution.py:229
  19.6 57.5 %collective-permute-start.8 = (bf16[2,1,256,12,128]{4,2,3,1,0:T(8,128)(2,1)}, bf16[2,1,256,12,128]{4,2,3,1,0:T(8,128)(2,1)}, u32[]{:S(2)}, u32[]{:S(2)}) collective-permute-start(bf16[2,1,256,12,128]{4,2,3,1,0:T(8,128)(2,1)} %copy.12), channel_id=1, source_target_pairs={{0,2},{2,0},{1,3},{3,1},{4,6},{6,4},{5,7},{7,5},{8,10},{10,8},{9,1... | collective-permute-start | bytes 4718600 | tf_op jit(solution)/shard_map/ppermute | solution.py:21
  31.7 4.8 %copy-start.5 = (s32[2,8]{1,0:T(2,128)S(1)}, s32[2,8]{1,0:T(2,128)}, u32[]{:S(2)}) copy-start(s32[2,8]{1,0:T(2,128)} %param.9) | copy-start | bytes 196
  31.7 4.9 %copy-start.1 = (bf16[1,1,32,8,1536]{4,3,2,1,0:T(8,128)(2,1)S(1)}, bf16[1,1,32,8,1536]{4,3,2,1,0:T(8,128)(2,1)}, u32[]{:S(2)}) copy-start(bf16[1,1,32,8,1536]{4,3,2,1,0:T(8,128)(2,1)} %param.5) | copy-start | bytes 2359300
  42.4 41.9 %collective-permute-start.3 = (bf16[2,1,32,8,1536]{4,3,2,1,0:T(8,128)(2,1)}, bf16[2,1,32,8,1536]{4,3,2,1,0:T(8,128)(2,1)S(1)}, u32[]{:S(2)}, u32[]{:S(2)}) collective-permute-start(bf16[2,1,32,8,1536]{4,3,2,1,0:T(8,128)(2,1)} %collective-permute-done), channel_id=1, source_target_pairs={{4,8},{8,12},{5,9},{9,13},{6,10},{10,14},{7,11},{11,15},{20,24},{2... | collective-permute-start | bytes 4718600 | tf_op jit(solution)/shard_map/ppermute | solution.py:246
  47.3 39.5 %collective-permute-start.2 = (bf16[2,1,32,8,1536]{4,3,2,1,0:T(8,128)(2,1)}, bf16[2,1,32,8,1536]{4,3,2,1,0:T(8,128)(2,1)}, u32[]{:S(2)}, u32[]{:S(2)}) collective-permute-start(bf16[2,1,32,8,1536]{4,3,2,1,0:T(8,128)(2,1)} %collective-permute-done.1), channel_id=1, source_target_pairs={{8,4},{4,0},{9,5},{5,1},{10,6},{6,2},{11,7},{7,3},{24,20},{20,16},... | collective-permute-start | bytes 4718600 | tf_op jit(solution)/shard_map/ppermute | solution.py:245
  55.7 33.8 %collective-permute-start.4 = (bf16[1,32,8,1536]{3,2,1,0:T(8,128)(2,1)S(1)}, bf16[1,32,8,1536]{3,2,1,0:T(8,128)(2,1)}, u32[]{:S(2)}, u32[]{:S(2)}) collective-permute-start(bf16[1,32,8,1536]{3,2,1,0:T(8,128)(2,1)S(1)} %bitcast.35), channel_id=1, source_target_pairs={{0,4},{12,8},{1,5},{13,9},{2,6},{14,10},{3,7},{15,11},{16,20},{28,... | collective-permute-start | bytes 2359304 | tf_op jit(solution)/shard_map/ppermute | solution.py:249
  77.1 4.1 %copy-start = (f32[256,12,128]{2,1,0:T(8,128)S(1)}, f32[256,12,128]{2,1,0:T(8,128)}, u32[]{:S(2)}) copy-start(f32[256,12,128]{2,1,0:T(8,128)} %reshape.557) | copy-start | bytes 4718596
  93.9 25.6 %collective-permute-start.6 = (bf16[1,256,1536]{2,1,0:T(8,128)(2,1)}, bf16[1,256,1536]{2,1,0:T(8,128)(2,1)S(1)}, u32[]{:S(2)}, u32[]{:S(2)}) collective-permute-start(bf16[1,256,1536]{2,1,0:T(8,128)(2,1)} %get-tuple-element.29), channel_id=1, source_target_pairs={{4,0},{8,12},{5,1},{9,13},{6,2},{10,14},{7,3},{11,15},{20,16},{24,... | collective-permute-start | bytes 2359304 | tf_op jit(solution)/shard_map/ppermute | solution.py:271
  100.1 2.1 %copy-start.6 = (f32[1,2,256,6]{3,2,1,0:T(8,128)S(1)}, f32[1,2,256,6]{3,2,1,0:T(8,128)}, u32[]{:S(2)}) copy-start(f32[1,2,256,6]{3,2,1,0:T(8,128)} %get-tuple-element.30) | copy-start | bytes 36868
  102.2 16.6 %collective-permute-start.7 = (f32[1,2,6,256]{2,3,1,0:T(8,128)S(1)}, f32[1,2,6,256]{2,3,1,0:T(8,128)S(1)}, u32[]{:S(2)}, u32[]{:S(2)}) collective-permute-start(f32[1,2,6,256]{2,3,1,0:T(8,128)S(1)} %bitcast.40), channel_id=1, source_target_pairs={{4,0},{8,12},{5,1},{9,13},{6,2},{10,14},{7,3},{11,15},{20,16},{24,... | collective-permute-start | bytes 36872 | tf_op jit(solution)/shard_map/ppermute | solution.py:271
  119.5 0.9 copy-start.3
  125.2 1.8 %collective-permute-start.9 = (bf16[1,32,8,768]{3,2,1,0:T(8,128)(2,1)S(1)}, bf16[1,32,8,768]{3,2,1,0:T(8,128)(2,1)S(1)}, u32[]{:S(2)}, u32[]{:S(2)}) collective-permute-start(bf16[1,32,8,768]{3,2,1,0:T(8,128)(2,1)S(1)} %constant_dynamic-slice_fusion), channel_id=1, source_target_pairs={{0,1},{1,0},{2,3},{3,2},{4,5},{5,4},{6,7},{7,6},{8,9},{9,8},{10,11... | collective-permute-start | bytes 1179656 | tf_op jit(solution)/shard_map/ppermute | solution.py:25
